TPU v7x, 32 devices: a whole 2x2x4 slice. The times are simulated.
32 devices in a mesh: section: 2 (over x), fsdp: 4 (over z), dp: 4 (over y, core).
Axes of the slice: x: 2, y: 2, z: 4, core: 2. Of those that a mesh axis runs over, the one named last changes fastest.
Arguments:
- activations: bfloat16 [2, 4, 512, 3584], P('section', None, ('fsdp', 'dp')), may hold values from -6 to 6
- out_grad: bfloat16 [2, 4, 512, 14336], P('section', None, ('fsdp', 'dp')), may hold values from -6 to 6
- blocks: bfloat16 [2, 16, 128, 128], P('section', 'fsdp'), may hold values from -0.5 to 0.5
- pattern: int32 [2, 16, 2], P('section', 'fsdp'), may hold values from 0 to 111, as said below
- order: int32 [4], replicated, may hold values from 0 to 3, each once
Outputs:
- received: bfloat16 [2, 4, 512, 3584], P('section', None, ('fsdp', 'dp'))
- weight_grad: float32 [2, 16, 128, 128], P('section', 'fsdp')
Inputs may be any that keep to these rules, and one draw needn't show every extreme that they name: pattern[s, b, 0] < 28 and pattern[s, b, 1] < 112; no two blocks of one section share both indices; within a section the blocks stand in ascending order of (row, column). `order`: a permutation of the microbatches.
All inputs are finite; a program needn't handle non-finite values.
Results may differ from a plain program's by a relative error of at most 0.0049.
Values may be sent and summed in bfloat16 or wider, within the bound.
No kernel may reach another device: no remote copies, remote signals or barrier semaphores. Data moves between devices by JAX's collectives and lax.ppermute only.
A program may use at most 128 MiB of HBM per device.

v0:
```python
import math

import jax
import jax.numpy as jnp
from jax import lax
from jax.sharding import PartitionSpec as P


def passed_along(block, axis, distance):
    devices = range(lax.axis_size(axis))
    route = [(i - distance, i) for i in devices if i - distance in devices]
    return lax.ppermute(block, axis, route)


def silu_slope(pre_act):
    sigmoid_val = jax.nn.sigmoid(pre_act)
    return sigmoid_val * (1.0 + pre_act * (1.0 - sigmoid_val))


def in_groups(step_fn, running, shard_blocks, first_block):
    block_count = shard_blocks.shape[0]
    group_size = math.gcd(block_count, 32)
    if group_size == block_count:
        return step_fn(running, shard_blocks, first_block)

    def one_group(number, carried):
        segment = lax.dynamic_slice_in_dim(shard_blocks, number * group_size, group_size, 0)
        return step_fn(carried, segment, first_block + number * group_size)

    return lax.fori_loop(0, block_count // group_size, one_group, running)


def local(activations, out_grad, blocks, pattern, order):
    block_size = blocks.shape[-1]
    micro_count = activations.shape[1]
    tok_rows = activations.shape[1] * activations.shape[2]
    row_count = activations.shape[3] // block_size
    col_count = out_grad.shape[3] // block_size
    features = activations[0].reshape(tok_rows, row_count, block_size)
    hidden_grad = out_grad[0].reshape(tok_rows, out_grad.shape[3])
    own_blocks = blocks[0]
    all_indices = lax.all_gather(pattern[0], "fsdp", axis=0, tiled=True)

    def forward_step(running, shard_blocks, first_block):
        indices = lax.dynamic_slice_in_dim(all_indices, first_block, shard_blocks.shape[0], 0)
        rows_in = jnp.take(features, indices[:, 0], axis=1)
        product = jnp.einsum(
            "tbk,bkn->tbn", rows_in, shard_blocks, preferred_element_type=jnp.float32
        )
        return running.at[:, indices[:, 1]].add(product)

    pre_zero = jnp.zeros((tok_rows, col_count, block_size), jnp.float32)
    pre_act = in_groups(
        forward_step, pre_zero, lax.all_gather(own_blocks, "fsdp", axis=0, tiled=True), jnp.int32(0)
    )
    act_grad = (hidden_grad.astype(jnp.float32) * silu_slope(pre_act.reshape(tok_rows, -1))).astype(
        jnp.bfloat16
    )
    grad_cols = act_grad.reshape(tok_rows, col_count, block_size)

    def backward_step(running, shard_blocks, first_block):
        indices = lax.dynamic_slice_in_dim(all_indices, first_block, shard_blocks.shape[0], 0)
        cols_in = jnp.take(grad_cols, indices[:, 1], axis=1)
        product = jnp.einsum(
            "tbn,bkn->tbk", cols_in, shard_blocks, preferred_element_type=jnp.float32
        )
        return running.at[:, indices[:, 0]].add(product)

    back_zero = jnp.zeros((tok_rows, row_count, block_size), jnp.float32)
    input_grad = in_groups(
        backward_step,
        back_zero,
        lax.all_gather(own_blocks, "fsdp", axis=0, tiled=True),
        jnp.int32(0),
    )
    input_grad = input_grad.astype(jnp.bfloat16).reshape(
        micro_count, activations.shape[2], activations.shape[3]
    )
    ordered = jnp.take(input_grad, order, axis=0)
    received = passed_along(ordered, "section", -1)
    indices = all_indices
    rows_in = jnp.take(features, indices[:, 0], axis=1)
    cols_in = jnp.take(grad_cols, indices[:, 1], axis=1)
    owned_grads = lax.psum_scatter(
        jnp.einsum("tbk,tbn->bkn", rows_in, cols_in, preferred_element_type=jnp.float32),
        "fsdp",
        scatter_dimension=0,
        tiled=True,
    )
    summed = lax.psum(owned_grads, "dp")
    grad_scale = 1.0 / math.sqrt(tok_rows * lax.axis_size("fsdp") * lax.axis_size("dp"))
    return (received[None], (summed * grad_scale)[None])


def solution(mesh):
    in_specs = (
        P("section", None, ("fsdp", "dp"), None),
        P("section", None, ("fsdp", "dp"), None),
        P("section", "fsdp", None, None),
        P("section", "fsdp", None),
        P(),
    )
    out_specs = (P("section", None, ("fsdp", "dp"), None), P("section", "fsdp", None, None))
    return jax.shard_map(local, mesh=mesh, in_specs=in_specs, out_specs=out_specs, check_vma=False)
```

profile of v0, /device:TPU:0, one launch (start us, length us, event | category | flops | bytes accessed | tf_op | source)
XLA Modules:
  0.0 135.6 jit_solution(16365849403868641486)
XLA Ops:
  7.2 0.0 reduce-scatter.2.cloned.1.call-start
  7.2 0.8 copy.12
  8.0 13.6 %all-gather = s32[1,16,2]{2,0,1:T(1,128)S(1)} all-gather(s32[1,4,2]{2,0,1:T(1,128)S(1)} %copy.12), channel_id=2, replica_groups=mesh['section'=2,'fsdp'=4,'dp'=4] {'fsdp'}, dimensions={1}, use_global_device_ids=true | all-gather | bytes 160 | tf_op jit(solution)/shard_map/all_gather | solution.py:42
  21.6 0.1 copy.13
  21.7 1.6 %reshape_squeeze.4 = bf16[128,28,128]{2,1,0:T(8,128)(2,1)S(1)} reshape(bf16[1,4,32,3584]{3,2,1,0:T(8,128)(2,1)} %param.9) | data formatting | bytes 1835008 | tf_op jit(solution)/shard_map/reshape;squeeze | solution.py:39
  23.3 0.4 copy.14
  23.7 16.1 %all-gather.1 = bf16[1,16,128,128]{3,2,0,1:T(8,128)(2,1)S(1)} all-gather(bf16[1,4,128,128]{3,2,0,1:T(8,128)(2,1)} %bitcast.40), channel_id=3, replica_groups=mesh['section'=2,'fsdp'=4,'dp'=4] {'fsdp'}, dimensions={1}, use_global_device_ids=true | all-gather | bytes 655360 | tf_op jit(solution)/shard_map/all_gather | solution.py:73
  39.8 5.9 %copy.20 = f32[16,8,112,128]{3,2,1,0:T(8,128)} copy(bf16[16,8,112,128]{3,1,2,0:T(8,128)(2,1)} %bitcast.38) | data formatting | bytes 11010048
  45.7 0.6 gather_fusion.1
  46.3 0.4 fusion.6
  46.7 3.9 %broadcast_in_dim.46 = f32[128,112,128]{2,0,1:T(8,128)} broadcast(f32[]{:T(128)} %constant.23.clone.1), dimensions={} | broadcast | bytes 7340036 | tf_op jit(solution)/shard_map/broadcast_in_dim | solution.py:52
  50.6 3.4 %scatter_fusion = f32[128,112,128]{2,0,1:T(8,128)} fusion(f32[128,112,128]{2,0,1:T(8,128)} %broadcast_in_dim.46, s32[16]{0:T(128)S(1)} %get-tuple-element.10, f32[16,128,128]{2,1,0:T(8,128)S(1)} %fusion.6), kind=kCustom, calls=%fused_computation.3 | custom fusion | flops 262144 | bytes 3145792 | tf_op jit(solution)/shard_map/scatter-add | solution.py:50
  54.0 8.4 %fusion = bf16[128,112,128]{2,0,1:T(8,128)(2,1)} fusion(f32[128,112,128]{2,1,0:T(8,128)} %bitcast.37, f32[128,112,128]{2,0,1:T(8,128)} %scatter_fusion), kind=kLoop, calls=%fused_computation.6 | loop fusion | flops 16515072 | bytes 18350080 | tf_op jit(solution)/shard_map/convert_element_type | solution.py:56
  62.5 2.7 %gather_fusion.2 = bf16[16,128,128]{2,1,0:T(8,128)(2,1)S(1)} fusion(bf16[128,112,128]{2,0,1:T(8,128)(2,1)} %fusion, s32[1024]{0:T(1024)S(1)} %get-tuple-element.12), kind=kCustom, calls=%fused_computation.1.clone | custom fusion | bytes 1048640 | tf_op jit(solution)/shard_map/jit(_take)/gather | solution.py:63
  65.2 1.4 %fusion.1 = f32[16,128,128]{2,1,0:T(8,128)} fusion(bf16[16,128,128]{2,1,0:T(8,128)(2,1)S(1)} %gather_fusion.1, pred[16]{0:T(512)(128)(4,1)S(1)} %get-tuple-element.8, bf16[16,128,128]{2,1,0:T(8,128)(2,1)S(1)} %gather_fusion.2, pred[16]{0:T(512)(128)(4,1)S(1)} %get-tuple-element.4), kind=kOutput, calls=%fused_computation.8 | convolution fusion | flops 67633152 | bytes 2097184 | tf_op jit(solution)/shard_map/tbk,tbn->bkn/dot_general | solution.py:85
  66.6 0.0 reduce-scatter.2.cloned.1.call-update
  66.6 0.0 all-reduce.2.cloned.1.call-start
  66.7 0.5 fusion.3
  67.2 0.2 broadcast_in_dim.45
  67.4 1.6 %scatter_fusion.1 = f32[128,28,128]{2,0,1:T(8,128)S(1)} fusion(f32[128,28,128]{2,0,1:T(8,128)S(1)} %broadcast_in_dim.45, s32[16]{0:T(128)S(1)} %get-tuple-element.11, f32[16,128,128]{2,1,0:T(8,128)S(1)} %fusion.3), kind=kCustom, calls=%fused_computation.4 | custom fusion | flops 262144 | bytes 3145792 | tf_op jit(solution)/shard_map/scatter-add | solution.py:67
  69.0 0.1 convert_element_type.17
  69.2 0.6 copy.17
  69.8 0.5 reshape.27
  70.3 0.6 gather_fusion
  70.9 0.2 broadcast_select_fusion
  71.1 1.3 collective-permute-start
  72.4 20.7 %reduce-scatter.2.cloned.1.call-done = f32[4,128,128]{2,1,0:T(8,128)} async-done(((f32[16,128,128]{2,1,0:T(8,128)}), f32[4,128,128]{2,1,0:T(8,128)}) %reduce-scatter.2.cloned.1.call-update) | async-done | bytes 262160 | tf_op jit(solution)/shard_map/reduce_scatter | solution.py:84
  93.0 0.0 all-reduce.2.cloned.1.call-update
  93.1 0.0 collective-permute-done
  93.1 33.1 %all-reduce.2.cloned.1.call-done = f32[4,128,128]{2,1,0:T(8,128)} async-done(((f32[4,128,128]{2,1,0:T(8,128)}), f32[4,128,128]{2,1,0:T(8,128)}) %all-reduce.2.cloned.1.call-update) | async-done | bytes 262160 | tf_op jit(solution)/shard_map/psum | solution.py:90
  126.2 1.7 %multiply_bitcast_fusion = f32[1,4,128,128]{3,2,1,0:T(8,128)} fusion(f32[4,128,128]{2,1,0:T(8,128)} %all-reduce.2.cloned.1.call-done), kind=kLoop, calls=%fused_computation.19 | loop fusion | flops 65536 | bytes 524288 | tf_op jit(solution)/shard_map/broadcast_in_dim | solution.py:92
  127.9 0.9 copy.28
  (8 shorter events, 0.0 us)
Async XLA Ops:
  7.2 85.9 %reduce-scatter.2.cloned.1.call-start = ((), (), s32[]{:S(2)}) async-start(), calls=%async_computation.1 | async-start | bytes 1310720 | tf_op jit(solution)/shard_map/reduce_scatter | solution.py:84
  54.0 13.1 %copy-start = (s32[4]{0:T(128)S(1)}, s32[4]{0:T(128)}, u32[]{:S(2)}) copy-start(s32[4]{0:T(128)} %param.13) | copy-start | bytes 52
  66.6 59.6 %all-reduce.2.cloned.1.call-start = ((), (), s32[]{:S(2)}) async-start(), calls=%async_computation.2 | async-start | bytes 524288 | tf_op jit(solution)/shard_map/psum | solution.py:90
  71.1 22.0 %collective-permute-start = (bf16[4,32,3584]{2,1,0:T(8,128)(2,1)S(1)}, bf16[4,32,3584]{2,1,0:T(8,128)(2,1)S(1)}, u32[]{:S(2)}, u32[]{:S(2)}) collective-permute-start(bf16[4,32,3584]{2,1,0:T(8,128)(2,1)S(1)} %broadcast_select_fusion), channel_id=1, source_target_pairs={{16,0},{17,1},{18,2},{19,3},{20,4},{21,5},{22,6},{23,7},{24,8},{25... | collective-permute-start | bytes 2752520 | tf_op jit(solution)/shard_map/ppermute | solution.py:12
Sparse Core Ops, SparseCore 0:
  66.7 26.2 reduce-scatter.1
  95.4 30.7 all-reduce.1
where the time goes:
time: 136 us
  waiting for transfers between devices  53.8 us (40%)
  blocking collectives  29.7 us (22%)
  local copies, waits for them, and re-layouts  18.8 us (14%)
  other arithmetic  15.5 us (11%)
  between operations  14.2 us (10%)
  matrix products  2.29 us (2%)
  starting transfers between devices  1.37 us (1%)
    psum x1, waiting for transfers between devices, local(): summed = lax.psum(owned_grads, 'dp')  33.1 us
    reduce_scatter x1, waiting for transfers between devices, local(): lax.psum_scatter(jnp.einsum('tbk,tbn->bkn', rows_in, cols_in, preferred_e...  20.7 us
    all_gather x1, blocking collectives, local(): lax.all_gather(own_blocks, 'fsdp', axis=0, tiled=True)  16.1 us
    all_gather x1, blocking collectives, local(): all_indices = lax.all_gather(pattern[0], 'fsdp', axis=0, tiled=True)  13.6 us
    convert_element_type x1, other arithmetic, local(): (hidden_grad.astype(jnp.float32) * silu_slope(pre_act.reshape(tok_rows, -...  8.43 us
    unnamed x5, local copies, waits for them, and re-layouts  7.54 us
    broadcast_in_dim x1, local copies, waits for them, and re-layouts, local(): pre_zero = jnp.zeros((tok_rows, col_count, block_size), jnp.float32)  3.95 us
    scatter-add x1, other arithmetic, forward_step(): return running.at[:, indices[:, 1]].add(product)  3.42 us
  transfers between devices with their start and end apart: 3, of which 2 were waited for; matrix products, arithmetic and copies ran while one was open for 3% of the time, Pallas kernels for 0%

commit v1 on v0

v1 whole, which is shorter than its diff:
```python
import math

import jax
import jax.numpy as jnp
from jax import lax
from jax.sharding import PartitionSpec as P


def passed_along(block, axis, distance):
    devices = range(lax.axis_size(axis))
    route = [(i - distance, i) for i in devices if i - distance in devices]
    return lax.ppermute(block, axis, route)


def shifted(x, axis, k):
    n = lax.axis_size(axis)
    return lax.ppermute(x, axis, [(i, (i + k) % n) for i in range(n)])


def swapped(x, axis, bit):
    n = lax.axis_size(axis)
    return lax.ppermute(x, axis, [(i, i ^ (1 << bit)) for i in range(n)])


def silu_slope(pre_act):
    sigmoid_val = jax.nn.sigmoid(pre_act)
    return sigmoid_val * (1.0 + pre_act * (1.0 - sigmoid_val))


def gather_over(x, axis):
    n = lax.axis_size(axis)
    return jnp.stack([x] + [shifted(x, axis, k) for k in range(1, n)])


def butterfly_gather(x, axis, bits):
    me = lax.axis_index(axis)
    held = x
    for bit in bits:
        other = swapped(held, axis, bit)
        mine_low = ((me >> bit) & 1) == 0
        held = jnp.where(mine_low, jnp.stack([held, other]), jnp.stack([other, held]))
    order = sorted(range(len(bits)), key=lambda a: -bits[len(bits) - 1 - a])
    perm = [order[i] for i in range(len(bits))] + list(range(len(bits), held.ndim))
    return jnp.transpose(held, perm)


def local(activations, out_grad, blocks, pattern, order):
    block_size = blocks.shape[-1]
    micro_count = activations.shape[1]
    tok_rows = activations.shape[1] * activations.shape[2]
    row_count = activations.shape[3] // block_size
    col_count = out_grad.shape[3] // block_size
    n_fsdp = lax.axis_size("fsdp")
    n_dp = lax.axis_size("dp")
    dp_bits = int(round(math.log2(n_dp)))
    assert 1 << dp_bits == n_dp and block_size % n_dp == 0
    chunk = block_size // n_dp
    me_dp = lax.axis_index("dp")

    features = activations[0].reshape(tok_rows, row_count, block_size)
    hidden_grad = out_grad[0].reshape(tok_rows, col_count, block_size)
    own_blocks = blocks[0]
    blocks_dev = own_blocks.shape[0]

    all_indices = gather_over(pattern[0], "fsdp").reshape(-1, 2)

    own_chunk = lax.dynamic_slice_in_dim(own_blocks, me_dp * chunk, chunk, 1)
    fetched = gather_over(own_chunk, "fsdp")
    gathered = butterfly_gather(fetched, "dp", list(reversed(range(dp_bits))))
    gathered = gathered.reshape((n_dp, n_fsdp, blocks_dev, chunk, block_size))
    weights = jnp.transpose(gathered, (1, 2, 0, 3, 4)).reshape(
        n_fsdp * blocks_dev, block_size, block_size
    )

    row_ids = all_indices[:, 0]
    col_ids = all_indices[:, 1]
    rows_in = jnp.take(features, row_ids, axis=1)
    product = jnp.einsum(
        "tbk,bkn->tbn", rows_in, weights, preferred_element_type=jnp.float32
    )
    same_col = (col_ids[:, None] == col_ids[None, :]).astype(jnp.float32)
    pre_act = jnp.einsum(
        "bc,tcn->tbn", same_col, product, precision=lax.Precision.HIGHEST
    )
    hidden_in = jnp.take(hidden_grad, col_ids, axis=1)
    act_cols = (hidden_in.astype(jnp.float32) * silu_slope(pre_act)).astype(jnp.bfloat16)

    backward = jnp.einsum(
        "tbn,bkn->tbk", act_cols, weights, preferred_element_type=jnp.float32
    )
    row_hit = (jnp.arange(row_count, dtype=jnp.int32)[:, None] == row_ids[None, :]).astype(
        jnp.float32
    )
    input_grad = jnp.einsum(
        "rb,tbk->trk", row_hit, backward, precision=lax.Precision.HIGHEST
    )
    input_grad = input_grad.astype(jnp.bfloat16).reshape(
        micro_count, activations.shape[2], activations.shape[3]
    )
    ordered = jnp.take(input_grad, order, axis=0)
    received = passed_along(ordered, "section", -1)

    partial = jnp.einsum(
        "tbk,tbn->bkn", rows_in, act_cols, preferred_element_type=jnp.float32
    )
    held = partial.reshape((n_fsdp, blocks_dev) + (2,) * dp_bits + (chunk, block_size))
    for bit in range(dp_bits):
        axis_at = 2 + (dp_bits - 1 - bit)
        mine = (me_dp >> bit) & 1
        keep = lax.dynamic_index_in_dim(held, mine, axis_at, keepdims=False)
        send = lax.dynamic_index_in_dim(held, 1 - mine, axis_at, keepdims=False)
        held = keep + swapped(send, "dp", bit)
    owned = held[0]
    for k in range(1, n_fsdp):
        owned = owned + shifted(held[k], "fsdp", -k)
    full = butterfly_gather(owned, "dp", list(reversed(range(dp_bits))))
    full = full.reshape((n_dp, blocks_dev, chunk, block_size))
    full = jnp.transpose(full, (1, 0, 2, 3)).reshape(blocks_dev, block_size, block_size)
    grad_scale = jnp.sqrt(jnp.float32(tok_rows * n_fsdp * n_dp))
    return (received[None], (full / grad_scale)[None])


def solution(mesh):
    in_specs = (
        P("section", None, ("fsdp", "dp"), None),
        P("section", None, ("fsdp", "dp"), None),
        P("section", "fsdp", None, None),
        P("section", "fsdp", None),
        P(),
    )
    out_specs = (P("section", None, ("fsdp", "dp"), None), P("section", "fsdp", None, None))
    return jax.shard_map(local, mesh=mesh, in_specs=in_specs, out_specs=out_specs, check_vma=False)
```

time: 136 us -> 74.2 us (0.55)
  waiting for transfers between devices: 53.8 us -> 23.8 us
  blocking collectives: 29.7 us -> 0 us
  starting transfers between devices: 1.37 us -> 21.5 us
  between operations: 14.2 us -> 0.92 us
  other arithmetic: 15.5 us -> 3.94 us
  matrix products: 2.29 us -> 4.42 us
    psum x1 -> x0, waiting for transfers between devices: 33.1 us -> none  [local(): summed = lax.psum(owned_grads, 'dp')]
    all_gather x2 -> x0, blocking collectives: 29.7 us -> none  [the longest x1 16.1 us: local(): lax.all_gather(own_blocks, 'fsdp', axis=0, tiled=True)]
    reduce_scatter x1 -> x0, waiting for transfers between devices: 20.7 us -> none  [local(): lax.psum_scatter(jnp.einsum('tbk,tbn->bkn', rows_in, cols_in, preferred_e...]
    ppermute x0 -> x15, starting transfers between devices: none -> 20.2 us  [the longest x9 14.8 us: shifted(): return lax.ppermute(x, axis, [(i, (i + k) % n) for i in range(n)])]
    ppermute x0 -> x15, waiting for transfers between devices: none -> 17.7 us  [the longest x6 9.98 us: swapped(): return lax.ppermute(x, axis, [(i, i ^ 1 << bit) for i in range(n)])]
    convert_element_type x2 -> x0, other arithmetic: 8.58 us -> none  [the longest x1 8.43 us: local(): (hidden_grad.astype(jnp.float32) * silu_slope(pre_act.reshape(tok_rows, -...]
    ppermute x1, waiting for transfers between devices: 0.01 us -> 6.06 us  [passed_along(): return lax.ppermute(block, axis, route)]
    scatter-add x2 -> x0, other arithmetic: 5.03 us -> none  [the longest x1 3.42 us: forward_step(): return running.at[:, indices[:, 1]].add(product)]
  transfers between devices with their start and end apart: 3 -> 16, of which waited for: 2 -> 8; matrix products, arithmetic and copies ran while one was open for 3% -> 26% of each run, Pallas kernels for 0% -> 0%
where the time goes in v1:
time: 74.2 us; the launch traced here: 73.8 us
  waiting for transfers between devices  23.8 us (32%)
  starting transfers between devices  21.5 us (29%)
  local copies, waits for them, and re-layouts  19.2 us (26%)
  matrix products  4.42 us (6%)
  other arithmetic  3.94 us (5%)
  between operations  0.92 us (1%)
    ppermute x9, starting transfers between devices, shifted(): return lax.ppermute(x, axis, [(i, (i + k) % n) for i in range(n)])  14.8 us
    ppermute x6, waiting for transfers between devices, swapped(): return lax.ppermute(x, axis, [(i, i ^ 1 << bit) for i in range(n)])  9.98 us
    ppermute x9, waiting for transfers between devices, shifted(): return lax.ppermute(x, axis, [(i, (i + k) % n) for i in range(n)])  7.77 us
    ppermute x1, waiting for transfers between devices, passed_along(): return lax.ppermute(block, axis, route)  6.06 us
    ppermute x6, starting transfers between devices, swapped(): return lax.ppermute(x, axis, [(i, i ^ 1 << bit) for i in range(n)])  5.38 us
    unnamed x6, local copies, waits for them, and re-layouts  4.67 us
    gather x1, local copies, waits for them, and re-layouts, local(): hidden_in = jnp.take(hidden_grad, col_ids, axis=1)  3.45 us
    another operation x1, local copies, waits for them, and re-layouts, local(): hidden_grad = out_grad[0].reshape(tok_rows, col_count, block_size)  2.76 us
  transfers between devices with their start and end apart: 16, of which 8 were waited for; matrix products, arithmetic and copies ran while one was open for 26% of the time, Pallas kernels for 0%

profile of v1, /device:TPU:0, one launch (start us, length us, event | category | flops | bytes accessed | tf_op | source)
XLA Modules:
  0.0 73.8 jit_solution(5864589147632713404)
XLA Ops:
  0.6 0.9 %copy-done = bf16[1,4,128,128]{3,2,1,0:T(8,128)(2,1)S(1)} copy-done((bf16[1,4,128,128]{3,2,1,0:T(8,128)(2,1)S(1)}, bf16[1,4,128,128]{3,2,1,0:T(8,128)(2,1)}, u32[]{:S(2)}) %copy-start) | copy-done | bytes 131096
  1.5 3.1 %collective-permute-start = (bf16[4,32,128]{2,1,0:T(8,128)(2,1)S(1)}, bf16[4,32,128]{2,1,0:T(8,128)(2,1)S(1)}, u32[]{:S(2)}, u32[]{:S(2)}) collective-permute-start(bf16[4,32,128]{2,1,0:T(8,128)(2,1)S(1)} %fusion.28), channel_id=1, source_target_pairs={{0,4},{4,8},{8,12},{12,0},{1,5},{5,9},{9,13},{13,1},{2,6},{6,10},{... | collective-permute-start | bytes 98312 | tf_op jit(solution)/shard_map/ppermute | solution.py:17
  4.6 2.6 %collective-permute-start.1 = (bf16[4,32,128]{2,1,0:T(8,128)(2,1)S(1)}, bf16[4,32,128]{2,1,0:T(8,128)(2,1)S(1)}, u32[]{:S(2)}, u32[]{:S(2)}) collective-permute-start(bf16[4,32,128]{2,1,0:T(8,128)(2,1)S(1)} %fusion.28), channel_id=1, source_target_pairs={{0,8},{4,12},{8,0},{12,4},{1,9},{5,13},{9,1},{13,5},{2,10},{6,14},... | collective-permute-start | bytes 98312 | tf_op jit(solution)/shard_map/ppermute | solution.py:17
  7.2 1.3 %collective-permute-start.2 = (bf16[4,32,128]{2,1,0:T(8,128)(2,1)S(1)}, bf16[4,32,128]{2,1,0:T(8,128)(2,1)S(1)}, u32[]{:S(2)}, u32[]{:S(2)}) collective-permute-start(bf16[4,32,128]{2,1,0:T(8,128)(2,1)S(1)} %fusion.28), channel_id=1, source_target_pairs={{0,12},{4,0},{8,4},{12,8},{1,13},{5,1},{9,5},{13,9},{2,14},{6,2},{... | collective-permute-start | bytes 98312 | tf_op jit(solution)/shard_map/ppermute | solution.py:17
  8.5 0.7 collective-permute-start.5
  10.2 0.7 compare_and_fusion
  10.9 1.6 %reshape_squeeze.7 = bf16[128,28,128]{2,1,0:T(8,128)(2,1)S(1)} reshape(bf16[1,4,32,3584]{3,2,1,0:T(8,128)(2,1)} %param.5) | data formatting | bytes 1835008 | tf_op jit(solution)/shard_map/reshape;squeeze | solution.py:60
  12.9 2.8 %copy.41 = bf16[16,8,112,128]{3,2,1,0:T(8,128)(2,1)S(1)} copy(bf16[16,8,112,128]{3,1,2,0:T(8,128)(2,1)} %bitcast.119) | data formatting | bytes 7340032
  15.7 2.8 %copy.27 = bf16[128,112,128]{2,0,1:T(8,128)(2,1)} copy(bf16[128,112,128]{2,1,0:T(8,128)(2,1)S(1)} %bitcast.114) | data formatting | bytes 7340032 | tf_op jit(solution)/shard_map/reshape;squeeze | solution.py:61
  18.5 2.9 %collective-permute-start.7 = (s32[4,2]{0,1:T(2,128)S(1)}, s32[4,2]{0,1:T(2,128)S(1)}, u32[]{:S(2)}, u32[]{:S(2)}) collective-permute-start(s32[4,2]{0,1:T(2,128)S(1)} %bitcast.136), channel_id=1, source_target_pairs={{0,12},{4,0},{8,4},{12,8},{1,13},{5,1},{9,5},{13,9},{2,14},{6,2},{... | collective-permute-start | bytes 104 | tf_op jit(solution)/shard_map/ppermute | solution.py:17
  21.4 2.1 %collective-permute-done.7 = s32[4,2]{0,1:T(2,128)S(1)} collective-permute-done((s32[4,2]{0,1:T(2,128)S(1)}, s32[4,2]{0,1:T(2,128)S(1)}, u32[]{:S(2)}, u32[]{:S(2)}) %collective-permute-start.7) | collective-permute-done | bytes 64 | tf_op jit(solution)/shard_map/ppermute | solution.py:17
  24.3 1.6 %collective-permute-start.3 = (bf16[4,4,32,128]{3,2,1,0:T(8,128)(2,1)S(1)}, bf16[4,4,32,128]{3,2,1,0:T(8,128)(2,1)S(1)}, u32[]{:S(2)}, u32[]{:S(2)}) collective-permute-start(bf16[4,4,32,128]{3,2,1,0:T(8,128)(2,1)S(1)} %get-tuple-element.9), channel_id=1, source_target_pairs={{0,2},{1,3},{2,0},{3,1},{4,6},{5,7},{6,4},{7,5},{8,10},{9,11},{10,... | collective-permute-start | bytes 393224 | tf_op jit(solution)/shard_map/ppermute | solution.py:22
  25.9 3.4 %collective-permute-done.3 = bf16[4,4,32,128]{3,2,1,0:T(8,128)(2,1)S(1)} collective-permute-done((bf16[4,4,32,128]{3,2,1,0:T(8,128)(2,1)S(1)}, bf16[4,4,32,128]{3,2,1,0:T(8,128)(2,1)S(1)}, u32[]{:S(2)}, u32[]{:S(2)}) %collective-permute-start.3) | collective-permute-done | bytes 131104 | tf_op jit(solution)/shard_map/ppermute | solution.py:22
  30.3 3.4 %gather_fusion = bf16[16,128,128]{2,1,0:T(8,128)(2,1)} fusion(bf16[128,112,128]{2,0,1:T(8,128)(2,1)} %copy.27, s32[1024]{0:T(1024)S(1)} %get-tuple-element.17), kind=kCustom, calls=%fused_computation | custom fusion | bytes 1048640 | tf_op jit(solution)/shard_map/jit(_take)/gather | solution.py:85
  34.8 2.2 %fusion.1 = bf16[128,16,128]{2,1,0:T(8,128)(2,1)S(1)} fusion(f32[128,16,128]{2,1,0:T(8,128)S(1)} %copy.33, bf16[16,128,128]{2,1,0:T(8,128)(2,1)} %gather_fusion, pred[16]{0:T(512)(128)(4,1)S(1)} %get-tuple-element.14, s32[16]{0:T(128)S(1)} %get-tuple-element.13), kind=kOutput, calls=%fused_computation.9 | convolution fusion | flops 53215488 | bytes 2097232 | tf_op jit(solution)/shard_map/bc,tcn->tbn/dot_general | solution.py:82
  37.2 0.9 %dynamic-slice_bitcast_fusion = f32[4,4,2,32,128]{4,3,2,1,0:T(8,128)} fusion(f32[4,4,2,2,32,128]{5,4,3,2,1,0:T(8,128)S(1)} %bitcast.117, s32[]{:T(128)S(6)} %select_n.117), kind=kLoop, calls=%fused_computation.16 | loop fusion | bytes 1048580 | tf_op jit(solution)/shard_map/jit(dynamic_index_in_dim)/squeeze | solution.py:111
  39.6 1.1 %fusion = bf16[128,28,128]{2,1,0:T(8,128)(2,1)S(1)} fusion(f32[128,16,128]{2,1,0:T(8,128)S(1)} %copy.35, s32[16]{0:T(128)S(1)} %get-tuple-element.10), kind=kOutput, calls=%fused_computation.4 | convolution fusion | flops 88539584 | bytes 1966144 | tf_op jit(solution)/shard_map/rb,tbk->trk/dot_general | solution.py:94
  40.7 1.4 %reshape.173 = bf16[4,32,3584]{2,1,0:T(8,128)(2,1)} reshape(bf16[128,28,128]{2,1,0:T(8,128)(2,1)S(1)} %fusion) | data formatting | bytes 1835008 | tf_op jit(solution)/shard_map/reshape | solution.py:97
  42.1 1.8 %gather_fusion.2 = bf16[4,32,3584]{2,1,0:T(8,128)(2,1)S(1)} fusion(bf16[4,32,3584]{2,1,0:T(8,128)(2,1)} %reshape.173, s32[1024]{0:T(1024)S(1)} %pad_clamp_fusion), kind=kCustom, calls=%fused_computation.2 | custom fusion | bytes 1835024 | tf_op jit(solution)/shard_map/jit(_take)/gather | solution.py:100
  43.9 1.1 %bitcast_add_fusion = f32[4,4,2,32,128]{4,3,2,1,0:T(8,128)S(1)} fusion(f32[4,4,2,32,128]{4,3,2,1,0:T(8,128)} %collective-permute-done.9, f32[4,4,2,2,32,128]{5,4,3,2,1,0:T(8,128)S(1)} %bitcast.118, s32[]{:T(128)S(6)} %select_n.116), kind=kLoop, calls=%fused_computation.12 | loop fusion | flops 131072 | bytes 1572868 | tf_op jit(solution)/shard_map/add | solution.py:112
  45.1 1.6 %collective-permute-start.10 = (f32[4,4,32,128]{3,2,1,0:T(8,128)S(1)}, f32[4,4,32,128]{3,2,1,0:T(8,128)S(1)}, u32[]{:S(2)}, u32[]{:S(2)}) collective-permute-start(f32[4,4,32,128]{3,2,1,0:T(8,128)S(1)} %dynamic-slice_bitcast_fusion.1), channel_id=1, source_target_pairs={{0,2},{1,3},{2,0},{3,1},{4,6},{5,7},{6,4},{7,5},{8,10},{9,11},{10,... | collective-permute-start | bytes 786440 | tf_op jit(solution)/shard_map/ppermute | solution.py:22
  46.8 1.3 %collective-permute-start.8 = (bf16[4,32,3584]{2,1,0:T(8,128)(2,1)S(1)}, bf16[4,32,3584]{2,1,0:T(8,128)(2,1)S(1)}, u32[]{:S(2)}, u32[]{:S(2)}) collective-permute-start(bf16[4,32,3584]{2,1,0:T(8,128)(2,1)S(1)} %broadcast_select_fusion), channel_id=1, source_target_pairs={{16,0},{17,1},{18,2},{19,3},{20,4},{21,5},{22,6},{23,7},{24,8},{25... | collective-permute-start | bytes 2752520 | tf_op jit(solution)/shard_map/ppermute | solution.py:12
  48.1 5.3 %collective-permute-done.10 = f32[4,4,32,128]{3,2,1,0:T(8,128)S(1)} collective-permute-done((f32[4,4,32,128]{3,2,1,0:T(8,128)S(1)}, f32[4,4,32,128]{3,2,1,0:T(8,128)S(1)}, u32[]{:S(2)}, u32[]{:S(2)}) %collective-permute-start.10) | collective-permute-done | bytes 262176 | tf_op jit(solution)/shard_map/ppermute | solution.py:22
  53.4 3.3 %collective-permute-start.11 = (f32[4,32,128]{2,1,0:T(8,128)S(1)}, f32[4,32,128]{2,1,0:T(8,128)S(1)}, u32[]{:S(2)}, u32[]{:S(2)}) collective-permute-start(f32[4,32,128]{2,1,0:T(8,128)S(1)} %get-tuple-element.2), channel_id=1, source_target_pairs={{0,12},{4,0},{8,4},{12,8},{1,13},{5,1},{9,5},{13,9},{2,14},{6,2},{... | collective-permute-start | bytes 196616 | tf_op jit(solution)/shard_map/ppermute | solution.py:17
  57.4 1.4 %collective-permute-done.11 = f32[4,32,128]{2,1,0:T(8,128)S(1)} collective-permute-done((f32[4,32,128]{2,1,0:T(8,128)S(1)}, f32[4,32,128]{2,1,0:T(8,128)S(1)}, u32[]{:S(2)}, u32[]{:S(2)}) %collective-permute-start.11) | collective-permute-done | bytes 65568 | tf_op jit(solution)/shard_map/ppermute | solution.py:17
  58.8 3.2 %collective-permute-done.12 = f32[4,32,128]{2,1,0:T(8,128)S(1)} collective-permute-done((f32[4,32,128]{2,1,0:T(8,128)S(1)}, f32[4,32,128]{2,1,0:T(8,128)S(1)}, u32[]{:S(2)}, u32[]{:S(2)}) %collective-permute-start.12) | collective-permute-done | bytes 65568 | tf_op jit(solution)/shard_map/ppermute | solution.py:17
  62.0 1.0 %collective-permute-done.13 = f32[4,32,128]{2,1,0:T(8,128)S(1)} collective-permute-done((f32[4,32,128]{2,1,0:T(8,128)S(1)}, f32[4,32,128]{2,1,0:T(8,128)S(1)}, u32[]{:S(2)}, u32[]{:S(2)}) %collective-permute-start.13) | collective-permute-done | bytes 65568 | tf_op jit(solution)/shard_map/ppermute | solution.py:17
  63.1 1.6 %collective-permute-start.14 = (f32[4,32,128]{2,1,0:T(8,128)S(1)}, f32[4,32,128]{2,1,0:T(8,128)S(1)}, u32[]{:S(2)}, u32[]{:S(2)}) collective-permute-start(f32[4,32,128]{2,1,0:T(8,128)S(1)} %fusion.10), channel_id=1, source_target_pairs={{0,2},{1,3},{2,0},{3,1},{4,6},{5,7},{6,4},{7,5},{8,10},{9,11},{10,... | collective-permute-start | bytes 196616 | tf_op jit(solution)/shard_map/ppermute | solution.py:22
  64.7 6.1 %collective-permute-done.8 = bf16[4,32,3584]{2,1,0:T(8,128)(2,1)S(1)} collective-permute-done((bf16[4,32,3584]{2,1,0:T(8,128)(2,1)S(1)}, bf16[4,32,3584]{2,1,0:T(8,128)(2,1)S(1)}, u32[]{:S(2)}, u32[]{:S(2)}) %collective-permute-start.8) | collective-permute-done | bytes 917536 | tf_op jit(solution)/shard_map/ppermute | solution.py:12
  70.9 1.3 %collective-permute-done.15 = f32[2,4,32,128]{3,2,0,1:T(8,128)S(1)} collective-permute-done((f32[2,4,32,128]{3,2,0,1:T(8,128)S(1)}, f32[2,4,32,128]{3,2,0,1:T(8,128)S(1)}, u32[]{:S(2)}, u32[]{:S(2)}) %collective-permute-start.15) | collective-permute-done | bytes 131104 | tf_op jit(solution)/shard_map/ppermute | solution.py:22
  72.1 0.7 fusion.7
  72.9 0.9 %copy.55 = bf16[1,4,32,3584]{3,2,1,0:T(8,128)(2,1)} copy(bf16[1,4,32,3584]{3,2,1,0:T(8,128)(2,1)S(1)} %bitcast.121) | data formatting | bytes 1835008
  (49 shorter events, 6.9 us)
Async XLA Ops:
  0.6 0.9 %copy-start = (bf16[1,4,128,128]{3,2,1,0:T(8,128)(2,1)S(1)}, bf16[1,4,128,128]{3,2,1,0:T(8,128)(2,1)}, u32[]{:S(2)}) copy-start(bf16[1,4,128,128]{3,2,1,0:T(8,128)(2,1)} %param.7) | copy-start | bytes 393220
  1.5 22.7 %collective-permute-start = (bf16[4,32,128]{2,1,0:T(8,128)(2,1)S(1)}, bf16[4,32,128]{2,1,0:T(8,128)(2,1)S(1)}, u32[]{:S(2)}, u32[]{:S(2)}) collective-permute-start(bf16[4,32,128]{2,1,0:T(8,128)(2,1)S(1)} %fusion.28), channel_id=1, source_target_pairs={{0,4},{4,8},{8,12},{12,0},{1,5},{5,9},{9,13},{13,1},{2,6},{6,10},{... | collective-permute-start | bytes 98312 | tf_op jit(solution)/shard_map/ppermute | solution.py:17
  4.6 19.7 %collective-permute-start.1 = (bf16[4,32,128]{2,1,0:T(8,128)(2,1)S(1)}, bf16[4,32,128]{2,1,0:T(8,128)(2,1)S(1)}, u32[]{:S(2)}, u32[]{:S(2)}) collective-permute-start(bf16[4,32,128]{2,1,0:T(8,128)(2,1)S(1)} %fusion.28), channel_id=1, source_target_pairs={{0,8},{4,12},{8,0},{12,4},{1,9},{5,13},{9,1},{13,5},{2,10},{6,14},... | collective-permute-start | bytes 98312 | tf_op jit(solution)/shard_map/ppermute | solution.py:17
  7.2 17.1 %collective-permute-start.2 = (bf16[4,32,128]{2,1,0:T(8,128)(2,1)S(1)}, bf16[4,32,128]{2,1,0:T(8,128)(2,1)S(1)}, u32[]{:S(2)}, u32[]{:S(2)}) collective-permute-start(bf16[4,32,128]{2,1,0:T(8,128)(2,1)S(1)} %fusion.28), channel_id=1, source_target_pairs={{0,12},{4,0},{8,4},{12,8},{1,13},{5,1},{9,5},{13,9},{2,14},{6,2},{... | collective-permute-start | bytes 98312 | tf_op jit(solution)/shard_map/ppermute | solution.py:17
  8.5 10.0 %collective-permute-start.5 = (s32[4,2]{0,1:T(2,128)}, s32[4,2]{0,1:T(2,128)S(1)}, u32[]{:S(2)}, u32[]{:S(2)}) collective-permute-start(s32[4,2]{0,1:T(2,128)} %bitcast.134), channel_id=1, source_target_pairs={{0,4},{4,8},{8,12},{12,0},{1,5},{5,9},{9,13},{13,1},{2,6},{6,10},{... | collective-permute-start | bytes 104 | tf_op jit(solution)/shard_map/ppermute | solution.py:17
  9.2 12.2 %collective-permute-start.6 = (s32[4,2]{0,1:T(2,128)}, s32[4,2]{0,1:T(2,128)S(1)}, u32[]{:S(2)}, u32[]{:S(2)}) collective-permute-start(s32[4,2]{0,1:T(2,128)} %bitcast.135), channel_id=1, source_target_pairs={{0,8},{4,12},{8,0},{12,4},{1,9},{5,13},{9,1},{13,5},{2,10},{6,14},... | collective-permute-start | bytes 104 | tf_op jit(solution)/shard_map/ppermute | solution.py:17
  15.7 2.8 %copy-start.1 = (s32[1,4,2]{1,2,0:T(2,128)S(1)}, s32[1,4,2]{1,2,0:T(2,128)}, u32[]{:S(2)}) copy-start(s32[1,4,2]{1,2,0:T(2,128)} %param.8) | copy-start | bytes 100
  18.5 5.0 %collective-permute-start.7 = (s32[4,2]{0,1:T(2,128)S(1)}, s32[4,2]{0,1:T(2,128)S(1)}, u32[]{:S(2)}, u32[]{:S(2)}) collective-permute-start(s32[4,2]{0,1:T(2,128)S(1)} %bitcast.136), channel_id=1, source_target_pairs={{0,12},{4,0},{8,4},{12,8},{1,13},{5,1},{9,5},{13,9},{2,14},{6,2},{... | collective-permute-start | bytes 104 | tf_op jit(solution)/shard_map/ppermute | solution.py:17
  24.3 5.0 %collective-permute-start.3 = (bf16[4,4,32,128]{3,2,1,0:T(8,128)(2,1)S(1)}, bf16[4,4,32,128]{3,2,1,0:T(8,128)(2,1)S(1)}, u32[]{:S(2)}, u32[]{:S(2)}) collective-permute-start(bf16[4,4,32,128]{3,2,1,0:T(8,128)(2,1)S(1)} %get-tuple-element.9), channel_id=1, source_target_pairs={{0,2},{1,3},{2,0},{3,1},{4,6},{5,7},{6,4},{7,5},{8,10},{9,11},{10,... | collective-permute-start | bytes 393224 | tf_op jit(solution)/shard_map/ppermute | solution.py:22
  29.4 4.4 %collective-permute-start.4 = (bf16[2,4,4,32,128]{4,3,2,1,0:T(8,128)(2,1)S(1)}, bf16[2,4,4,32,128]{4,3,2,1,0:T(8,128)(2,1)S(1)}, u32[]{:S(2)}, u32[]{:S(2)}) collective-permute-start(bf16[2,4,4,32,128]{4,3,2,1,0:T(8,128)(2,1)S(1)} %maximum_select_fusion.1), channel_id=1, source_target_pairs={{0,1},{1,0},{2,3},{3,2},{4,5},{5,4},{6,7},{7,6},{8,9},{9,8},{10,11... | collective-permute-start | bytes 786440 | tf_op jit(solution)/shard_map/ppermute | solution.py:22
  38.1 5.8 %collective-permute-start.9 = (f32[4,4,2,32,128]{4,3,2,1,0:T(8,128)}, f32[4,4,2,32,128]{4,3,2,1,0:T(8,128)}, u32[]{:S(2)}, u32[]{:S(2)}) collective-permute-start(f32[4,4,2,32,128]{4,3,2,1,0:T(8,128)} %dynamic-slice_bitcast_fusion), channel_id=1, source_target_pairs={{0,1},{1,0},{2,3},{3,2},{4,5},{5,4},{6,7},{7,6},{8,9},{9,8},{10,11... | collective-permute-start | bytes 1572872 | tf_op jit(solution)/shard_map/ppermute | solution.py:22
  45.1 8.3 %collective-permute-start.10 = (f32[4,4,32,128]{3,2,1,0:T(8,128)S(1)}, f32[4,4,32,128]{3,2,1,0:T(8,128)S(1)}, u32[]{:S(2)}, u32[]{:S(2)}) collective-permute-start(f32[4,4,32,128]{3,2,1,0:T(8,128)S(1)} %dynamic-slice_bitcast_fusion.1), channel_id=1, source_target_pairs={{0,2},{1,3},{2,0},{3,1},{4,6},{5,7},{6,4},{7,5},{8,10},{9,11},{10,... | collective-permute-start | bytes 786440 | tf_op jit(solution)/shard_map/ppermute | solution.py:22
  46.8 23.9 %collective-permute-start.8 = (bf16[4,32,3584]{2,1,0:T(8,128)(2,1)S(1)}, bf16[4,32,3584]{2,1,0:T(8,128)(2,1)S(1)}, u32[]{:S(2)}, u32[]{:S(2)}) collective-permute-start(bf16[4,32,3584]{2,1,0:T(8,128)(2,1)S(1)} %broadcast_select_fusion), channel_id=1, source_target_pairs={{16,0},{17,1},{18,2},{19,3},{20,4},{21,5},{22,6},{23,7},{24,8},{25... | collective-permute-start | bytes 2752520 | tf_op jit(solution)/shard_map/ppermute | solution.py:12
  53.4 5.4 %collective-permute-start.11 = (f32[4,32,128]{2,1,0:T(8,128)S(1)}, f32[4,32,128]{2,1,0:T(8,128)S(1)}, u32[]{:S(2)}, u32[]{:S(2)}) collective-permute-start(f32[4,32,128]{2,1,0:T(8,128)S(1)} %get-tuple-element.2), channel_id=1, source_target_pairs={{0,12},{4,0},{8,4},{12,8},{1,13},{5,1},{9,5},{13,9},{2,14},{6,2},{... | collective-permute-start | bytes 196616 | tf_op jit(solution)/shard_map/ppermute | solution.py:17
  56.8 5.3 %collective-permute-start.12 = (f32[4,32,128]{2,1,0:T(8,128)S(1)}, f32[4,32,128]{2,1,0:T(8,128)S(1)}, u32[]{:S(2)}, u32[]{:S(2)}) collective-permute-start(f32[4,32,128]{2,1,0:T(8,128)S(1)} %get-tuple-element.4), channel_id=1, source_target_pairs={{0,8},{4,12},{8,0},{12,4},{1,9},{5,13},{9,1},{13,5},{2,10},{6,14},... | collective-permute-start | bytes 196616 | tf_op jit(solution)/shard_map/ppermute | solution.py:17
  57.0 6.1 %collective-permute-start.13 = (f32[4,32,128]{2,1,0:T(8,128)S(1)}, f32[4,32,128]{2,1,0:T(8,128)S(1)}, u32[]{:S(2)}, u32[]{:S(2)}) collective-permute-start(f32[4,32,128]{2,1,0:T(8,128)S(1)} %get-tuple-element.3), channel_id=1, source_target_pairs={{0,4},{4,8},{8,12},{12,0},{1,5},{5,9},{9,13},{13,1},{2,6},{6,10},{... | collective-permute-start | bytes 196616 | tf_op jit(solution)/shard_map/ppermute | solution.py:17
  63.1 7.6 %collective-permute-start.14 = (f32[4,32,128]{2,1,0:T(8,128)S(1)}, f32[4,32,128]{2,1,0:T(8,128)S(1)}, u32[]{:S(2)}, u32[]{:S(2)}) collective-permute-start(f32[4,32,128]{2,1,0:T(8,128)S(1)} %fusion.10), channel_id=1, source_target_pairs={{0,2},{1,3},{2,0},{3,1},{4,6},{5,7},{6,4},{7,5},{8,10},{9,11},{10,... | collective-permute-start | bytes 196616 | tf_op jit(solution)/shard_map/ppermute | solution.py:22
  70.7 1.4 %collective-permute-start.15 = (f32[2,4,32,128]{3,2,0,1:T(8,128)S(1)}, f32[2,4,32,128]{3,2,0,1:T(8,128)S(1)}, u32[]{:S(2)}, u32[]{:S(2)}) collective-permute-start(f32[2,4,32,128]{3,2,0,1:T(8,128)S(1)} %maximum_select_fusion.3), channel_id=1, source_target_pairs={{0,1},{1,0},{2,3},{3,2},{4,5},{5,4},{6,7},{7,6},{8,9},{9,8},{10,11... | collective-permute-start | bytes 393224 | tf_op jit(solution)/shard_map/ppermute | solution.py:22

commit v2 on v1

--- a/solution.py
+++ b/solution.py
@@ -57,51 +57,80 @@
     chunk = block_size // n_dp
     me_dp = lax.axis_index("dp")
 
-    features = activations[0].reshape(tok_rows, row_count, block_size)
-    hidden_grad = out_grad[0].reshape(tok_rows, col_count, block_size)
     own_blocks = blocks[0]
     blocks_dev = own_blocks.shape[0]
 
-    all_indices = gather_over(pattern[0], "fsdp").reshape(-1, 2)
-
-    own_chunk = lax.dynamic_slice_in_dim(own_blocks, me_dp * chunk, chunk, 1)
-    fetched = gather_over(own_chunk, "fsdp")
-    gathered = butterfly_gather(fetched, "dp", list(reversed(range(dp_bits))))
-    gathered = gathered.reshape((n_dp, n_fsdp, blocks_dev, chunk, block_size))
-    weights = jnp.transpose(gathered, (1, 2, 0, 3, 4)).reshape(
-        n_fsdp * blocks_dev, block_size, block_size
+    assert n_fsdp % n_dp == 0
+    per_dp = n_fsdp // n_dp
+    weight_len = blocks_dev * block_size * block_size
+    payload = jnp.concatenate(
+        [own_blocks.reshape(-1), pattern[0].reshape(-1).astype(jnp.bfloat16)]
     )
+    fetched = []
+    for m in range(per_dp):
+        pairs = []
+        for f in range(n_fsdp):
+            for d in range(n_dp):
+                k = d + n_dp * m
+                pairs.append((((f - k) % n_fsdp) * n_dp + d, f * n_dp + d))
+        fetched.append(lax.ppermute(payload, ("fsdp", "dp"), pairs))
+    fetched = jnp.stack(fetched)
+    pieces = butterfly_gather(fetched, "dp", list(reversed(range(dp_bits))))
+    pieces = pieces.reshape((n_dp, per_dp, -1))
+    pieces = jnp.transpose(pieces, (1, 0, 2)).reshape(n_fsdp, -1)
+    weights = pieces[:, :weight_len].reshape(n_fsdp * blocks_dev, block_size, block_size)
+    all_indices = pieces[:, weight_len:].reshape(n_fsdp * blocks_dev, 2).astype(jnp.int32)
+    block_count = n_fsdp * blocks_dev
 
     row_ids = all_indices[:, 0]
     col_ids = all_indices[:, 1]
-    rows_in = jnp.take(features, row_ids, axis=1)
+    features = activations[0].reshape(tok_rows, -1)
+    hidden_grad = out_grad[0].reshape(tok_rows, -1)
+    rows_in = jnp.stack(
+        [
+            lax.dynamic_slice(features, (0, row_ids[b] * block_size), (tok_rows, block_size))
+            for b in range(block_count)
+        ]
+    )
+    hidden_in = jnp.stack(
+        [
+            lax.dynamic_slice(hidden_grad, (0, col_ids[b] * block_size), (tok_rows, block_size))
+            for b in range(block_count)
+        ]
+    )
+    tok_mb = activations.shape[2]
+    rows_in = jnp.take(
+        rows_in.reshape(block_count, micro_count, tok_mb, block_size), order, axis=1
+    ).reshape(block_count, tok_rows, block_size)
+    hidden_in = jnp.take(
+        hidden_in.reshape(block_count, micro_count, tok_mb, block_size), order, axis=1
+    ).reshape(block_count, tok_rows, block_size)
+
     product = jnp.einsum(
-        "tbk,bkn->tbn", rows_in, weights, preferred_element_type=jnp.float32
+        "btk,bkn->btn", rows_in, weights, preferred_element_type=jnp.float32
     )
     same_col = (col_ids[:, None] == col_ids[None, :]).astype(jnp.float32)
     pre_act = jnp.einsum(
-        "bc,tcn->tbn", same_col, product, precision=lax.Precision.HIGHEST
+        "bc,ctn->btn", same_col, product, precision=lax.Precision.HIGHEST
     )
-    hidden_in = jnp.take(hidden_grad, col_ids, axis=1)
     act_cols = (hidden_in.astype(jnp.float32) * silu_slope(pre_act)).astype(jnp.bfloat16)
 
     backward = jnp.einsum(
-        "tbn,bkn->tbk", act_cols, weights, preferred_element_type=jnp.float32
+        "btn,bkn->btk", act_cols, weights, preferred_element_type=jnp.float32
     )
     row_hit = (jnp.arange(row_count, dtype=jnp.int32)[:, None] == row_ids[None, :]).astype(
         jnp.float32
     )
     input_grad = jnp.einsum(
-        "rb,tbk->trk", row_hit, backward, precision=lax.Precision.HIGHEST
+        "rb,btk->trk", row_hit, backward, precision=lax.Precision.HIGHEST
     )
-    input_grad = input_grad.astype(jnp.bfloat16).reshape(
-        micro_count, activations.shape[2], activations.shape[3]
+    ordered = input_grad.astype(jnp.bfloat16).reshape(
+        micro_count, tok_mb, activations.shape[3]
     )
-    ordered = jnp.take(input_grad, order, axis=0)
     received = passed_along(ordered, "section", -1)
 
     partial = jnp.einsum(
-        "tbk,tbn->bkn", rows_in, act_cols, preferred_element_type=jnp.float32
+        "btk,btn->bkn", rows_in, act_cols, preferred_element_type=jnp.float32
     )
     held = partial.reshape((n_fsdp, blocks_dev) + (2,) * dp_bits + (chunk, block_size))
     for bit in range(dp_bits):

time: 74.2 us -> 89 us (1.20)
  between operations: 0.92 us -> 21.4 us
  local copies, waits for them, and re-layouts: 19.2 us -> 9.56 us
  other arithmetic: 3.94 us -> 7.72 us
    ppermute x9 -> x3, starting transfers between devices: 14.8 us -> 4.66 us  [shifted(): return lax.ppermute(x, axis, [(i, (i + k) % n) for i in range(n)])]
    ppermute x6, starting transfers between devices: 5.38 us -> 15.3 us  [swapped(): return lax.ppermute(x, axis, [(i, i ^ 1 << bit) for i in range(n)])]
    gather x3 -> x2, local copies, waits for them, and re-layouts: 5.88 us -> 1.3 us  [the longest x1 0.65 us: local(): jnp.take(rows_in.reshape(block_count, micro_count, tok_mb, block_size), o...]
    another operation x4 -> x5, local copies, waits for them, and re-layouts: 4.74 us -> 1.2 us  [the longest x1 0.9 us: local(): pieces = jnp.transpose(pieces, (1, 0, 2)).reshape(n_fsdp, -1)]
    unnamed x6 -> x33, local copies, waits for them, and re-layouts: 4.67 us -> 1.23 us
    ppermute x9 -> x3, waiting for transfers between devices: 7.77 us -> 4.51 us  [shifted(): return lax.ppermute(x, axis, [(i, (i + k) % n) for i in range(n)])]
    ppermute x1, waiting for transfers between devices: 6.06 us -> 8.59 us  [passed_along(): return lax.ppermute(block, axis, route)]
    slice x0 -> x4, local copies, waits for them, and re-layouts: none -> 1.73 us  [the longest x1 0.69 us: local(): col_ids[b] * block_size]
  transfers between devices with their start and end apart: 16 -> 11, of which waited for: 8 -> 9; matrix products, arithmetic and copies ran while one was open for 26% -> 6% of each run, Pallas kernels for 0% -> 0%
where the time goes in v2:
time: 89 us; the launch traced here: 88.5 us
  waiting for transfers between devices  23.5 us (26%)
  starting transfers between devices  21.9 us (25%)
  between operations  21.4 us (24%)
  local copies, waits for them, and re-layouts  9.56 us (11%)
  other arithmetic  7.72 us (9%)
  matrix products  4.42 us (5%)
    ppermute x6, starting transfers between devices, swapped(): return lax.ppermute(x, axis, [(i, i ^ 1 << bit) for i in range(n)])  15.3 us
    ppermute x6, waiting for transfers between devices, swapped(): return lax.ppermute(x, axis, [(i, i ^ 1 << bit) for i in range(n)])  10.3 us
    ppermute x1, waiting for transfers between devices, passed_along(): return lax.ppermute(block, axis, route)  8.59 us
    ppermute x3, starting transfers between devices, shifted(): return lax.ppermute(x, axis, [(i, (i + k) % n) for i in range(n)])  4.66 us
    ppermute x3, waiting for transfers between devices, shifted(): return lax.ppermute(x, axis, [(i, (i + k) % n) for i in range(n)])  4.51 us
  transfers between devices with their start and end apart: 11, of which 9 were waited for; matrix products, arithmetic and copies ran while one was open for 6% of the time, Pallas kernels for 0%

profile of v2, /device:TPU:0, one launch (start us, length us, event | category | flops | bytes accessed | tf_op | source)
XLA Modules:
  0.0 88.5 jit_solution(9460385224124580429)
XLA Ops:
  0.6 0.7 convert_element_type.29
  1.5 0.9 %pad_maximum_fusion = bf16[65544]{0:T(1024)(128)(2,1)S(1)} fusion(bf16[8]{0:T(256)(128)(2,1)S(1)} %convert_element_type.30, bf16[65536]{0:T(1024)(128)(2,1)} %bitcast.179), kind=kLoop, calls=%fused_computation.26 | loop fusion | flops 262176 | bytes 262176 | tf_op jit(solution)/shard_map/concatenate | solution.py:66
  2.4 0.7 collective-permute-start
  3.1 0.7 compare_select_fusion
  3.9 11.3 %collective-permute-start.1 = (bf16[1,65544]{1,0:T(2,128)(2,1)S(1)}, bf16[1,65544]{1,0:T(2,128)(2,1)S(1)}, u32[]{:S(2)}, u32[]{:S(2)}) collective-permute-start(bf16[1,65544]{1,0:T(2,128)(2,1)S(1)} %stack.170), channel_id=1, source_target_pairs={{0,2},{1,3},{2,0},{3,1},{4,6},{5,7},{6,4},{7,5},{8,10},{9,11},{10,... | collective-permute-start | bytes 393272 | tf_op jit(solution)/shard_map/ppermute | solution.py:22
  15.2 0.7 compare_and_fusion
  16.1 4.4 %collective-permute-done.1 = bf16[1,65544]{1,0:T(2,128)(2,1)S(1)} collective-permute-done((bf16[1,65544]{1,0:T(2,128)(2,1)S(1)}, bf16[1,65544]{1,0:T(2,128)(2,1)S(1)}, u32[]{:S(2)}, u32[]{:S(2)}) %collective-permute-start.1) | collective-permute-done | bytes 131120 | tf_op jit(solution)/shard_map/ppermute | solution.py:22
  20.4 1.6 %broadcast_select_fusion = bf16[2,1,65544]{2,1,0:T(2,128)(2,1)S(1)} fusion(pred[]{:T(512)S(6)} %eq.39, bf16[1,1,65544]{2,1,0:T(2,128)(2,1)S(1)} %bitcast.136, bf16[1,1,65544]{2,1,0:T(2,128)(2,1)S(1)} %stack.169), kind=kLoop, calls=%fused_computation.4 | loop fusion | flops 393264 | bytes 524353 | tf_op jit(solution)/shard_map/jit(_where)/select_n | solution.py:41
  22.4 1.2 %fusion.12 = bf16[1,2,1,65544]{3,1,2,0:T(2,128)(2,1)S(1)} fusion(pred[]{:T(512)S(6)} %eq.39, bf16[1,1,65544]{2,1,0:T(2,128)(2,1)S(1)} %bitcast.137, bf16[1,1,65544]{2,1,0:T(2,128)(2,1)S(1)} %stack.169), kind=kLoop, calls=%fused_computation.21 | loop fusion | flops 1179792 | bytes 524353 | tf_op jit(solution)/shard_map/stack | solution.py:41
  23.9 0.9 %fusion.7 = bf16[2,2,1,65544]{3,0,2,1:T(2,128)(2,1)S(1)} fusion(pred[]{:T(512)S(6)} %eq.38, bf16[1,2,1,65544]{3,1,2,0:T(2,128)(2,1)S(1)} %bitcast.142, bf16[1,2,1,65544]{3,1,2,0:T(2,128)(2,1)S(1)} %fusion.12), kind=kLoop, calls=%fused_computation.11 | loop fusion | flops 786528 | bytes 1048705 | tf_op jit(solution)/shard_map/transpose | solution.py:44
  25.3 0.9 %reshape_transpose_reshape.3 = bf16[4,65544]{1,0:T(4,128)(2,1)S(1)} reshape(bf16[2,2,1,65544]{3,1,0,2:T(2,128)(2,1)S(1)} %copy.31) | data formatting | bytes 1048704 | tf_op jit(solution)/shard_map/reshape;transpose;reshape | solution.py:80
  26.5 0.7 fusion.24
  39.3 0.7 fusion.25
  49.1 1.2 %constant_dynamic-slice_fusion.16 = (bf16[128,128]{1,0:T(8,128)(2,1)S(1)}, bf16[128,128]{1,0:T(8,128)(2,1)S(1)}, bf16[128,128]{1,0:T(8,128)(2,1)S(1)}, bf16[128,...) fusion(bf16[128,14336]{1,0:T(8,128)(2,1)} %bitcast.180, ...), kind=kLoop, calls=%fused_computation.86 | loop fusion | bytes 1048640 | tf_op jit(solution)/shard_map/dynamic_slice | solution.py:97
  50.5 0.6 gather_fusion.1
  51.4 0.6 gather_fusion
  52.3 0.6 copy.32
  53.2 1.5 %fusion.1 = bf16[16,128,128]{2,0,1:T(8,128)(2,1)S(1)} fusion(f32[16,4,32,128]{3,0,2,1:T(8,128)S(1)} %copy.32, f32[16,128,128]{2,1,0:T(8,128)S(1)} %fusion.26, s32[16]{0:T(128)S(1)} %get-tuple-element.4), kind=kOutput, calls=%fused_computation.7 | convolution fusion | flops 52691200 | bytes 2621504 | tf_op jit(solution)/shard_map/bc,ctn->btn/dot_general | solution.py:113
  55.9 1.3 %collective-permute-done.4 = f32[4,4,2,32,128]{4,3,2,1,0:T(8,128)S(1)} collective-permute-done((f32[4,4,2,32,128]{4,3,2,1,0:T(8,128)S(1)}, f32[4,4,2,32,128]{4,3,2,1,0:T(8,128)S(1)}, u32[]{:S(2)}, u32[]{:S(2)}) %collective-permute-start.4) | collective-permute-done | bytes 524320 | tf_op jit(solution)/shard_map/ppermute | solution.py:22
  57.3 1.8 %collective-permute-start.5 = (f32[4,4,32,128]{3,2,1,0:T(8,128)S(1)}, f32[4,4,32,128]{3,2,1,0:T(8,128)S(1)}, u32[]{:S(2)}, u32[]{:S(2)}) collective-permute-start(f32[4,4,32,128]{3,2,1,0:T(8,128)S(1)} %dynamic-slice_bitcast_fusion.1), channel_id=1, source_target_pairs={{0,2},{1,3},{2,0},{3,1},{4,6},{5,7},{6,4},{7,5},{8,10},{9,11},{10,... | collective-permute-start | bytes 786440 | tf_op jit(solution)/shard_map/ppermute | solution.py:22
  59.1 1.8 %fusion = bf16[128,28,128]{2,1,0:T(8,128)(2,1)S(1)} fusion(f32[16,128,128]{2,1,0:T(8,128)S(1)} %fusion.10, s32[16]{0:T(128)S(1)} %get-tuple-element.3), kind=kOutput, calls=%fused_computation.3 | convolution fusion | flops 88539584 | bytes 1966144 | tf_op jit(solution)/shard_map/rb,btk->trk/dot_general | solution.py:124
  61.4 1.3 %collective-permute-start.3 = (bf16[4,32,3584]{2,1,0:T(8,128)(2,1)S(1)}, bf16[4,32,3584]{2,1,0:T(8,128)(2,1)S(1)}, u32[]{:S(2)}, u32[]{:S(2)}) collective-permute-start(bf16[4,32,3584]{2,1,0:T(8,128)(2,1)S(1)} %reshape.568), channel_id=1, source_target_pairs={{16,0},{17,1},{18,2},{19,3},{20,4},{21,5},{22,6},{23,7},{24,8},{25... | collective-permute-start | bytes 2752520 | tf_op jit(solution)/shard_map/ppermute | solution.py:12
  62.7 3.1 %collective-permute-done.5 = f32[4,4,32,128]{3,2,1,0:T(8,128)S(1)} collective-permute-done((f32[4,4,32,128]{3,2,1,0:T(8,128)S(1)}, f32[4,4,32,128]{3,2,1,0:T(8,128)S(1)}, u32[]{:S(2)}, u32[]{:S(2)}) %collective-permute-start.5) | collective-permute-done | bytes 262176 | tf_op jit(solution)/shard_map/ppermute | solution.py:22
  65.8 1.1 %collective-permute-start.8 = (f32[4,32,128]{2,1,0:T(8,128)S(1)}, f32[4,32,128]{2,1,0:T(8,128)S(1)}, u32[]{:S(2)}, u32[]{:S(2)}) collective-permute-start(f32[4,32,128]{2,1,0:T(8,128)S(1)} %get-tuple-element.38), channel_id=1, source_target_pairs={{0,4},{4,8},{8,12},{12,0},{1,5},{5,9},{9,13},{13,1},{2,6},{6,10},{... | collective-permute-start | bytes 196616 | tf_op jit(solution)/shard_map/ppermute | solution.py:17
  66.9 3.6 %collective-permute-start.7 = (f32[4,32,128]{2,1,0:T(8,128)S(1)}, f32[4,32,128]{2,1,0:T(8,128)S(1)}, u32[]{:S(2)}, u32[]{:S(2)}) collective-permute-start(f32[4,32,128]{2,1,0:T(8,128)S(1)} %get-tuple-element.39), channel_id=1, source_target_pairs={{0,8},{4,12},{8,0},{12,4},{1,9},{5,13},{9,1},{13,5},{2,10},{6,14},... | collective-permute-start | bytes 196616 | tf_op jit(solution)/shard_map/ppermute | solution.py:17
  70.5 2.4 %collective-permute-done.8 = f32[4,32,128]{2,1,0:T(8,128)S(1)} collective-permute-done((f32[4,32,128]{2,1,0:T(8,128)S(1)}, f32[4,32,128]{2,1,0:T(8,128)S(1)}, u32[]{:S(2)}, u32[]{:S(2)}) %collective-permute-start.8) | collective-permute-done | bytes 65568 | tf_op jit(solution)/shard_map/ppermute | solution.py:17
  72.9 1.6 %collective-permute-done.7 = f32[4,32,128]{2,1,0:T(8,128)S(1)} collective-permute-done((f32[4,32,128]{2,1,0:T(8,128)S(1)}, f32[4,32,128]{2,1,0:T(8,128)S(1)}, u32[]{:S(2)}, u32[]{:S(2)}) %collective-permute-start.7) | collective-permute-done | bytes 65568 | tf_op jit(solution)/shard_map/ppermute | solution.py:17
  75.0 1.8 %collective-permute-start.9 = (f32[4,32,128]{2,1,0:T(8,128)S(1)}, f32[4,32,128]{2,1,0:T(8,128)S(1)}, u32[]{:S(2)}, u32[]{:S(2)}) collective-permute-start(f32[4,32,128]{2,1,0:T(8,128)S(1)} %fusion.16), channel_id=1, source_target_pairs={{0,2},{1,3},{2,0},{3,1},{4,6},{5,7},{6,4},{7,5},{8,10},{9,11},{10,... | collective-permute-start | bytes 196616 | tf_op jit(solution)/shard_map/ppermute | solution.py:22
  76.8 8.6 %collective-permute-done.3 = bf16[4,32,3584]{2,1,0:T(8,128)(2,1)S(1)} collective-permute-done((bf16[4,32,3584]{2,1,0:T(8,128)(2,1)S(1)}, bf16[4,32,3584]{2,1,0:T(8,128)(2,1)S(1)}, u32[]{:S(2)}, u32[]{:S(2)}) %collective-permute-start.3) | collective-permute-done | bytes 917536 | tf_op jit(solution)/shard_map/ppermute | solution.py:12
  85.6 1.3 %collective-permute-done.10 = f32[2,4,32,128]{3,2,0,1:T(8,128)S(1)} collective-permute-done((f32[2,4,32,128]{3,2,0,1:T(8,128)S(1)}, f32[2,4,32,128]{3,2,0,1:T(8,128)S(1)}, u32[]{:S(2)}, u32[]{:S(2)}) %collective-permute-start.10) | collective-permute-done | bytes 131104 | tf_op jit(solution)/shard_map/ppermute | solution.py:22
  86.8 0.7 fusion.13
  87.6 0.9 %copy.85 = bf16[1,4,32,3584]{3,2,1,0:T(8,128)(2,1)} copy(bf16[1,4,32,3584]{3,2,1,0:T(8,128)(2,1)S(1)} %bitcast.138) | data formatting | bytes 1835008
  (70 shorter events, 5.9 us)
Async XLA Ops:
  2.4 1.3 %collective-permute-start = (bf16[65544]{0:T(1024)(128)(2,1)S(1)}, bf16[65544]{0:T(1024)(128)(2,1)S(1)}, u32[]{:S(2)}, u32[]{:S(2)}) collective-permute-start(bf16[65544]{0:T(1024)(128)(2,1)S(1)} %pad_maximum_fusion), channel_id=1, source_target_pairs={{0,0},{13,1},{10,2},{7,3},{4,4},{1,5},{14,6},{11,7},{8,8},{5,9},{2... | collective-permute-start | bytes 393272 | tf_op jit(solution)/shard_map/ppermute | solution.py:76
  3.9 16.5 %collective-permute-start.1 = (bf16[1,65544]{1,0:T(2,128)(2,1)S(1)}, bf16[1,65544]{1,0:T(2,128)(2,1)S(1)}, u32[]{:S(2)}, u32[]{:S(2)}) collective-permute-start(bf16[1,65544]{1,0:T(2,128)(2,1)S(1)} %stack.170), channel_id=1, source_target_pairs={{0,2},{1,3},{2,0},{3,1},{4,6},{5,7},{6,4},{7,5},{8,10},{9,11},{10,... | collective-permute-start | bytes 393272 | tf_op jit(solution)/shard_map/ppermute | solution.py:22
  22.0 26.8 %copy-start = (bf16[1,4,32,3584]{3,2,1,0:T(8,128)(2,1)S(1)}, bf16[1,4,32,3584]{3,2,1,0:T(8,128)(2,1)}, u32[]{:S(2)}) copy-start(bf16[1,4,32,3584]{3,2,1,0:T(8,128)(2,1)} %param.7) | copy-start | bytes 2752516
  22.3 1.6 %collective-permute-start.2 = (bf16[2,1,65544]{2,0,1:T(2,128)(2,1)S(1)}, bf16[2,1,65544]{2,0,1:T(2,128)(2,1)S(1)}, u32[]{:S(2)}, u32[]{:S(2)}) collective-permute-start(bf16[2,1,65544]{2,0,1:T(2,128)(2,1)S(1)} %copy.30), channel_id=1, source_target_pairs={{0,1},{1,0},{2,3},{3,2},{4,5},{5,4},{6,7},{7,6},{8,9},{9,8},{10,11... | collective-permute-start | bytes 786536 | tf_op jit(solution)/shard_map/ppermute | solution.py:22
  55.2 2.0 %collective-permute-start.4 = (f32[4,4,2,32,128]{4,3,2,1,0:T(8,128)S(1)}, f32[4,4,2,32,128]{4,3,2,1,0:T(8,128)S(1)}, u32[]{:S(2)}, u32[]{:S(2)}) collective-permute-start(f32[4,4,2,32,128]{4,3,2,1,0:T(8,128)S(1)} %dynamic-slice_bitcast_fusion), channel_id=1, source_target_pairs={{0,1},{1,0},{2,3},{3,2},{4,5},{5,4},{6,7},{7,6},{8,9},{9,8},{10,11... | collective-permute-start | bytes 1572872 | tf_op jit(solution)/shard_map/ppermute | solution.py:22
  57.3 8.4 %collective-permute-start.5 = (f32[4,4,32,128]{3,2,1,0:T(8,128)S(1)}, f32[4,4,32,128]{3,2,1,0:T(8,128)S(1)}, u32[]{:S(2)}, u32[]{:S(2)}) collective-permute-start(f32[4,4,32,128]{3,2,1,0:T(8,128)S(1)} %dynamic-slice_bitcast_fusion.1), channel_id=1, source_target_pairs={{0,2},{1,3},{2,0},{3,1},{4,6},{5,7},{6,4},{7,5},{8,10},{9,11},{10,... | collective-permute-start | bytes 786440 | tf_op jit(solution)/shard_map/ppermute | solution.py:22
  61.4 24.0 %collective-permute-start.3 = (bf16[4,32,3584]{2,1,0:T(8,128)(2,1)S(1)}, bf16[4,32,3584]{2,1,0:T(8,128)(2,1)S(1)}, u32[]{:S(2)}, u32[]{:S(2)}) collective-permute-start(bf16[4,32,3584]{2,1,0:T(8,128)(2,1)S(1)} %reshape.568), channel_id=1, source_target_pairs={{16,0},{17,1},{18,2},{19,3},{20,4},{21,5},{22,6},{23,7},{24,8},{25... | collective-permute-start | bytes 2752520 | tf_op jit(solution)/shard_map/ppermute | solution.py:12
  65.8 7.1 %collective-permute-start.8 = (f32[4,32,128]{2,1,0:T(8,128)S(1)}, f32[4,32,128]{2,1,0:T(8,128)S(1)}, u32[]{:S(2)}, u32[]{:S(2)}) collective-permute-start(f32[4,32,128]{2,1,0:T(8,128)S(1)} %get-tuple-element.38), channel_id=1, source_target_pairs={{0,4},{4,8},{8,12},{12,0},{1,5},{5,9},{9,13},{13,1},{2,6},{6,10},{... | collective-permute-start | bytes 196616 | tf_op jit(solution)/shard_map/ppermute | solution.py:17
  66.9 7.6 %collective-permute-start.7 = (f32[4,32,128]{2,1,0:T(8,128)S(1)}, f32[4,32,128]{2,1,0:T(8,128)S(1)}, u32[]{:S(2)}, u32[]{:S(2)}) collective-permute-start(f32[4,32,128]{2,1,0:T(8,128)S(1)} %get-tuple-element.39), channel_id=1, source_target_pairs={{0,8},{4,12},{8,0},{12,4},{1,9},{5,13},{9,1},{13,5},{2,10},{6,14},... | collective-permute-start | bytes 196616 | tf_op jit(solution)/shard_map/ppermute | solution.py:17
  70.5 4.5 %collective-permute-start.6 = (f32[4,32,128]{2,1,0:T(8,128)S(1)}, f32[4,32,128]{2,1,0:T(8,128)S(1)}, u32[]{:S(2)}, u32[]{:S(2)}) collective-permute-start(f32[4,32,128]{2,1,0:T(8,128)S(1)} %get-tuple-element.37), channel_id=1, source_target_pairs={{0,12},{4,0},{8,4},{12,8},{1,13},{5,1},{9,5},{13,9},{2,14},{6,2},{... | collective-permute-start | bytes 196616 | tf_op jit(solution)/shard_map/ppermute | solution.py:17
  75.0 10.4 %collective-permute-start.9 = (f32[4,32,128]{2,1,0:T(8,128)S(1)}, f32[4,32,128]{2,1,0:T(8,128)S(1)}, u32[]{:S(2)}, u32[]{:S(2)}) collective-permute-start(f32[4,32,128]{2,1,0:T(8,128)S(1)} %fusion.16), channel_id=1, source_target_pairs={{0,2},{1,3},{2,0},{3,1},{4,6},{5,7},{6,4},{7,5},{8,10},{9,11},{10,... | collective-permute-start | bytes 196616 | tf_op jit(solution)/shard_map/ppermute | solution.py:22
  85.4 1.4 %collective-permute-start.10 = (f32[2,4,32,128]{3,2,0,1:T(8,128)S(1)}, f32[2,4,32,128]{3,2,0,1:T(8,128)S(1)}, u32[]{:S(2)}, u32[]{:S(2)}) collective-permute-start(f32[2,4,32,128]{3,2,0,1:T(8,128)S(1)} %maximum_select_fusion.1), channel_id=1, source_target_pairs={{0,1},{1,0},{2,3},{3,2},{4,5},{5,4},{6,7},{7,6},{8,9},{9,8},{10,11... | collective-permute-start | bytes 393224 | tf_op jit(solution)/shard_map/ppermute | solution.py:22

commit v3 on v1

--- a/solution.py
+++ b/solution.py
@@ -57,21 +57,32 @@
     chunk = block_size // n_dp
     me_dp = lax.axis_index("dp")
 
-    features = activations[0].reshape(tok_rows, row_count, block_size)
-    hidden_grad = out_grad[0].reshape(tok_rows, col_count, block_size)
     own_blocks = blocks[0]
     blocks_dev = own_blocks.shape[0]
 
-    all_indices = gather_over(pattern[0], "fsdp").reshape(-1, 2)
+    assert n_fsdp % n_dp == 0
+    per_dp = n_fsdp // n_dp
+    weight_len = blocks_dev * block_size * block_size
+    payload = jnp.concatenate(
+        [own_blocks.reshape(-1), pattern[0].reshape(-1).astype(jnp.bfloat16)]
+    )
+    fetched = []
+    for m in range(per_dp):
+        pairs = []
+        for f in range(n_fsdp):
+            for d in range(n_dp):
+                k = d + n_dp * m
+                pairs.append((((f - k) % n_fsdp) * n_dp + d, f * n_dp + d))
+        fetched.append(lax.ppermute(payload, ("fsdp", "dp"), pairs))
+    fetched = jnp.stack(fetched)
+    pieces = butterfly_gather(fetched, "dp", list(reversed(range(dp_bits))))
+    pieces = pieces.reshape((n_dp, per_dp, -1))
+    pieces = jnp.transpose(pieces, (1, 0, 2)).reshape(n_fsdp, -1)
+    weights = pieces[:, :weight_len].reshape(n_fsdp * blocks_dev, block_size, block_size)
+    all_indices = pieces[:, weight_len:].reshape(n_fsdp * blocks_dev, 2).astype(jnp.int32)
 
-    own_chunk = lax.dynamic_slice_in_dim(own_blocks, me_dp * chunk, chunk, 1)
-    fetched = gather_over(own_chunk, "fsdp")
-    gathered = butterfly_gather(fetched, "dp", list(reversed(range(dp_bits))))
-    gathered = gathered.reshape((n_dp, n_fsdp, blocks_dev, chunk, block_size))
-    weights = jnp.transpose(gathered, (1, 2, 0, 3, 4)).reshape(
-        n_fsdp * blocks_dev, block_size, block_size
-    )
-
+    features = activations[0].reshape(tok_rows, row_count, block_size)
+    hidden_grad = out_grad[0].reshape(tok_rows, col_count, block_size)
     row_ids = all_indices[:, 0]
     col_ids = all_indices[:, 1]
     rows_in = jnp.take(features, row_ids, axis=1)

time: 74.2 us -> 73 us (0.984)
  other arithmetic: 3.94 us -> 9.48 us
  waiting for transfers between devices: 23.8 us -> 19.1 us
  starting transfers between devices: 21.5 us -> 19.3 us
  local copies, waits for them, and re-layouts: 19.2 us -> 20.3 us
  matrix products: 4.42 us -> 3.55 us
    ppermute x9 -> x3, starting transfers between devices: 14.8 us -> 5.08 us  [shifted(): return lax.ppermute(x, axis, [(i, (i + k) % n) for i in range(n)])]
    ppermute x6, starting transfers between devices: 5.38 us -> 12.2 us  [swapped(): return lax.ppermute(x, axis, [(i, i ^ 1 << bit) for i in range(n)])]
    ppermute x9 -> x3, waiting for transfers between devices: 7.77 us -> 5.42 us  [shifted(): return lax.ppermute(x, axis, [(i, (i + k) % n) for i in range(n)])]
    select_n x5 -> x3, other arithmetic: 0.13 us -> 1.62 us  [butterfly_gather(): jnp.where(mine_low, jnp.stack([held, other]), jnp.stack([other, held]))]
    ppermute x6, waiting for transfers between devices: 9.98 us -> 8.71 us  [swapped(): return lax.ppermute(x, axis, [(i, i ^ 1 << bit) for i in range(n)])]
    another operation x1 -> x3, local copies, waits for them, and re-layouts: 0.01 us -> 1.18 us  [the longest x1 0.9 us: local(): pieces = jnp.transpose(pieces, (1, 0, 2)).reshape(n_fsdp, -1)]
    another operation x2, other arithmetic: 0.05 us -> 1.2 us  [butterfly_gather(): jnp.stack([held, other])]
    ppermute x1, waiting for transfers between devices: 6.06 us -> 5 us  [passed_along(): return lax.ppermute(block, axis, route)]
  transfers between devices with their start and end apart: 16 -> 11, of which waited for: 8 -> 7; matrix products, arithmetic and copies ran while one was open for 26% -> 22% of each run, Pallas kernels for 0% -> 0%
where the time goes in v3:
time: 73 us; the launch traced here: 72.6 us
  local copies, waits for them, and re-layouts  20.3 us (28%)
  starting transfers between devices  19.3 us (26%)
  waiting for transfers between devices  19.1 us (26%)
  other arithmetic  9.48 us (13%)
  matrix products  3.55 us (5%)
  between operations  0.92 us (1%)
    ppermute x6, starting transfers between devices, swapped(): return lax.ppermute(x, axis, [(i, i ^ 1 << bit) for i in range(n)])  12.2 us
    ppermute x6, waiting for transfers between devices, swapped(): return lax.ppermute(x, axis, [(i, i ^ 1 << bit) for i in range(n)])  8.71 us
    ppermute x3, waiting for transfers between devices, shifted(): return lax.ppermute(x, axis, [(i, (i + k) % n) for i in range(n)])  5.42 us
    ppermute x3, starting transfers between devices, shifted(): return lax.ppermute(x, axis, [(i, (i + k) % n) for i in range(n)])  5.08 us
    ppermute x1, waiting for transfers between devices, passed_along(): return lax.ppermute(block, axis, route)  5 us
    unnamed x2, local copies, waits for them, and re-layouts  3.77 us
    another operation x1, local copies, waits for them, and re-layouts, local(): hidden_grad = out_grad[0].reshape(tok_rows, col_count, block_size)  2.77 us
    gather x1, local copies, waits for them, and re-layouts, local(): hidden_in = jnp.take(hidden_grad, col_ids, axis=1)  2.69 us
  transfers between devices with their start and end apart: 11, of which 7 were waited for; matrix products, arithmetic and copies ran while one was open for 22% of the time, Pallas kernels for 0%

profile of v3, /device:TPU:0, one launch (start us, length us, event | category | flops | bytes accessed | tf_op | source)
XLA Modules:
  0.0 72.6 jit_solution(17571908057759940549)
XLA Ops:
  0.6 0.7 convert_element_type.26
  1.5 0.9 %pad_maximum_fusion = bf16[65544]{0:T(1024)(128)(2,1)S(1)} fusion(bf16[8]{0:T(256)(128)(2,1)S(1)} %convert_element_type.27, bf16[65536]{0:T(1024)(128)(2,1)} %bitcast.93), kind=kLoop, calls=%fused_computation.28 | loop fusion | flops 262176 | bytes 262176 | tf_op jit(solution)/shard_map/concatenate | solution.py:66
  2.4 0.7 collective-permute-start
  3.1 0.7 compare_select_fusion.2
  3.9 11.3 %collective-permute-start.1 = (bf16[1,65544]{1,0:T(2,128)(2,1)S(1)}, bf16[1,65544]{1,0:T(2,128)(2,1)S(1)}, u32[]{:S(2)}, u32[]{:S(2)}) collective-permute-start(bf16[1,65544]{1,0:T(2,128)(2,1)S(1)} %stack.68), channel_id=1, source_target_pairs={{0,2},{1,3},{2,0},{3,1},{4,6},{5,7},{6,4},{7,5},{8,10},{9,11},{10,... | collective-permute-start | bytes 393272 | tf_op jit(solution)/shard_map/ppermute | solution.py:22
  15.2 0.7 compare_and_fusion
  15.9 1.6 %reshape_squeeze.12 = bf16[128,28,128]{2,1,0:T(8,128)(2,1)S(1)} reshape(bf16[1,4,32,3584]{3,2,1,0:T(8,128)(2,1)} %param.5) | data formatting | bytes 1835008 | tf_op jit(solution)/shard_map/reshape;squeeze | solution.py:84
  17.9 2.8 %copy.67 = bf16[16,8,112,128]{3,2,1,0:T(8,128)(2,1)S(1)} copy(bf16[16,8,112,128]{3,1,2,0:T(8,128)(2,1)} %bitcast.82) | data formatting | bytes 7340032
  20.7 2.8 %copy.53 = bf16[128,112,128]{2,0,1:T(8,128)(2,1)} copy(bf16[128,112,128]{2,1,0:T(8,128)(2,1)S(1)} %bitcast.79) | data formatting | bytes 7340032 | tf_op jit(solution)/shard_map/reshape;squeeze | solution.py:85
  23.7 1.6 %broadcast_select_fusion = bf16[2,1,65544]{2,1,0:T(2,128)(2,1)S(1)} fusion(pred[]{:T(512)S(6)} %eq.39, bf16[1,1,65544]{2,1,0:T(2,128)(2,1)S(1)} %bitcast.83, bf16[1,1,65544]{2,1,0:T(2,128)(2,1)S(1)} %stack.67), kind=kLoop, calls=%fused_computation.8 | loop fusion | flops 393264 | bytes 524353 | tf_op jit(solution)/shard_map/jit(_where)/select_n | solution.py:41
  25.6 1.2 %fusion.7 = bf16[1,2,1,65544]{3,1,2,0:T(2,128)(2,1)S(1)} fusion(pred[]{:T(512)S(6)} %eq.39, bf16[1,1,65544]{2,1,0:T(2,128)(2,1)S(1)} %bitcast.84, bf16[1,1,65544]{2,1,0:T(2,128)(2,1)S(1)} %stack.67), kind=kLoop, calls=%fused_computation.23 | loop fusion | flops 1179792 | bytes 524353 | tf_op jit(solution)/shard_map/stack | solution.py:41
  27.2 0.9 %fusion.2 = bf16[2,2,1,65544]{3,0,2,1:T(2,128)(2,1)S(1)} fusion(pred[]{:T(512)S(6)} %eq.38, bf16[1,2,1,65544]{3,1,2,0:T(2,128)(2,1)S(1)} %bitcast.88, bf16[1,2,1,65544]{3,1,2,0:T(2,128)(2,1)S(1)} %fusion.7), kind=kLoop, calls=%fused_computation.13 | loop fusion | flops 786528 | bytes 1048705 | tf_op jit(solution)/shard_map/transpose | solution.py:44
  28.5 0.9 %reshape_transpose_reshape.3 = bf16[4,65544]{1,0:T(4,128)(2,1)S(1)} reshape(bf16[2,2,1,65544]{3,1,0,2:T(2,128)(2,1)S(1)} %copy.52) | data formatting | bytes 1048704 | tf_op jit(solution)/shard_map/reshape;transpose;reshape | solution.py:80
  30.1 0.6 gather_fusion.1
  33.0 2.7 %gather_fusion = bf16[16,128,128]{2,1,0:T(8,128)(2,1)S(1)} fusion(bf16[128,112,128]{2,0,1:T(8,128)(2,1)} %copy.53, s32[1024]{0:T(1024)S(1)} %get-tuple-element.14), kind=kCustom, calls=%fused_computation | custom fusion | bytes 1048640 | tf_op jit(solution)/shard_map/jit(_take)/gather | solution.py:96
  35.7 1.1 %fusion.1 = bf16[128,16,128]{2,1,0:T(8,128)(2,1)S(1)} fusion(f32[128,16,128]{2,1,0:T(8,128)S(1)} %copy.59, bf16[16,128,128]{2,1,0:T(8,128)(2,1)S(1)} %gather_fusion, pred[16]{0:T(512)(128)(4,1)S(1)} %get-tuple-element.6, s32[16]{0:T(128)S(1)} %get-tuple-element.5), kind=kOutput, calls=%fused_computation.11 | convolution fusion | flops 53215488 | bytes 2097232 | tf_op jit(solution)/shard_map/bc,tcn->tbn/dot_general | solution.py:93
  37.1 0.8 %dynamic-slice_bitcast_fusion = f32[4,4,2,32,128]{4,3,2,1,0:T(8,128)} fusion(f32[4,4,2,2,32,128]{5,4,3,2,1,0:T(8,128)S(1)} %bitcast.80, s32[]{:T(128)S(6)} %select_n.140), kind=kLoop, calls=%fused_computation.19 | loop fusion | bytes 1048580 | tf_op jit(solution)/shard_map/jit(dynamic_index_in_dim)/squeeze | solution.py:122
  38.1 0.7 convolution_bitcast_fusion
  39.3 1.1 %fusion = bf16[128,28,128]{2,1,0:T(8,128)(2,1)S(1)} fusion(f32[128,16,128]{2,1,0:T(8,128)S(1)} %copy.61, s32[16]{0:T(128)S(1)} %get-tuple-element.2), kind=kOutput, calls=%fused_computation.4 | convolution fusion | flops 88539584 | bytes 1966144 | tf_op jit(solution)/shard_map/rb,tbk->trk/dot_general | solution.py:105
  40.4 1.4 %reshape.375 = bf16[4,32,3584]{2,1,0:T(8,128)(2,1)} reshape(bf16[128,28,128]{2,1,0:T(8,128)(2,1)S(1)} %fusion) | data formatting | bytes 1835008 | tf_op jit(solution)/shard_map/reshape | solution.py:108
  41.8 1.8 %gather_fusion.2 = bf16[4,32,3584]{2,1,0:T(8,128)(2,1)S(1)} fusion(bf16[4,32,3584]{2,1,0:T(8,128)(2,1)} %reshape.375, s32[1024]{0:T(1024)S(1)} %pad_clamp_fusion), kind=kCustom, calls=%fused_computation.2 | custom fusion | bytes 1835024 | tf_op jit(solution)/shard_map/jit(_take)/gather | solution.py:111
  43.6 1.1 %bitcast_add_fusion = f32[4,4,2,32,128]{4,3,2,1,0:T(8,128)S(1)} fusion(f32[4,4,2,32,128]{4,3,2,1,0:T(8,128)} %collective-permute-done.4, f32[4,4,2,2,32,128]{5,4,3,2,1,0:T(8,128)S(1)} %bitcast.81, s32[]{:T(128)S(6)} %select_n.139), kind=kLoop, calls=%fused_computation.15 | loop fusion | flops 131072 | bytes 1572868 | tf_op jit(solution)/shard_map/add | solution.py:123
  45.0 1.3 %collective-permute-start.3 = (bf16[4,32,3584]{2,1,0:T(8,128)(2,1)S(1)}, bf16[4,32,3584]{2,1,0:T(8,128)(2,1)S(1)}, u32[]{:S(2)}, u32[]{:S(2)}) collective-permute-start(bf16[4,32,3584]{2,1,0:T(8,128)(2,1)S(1)} %broadcast_select_fusion.2), channel_id=1, source_target_pairs={{16,0},{17,1},{18,2},{19,3},{20,4},{21,5},{22,6},{23,7},{24,8},{25... | collective-permute-start | bytes 2752520 | tf_op jit(solution)/shard_map/ppermute | solution.py:12
  46.3 7.1 %collective-permute-done.5 = f32[4,4,32,128]{3,2,1,0:T(8,128)S(1)} collective-permute-done((f32[4,4,32,128]{3,2,1,0:T(8,128)S(1)}, f32[4,4,32,128]{3,2,1,0:T(8,128)S(1)}, u32[]{:S(2)}, u32[]{:S(2)}) %collective-permute-start.5) | collective-permute-done | bytes 262176 | tf_op jit(solution)/shard_map/ppermute | solution.py:22
  53.5 4.4 %collective-permute-start.6 = (f32[4,32,128]{2,1,0:T(8,128)S(1)}, f32[4,32,128]{2,1,0:T(8,128)S(1)}, u32[]{:S(2)}, u32[]{:S(2)}) collective-permute-start(f32[4,32,128]{2,1,0:T(8,128)S(1)} %get-tuple-element.8), channel_id=1, source_target_pairs={{0,12},{4,0},{8,4},{12,8},{1,13},{5,1},{9,5},{13,9},{2,14},{6,2},{... | collective-permute-start | bytes 196616 | tf_op jit(solution)/shard_map/ppermute | solution.py:17
  58.6 1.8 %collective-permute-done.6 = f32[4,32,128]{2,1,0:T(8,128)S(1)} collective-permute-done((f32[4,32,128]{2,1,0:T(8,128)S(1)}, f32[4,32,128]{2,1,0:T(8,128)S(1)}, u32[]{:S(2)}, u32[]{:S(2)}) %collective-permute-start.6) | collective-permute-done | bytes 65568 | tf_op jit(solution)/shard_map/ppermute | solution.py:17
  60.4 2.8 %collective-permute-done.7 = f32[4,32,128]{2,1,0:T(8,128)S(1)} collective-permute-done((f32[4,32,128]{2,1,0:T(8,128)S(1)}, f32[4,32,128]{2,1,0:T(8,128)S(1)}, u32[]{:S(2)}, u32[]{:S(2)}) %collective-permute-start.7) | collective-permute-done | bytes 65568 | tf_op jit(solution)/shard_map/ppermute | solution.py:17
  63.2 0.8 %collective-permute-done.8 = f32[4,32,128]{2,1,0:T(8,128)S(1)} collective-permute-done((f32[4,32,128]{2,1,0:T(8,128)S(1)}, f32[4,32,128]{2,1,0:T(8,128)S(1)}, u32[]{:S(2)}, u32[]{:S(2)}) %collective-permute-start.8) | collective-permute-done | bytes 65568 | tf_op jit(solution)/shard_map/ppermute | solution.py:17
  64.5 5.0 %collective-permute-done.3 = bf16[4,32,3584]{2,1,0:T(8,128)(2,1)S(1)} collective-permute-done((bf16[4,32,3584]{2,1,0:T(8,128)(2,1)S(1)}, bf16[4,32,3584]{2,1,0:T(8,128)(2,1)S(1)}, u32[]{:S(2)}, u32[]{:S(2)}) %collective-permute-start.3) | collective-permute-done | bytes 917536 | tf_op jit(solution)/shard_map/ppermute | solution.py:12
  69.7 1.3 %collective-permute-done.10 = f32[2,4,32,128]{3,2,0,1:T(8,128)S(1)} collective-permute-done((f32[2,4,32,128]{3,2,0,1:T(8,128)S(1)}, f32[2,4,32,128]{3,2,0,1:T(8,128)S(1)}, u32[]{:S(2)}, u32[]{:S(2)}) %collective-permute-start.10) | collective-permute-done | bytes 131104 | tf_op jit(solution)/shard_map/ppermute | solution.py:22
  71.0 0.7 %fusion.8 = f32[2,2,4,32,128]{4,3,0,1,2:T(8,128)} fusion(f32[1,2,4,32,128]{4,3,0,1,2:T(8,128)S(1)} %bitcast.92, f32[1,2,4,32,128]{4,3,0,1,2:T(8,128)S(1)} %copy_select_fusion.2, pred[]{:T(512)S(6)} %eq.38), kind=kLoop, calls=%fused_computation.25 | loop fusion | flops 262144 | bytes 524289 | tf_op jit(solution)/shard_map/div | solution.py:131
  71.7 0.9 %copy.81 = bf16[1,4,32,3584]{3,2,1,0:T(8,128)(2,1)} copy(bf16[1,4,32,3584]{3,2,1,0:T(8,128)(2,1)S(1)} %bitcast.85) | data formatting | bytes 1835008
  (41 shorter events, 7.4 us)
Async XLA Ops:
  2.4 1.3 %collective-permute-start = (bf16[65544]{0:T(1024)(128)(2,1)S(1)}, bf16[65544]{0:T(1024)(128)(2,1)S(1)}, u32[]{:S(2)}, u32[]{:S(2)}) collective-permute-start(bf16[65544]{0:T(1024)(128)(2,1)S(1)} %pad_maximum_fusion), channel_id=1, source_target_pairs={{0,0},{13,1},{10,2},{7,3},{4,4},{1,5},{14,6},{11,7},{8,8},{5,9},{2... | collective-permute-start | bytes 393272 | tf_op jit(solution)/shard_map/ppermute | solution.py:76
  3.9 19.8 %collective-permute-start.1 = (bf16[1,65544]{1,0:T(2,128)(2,1)S(1)}, bf16[1,65544]{1,0:T(2,128)(2,1)S(1)}, u32[]{:S(2)}, u32[]{:S(2)}) collective-permute-start(bf16[1,65544]{1,0:T(2,128)(2,1)S(1)} %stack.68), channel_id=1, source_target_pairs={{0,2},{1,3},{2,0},{3,1},{4,6},{5,7},{6,4},{7,5},{8,10},{9,11},{10,... | collective-permute-start | bytes 393272 | tf_op jit(solution)/shard_map/ppermute | solution.py:22
  25.5 1.6 %collective-permute-start.2 = (bf16[2,1,65544]{2,0,1:T(2,128)(2,1)S(1)}, bf16[2,1,65544]{2,0,1:T(2,128)(2,1)S(1)}, u32[]{:S(2)}, u32[]{:S(2)}) collective-permute-start(bf16[2,1,65544]{2,0,1:T(2,128)(2,1)S(1)} %copy.51), channel_id=1, source_target_pairs={{0,1},{1,0},{2,3},{3,2},{4,5},{5,4},{6,7},{7,6},{8,9},{9,8},{10,11... | collective-permute-start | bytes 786536 | tf_op jit(solution)/shard_map/ppermute | solution.py:22
  38.0 5.7 %collective-permute-start.4 = (f32[4,4,2,32,128]{4,3,2,1,0:T(8,128)}, f32[4,4,2,32,128]{4,3,2,1,0:T(8,128)}, u32[]{:S(2)}, u32[]{:S(2)}) collective-permute-start(f32[4,4,2,32,128]{4,3,2,1,0:T(8,128)} %dynamic-slice_bitcast_fusion), channel_id=1, source_target_pairs={{0,1},{1,0},{2,3},{3,2},{4,5},{5,4},{6,7},{7,6},{8,9},{9,8},{10,11... | collective-permute-start | bytes 1572872 | tf_op jit(solution)/shard_map/ppermute | solution.py:22
  44.8 8.6 %collective-permute-start.5 = (f32[4,4,32,128]{3,2,1,0:T(8,128)S(1)}, f32[4,4,32,128]{3,2,1,0:T(8,128)S(1)}, u32[]{:S(2)}, u32[]{:S(2)}) collective-permute-start(f32[4,4,32,128]{3,2,1,0:T(8,128)S(1)} %dynamic-slice_bitcast_fusion.1), channel_id=1, source_target_pairs={{0,2},{1,3},{2,0},{3,1},{4,6},{5,7},{6,4},{7,5},{8,10},{9,11},{10,... | collective-permute-start | bytes 786440 | tf_op jit(solution)/shard_map/ppermute | solution.py:22
  45.0 24.5 %collective-permute-start.3 = (bf16[4,32,3584]{2,1,0:T(8,128)(2,1)S(1)}, bf16[4,32,3584]{2,1,0:T(8,128)(2,1)S(1)}, u32[]{:S(2)}, u32[]{:S(2)}) collective-permute-start(bf16[4,32,3584]{2,1,0:T(8,128)(2,1)S(1)} %broadcast_select_fusion.2), channel_id=1, source_target_pairs={{16,0},{17,1},{18,2},{19,3},{20,4},{21,5},{22,6},{23,7},{24,8},{25... | collective-permute-start | bytes 2752520 | tf_op jit(solution)/shard_map/ppermute | solution.py:12
  53.5 6.9 %collective-permute-start.6 = (f32[4,32,128]{2,1,0:T(8,128)S(1)}, f32[4,32,128]{2,1,0:T(8,128)S(1)}, u32[]{:S(2)}, u32[]{:S(2)}) collective-permute-start(f32[4,32,128]{2,1,0:T(8,128)S(1)} %get-tuple-element.8), channel_id=1, source_target_pairs={{0,12},{4,0},{8,4},{12,8},{1,13},{5,1},{9,5},{13,9},{2,14},{6,2},{... | collective-permute-start | bytes 196616 | tf_op jit(solution)/shard_map/ppermute | solution.py:17
  57.9 5.3 %collective-permute-start.7 = (f32[4,32,128]{2,1,0:T(8,128)S(1)}, f32[4,32,128]{2,1,0:T(8,128)S(1)}, u32[]{:S(2)}, u32[]{:S(2)}) collective-permute-start(f32[4,32,128]{2,1,0:T(8,128)S(1)} %get-tuple-element.10), channel_id=1, source_target_pairs={{0,8},{4,12},{8,0},{12,4},{1,9},{5,13},{9,1},{13,5},{2,10},{6,14},... | collective-permute-start | bytes 196616 | tf_op jit(solution)/shard_map/ppermute | solution.py:17
  57.9 6.1 %collective-permute-start.8 = (f32[4,32,128]{2,1,0:T(8,128)S(1)}, f32[4,32,128]{2,1,0:T(8,128)S(1)}, u32[]{:S(2)}, u32[]{:S(2)}) collective-permute-start(f32[4,32,128]{2,1,0:T(8,128)S(1)} %get-tuple-element.9), channel_id=1, source_target_pairs={{0,4},{4,8},{8,12},{12,0},{1,5},{5,9},{9,13},{13,1},{2,6},{6,10},{... | collective-permute-start | bytes 196616 | tf_op jit(solution)/shard_map/ppermute | solution.py:17
  64.0 5.5 %collective-permute-start.9 = (f32[4,32,128]{2,1,0:T(8,128)S(1)}, f32[4,32,128]{2,1,0:T(8,128)S(1)}, u32[]{:S(2)}, u32[]{:S(2)}) collective-permute-start(f32[4,32,128]{2,1,0:T(8,128)S(1)} %fusion.11), channel_id=1, source_target_pairs={{0,2},{1,3},{2,0},{3,1},{4,6},{5,7},{6,4},{7,5},{8,10},{9,11},{10,... | collective-permute-start | bytes 196616 | tf_op jit(solution)/shard_map/ppermute | solution.py:22
  69.6 1.4 %collective-permute-start.10 = (f32[2,4,32,128]{3,2,0,1:T(8,128)S(1)}, f32[2,4,32,128]{3,2,0,1:T(8,128)S(1)}, u32[]{:S(2)}, u32[]{:S(2)}) collective-permute-start(f32[2,4,32,128]{3,2,0,1:T(8,128)S(1)} %maximum_select_fusion.1), channel_id=1, source_target_pairs={{0,1},{1,0},{2,3},{3,2},{4,5},{5,4},{6,7},{7,6},{8,9},{9,8},{10,11... | collective-permute-start | bytes 393224 | tf_op jit(solution)/shard_map/ppermute | solution.py:22

commit v4 on v3

--- a/solution.py
+++ b/solution.py
@@ -105,11 +105,9 @@
     input_grad = jnp.einsum(
         "rb,tbk->trk", row_hit, backward, precision=lax.Precision.HIGHEST
     )
-    input_grad = input_grad.astype(jnp.bfloat16).reshape(
-        micro_count, activations.shape[2], activations.shape[3]
-    )
-    ordered = jnp.take(input_grad, order, axis=0)
-    received = passed_along(ordered, "section", -1)
+    arrived = passed_along(input_grad.astype(jnp.bfloat16), "section", -1)
+    arrived = arrived.reshape(micro_count, activations.shape[2], activations.shape[3])
+    received = jnp.take(arrived, order, axis=0)
 
     partial = jnp.einsum(
         "tbk,tbn->bkn", rows_in, act_cols, preferred_element_type=jnp.float32

time: 73 us -> 72.7 us (level)
  local copies, waits for them, and re-layouts: 20.3 us -> 18.7 us
  matrix products: 3.55 us -> 4.59 us
    ppermute x6, waiting for transfers between devices: 8.71 us -> 7.35 us  [swapped(): return lax.ppermute(x, axis, [(i, i ^ 1 << bit) for i in range(n)])]
    ppermute x1, waiting for transfers between devices: 5 us -> 6.34 us  [passed_along(): return lax.ppermute(block, axis, route)]
    gather x1, local copies, waits for them, and re-layouts: 1.78 us -> 0.61 us  [local(): received = jnp.take(arrived, order, axis=0)]
    dot_general x1, matrix products: 0.66 us -> 1.7 us  [local(): jnp.einsum('tbn,bkn->tbk', act_cols, weights, preferred_element_type=jnp....]
    reshape x1, local copies, waits for them, and re-layouts: 1.41 us -> 0.49 us  [local(): arrived.reshape(micro_count, activations.shape[2], activations.shape[3])]
    unnamed x2 -> x5, local copies, waits for them, and re-layouts: 3.77 us -> 3.34 us
  transfers between devices with their start and end apart: 11 -> 11, of which waited for: 7 -> 7; matrix products, arithmetic and copies ran while one was open for 22% -> 21% of each run, Pallas kernels for 0% -> 0%
where the time goes in v4:
time: 72.7 us; the launch traced here: 72.4 us
  starting transfers between devices  19.9 us (27%)
  waiting for transfers between devices  19.1 us (26%)
  local copies, waits for them, and re-layouts  18.7 us (26%)
  other arithmetic  9.09 us (13%)
  matrix products  4.59 us (6%)
  between operations  0.97 us (1%)
    ppermute x6, starting transfers between devices, swapped(): return lax.ppermute(x, axis, [(i, i ^ 1 << bit) for i in range(n)])  12.9 us
    ppermute x6, waiting for transfers between devices, swapped(): return lax.ppermute(x, axis, [(i, i ^ 1 << bit) for i in range(n)])  7.35 us
    ppermute x1, waiting for transfers between devices, passed_along(): return lax.ppermute(block, axis, route)  6.34 us
    ppermute x3, waiting for transfers between devices, shifted(): return lax.ppermute(x, axis, [(i, (i + k) % n) for i in range(n)])  5.42 us
    ppermute x3, starting transfers between devices, shifted(): return lax.ppermute(x, axis, [(i, (i + k) % n) for i in range(n)])  5.08 us
    unnamed x5, local copies, waits for them, and re-layouts  3.34 us
    another operation x1, local copies, waits for them, and re-layouts, local(): hidden_grad = out_grad[0].reshape(tok_rows, col_count, block_size)  2.76 us
    gather x1, local copies, waits for them, and re-layouts, local(): hidden_in = jnp.take(hidden_grad, col_ids, axis=1)  2.69 us
  transfers between devices with their start and end apart: 11, of which 7 were waited for; matrix products, arithmetic and copies ran while one was open for 21% of the time, Pallas kernels for 0%

profile of v4, /device:TPU:0, one launch (start us, length us, event | category | flops | bytes accessed | tf_op | source)
XLA Modules:
  0.0 72.4 jit_solution(10813592726025845470)
XLA Ops:
  0.6 0.7 convert_element_type.26
  1.5 0.9 %pad_maximum_fusion = bf16[65544]{0:T(1024)(128)(2,1)S(1)} fusion(bf16[8]{0:T(256)(128)(2,1)S(1)} %convert_element_type.27, bf16[65536]{0:T(1024)(128)(2,1)} %bitcast.93), kind=kLoop, calls=%fused_computation.28 | loop fusion | flops 262176 | bytes 262176 | tf_op jit(solution)/shard_map/concatenate | solution.py:66
  2.4 0.7 collective-permute-start
  3.3 12.0 %collective-permute-start.1 = (bf16[1,65544]{1,0:T(2,128)(2,1)S(1)}, bf16[1,65544]{1,0:T(2,128)(2,1)S(1)}, u32[]{:S(2)}, u32[]{:S(2)}) collective-permute-start(bf16[1,65544]{1,0:T(2,128)(2,1)S(1)} %stack.68), channel_id=1, source_target_pairs={{0,2},{1,3},{2,0},{3,1},{4,6},{5,7},{6,4},{7,5},{8,10},{9,11},{10,... | collective-permute-start | bytes 393272 | tf_op jit(solution)/shard_map/ppermute | solution.py:22
  15.2 1.6 %reshape_squeeze.12 = bf16[128,28,128]{2,1,0:T(8,128)(2,1)S(1)} reshape(bf16[1,4,32,3584]{3,2,1,0:T(8,128)(2,1)} %param.5) | data formatting | bytes 1835008 | tf_op jit(solution)/shard_map/reshape;squeeze | solution.py:84
  17.2 2.8 %copy.69 = bf16[16,8,112,128]{3,2,1,0:T(8,128)(2,1)S(1)} copy(bf16[16,8,112,128]{3,1,2,0:T(8,128)(2,1)} %bitcast.83) | data formatting | bytes 7340032
  20.1 2.8 %copy.53 = bf16[128,112,128]{2,0,1:T(8,128)(2,1)} copy(bf16[128,112,128]{2,1,0:T(8,128)(2,1)S(1)} %bitcast.80) | data formatting | bytes 7340032 | tf_op jit(solution)/shard_map/reshape;squeeze | solution.py:85
  23.0 1.6 %broadcast_select_fusion = bf16[2,1,65544]{2,1,0:T(2,128)(2,1)S(1)} fusion(pred[]{:T(512)S(6)} %eq.39, bf16[1,1,65544]{2,1,0:T(2,128)(2,1)S(1)} %bitcast.84, bf16[1,1,65544]{2,1,0:T(2,128)(2,1)S(1)} %stack.67), kind=kLoop, calls=%fused_computation.8 | loop fusion | flops 393264 | bytes 524353 | tf_op jit(solution)/shard_map/jit(_where)/select_n | solution.py:41
  25.0 1.2 %fusion.7 = bf16[1,2,1,65544]{3,1,2,0:T(2,128)(2,1)S(1)} fusion(pred[]{:T(512)S(6)} %eq.39, bf16[1,1,65544]{2,1,0:T(2,128)(2,1)S(1)} %bitcast.85, bf16[1,1,65544]{2,1,0:T(2,128)(2,1)S(1)} %stack.67), kind=kLoop, calls=%fused_computation.23 | loop fusion | flops 1179792 | bytes 524353 | tf_op jit(solution)/shard_map/stack | solution.py:41
  26.5 0.9 %fusion.2 = bf16[2,2,1,65544]{3,0,2,1:T(2,128)(2,1)S(1)} fusion(pred[]{:T(512)S(6)} %eq.38, bf16[1,2,1,65544]{3,1,2,0:T(2,128)(2,1)S(1)} %bitcast.88, bf16[1,2,1,65544]{3,1,2,0:T(2,128)(2,1)S(1)} %fusion.7), kind=kLoop, calls=%fused_computation.13 | loop fusion | flops 786528 | bytes 1048705 | tf_op jit(solution)/shard_map/transpose | solution.py:44
  27.8 0.9 %reshape_transpose_reshape.3 = bf16[4,65544]{1,0:T(4,128)(2,1)S(1)} reshape(bf16[2,2,1,65544]{3,1,0,2:T(2,128)(2,1)S(1)} %copy.52) | data formatting | bytes 1048704 | tf_op jit(solution)/shard_map/reshape;transpose;reshape | solution.py:80
  29.4 0.6 gather_fusion.1
  30.9 0.5 reshape.381
  32.3 2.7 %gather_fusion = bf16[16,128,128]{2,1,0:T(8,128)(2,1)S(1)} fusion(bf16[128,112,128]{2,0,1:T(8,128)(2,1)} %copy.53, s32[1024]{0:T(1024)S(1)} %get-tuple-element.14), kind=kCustom, calls=%fused_computation | custom fusion | bytes 1048640 | tf_op jit(solution)/shard_map/jit(_take)/gather | solution.py:96
  35.0 1.1 %fusion.1 = bf16[128,16,128]{2,1,0:T(8,128)(2,1)S(1)} fusion(f32[128,16,128]{2,1,0:T(8,128)S(1)} %copy.59, bf16[16,128,128]{2,1,0:T(8,128)(2,1)S(1)} %gather_fusion, pred[16]{0:T(512)(128)(4,1)S(1)} %get-tuple-element.6, s32[16]{0:T(128)S(1)} %get-tuple-element.5), kind=kOutput, calls=%fused_computation.11 | convolution fusion | flops 53215488 | bytes 2097232 | tf_op jit(solution)/shard_map/bc,tcn->tbn/dot_general | solution.py:93
  37.0 0.8 %dynamic-slice_bitcast_fusion = f32[4,4,2,32,128]{4,3,2,1,0:T(8,128)} fusion(f32[4,4,2,2,32,128]{5,4,3,2,1,0:T(8,128)S(1)} %bitcast.81, s32[]{:T(128)S(6)} %select_n.147), kind=kLoop, calls=%fused_computation.19 | loop fusion | bytes 1048580 | tf_op jit(solution)/shard_map/jit(dynamic_index_in_dim)/squeeze | solution.py:120
  38.0 1.7 %convolution_bitcast_fusion = f32[128,16,128]{0,2,1:T(8,128)S(1)} fusion(bf16[16,128,128]{2,1,0:T(8,128)(2,1)S(1)} %reshape.381, bf16[128,16,128]{2,1,0:T(8,128)(2,1)} %copy-done), kind=kOutput, calls=%fused_computation.5 | convolution fusion | flops 67108864 | bytes 2097152 | tf_op jit(solution)/shard_map/tbn,bkn->tbk/dot_general | solution.py:99
  40.2 1.1 %bitcast_add_fusion = f32[4,4,2,32,128]{4,3,2,1,0:T(8,128)S(1)} fusion(f32[4,4,2,32,128]{4,3,2,1,0:T(8,128)} %collective-permute-done.4, f32[4,4,2,2,32,128]{5,4,3,2,1,0:T(8,128)S(1)} %bitcast.82, s32[]{:T(128)S(6)} %select_n.146), kind=kLoop, calls=%fused_computation.15 | loop fusion | flops 131072 | bytes 1572868 | tf_op jit(solution)/shard_map/add | solution.py:121
  41.5 1.1 %fusion = bf16[128,28,128]{2,1,0:T(8,128)(2,1)S(1)} fusion(f32[128,16,128]{2,1,0:T(8,128)S(1)} %copy.61, s32[16]{0:T(128)S(1)} %get-tuple-element.2), kind=kOutput, calls=%fused_computation.4 | convolution fusion | flops 88539584 | bytes 1966144 | tf_op jit(solution)/shard_map/rb,tbk->trk/dot_general | solution.py:105
  42.9 1.3 %collective-permute-start.3 = (bf16[128,28,128]{2,0,1:T(8,128)(2,1)S(1)}, bf16[128,28,128]{2,0,1:T(8,128)(2,1)S(1)}, u32[]{:S(2)}, u32[]{:S(2)}) collective-permute-start(bf16[128,28,128]{2,0,1:T(8,128)(2,1)S(1)} %copy.62), channel_id=1, source_target_pairs={{16,0},{17,1},{18,2},{19,3},{20,4},{21,5},{22,6},{23,7},{24,8},{25... | collective-permute-start | bytes 2752520 | tf_op jit(solution)/shard_map/ppermute | solution.py:12
  44.2 5.7 %collective-permute-done.5 = f32[4,4,32,128]{3,2,1,0:T(8,128)S(1)} collective-permute-done((f32[4,4,32,128]{3,2,1,0:T(8,128)S(1)}, f32[4,4,32,128]{3,2,1,0:T(8,128)S(1)}, u32[]{:S(2)}, u32[]{:S(2)}) %collective-permute-start.5) | collective-permute-done | bytes 262176 | tf_op jit(solution)/shard_map/ppermute | solution.py:22
  50.0 4.4 %collective-permute-start.6 = (f32[4,32,128]{2,1,0:T(8,128)S(1)}, f32[4,32,128]{2,1,0:T(8,128)S(1)}, u32[]{:S(2)}, u32[]{:S(2)}) collective-permute-start(f32[4,32,128]{2,1,0:T(8,128)S(1)} %get-tuple-element.8), channel_id=1, source_target_pairs={{0,12},{4,0},{8,4},{12,8},{1,13},{5,1},{9,5},{13,9},{2,14},{6,2},{... | collective-permute-start | bytes 196616 | tf_op jit(solution)/shard_map/ppermute | solution.py:17
  54.5 0.6 collective-permute-start.8
  55.1 1.8 %collective-permute-done.6 = f32[4,32,128]{2,1,0:T(8,128)S(1)} collective-permute-done((f32[4,32,128]{2,1,0:T(8,128)S(1)}, f32[4,32,128]{2,1,0:T(8,128)S(1)}, u32[]{:S(2)}, u32[]{:S(2)}) %collective-permute-start.6) | collective-permute-done | bytes 65568 | tf_op jit(solution)/shard_map/ppermute | solution.py:17
  56.9 2.8 %collective-permute-done.7 = f32[4,32,128]{2,1,0:T(8,128)S(1)} collective-permute-done((f32[4,32,128]{2,1,0:T(8,128)S(1)}, f32[4,32,128]{2,1,0:T(8,128)S(1)}, u32[]{:S(2)}, u32[]{:S(2)}) %collective-permute-start.7) | collective-permute-done | bytes 65568 | tf_op jit(solution)/shard_map/ppermute | solution.py:17
  59.7 0.8 %collective-permute-done.8 = f32[4,32,128]{2,1,0:T(8,128)S(1)} collective-permute-done((f32[4,32,128]{2,1,0:T(8,128)S(1)}, f32[4,32,128]{2,1,0:T(8,128)S(1)}, u32[]{:S(2)}, u32[]{:S(2)}) %collective-permute-start.8) | collective-permute-done | bytes 65568 | tf_op jit(solution)/shard_map/ppermute | solution.py:17
  61.1 6.3 %collective-permute-done.3 = bf16[128,28,128]{2,0,1:T(8,128)(2,1)S(1)} collective-permute-done((bf16[128,28,128]{2,0,1:T(8,128)(2,1)S(1)}, bf16[128,28,128]{2,0,1:T(8,128)(2,1)S(1)}, u32[]{:S(2)}, u32[]{:S(2)}) %collective-permute-start.3) | collective-permute-done | bytes 917536 | tf_op jit(solution)/shard_map/ppermute | solution.py:12
  67.4 0.6 copy.63
  68.5 0.6 gather_fusion.2
  69.1 1.1 %bitcast_select_fusion = bf16[1,4,32,3584]{3,2,1,0:T(8,128)(2,1)} fusion(bf16[4,32,3584]{2,1,0:T(8,128)(2,1)S(1)} %gather_fusion.2, pred[4]{0:T(512)(128)(4,1)S(1)} %compare_and_fusion), kind=kLoop, calls=%fused_computation.12 | loop fusion | flops 458752 | bytes 1835012 | tf_op jit(solution)/shard_map/jit(_take)/select_n | solution.py:110
  70.4 1.3 %collective-permute-done.10 = f32[2,4,32,128]{3,2,0,1:T(8,128)S(1)} collective-permute-done((f32[2,4,32,128]{3,2,0,1:T(8,128)S(1)}, f32[2,4,32,128]{3,2,0,1:T(8,128)S(1)}, u32[]{:S(2)}, u32[]{:S(2)}) %collective-permute-start.10) | collective-permute-done | bytes 131104 | tf_op jit(solution)/shard_map/ppermute | solution.py:22
  71.6 0.7 %fusion.8 = f32[2,2,4,32,128]{4,3,0,1,2:T(8,128)} fusion(f32[1,2,4,32,128]{4,3,0,1,2:T(8,128)S(1)} %bitcast.92, f32[1,2,4,32,128]{4,3,0,1,2:T(8,128)S(1)} %copy_select_fusion.2, pred[]{:T(512)S(6)} %eq.38), kind=kLoop, calls=%fused_computation.25 | loop fusion | flops 262144 | bytes 524289 | tf_op jit(solution)/shard_map/div | solution.py:129
  (46 shorter events, 7.4 us)
Async XLA Ops:
  2.4 0.7 collective-permute-start
  3.3 19.7 %collective-permute-start.1 = (bf16[1,65544]{1,0:T(2,128)(2,1)S(1)}, bf16[1,65544]{1,0:T(2,128)(2,1)S(1)}, u32[]{:S(2)}, u32[]{:S(2)}) collective-permute-start(bf16[1,65544]{1,0:T(2,128)(2,1)S(1)} %stack.68), channel_id=1, source_target_pairs={{0,2},{1,3},{2,0},{3,1},{4,6},{5,7},{6,4},{7,5},{8,10},{9,11},{10,... | collective-permute-start | bytes 393272 | tf_op jit(solution)/shard_map/ppermute | solution.py:22
  24.9 1.6 %collective-permute-start.2 = (bf16[2,1,65544]{2,0,1:T(2,128)(2,1)S(1)}, bf16[2,1,65544]{2,0,1:T(2,128)(2,1)S(1)}, u32[]{:S(2)}, u32[]{:S(2)}) collective-permute-start(bf16[2,1,65544]{2,0,1:T(2,128)(2,1)S(1)} %copy.51), channel_id=1, source_target_pairs={{0,1},{1,0},{2,3},{3,2},{4,5},{5,4},{6,7},{7,6},{8,9},{9,8},{10,11... | collective-permute-start | bytes 786536 | tf_op jit(solution)/shard_map/ppermute | solution.py:22
  35.0 2.9 %copy-start.1 = (s32[4]{0:T(128)S(1)}, s32[4]{0:T(128)}, u32[]{:S(2)}) copy-start(s32[4]{0:T(128)} %param.9) | copy-start | bytes 52
  36.2 0.8 %copy-start = (bf16[128,16,128]{2,1,0:T(8,128)(2,1)}, bf16[128,16,128]{2,1,0:T(8,128)(2,1)S(1)}, u32[]{:S(2)}) copy-start(bf16[128,16,128]{2,1,0:T(8,128)(2,1)S(1)} %fusion.1) | copy-start | bytes 1572868
  37.8 2.4 %collective-permute-start.4 = (f32[4,4,2,32,128]{4,3,2,1,0:T(8,128)}, f32[4,4,2,32,128]{4,3,2,1,0:T(8,128)}, u32[]{:S(2)}, u32[]{:S(2)}) collective-permute-start(f32[4,4,2,32,128]{4,3,2,1,0:T(8,128)} %dynamic-slice_bitcast_fusion), channel_id=1, source_target_pairs={{0,1},{1,0},{2,3},{3,2},{4,5},{5,4},{6,7},{7,6},{8,9},{9,8},{10,11... | collective-permute-start | bytes 1572872 | tf_op jit(solution)/shard_map/ppermute | solution.py:22
  41.4 8.6 %collective-permute-start.5 = (f32[4,4,32,128]{3,2,1,0:T(8,128)S(1)}, f32[4,4,32,128]{3,2,1,0:T(8,128)S(1)}, u32[]{:S(2)}, u32[]{:S(2)}) collective-permute-start(f32[4,4,32,128]{3,2,1,0:T(8,128)S(1)} %dynamic-slice_bitcast_fusion.1), channel_id=1, source_target_pairs={{0,2},{1,3},{2,0},{3,1},{4,6},{5,7},{6,4},{7,5},{8,10},{9,11},{10,... | collective-permute-start | bytes 786440 | tf_op jit(solution)/shard_map/ppermute | solution.py:22
  42.9 24.5 %collective-permute-start.3 = (bf16[128,28,128]{2,0,1:T(8,128)(2,1)S(1)}, bf16[128,28,128]{2,0,1:T(8,128)(2,1)S(1)}, u32[]{:S(2)}, u32[]{:S(2)}) collective-permute-start(bf16[128,28,128]{2,0,1:T(8,128)(2,1)S(1)} %copy.62), channel_id=1, source_target_pairs={{16,0},{17,1},{18,2},{19,3},{20,4},{21,5},{22,6},{23,7},{24,8},{25... | collective-permute-start | bytes 2752520 | tf_op jit(solution)/shard_map/ppermute | solution.py:12
  50.0 6.9 %collective-permute-start.6 = (f32[4,32,128]{2,1,0:T(8,128)S(1)}, f32[4,32,128]{2,1,0:T(8,128)S(1)}, u32[]{:S(2)}, u32[]{:S(2)}) collective-permute-start(f32[4,32,128]{2,1,0:T(8,128)S(1)} %get-tuple-element.8), channel_id=1, source_target_pairs={{0,12},{4,0},{8,4},{12,8},{1,13},{5,1},{9,5},{13,9},{2,14},{6,2},{... | collective-permute-start | bytes 196616 | tf_op jit(solution)/shard_map/ppermute | solution.py:17
  54.5 5.3 %collective-permute-start.7 = (f32[4,32,128]{2,1,0:T(8,128)S(1)}, f32[4,32,128]{2,1,0:T(8,128)S(1)}, u32[]{:S(2)}, u32[]{:S(2)}) collective-permute-start(f32[4,32,128]{2,1,0:T(8,128)S(1)} %get-tuple-element.10), channel_id=1, source_target_pairs={{0,8},{4,12},{8,0},{12,4},{1,9},{5,13},{9,1},{13,5},{2,10},{6,14},... | collective-permute-start | bytes 196616 | tf_op jit(solution)/shard_map/ppermute | solution.py:17
  54.5 6.1 %collective-permute-start.8 = (f32[4,32,128]{2,1,0:T(8,128)S(1)}, f32[4,32,128]{2,1,0:T(8,128)S(1)}, u32[]{:S(2)}, u32[]{:S(2)}) collective-permute-start(f32[4,32,128]{2,1,0:T(8,128)S(1)} %get-tuple-element.9), channel_id=1, source_target_pairs={{0,4},{4,8},{8,12},{12,0},{1,5},{5,9},{9,13},{13,1},{2,6},{6,10},{... | collective-permute-start | bytes 196616 | tf_op jit(solution)/shard_map/ppermute | solution.py:17
  60.6 9.6 %collective-permute-start.9 = (f32[4,32,128]{2,1,0:T(8,128)S(1)}, f32[4,32,128]{2,1,0:T(8,128)S(1)}, u32[]{:S(2)}, u32[]{:S(2)}) collective-permute-start(f32[4,32,128]{2,1,0:T(8,128)S(1)} %fusion.11), channel_id=1, source_target_pairs={{0,2},{1,3},{2,0},{3,1},{4,6},{5,7},{6,4},{7,5},{8,10},{9,11},{10,... | collective-permute-start | bytes 196616 | tf_op jit(solution)/shard_map/ppermute | solution.py:22
  70.2 1.4 %collective-permute-start.10 = (f32[2,4,32,128]{3,2,0,1:T(8,128)S(1)}, f32[2,4,32,128]{3,2,0,1:T(8,128)S(1)}, u32[]{:S(2)}, u32[]{:S(2)}) collective-permute-start(f32[2,4,32,128]{3,2,0,1:T(8,128)S(1)} %maximum_select_fusion.1), channel_id=1, source_target_pairs={{0,1},{1,0},{2,3},{3,2},{4,5},{5,4},{6,7},{7,6},{8,9},{9,8},{10,11... | collective-permute-start | bytes 393224 | tf_op jit(solution)/shard_map/ppermute | solution.py:22

commit v5 on v4

--- a/solution.py
+++ b/solution.py
@@ -118,10 +118,13 @@
         mine = (me_dp >> bit) & 1
         keep = lax.dynamic_index_in_dim(held, mine, axis_at, keepdims=False)
         send = lax.dynamic_index_in_dim(held, 1 - mine, axis_at, keepdims=False)
-        held = keep + swapped(send, "dp", bit)
+        if bit == 0:
+            held = keep + swapped(send, "dp", bit)
+        else:
+            held = keep + swapped(send.astype(jnp.bfloat16), "dp", bit).astype(jnp.float32)
     owned = held[0]
     for k in range(1, n_fsdp):
-        owned = owned + shifted(held[k], "fsdp", -k)
+        owned = owned + shifted(held[k].astype(jnp.bfloat16), "fsdp", -k).astype(jnp.float32)
     full = butterfly_gather(owned, "dp", list(reversed(range(dp_bits))))
     full = full.reshape((n_dp, blocks_dev, chunk, block_size))
     full = jnp.transpose(full, (1, 0, 2, 3)).reshape(blocks_dev, block_size, block_size)

time: 72.7 us -> 69.8 us (0.960)
  matrix products: 4.59 us -> 3.37 us
  waiting for transfers between devices: 19.1 us -> 18 us
  other arithmetic: 9.09 us -> 8.36 us
    ppermute x1, waiting for transfers between devices: 6.34 us -> 3.45 us  [passed_along(): return lax.ppermute(block, axis, route)]
    ppermute x6, waiting for transfers between devices: 7.35 us -> 9.44 us  [swapped(): return lax.ppermute(x, axis, [(i, i ^ 1 << bit) for i in range(n)])]
    dot_general x1, matrix products: 1.7 us -> 0.48 us  [local(): jnp.einsum('tbn,bkn->tbk', act_cols, weights, preferred_element_type=jnp....]
    dynamic_slice x0 -> x2, local copies, waits for them, and re-layouts: none -> 0.92 us  [the longest x1 0.84 us: local(): send = lax.dynamic_index_in_dim(held, 1 - mine, axis_at, keepdims=False)]
    squeeze x3 -> x0, local copies, waits for them, and re-layouts: 0.88 us -> none  [the longest x2 0.86 us: local(): send = lax.dynamic_index_in_dim(held, 1 - mine, axis_at, keepdims=False)]
    div x0 -> x2, local copies, waits for them, and re-layouts: none -> 0.74 us  [local(): return (received[None], (full / grad_scale)[None])]
    unnamed x5 -> x3, local copies, waits for them, and re-layouts: 3.34 us -> 2.85 us
  transfers between devices with their start and end apart: 11 -> 11, of which waited for: 7 -> 9; matrix products, arithmetic and copies ran while one was open for 21% -> 18% of each run, Pallas kernels for 0% -> 0%
where the time goes in v5:
time: 69.8 us; the launch traced here: 69.5 us
  starting transfers between devices  19.8 us (28%)
  local copies, waits for them, and re-layouts  19 us (27%)
  waiting for transfers between devices  18 us (26%)
  other arithmetic  8.36 us (12%)
  matrix products  3.37 us (5%)
  between operations  0.98 us (1%)
    ppermute x6, starting transfers between devices, swapped(): return lax.ppermute(x, axis, [(i, i ^ 1 << bit) for i in range(n)])  12.7 us
    ppermute x6, waiting for transfers between devices, swapped(): return lax.ppermute(x, axis, [(i, i ^ 1 << bit) for i in range(n)])  9.44 us
    ppermute x3, starting transfers between devices, shifted(): return lax.ppermute(x, axis, [(i, (i + k) % n) for i in range(n)])  5.08 us
    ppermute x3, waiting for transfers between devices, shifted(): return lax.ppermute(x, axis, [(i, (i + k) % n) for i in range(n)])  5.07 us
    ppermute x1, waiting for transfers between devices, passed_along(): return lax.ppermute(block, axis, route)  3.45 us
    unnamed x3, local copies, waits for them, and re-layouts  2.85 us
    another operation x1, local copies, waits for them, and re-layouts, local(): hidden_grad = out_grad[0].reshape(tok_rows, col_count, block_size)  2.76 us
    gather x1, local copies, waits for them, and re-layouts, local(): hidden_in = jnp.take(hidden_grad, col_ids, axis=1)  2.69 us
  transfers between devices with their start and end apart: 11, of which 9 were waited for; matrix products, arithmetic and copies ran while one was open for 18% of the time, Pallas kernels for 0%

profile of v5, /device:TPU:0, one launch (start us, length us, event | category | flops | bytes accessed | tf_op | source)
XLA Modules:
  0.0 69.5 jit_solution(10542977688207801007)
XLA Ops:
  0.6 0.7 convert_element_type.56
  1.5 0.9 %pad_maximum_fusion = bf16[65544]{0:T(1024)(128)(2,1)S(1)} fusion(bf16[8]{0:T(256)(128)(2,1)S(1)} %convert_element_type.57, bf16[65536]{0:T(1024)(128)(2,1)} %bitcast.94), kind=kLoop, calls=%fused_computation.29 | loop fusion | flops 262176 | bytes 262176 | tf_op jit(solution)/shard_map/concatenate | solution.py:66
  2.4 0.7 collective-permute-start
  3.3 12.0 %collective-permute-start.1 = (bf16[1,65544]{1,0:T(2,128)(2,1)S(1)}, bf16[1,65544]{1,0:T(2,128)(2,1)S(1)}, u32[]{:S(2)}, u32[]{:S(2)}) collective-permute-start(bf16[1,65544]{1,0:T(2,128)(2,1)S(1)} %stack.68), channel_id=1, source_target_pairs={{0,2},{1,3},{2,0},{3,1},{4,6},{5,7},{6,4},{7,5},{8,10},{9,11},{10,... | collective-permute-start | bytes 393272 | tf_op jit(solution)/shard_map/ppermute | solution.py:22
  15.2 1.6 %reshape_squeeze.12 = bf16[128,28,128]{2,1,0:T(8,128)(2,1)S(1)} reshape(bf16[1,4,32,3584]{3,2,1,0:T(8,128)(2,1)} %param.5) | data formatting | bytes 1835008 | tf_op jit(solution)/shard_map/reshape;squeeze | solution.py:84
  17.2 2.8 %copy.75 = bf16[16,8,112,128]{3,2,1,0:T(8,128)(2,1)S(1)} copy(bf16[16,8,112,128]{3,1,2,0:T(8,128)(2,1)} %bitcast.83) | data formatting | bytes 7340032
  20.1 2.8 %copy.57 = bf16[128,112,128]{2,0,1:T(8,128)(2,1)} copy(bf16[128,112,128]{2,1,0:T(8,128)(2,1)S(1)} %bitcast.81) | data formatting | bytes 7340032 | tf_op jit(solution)/shard_map/reshape;squeeze | solution.py:85
  23.0 1.6 %broadcast_select_fusion = bf16[2,1,65544]{2,1,0:T(2,128)(2,1)S(1)} fusion(pred[]{:T(512)S(6)} %eq.39, bf16[1,1,65544]{2,1,0:T(2,128)(2,1)S(1)} %bitcast.84, bf16[1,1,65544]{2,1,0:T(2,128)(2,1)S(1)} %stack.67), kind=kLoop, calls=%fused_computation.8 | loop fusion | flops 393264 | bytes 524353 | tf_op jit(solution)/shard_map/jit(_where)/select_n | solution.py:41
  25.0 1.2 %fusion.7 = bf16[1,2,1,65544]{3,1,2,0:T(2,128)(2,1)S(1)} fusion(pred[]{:T(512)S(6)} %eq.39, bf16[1,1,65544]{2,1,0:T(2,128)(2,1)S(1)} %bitcast.85, bf16[1,1,65544]{2,1,0:T(2,128)(2,1)S(1)} %stack.67), kind=kLoop, calls=%fused_computation.23 | loop fusion | flops 1179792 | bytes 524353 | tf_op jit(solution)/shard_map/stack | solution.py:41
  26.5 0.9 %fusion.2 = bf16[2,2,1,65544]{3,0,2,1:T(2,128)(2,1)S(1)} fusion(pred[]{:T(512)S(6)} %eq.38, bf16[1,2,1,65544]{3,1,2,0:T(2,128)(2,1)S(1)} %bitcast.89, bf16[1,2,1,65544]{3,1,2,0:T(2,128)(2,1)S(1)} %fusion.7), kind=kLoop, calls=%fused_computation.13 | loop fusion | flops 786528 | bytes 1048705 | tf_op jit(solution)/shard_map/transpose | solution.py:44
  27.8 0.9 %reshape_transpose_reshape.3 = bf16[4,65544]{1,0:T(4,128)(2,1)S(1)} reshape(bf16[2,2,1,65544]{3,1,0,2:T(2,128)(2,1)S(1)} %copy.56) | data formatting | bytes 1048704 | tf_op jit(solution)/shard_map/reshape;transpose;reshape | solution.py:80
  29.4 0.6 gather_fusion.1
  32.3 2.7 %gather_fusion = bf16[16,128,128]{2,1,0:T(8,128)(2,1)S(1)} fusion(bf16[128,112,128]{2,0,1:T(8,128)(2,1)} %copy.57, s32[1024]{0:T(1024)S(1)} %get-tuple-element.16), kind=kCustom, calls=%fused_computation | custom fusion | bytes 1048640 | tf_op jit(solution)/shard_map/jit(_take)/gather | solution.py:96
  35.0 1.1 %fusion.1 = bf16[128,16,128]{2,1,0:T(8,128)(2,1)S(1)} fusion(f32[128,16,128]{2,1,0:T(8,128)S(1)} %copy.63, bf16[16,128,128]{2,1,0:T(8,128)(2,1)S(1)} %gather_fusion, pred[16]{0:T(512)(128)(4,1)S(1)} %get-tuple-element.6, s32[16]{0:T(128)S(1)} %get-tuple-element.5), kind=kOutput, calls=%fused_computation.11 | convolution fusion | flops 53215488 | bytes 2097232 | tf_op jit(solution)/shard_map/bc,tcn->tbn/dot_general | solution.py:93
  36.5 0.8 %copy.88 = f32[4,4,2,1,32,128]{5,4,1,0,2,3:T(8,128)} copy(f32[4,4,2,1,32,128]{5,4,3,2,1,0:T(8,128)S(1)} %get-tuple-element.11) | data formatting | bytes 1048576 | tf_op jit(solution)/shard_map/jit(dynamic_index_in_dim)/dynamic_slice | solution.py:120
  38.5 1.1 %collective-permute-done.4 = f32[4,4,2,32,128]{4,3,1,0,2:T(8,128)} collective-permute-done((f32[4,4,2,32,128]{4,3,1,0,2:T(8,128)}, f32[4,4,2,32,128]{4,3,1,0,2:T(8,128)}, u32[]{:S(2)}, u32[]{:S(2)}) %collective-permute-start.4) | collective-permute-done | bytes 524320 | tf_op jit(solution)/shard_map/ppermute | solution.py:22
  39.6 1.1 %bitcast_add_fusion = f32[4,4,2,32,128]{4,3,1,0,2:T(8,128)S(1)} fusion(f32[4,4,2,32,128]{4,3,1,0,2:T(8,128)} %collective-permute-done.4, f32[4,4,2,1,32,128]{5,4,3,2,1,0:T(8,128)S(1)} %get-tuple-element.10), kind=kLoop, calls=%fused_computation.15 | loop fusion | flops 131072 | bytes 1572864 | tf_op jit(solution)/shard_map/add | solution.py:122
  40.9 1.1 %fusion = bf16[128,28,128]{2,1,0:T(8,128)(2,1)S(1)} fusion(f32[128,16,128]{2,1,0:T(8,128)S(1)} %copy.65, s32[16]{0:T(128)S(1)} %get-tuple-element.2), kind=kOutput, calls=%fused_computation.4 | convolution fusion | flops 88539584 | bytes 1966144 | tf_op jit(solution)/shard_map/rb,tbk->trk/dot_general | solution.py:105
  42.4 1.3 %collective-permute-start.3 = (bf16[128,28,128]{2,0,1:T(8,128)(2,1)S(1)}, bf16[128,28,128]{2,0,1:T(8,128)(2,1)S(1)}, u32[]{:S(2)}, u32[]{:S(2)}) collective-permute-start(bf16[128,28,128]{2,0,1:T(8,128)(2,1)S(1)} %copy.66), channel_id=1, source_target_pairs={{16,0},{17,1},{18,2},{19,3},{20,4},{21,5},{22,6},{23,7},{24,8},{25... | collective-permute-start | bytes 2752520 | tf_op jit(solution)/shard_map/ppermute | solution.py:12
  43.7 2.8 %collective-permute-done.5 = bf16[4,4,32,128]{3,2,1,0:T(8,128)(2,1)S(1)} collective-permute-done((bf16[4,4,32,128]{3,2,1,0:T(8,128)(2,1)S(1)}, bf16[4,4,32,128]{3,2,1,0:T(8,128)(2,1)S(1)}, u32[]{:S(2)}, u32[]{:S(2)}) %collective-permute-start.5) | collective-permute-done | bytes 131104 | tf_op jit(solution)/shard_map/ppermute | solution.py:22
  46.5 4.4 %collective-permute-start.6 = (bf16[4,32,128]{2,1,0:T(8,128)(2,1)S(1)}, bf16[4,32,128]{2,1,0:T(8,128)(2,1)S(1)}, u32[]{:S(2)}, u32[]{:S(2)}) collective-permute-start(bf16[4,32,128]{2,1,0:T(8,128)(2,1)S(1)} %get-tuple-element.12), channel_id=1, source_target_pairs={{0,12},{4,0},{8,4},{12,8},{1,13},{5,1},{9,5},{13,9},{2,14},{6,2},{... | collective-permute-start | bytes 98312 | tf_op jit(solution)/shard_map/ppermute | solution.py:17
  50.9 0.6 collective-permute-start.8
  51.6 0.9 %collective-permute-done.6 = bf16[4,32,128]{2,1,0:T(8,128)(2,1)S(1)} collective-permute-done((bf16[4,32,128]{2,1,0:T(8,128)(2,1)S(1)}, bf16[4,32,128]{2,1,0:T(8,128)(2,1)S(1)}, u32[]{:S(2)}, u32[]{:S(2)}) %collective-permute-start.6) | collective-permute-done | bytes 32800 | tf_op jit(solution)/shard_map/ppermute | solution.py:17
  52.5 3.2 %collective-permute-done.7 = bf16[4,32,128]{2,1,0:T(8,128)(2,1)S(1)} collective-permute-done((bf16[4,32,128]{2,1,0:T(8,128)(2,1)S(1)}, bf16[4,32,128]{2,1,0:T(8,128)(2,1)S(1)}, u32[]{:S(2)}, u32[]{:S(2)}) %collective-permute-start.7) | collective-permute-done | bytes 32800 | tf_op jit(solution)/shard_map/ppermute | solution.py:17
  55.7 0.9 %collective-permute-done.8 = bf16[4,32,128]{2,1,0:T(8,128)(2,1)S(1)} collective-permute-done((bf16[4,32,128]{2,1,0:T(8,128)(2,1)S(1)}, bf16[4,32,128]{2,1,0:T(8,128)(2,1)S(1)}, u32[]{:S(2)}, u32[]{:S(2)}) %collective-permute-start.8) | collective-permute-done | bytes 32800 | tf_op jit(solution)/shard_map/ppermute | solution.py:17
  57.0 4.0 %collective-permute-done.9 = f32[4,32,128]{2,1,0:T(8,128)S(1)} collective-permute-done((f32[4,32,128]{2,1,0:T(8,128)S(1)}, f32[4,32,128]{2,1,0:T(8,128)S(1)}, u32[]{:S(2)}, u32[]{:S(2)}) %collective-permute-start.9) | collective-permute-done | bytes 65568 | tf_op jit(solution)/shard_map/ppermute | solution.py:22
  61.1 1.3 %collective-permute-done.10 = f32[2,4,32,128]{3,2,1,0:T(8,128)S(1)} collective-permute-done((f32[2,4,32,128]{3,2,1,0:T(8,128)S(1)}, f32[2,4,32,128]{3,2,1,0:T(8,128)S(1)}, u32[]{:S(2)}, u32[]{:S(2)}) %collective-permute-start.10) | collective-permute-done | bytes 131104 | tf_op jit(solution)/shard_map/ppermute | solution.py:22
  62.5 0.7 %copy.73 = f32[4,4,32,128]{3,2,1,0:T(8,128)} copy(f32[4,4,32,128]{3,2,0,1:T(8,128)S(1)} %bitcast.86) | data formatting | bytes 524288 | tf_op jit(solution)/shard_map/div | solution.py:132
  63.2 3.4 %collective-permute-done.3 = bf16[128,28,128]{2,0,1:T(8,128)(2,1)S(1)} collective-permute-done((bf16[128,28,128]{2,0,1:T(8,128)(2,1)S(1)}, bf16[128,28,128]{2,0,1:T(8,128)(2,1)S(1)}, u32[]{:S(2)}, u32[]{:S(2)}) %collective-permute-start.3) | collective-permute-done | bytes 917536 | tf_op jit(solution)/shard_map/ppermute | solution.py:12
  66.7 0.6 copy.67
  67.8 0.6 gather_fusion.2
  68.4 1.1 %bitcast_select_fusion = bf16[1,4,32,3584]{3,2,1,0:T(8,128)(2,1)} fusion(bf16[4,32,3584]{2,1,0:T(8,128)(2,1)S(1)} %gather_fusion.2, pred[4]{0:T(512)(128)(4,1)S(1)} %compare_and_fusion), kind=kLoop, calls=%fused_computation.12 | loop fusion | flops 458752 | bytes 1835012 | tf_op jit(solution)/shard_map/jit(_take)/select_n | solution.py:110
  (46 shorter events, 7.9 us)
Async XLA Ops:
  2.4 0.7 collective-permute-start
  3.3 19.7 %collective-permute-start.1 = (bf16[1,65544]{1,0:T(2,128)(2,1)S(1)}, bf16[1,65544]{1,0:T(2,128)(2,1)S(1)}, u32[]{:S(2)}, u32[]{:S(2)}) collective-permute-start(bf16[1,65544]{1,0:T(2,128)(2,1)S(1)} %stack.68), channel_id=1, source_target_pairs={{0,2},{1,3},{2,0},{3,1},{4,6},{5,7},{6,4},{7,5},{8,10},{9,11},{10,... | collective-permute-start | bytes 393272 | tf_op jit(solution)/shard_map/ppermute | solution.py:22
  24.9 1.6 %collective-permute-start.2 = (bf16[2,1,65544]{2,0,1:T(2,128)(2,1)S(1)}, bf16[2,1,65544]{2,0,1:T(2,128)(2,1)S(1)}, u32[]{:S(2)}, u32[]{:S(2)}) collective-permute-start(bf16[2,1,65544]{2,0,1:T(2,128)(2,1)S(1)} %copy.55), channel_id=1, source_target_pairs={{0,1},{1,0},{2,3},{3,2},{4,5},{5,4},{6,7},{7,6},{8,9},{9,8},{10,11... | collective-permute-start | bytes 786536 | tf_op jit(solution)/shard_map/ppermute | solution.py:22
  37.4 2.3 %collective-permute-start.4 = (f32[4,4,2,32,128]{4,3,1,0,2:T(8,128)}, f32[4,4,2,32,128]{4,3,1,0,2:T(8,128)}, u32[]{:S(2)}, u32[]{:S(2)}) collective-permute-start(f32[4,4,2,32,128]{4,3,1,0,2:T(8,128)} %bitcast.80), channel_id=1, source_target_pairs={{0,1},{1,0},{2,3},{3,2},{4,5},{5,4},{6,7},{7,6},{8,9},{9,8},{10,11... | collective-permute-start | bytes 1572872 | tf_op jit(solution)/shard_map/ppermute | solution.py:22
  38.5 13.0 %copy-start = (s32[4]{0:T(128)S(1)}, s32[4]{0:T(128)}, u32[]{:S(2)}) copy-start(s32[4]{0:T(128)} %param.9) | copy-start | bytes 52
  40.8 5.6 %collective-permute-start.5 = (bf16[4,4,32,128]{3,2,1,0:T(8,128)(2,1)S(1)}, bf16[4,4,32,128]{3,2,1,0:T(8,128)(2,1)S(1)}, u32[]{:S(2)}, u32[]{:S(2)}) collective-permute-start(bf16[4,4,32,128]{3,2,1,0:T(8,128)(2,1)S(1)} %fusion.10), channel_id=1, source_target_pairs={{0,2},{1,3},{2,0},{3,1},{4,6},{5,7},{6,4},{7,5},{8,10},{9,11},{10,... | collective-permute-start | bytes 393224 | tf_op jit(solution)/shard_map/ppermute | solution.py:22
  42.4 24.3 %collective-permute-start.3 = (bf16[128,28,128]{2,0,1:T(8,128)(2,1)S(1)}, bf16[128,28,128]{2,0,1:T(8,128)(2,1)S(1)}, u32[]{:S(2)}, u32[]{:S(2)}) collective-permute-start(bf16[128,28,128]{2,0,1:T(8,128)(2,1)S(1)} %copy.66), channel_id=1, source_target_pairs={{16,0},{17,1},{18,2},{19,3},{20,4},{21,5},{22,6},{23,7},{24,8},{25... | collective-permute-start | bytes 2752520 | tf_op jit(solution)/shard_map/ppermute | solution.py:12
  46.5 6.0 %collective-permute-start.6 = (bf16[4,32,128]{2,1,0:T(8,128)(2,1)S(1)}, bf16[4,32,128]{2,1,0:T(8,128)(2,1)S(1)}, u32[]{:S(2)}, u32[]{:S(2)}) collective-permute-start(bf16[4,32,128]{2,1,0:T(8,128)(2,1)S(1)} %get-tuple-element.12), channel_id=1, source_target_pairs={{0,12},{4,0},{8,4},{12,8},{1,13},{5,1},{9,5},{13,9},{2,14},{6,2},{... | collective-permute-start | bytes 98312 | tf_op jit(solution)/shard_map/ppermute | solution.py:17
  50.9 4.8 %collective-permute-start.7 = (bf16[4,32,128]{2,1,0:T(8,128)(2,1)S(1)}, bf16[4,32,128]{2,1,0:T(8,128)(2,1)S(1)}, u32[]{:S(2)}, u32[]{:S(2)}) collective-permute-start(bf16[4,32,128]{2,1,0:T(8,128)(2,1)S(1)} %get-tuple-element.14), channel_id=1, source_target_pairs={{0,8},{4,12},{8,0},{12,4},{1,9},{5,13},{9,1},{13,5},{2,10},{6,14},... | collective-permute-start | bytes 98312 | tf_op jit(solution)/shard_map/ppermute | solution.py:17
  50.9 5.7 %collective-permute-start.8 = (bf16[4,32,128]{2,1,0:T(8,128)(2,1)S(1)}, bf16[4,32,128]{2,1,0:T(8,128)(2,1)S(1)}, u32[]{:S(2)}, u32[]{:S(2)}) collective-permute-start(bf16[4,32,128]{2,1,0:T(8,128)(2,1)S(1)} %get-tuple-element.13), channel_id=1, source_target_pairs={{0,4},{4,8},{8,12},{12,0},{1,5},{5,9},{9,13},{13,1},{2,6},{6,10},{... | collective-permute-start | bytes 98312 | tf_op jit(solution)/shard_map/ppermute | solution.py:17
  56.7 4.3 %collective-permute-start.9 = (f32[4,32,128]{2,1,0:T(8,128)S(1)}, f32[4,32,128]{2,1,0:T(8,128)S(1)}, u32[]{:S(2)}, u32[]{:S(2)}) collective-permute-start(f32[4,32,128]{2,1,0:T(8,128)S(1)} %fusion.13), channel_id=1, source_target_pairs={{0,2},{1,3},{2,0},{3,1},{4,6},{5,7},{6,4},{7,5},{8,10},{9,11},{10,... | collective-permute-start | bytes 196616 | tf_op jit(solution)/shard_map/ppermute | solution.py:22
  61.0 1.4 %collective-permute-start.10 = (f32[2,4,32,128]{3,2,1,0:T(8,128)S(1)}, f32[2,4,32,128]{3,2,1,0:T(8,128)S(1)}, u32[]{:S(2)}, u32[]{:S(2)}) collective-permute-start(f32[2,4,32,128]{3,2,1,0:T(8,128)S(1)} %maximum_select_fusion.2), channel_id=1, source_target_pairs={{0,1},{1,0},{2,3},{3,2},{4,5},{5,4},{6,7},{7,6},{8,9},{9,8},{10,11... | collective-permute-start | bytes 393224 | tf_op jit(solution)/shard_map/ppermute | solution.py:22

commit v6 on v5

--- a/solution.py
+++ b/solution.py
@@ -3,6 +3,8 @@
 import jax
 import jax.numpy as jnp
 from jax import lax
+from jax.experimental import pallas as pl
+from jax.experimental.pallas import tpu as pltpu
 from jax.sharding import PartitionSpec as P
 
 
@@ -25,6 +27,88 @@
 def silu_slope(pre_act):
     sigmoid_val = jax.nn.sigmoid(pre_act)
     return sigmoid_val * (1.0 + pre_act * (1.0 - sigmoid_val))
+
+
+def block_kernel(rows_ref, cols_ref, rep_ref, feat_hbm, hid_hbm, w_ref, ig_ref, pg_ref,
+                 xs, hs, pr, acc, sems):
+    block_count = w_ref.shape[0]
+    width = w_ref.shape[-1]
+
+    def copies(b):
+        r = pl.multiple_of(rows_ref[b] * width, width)
+        c = pl.multiple_of(cols_ref[b] * width, width)
+        return (
+            pltpu.make_async_copy(feat_hbm.at[:, pl.ds(r, width)], xs.at[b], sems.at[0, b]),
+            pltpu.make_async_copy(hid_hbm.at[:, pl.ds(c, width)], hs.at[b], sems.at[1, b]),
+        )
+
+    @pl.loop(0, block_count)
+    def _(b):
+        for cp in copies(b):
+            cp.start()
+
+    acc[...] = jnp.zeros(acc.shape, acc.dtype)
+
+    @pl.loop(0, block_count)
+    def _(b):
+        for cp in copies(b):
+            cp.wait()
+        pr[b] = jnp.dot(xs[b], w_ref[b], preferred_element_type=jnp.float32)
+
+    @pl.loop(0, block_count)
+    def _(b):
+        first = rep_ref[b]
+
+        @pl.when(first != b)
+        def _():
+            pr[first] = pr[first] + pr[b]
+
+    @pl.loop(0, block_count)
+    def _(b):
+        pre_act = pr[rep_ref[b]]
+        act = (hs[b].astype(jnp.float32) * silu_slope(pre_act)).astype(jnp.bfloat16)
+        back = lax.dot_general(
+            act, w_ref[b], (((1,), (1,)), ((), ())), preferred_element_type=jnp.float32
+        )
+        row = rows_ref[b]
+        acc[row] = acc[row] + back
+        pg_ref[b] = lax.dot_general(
+            xs[b], act, (((0,), (0,)), ((), ())), preferred_element_type=jnp.float32
+        )
+
+    ig_ref[...] = acc[...].astype(ig_ref.dtype)
+
+
+def block_pass(features, hidden_grad, weights, row_ids, col_ids, row_count):
+    tokens = features.shape[0]
+    block_count, width, _ = weights.shape
+    same = col_ids[:, None] == col_ids[None, :]
+    first = jnp.argmax(same, axis=1).astype(jnp.int32)
+    smem = pl.BlockSpec(memory_space=pltpu.SMEM)
+    anyspace = pl.BlockSpec(memory_space=pl.ANY)
+    vmem = pl.BlockSpec(memory_space=pltpu.VMEM)
+    return pl.pallas_call(
+        block_kernel,
+        out_shape=(
+            jax.ShapeDtypeStruct((row_count, tokens, width), jnp.bfloat16),
+            jax.ShapeDtypeStruct((block_count, width, width), jnp.float32),
+        ),
+        in_specs=[smem, smem, smem, anyspace, anyspace, vmem],
+        out_specs=(vmem, vmem),
+        scratch_shapes=[
+            pltpu.VMEM((block_count, tokens, width), jnp.bfloat16),
+            pltpu.VMEM((block_count, tokens, width), jnp.bfloat16),
+            pltpu.VMEM((block_count, tokens, width), jnp.float32),
+            pltpu.VMEM((row_count, tokens, width), jnp.float32),
+            pltpu.SemaphoreType.DMA((2, block_count)),
+        ],
+        cost_estimate=pl.CostEstimate(
+            flops=6 * block_count * tokens * width * width,
+            transcendentals=block_count * tokens * width,
+            bytes_accessed=block_count * width * (4 * tokens + 6 * width)
+            + row_count * tokens * width * 2,
+        ),
+    )(row_ids, col_ids, first, features, hidden_grad, weights)
 
 
 def gather_over(x, axis):
@@ -81,37 +165,22 @@
     weights = pieces[:, :weight_len].reshape(n_fsdp * blocks_dev, block_size, block_size)
     all_indices = pieces[:, weight_len:].reshape(n_fsdp * blocks_dev, 2).astype(jnp.int32)
 
-    features = activations[0].reshape(tok_rows, row_count, block_size)
-    hidden_grad = out_grad[0].reshape(tok_rows, col_count, block_size)
     row_ids = all_indices[:, 0]
     col_ids = all_indices[:, 1]
-    rows_in = jnp.take(features, row_ids, axis=1)
-    product = jnp.einsum(
-        "tbk,bkn->tbn", rows_in, weights, preferred_element_type=jnp.float32
-    )
-    same_col = (col_ids[:, None] == col_ids[None, :]).astype(jnp.float32)
-    pre_act = jnp.einsum(
-        "bc,tcn->tbn", same_col, product, precision=lax.Precision.HIGHEST
-    )
-    hidden_in = jnp.take(hidden_grad, col_ids, axis=1)
-    act_cols = (hidden_in.astype(jnp.float32) * silu_slope(pre_act)).astype(jnp.bfloat16)
-
-    backward = jnp.einsum(
-        "tbn,bkn->tbk", act_cols, weights, preferred_element_type=jnp.float32
-    )
-    row_hit = (jnp.arange(row_count, dtype=jnp.int32)[:, None] == row_ids[None, :]).astype(
-        jnp.float32
-    )
-    input_grad = jnp.einsum(
-        "rb,tbk->trk", row_hit, backward, precision=lax.Precision.HIGHEST
-    )
-    arrived = passed_along(input_grad.astype(jnp.bfloat16), "section", -1)
-    arrived = arrived.reshape(micro_count, activations.shape[2], activations.shape[3])
+    input_grad, partial = block_pass(
+        activations[0].reshape(tok_rows, -1),
+        out_grad[0].reshape(tok_rows, -1),
+        weights,
+        row_ids,
+        col_ids,
+        row_count,
+    )
+    arrived = passed_along(input_grad, "section", -1)
+    arrived = jnp.transpose(arrived, (1, 0, 2)).reshape(
+        micro_count, activations.shape[2], activations.shape[3]
+    )
     received = jnp.take(arrived, order, axis=0)
 
-    partial = jnp.einsum(
-        "tbk,tbn->bkn", rows_in, act_cols, preferred_element_type=jnp.float32
-    )
     held = partial.reshape((n_fsdp, blocks_dev) + (2,) * dp_bits + (chunk, block_size))
     for bit in range(dp_bits):
         axis_at = 2 + (dp_bits - 1 - bit)

time: 69.8 us -> 70.3 us (level)
  local copies, waits for them, and re-layouts: 19 us -> 8.2 us
  Pallas kernels: 0 us -> 8.72 us
  waiting for transfers between devices: 18 us -> 22.4 us
  matrix products: 3.37 us -> 0 us
  starting transfers between devices: 19.8 us -> 22.6 us
  other arithmetic: 8.36 us -> 7.27 us
    pallas_call x0 -> x1, Pallas kernels: none -> 8.72 us  [block_pass(): pl.pallas_call(block_kernel, out_shape=(jax.ShapeDtypeStruct((row_count,...]
    another operation x3 -> x0, local copies, waits for them, and re-layouts: 4.74 us -> none  [the longest x1 2.76 us: local(): hidden_grad = out_grad[0].reshape(tok_rows, col_count, block_size)]
    ppermute x6, waiting for transfers between devices: 9.44 us -> 13.5 us  [swapped(): return lax.ppermute(x, axis, [(i, i ^ 1 << bit) for i in range(n)])]
    dot_general x5 -> x0, matrix products: 3.37 us -> none  [the longest x1 1.13 us: local(): jnp.einsum('bc,tcn->tbn', same_col, product, precision=lax.Precision.HIGH...]
    gather x2 -> x0, local copies, waits for them, and re-layouts: 3.33 us -> none  [the longest x1 2.69 us: local(): hidden_in = jnp.take(hidden_grad, col_ids, axis=1)]
    ppermute x6, starting transfers between devices: 12.7 us -> 16 us  [swapped(): return lax.ppermute(x, axis, [(i, i ^ 1 << bit) for i in range(n)])]
    unnamed x3 -> x6, local copies, waits for them, and re-layouts: 2.85 us -> 0.02 us
    ppermute x1, waiting for transfers between devices: 3.45 us -> 4.99 us  [passed_along(): return lax.ppermute(block, axis, route)]
  transfers between devices with their start and end apart: 11 -> 11, of which waited for: 9 -> 10; matrix products, arithmetic and copies ran while one was open for 18% -> 3% of each run, Pallas kernels for 0% -> 0%
where the time goes in v6:
time: 70.3 us; the launch traced here: 70 us
  starting transfers between devices  22.6 us (32%)
  waiting for transfers between devices  22.4 us (32%)
  Pallas kernels  8.72 us (12%)
  local copies, waits for them, and re-layouts  8.2 us (12%)
  other arithmetic  7.27 us (10%)
  between operations  0.87 us (1%)
    ppermute x6, starting transfers between devices, swapped(): return lax.ppermute(x, axis, [(i, i ^ 1 << bit) for i in range(n)])  16 us
    ppermute x6, waiting for transfers between devices, swapped(): return lax.ppermute(x, axis, [(i, i ^ 1 << bit) for i in range(n)])  13.5 us
    pallas_call x1, Pallas kernels, block_pass(): pl.pallas_call(block_kernel, out_shape=(jax.ShapeDtypeStruct((row_count,...  8.72 us
    ppermute x1, waiting for transfers between devices, passed_along(): return lax.ppermute(block, axis, route)  4.99 us
    ppermute x3, starting transfers between devices, shifted(): return lax.ppermute(x, axis, [(i, (i + k) % n) for i in range(n)])  4.66 us
    ppermute x3, waiting for transfers between devices, shifted(): return lax.ppermute(x, axis, [(i, (i + k) % n) for i in range(n)])  3.9 us
    select_n x3, other arithmetic, butterfly_gather(): jnp.where(mine_low, jnp.stack([held, other]), jnp.stack([other, held]))  1.61 us
  transfers between devices with their start and end apart: 11, of which 10 were waited for; matrix products, arithmetic and copies ran while one was open for 3% of the time, Pallas kernels for 0%

profile of v6, /device:TPU:0, one launch (start us, length us, event | category | flops | bytes accessed | tf_op | source)
XLA Modules:
  0.0 70.0 jit_solution(1676386726660727148)
XLA Ops:
  0.6 0.7 convert_element_type.42
  1.5 0.9 %pad_maximum_fusion = bf16[65544]{0:T(1024)(128)(2,1)S(1)} fusion(bf16[8]{0:T(256)(128)(2,1)S(1)} %convert_element_type.43, bf16[65536]{0:T(1024)(128)(2,1)} %bitcast.65), kind=kLoop, calls=%fused_computation.14 | loop fusion | flops 262176 | bytes 262176 | tf_op jit(solution)/shard_map/concatenate | solution.py:150
  2.4 0.7 collective-permute-start
  3.3 12.0 %collective-permute-start.1 = (bf16[1,65544]{1,0:T(2,128)(2,1)S(1)}, bf16[1,65544]{1,0:T(2,128)(2,1)S(1)}, u32[]{:S(2)}, u32[]{:S(2)}) collective-permute-start(bf16[1,65544]{1,0:T(2,128)(2,1)S(1)} %stack.68), channel_id=1, source_target_pairs={{0,2},{1,3},{2,0},{3,1},{4,6},{5,7},{6,4},{7,5},{8,10},{9,11},{10,... | collective-permute-start | bytes 393272 | tf_op jit(solution)/shard_map/ppermute | solution.py:24
  15.4 5.1 %collective-permute-done.1 = bf16[1,65544]{1,0:T(2,128)(2,1)S(1)} collective-permute-done((bf16[1,65544]{1,0:T(2,128)(2,1)S(1)}, bf16[1,65544]{1,0:T(2,128)(2,1)S(1)}, u32[]{:S(2)}, u32[]{:S(2)}) %collective-permute-start.1) | collective-permute-done | bytes 131120 | tf_op jit(solution)/shard_map/ppermute | solution.py:24
  20.4 1.6 %broadcast_select_fusion = bf16[2,1,65544]{2,1,0:T(2,128)(2,1)S(1)} fusion(pred[]{:T(512)S(6)} %eq.24, bf16[1,1,65544]{2,1,0:T(2,128)(2,1)S(1)} %bitcast.51, bf16[1,1,65544]{2,1,0:T(2,128)(2,1)S(1)} %stack.67), kind=kLoop, calls=%fused_computation.1 | loop fusion | flops 393264 | bytes 524353 | tf_op jit(solution)/shard_map/jit(_where)/select_n | solution.py:125
  22.4 1.2 %fusion.1 = bf16[1,2,1,65544]{3,1,2,0:T(2,128)(2,1)S(1)} fusion(pred[]{:T(512)S(6)} %eq.24, bf16[1,1,65544]{2,1,0:T(2,128)(2,1)S(1)} %bitcast.52, bf16[1,1,65544]{2,1,0:T(2,128)(2,1)S(1)} %stack.67), kind=kLoop, calls=%fused_computation.8 | loop fusion | flops 1179792 | bytes 524353 | tf_op jit(solution)/shard_map/stack | solution.py:125
  23.9 0.9 %fusion = bf16[2,2,1,65544]{3,0,2,1:T(2,128)(2,1)S(1)} fusion(pred[]{:T(512)S(6)} %eq.12, bf16[1,2,1,65544]{3,1,2,0:T(2,128)(2,1)S(1)} %bitcast.60, bf16[1,2,1,65544]{3,1,2,0:T(2,128)(2,1)S(1)} %fusion.1), kind=kLoop, calls=%fused_computation.4 | loop fusion | flops 786528 | bytes 1048705 | tf_op jit(solution)/shard_map/transpose | solution.py:128
  25.2 0.9 %reshape_transpose_reshape.3 = bf16[4,65544]{1,0:T(4,128)(2,1)S(1)} reshape(bf16[2,2,1,65544]{3,1,0,2:T(2,128)(2,1)S(1)} %copy.38) | data formatting | bytes 1048704 | tf_op jit(solution)/shard_map/reshape;transpose;reshape | solution.py:164
  26.4 0.6 slice_reduce_fusion
  27.1 0.7 iota_reduce_fusion
  27.8 1.3 %reshape.376.w_ref = bf16[16,128,128]{2,1,0:T(8,128)(2,1)} reshape(bf16[4,65536]{1,0:T(4,128)(2,1)S(1)} %slice.40) | data formatting | bytes 1048576 | tf_op jit(solution)/shard_map/reshape | solution.py:165
  29.1 8.7 %shard_map.68 = (bf16[28,128,128]{2,1,0:T(8,128)(2,1)}, f32[16,128,128]{2,1,0:T(8,128)}) custom-call(s32[16]{0:T(128)} %get-tuple-element.9.rows_ref, s32[16]{0:T(128)} %copy-done, s32[16]{0:T(128)} %get-tuple-element.5.rep_ref, bf16[128,3584]{1,0:T(8,128)(2,1)} %bitcast.56, bf16[128,14336]{1,0:T(8,128)(2,1)} %bitcast.50, bf16[16,128,128]{2,1,0:T(8,128)(2,1)} %reshape.376.w_ref), custom_call_target="tpu_custom_call" | custom-call | flops 201326592 | bytes 3538944 | tf_op jit(solution)/shard_map/pallas_call | solution.py:90
  37.9 1.4 %constant_dynamic-slice_fusion.1 = (f32[4,4,2,1,32,128]{5,4,3,2,1,0:T(8,128)S(1)}, f32[4,4,2,1,32,128]{5,4,3,2,1,0:T(8,128)S(1)}) fusion(f32[4,4,2,2,32,128]{5,4,3,2,1,0:T(8,128)} %bitcast.54, s32[]{:T(128)S(6)} %select_n.125, s32[]{:T(128)S(6)} %select_n.126), kind=kLoop, calls=%fused_computation.33 | loop fusion | bytes 2097160 | tf_op jit(solution)/shard_map/jit(dynamic_index_in_dim)/dynamic_slice | solution.py:188
  39.5 1.7 %collective-permute-done.4 = f32[4,4,2,32,128]{4,3,1,0,2:T(8,128)S(1)} collective-permute-done((f32[4,4,2,32,128]{4,3,1,0,2:T(8,128)S(1)}, f32[4,4,2,32,128]{4,3,1,0,2:T(8,128)S(1)}, u32[]{:S(2)}, u32[]{:S(2)}) %collective-permute-start.4) | collective-permute-done | bytes 524320 | tf_op jit(solution)/shard_map/ppermute | solution.py:24
  41.4 1.8 %collective-permute-start.5 = (bf16[4,4,32,128]{3,2,1,0:T(8,128)(2,1)S(1)}, bf16[4,4,32,128]{3,2,1,0:T(8,128)(2,1)S(1)}, u32[]{:S(2)}, u32[]{:S(2)}) collective-permute-start(bf16[4,4,32,128]{3,2,1,0:T(8,128)(2,1)S(1)} %fusion.4), channel_id=1, source_target_pairs={{0,2},{1,3},{2,0},{3,1},{4,6},{5,7},{6,4},{7,5},{8,10},{9,11},{10,... | collective-permute-start | bytes 393224 | tf_op jit(solution)/shard_map/ppermute | solution.py:24
  43.2 1.3 %collective-permute-start.3 = (bf16[28,128,128]{2,1,0:T(8,128)(2,1)S(1)}, bf16[28,128,128]{2,1,0:T(8,128)(2,1)S(1)}, u32[]{:S(2)}, u32[]{:S(2)}) collective-permute-start(bf16[28,128,128]{2,1,0:T(8,128)(2,1)S(1)} %copy-done.1), channel_id=1, source_target_pairs={{16,0},{17,1},{18,2},{19,3},{20,4},{21,5},{22,6},{23,7},{24,8},{25... | collective-permute-start | bytes 2752520 | tf_op jit(solution)/shard_map/ppermute | solution.py:14
  44.5 2.5 %collective-permute-done.5 = bf16[4,4,32,128]{3,2,1,0:T(8,128)(2,1)S(1)} collective-permute-done((bf16[4,4,32,128]{3,2,1,0:T(8,128)(2,1)S(1)}, bf16[4,4,32,128]{3,2,1,0:T(8,128)(2,1)S(1)}, u32[]{:S(2)}, u32[]{:S(2)}) %collective-permute-start.5) | collective-permute-done | bytes 131104 | tf_op jit(solution)/shard_map/ppermute | solution.py:24
  47.1 1.1 %collective-permute-start.8 = (bf16[4,32,128]{2,1,0:T(8,128)(2,1)S(1)}, bf16[4,32,128]{2,1,0:T(8,128)(2,1)S(1)}, u32[]{:S(2)}, u32[]{:S(2)}) collective-permute-start(bf16[4,32,128]{2,1,0:T(8,128)(2,1)S(1)} %get-tuple-element.15), channel_id=1, source_target_pairs={{0,4},{4,8},{8,12},{12,0},{1,5},{5,9},{9,13},{13,1},{2,6},{6,10},{... | collective-permute-start | bytes 98312 | tf_op jit(solution)/shard_map/ppermute | solution.py:19
  48.2 3.6 %collective-permute-start.7 = (bf16[4,32,128]{2,1,0:T(8,128)(2,1)S(1)}, bf16[4,32,128]{2,1,0:T(8,128)(2,1)S(1)}, u32[]{:S(2)}, u32[]{:S(2)}) collective-permute-start(bf16[4,32,128]{2,1,0:T(8,128)(2,1)S(1)} %get-tuple-element.16), channel_id=1, source_target_pairs={{0,8},{4,12},{8,0},{12,4},{1,9},{5,13},{9,1},{13,5},{2,10},{6,14},... | collective-permute-start | bytes 98312 | tf_op jit(solution)/shard_map/ppermute | solution.py:19
  51.8 1.7 %collective-permute-done.8 = bf16[4,32,128]{2,1,0:T(8,128)(2,1)S(1)} collective-permute-done((bf16[4,32,128]{2,1,0:T(8,128)(2,1)S(1)}, bf16[4,32,128]{2,1,0:T(8,128)(2,1)S(1)}, u32[]{:S(2)}, u32[]{:S(2)}) %collective-permute-start.8) | collective-permute-done | bytes 32800 | tf_op jit(solution)/shard_map/ppermute | solution.py:19
  53.4 0.7 %collective-permute-done.7 = bf16[4,32,128]{2,1,0:T(8,128)(2,1)S(1)} collective-permute-done((bf16[4,32,128]{2,1,0:T(8,128)(2,1)S(1)}, bf16[4,32,128]{2,1,0:T(8,128)(2,1)S(1)}, u32[]{:S(2)}, u32[]{:S(2)}) %collective-permute-start.7) | collective-permute-done | bytes 32800 | tf_op jit(solution)/shard_map/ppermute | solution.py:19
  54.2 1.5 %collective-permute-done.6 = bf16[4,32,128]{2,1,0:T(8,128)(2,1)S(1)} collective-permute-done((bf16[4,32,128]{2,1,0:T(8,128)(2,1)S(1)}, bf16[4,32,128]{2,1,0:T(8,128)(2,1)S(1)}, u32[]{:S(2)}, u32[]{:S(2)}) %collective-permute-start.6) | collective-permute-done | bytes 32800 | tf_op jit(solution)/shard_map/ppermute | solution.py:19
  55.7 1.8 %collective-permute-start.9 = (f32[4,32,128]{2,1,0:T(8,128)S(1)}, f32[4,32,128]{2,1,0:T(8,128)S(1)}, u32[]{:S(2)}, u32[]{:S(2)}) collective-permute-start(f32[4,32,128]{2,1,0:T(8,128)S(1)} %fusion.7), channel_id=1, source_target_pairs={{0,2},{1,3},{2,0},{3,1},{4,6},{5,7},{6,4},{7,5},{8,10},{9,11},{10,... | collective-permute-start | bytes 196616 | tf_op jit(solution)/shard_map/ppermute | solution.py:24
  57.5 2.5 %collective-permute-done.9 = f32[4,32,128]{2,1,0:T(8,128)S(1)} collective-permute-done((f32[4,32,128]{2,1,0:T(8,128)S(1)}, f32[4,32,128]{2,1,0:T(8,128)S(1)}, u32[]{:S(2)}, u32[]{:S(2)}) %collective-permute-start.9) | collective-permute-done | bytes 65568 | tf_op jit(solution)/shard_map/ppermute | solution.py:24
  60.2 1.3 %collective-permute-done.10 = f32[2,4,32,128]{3,2,1,0:T(8,128)S(1)} collective-permute-done((f32[2,4,32,128]{3,2,1,0:T(8,128)S(1)}, f32[2,4,32,128]{3,2,1,0:T(8,128)S(1)}, u32[]{:S(2)}, u32[]{:S(2)}) %collective-permute-start.10) | collective-permute-done | bytes 131104 | tf_op jit(solution)/shard_map/ppermute | solution.py:24
  61.5 0.7 %copy.43 = f32[4,4,32,128]{3,2,1,0:T(8,128)} copy(f32[4,4,32,128]{3,2,0,1:T(8,128)S(1)} %bitcast.53) | data formatting | bytes 524288 | tf_op jit(solution)/shard_map/div | solution.py:201
  62.2 5.0 %collective-permute-done.3 = bf16[28,128,128]{2,1,0:T(8,128)(2,1)S(1)} collective-permute-done((bf16[28,128,128]{2,1,0:T(8,128)(2,1)S(1)}, bf16[28,128,128]{2,1,0:T(8,128)(2,1)S(1)}, u32[]{:S(2)}, u32[]{:S(2)}) %collective-permute-start.3) | collective-permute-done | bytes 917536 | tf_op jit(solution)/shard_map/ppermute | solution.py:14
  67.2 0.6 copy.39
  67.8 0.5 reshape.377
  68.3 0.6 gather_fusion
  69.0 1.1 %bitcast_select_fusion = bf16[1,4,32,3584]{3,2,1,0:T(8,128)(2,1)} fusion(bf16[4,32,3584]{2,1,0:T(8,128)(2,1)S(1)} %gather_fusion, pred[4]{0:T(512)(128)(4,1)S(1)} %compare_and_fusion), kind=kLoop, calls=%fused_computation.3 | loop fusion | flops 458752 | bytes 1835012 | tf_op jit(solution)/shard_map/jit(_take)/select_n | solution.py:182
  (34 shorter events, 2.5 us)
Async XLA Ops:
  2.4 0.7 collective-permute-start
  3.3 17.2 %collective-permute-start.1 = (bf16[1,65544]{1,0:T(2,128)(2,1)S(1)}, bf16[1,65544]{1,0:T(2,128)(2,1)S(1)}, u32[]{:S(2)}, u32[]{:S(2)}) collective-permute-start(bf16[1,65544]{1,0:T(2,128)(2,1)S(1)} %stack.68), channel_id=1, source_target_pairs={{0,2},{1,3},{2,0},{3,1},{4,6},{5,7},{6,4},{7,5},{8,10},{9,11},{10,... | collective-permute-start | bytes 393272 | tf_op jit(solution)/shard_map/ppermute | solution.py:24
  22.3 1.6 %collective-permute-start.2 = (bf16[2,1,65544]{2,0,1:T(2,128)(2,1)S(1)}, bf16[2,1,65544]{2,0,1:T(2,128)(2,1)S(1)}, u32[]{:S(2)}, u32[]{:S(2)}) collective-permute-start(bf16[2,1,65544]{2,0,1:T(2,128)(2,1)S(1)} %copy.37), channel_id=1, source_target_pairs={{0,1},{1,0},{2,3},{3,2},{4,5},{5,4},{6,7},{7,6},{8,9},{9,8},{10,11... | collective-permute-start | bytes 786536 | tf_op jit(solution)/shard_map/ppermute | solution.py:24
  27.1 2.0 %copy-start = (s32[16]{0:T(128)}, s32[16]{0:T(128)S(1)}, u32[]{:S(2)}) copy-start(s32[16]{0:T(128)S(1)} %get-tuple-element.8.cols_ref) | copy-start | bytes 196
  37.8 5.4 %copy-start.1 = (bf16[28,128,128]{2,1,0:T(8,128)(2,1)S(1)}, bf16[28,128,128]{2,1,0:T(8,128)(2,1)}, u32[]{:S(2)}) copy-start(bf16[28,128,128]{2,1,0:T(8,128)(2,1)} %get-tuple-element.6) | copy-start | bytes 2752516
  37.9 13.9 %copy-start.2 = (s32[4]{0:T(128)S(1)}, s32[4]{0:T(128)}, u32[]{:S(2)}) copy-start(s32[4]{0:T(128)} %param.9) | copy-start | bytes 52
  39.3 2.0 %collective-permute-start.4 = (f32[4,4,2,32,128]{4,3,1,0,2:T(8,128)S(1)}, f32[4,4,2,32,128]{4,3,1,0,2:T(8,128)S(1)}, u32[]{:S(2)}, u32[]{:S(2)}) collective-permute-start(f32[4,4,2,32,128]{4,3,1,0,2:T(8,128)S(1)} %bitcast.59), channel_id=1, source_target_pairs={{0,1},{1,0},{2,3},{3,2},{4,5},{5,4},{6,7},{7,6},{8,9},{9,8},{10,11... | collective-permute-start | bytes 1572872 | tf_op jit(solution)/shard_map/ppermute | solution.py:24
  41.4 5.6 %collective-permute-start.5 = (bf16[4,4,32,128]{3,2,1,0:T(8,128)(2,1)S(1)}, bf16[4,4,32,128]{3,2,1,0:T(8,128)(2,1)S(1)}, u32[]{:S(2)}, u32[]{:S(2)}) collective-permute-start(bf16[4,4,32,128]{3,2,1,0:T(8,128)(2,1)S(1)} %fusion.4), channel_id=1, source_target_pairs={{0,2},{1,3},{2,0},{3,1},{4,6},{5,7},{6,4},{7,5},{8,10},{9,11},{10,... | collective-permute-start | bytes 393224 | tf_op jit(solution)/shard_map/ppermute | solution.py:24
  43.2 24.0 %collective-permute-start.3 = (bf16[28,128,128]{2,1,0:T(8,128)(2,1)S(1)}, bf16[28,128,128]{2,1,0:T(8,128)(2,1)S(1)}, u32[]{:S(2)}, u32[]{:S(2)}) collective-permute-start(bf16[28,128,128]{2,1,0:T(8,128)(2,1)S(1)} %copy-done.1), channel_id=1, source_target_pairs={{16,0},{17,1},{18,2},{19,3},{20,4},{21,5},{22,6},{23,7},{24,8},{25... | collective-permute-start | bytes 2752520 | tf_op jit(solution)/shard_map/ppermute | solution.py:14
  47.1 6.3 %collective-permute-start.8 = (bf16[4,32,128]{2,1,0:T(8,128)(2,1)S(1)}, bf16[4,32,128]{2,1,0:T(8,128)(2,1)S(1)}, u32[]{:S(2)}, u32[]{:S(2)}) collective-permute-start(bf16[4,32,128]{2,1,0:T(8,128)(2,1)S(1)} %get-tuple-element.15), channel_id=1, source_target_pairs={{0,4},{4,8},{8,12},{12,0},{1,5},{5,9},{9,13},{13,1},{2,6},{6,10},{... | collective-permute-start | bytes 98312 | tf_op jit(solution)/shard_map/ppermute | solution.py:19
  48.2 6.0 %collective-permute-start.7 = (bf16[4,32,128]{2,1,0:T(8,128)(2,1)S(1)}, bf16[4,32,128]{2,1,0:T(8,128)(2,1)S(1)}, u32[]{:S(2)}, u32[]{:S(2)}) collective-permute-start(bf16[4,32,128]{2,1,0:T(8,128)(2,1)S(1)} %get-tuple-element.16), channel_id=1, source_target_pairs={{0,8},{4,12},{8,0},{12,4},{1,9},{5,13},{9,1},{13,5},{2,10},{6,14},... | collective-permute-start | bytes 98312 | tf_op jit(solution)/shard_map/ppermute | solution.py:19
  51.8 3.9 %collective-permute-start.6 = (bf16[4,32,128]{2,1,0:T(8,128)(2,1)S(1)}, bf16[4,32,128]{2,1,0:T(8,128)(2,1)S(1)}, u32[]{:S(2)}, u32[]{:S(2)}) collective-permute-start(bf16[4,32,128]{2,1,0:T(8,128)(2,1)S(1)} %get-tuple-element.14), channel_id=1, source_target_pairs={{0,12},{4,0},{8,4},{12,8},{1,13},{5,1},{9,5},{13,9},{2,14},{6,2},{... | collective-permute-start | bytes 98312 | tf_op jit(solution)/shard_map/ppermute | solution.py:19
  55.7 4.3 %collective-permute-start.9 = (f32[4,32,128]{2,1,0:T(8,128)S(1)}, f32[4,32,128]{2,1,0:T(8,128)S(1)}, u32[]{:S(2)}, u32[]{:S(2)}) collective-permute-start(f32[4,32,128]{2,1,0:T(8,128)S(1)} %fusion.7), channel_id=1, source_target_pairs={{0,2},{1,3},{2,0},{3,1},{4,6},{5,7},{6,4},{7,5},{8,10},{9,11},{10,... | collective-permute-start | bytes 196616 | tf_op jit(solution)/shard_map/ppermute | solution.py:24
  60.0 1.4 %collective-permute-start.10 = (f32[2,4,32,128]{3,2,1,0:T(8,128)S(1)}, f32[2,4,32,128]{3,2,1,0:T(8,128)S(1)}, u32[]{:S(2)}, u32[]{:S(2)}) collective-permute-start(f32[2,4,32,128]{3,2,1,0:T(8,128)S(1)} %maximum_select_fusion.2), channel_id=1, source_target_pairs={{0,1},{1,0},{2,3},{3,2},{4,5},{5,4},{6,7},{7,6},{8,9},{9,8},{10,11... | collective-permute-start | bytes 393224 | tf_op jit(solution)/shard_map/ppermute | solution.py:24

commit v7 on v6

--- a/solution.py
+++ b/solution.py
@@ -175,7 +175,16 @@
         col_ids,
         row_count,
     )
-    arrived = passed_along(input_grad, "section", -1)
+    block_count = row_ids.shape[0]
+    if block_count < row_count:
+        hit = jnp.take(input_grad, row_ids, axis=0)
+        payload = jnp.concatenate([hit.reshape(-1), row_ids.astype(jnp.bfloat16)])
+        payload = passed_along(payload, "section", -1)
+        got_rows = payload[hit.size:].astype(jnp.int32)
+        got = payload[: hit.size].reshape(hit.shape)
+        arrived = jnp.zeros_like(input_grad).at[got_rows].set(got)
+    else:
+        arrived = passed_along(input_grad, "section", -1)
     arrived = jnp.transpose(arrived, (1, 0, 2)).reshape(
         micro_count, activations.shape[2], activations.shape[3]
     )

time: 70.3 us -> 64.7 us (0.920)
  waiting for transfers between devices: 22.4 us -> 12.8 us
  local copies, waits for them, and re-layouts: 8.2 us -> 10.4 us
  other arithmetic: 7.27 us -> 8.92 us
    ppermute x6, waiting for transfers between devices: 13.5 us -> 7.48 us  [swapped(): return lax.ppermute(x, axis, [(i, i ^ 1 << bit) for i in range(n)])]
    ppermute x1, waiting for transfers between devices: 4.99 us -> 0.24 us  [passed_along(): return lax.ppermute(block, axis, route)]
    ppermute x3, waiting for transfers between devices: 3.9 us -> 5.07 us  [shifted(): return lax.ppermute(x, axis, [(i, (i + k) % n) for i in range(n)])]
    scatter x0 -> x1, local copies, waits for them, and re-layouts: none -> 1.14 us  [local(): arrived = jnp.zeros_like(input_grad).at[got_rows].set(got)]
    unnamed x6 -> x8, local copies, waits for them, and re-layouts: 0.02 us -> 0.89 us
    select_n x0 -> x3, other arithmetic: none -> 0.76 us  [the longest x2 0.75 us: local(): hit = jnp.take(input_grad, row_ids, axis=0)]
  transfers between devices with their start and end apart: 11 -> 11, of which waited for: 10 -> 8; matrix products, arithmetic and copies ran while one was open for 3% -> 11% of each run, Pallas kernels for 0% -> 0%
where the time goes in v7:
time: 64.7 us; the launch traced here: 64.4 us
  starting transfers between devices  22.6 us (35%)
  waiting for transfers between devices  12.8 us (20%)
  local copies, waits for them, and re-layouts  10.4 us (16%)
  other arithmetic  8.92 us (14%)
  Pallas kernels  8.81 us (14%)
  between operations  0.95 us (1%)
    ppermute x6, starting transfers between devices, swapped(): return lax.ppermute(x, axis, [(i, i ^ 1 << bit) for i in range(n)])  16 us
    pallas_call x1, Pallas kernels, block_pass(): pl.pallas_call(block_kernel, out_shape=(jax.ShapeDtypeStruct((row_count,...  8.81 us
    ppermute x6, waiting for transfers between devices, swapped(): return lax.ppermute(x, axis, [(i, i ^ 1 << bit) for i in range(n)])  7.48 us
    ppermute x3, waiting for transfers between devices, shifted(): return lax.ppermute(x, axis, [(i, (i + k) % n) for i in range(n)])  5.07 us
    ppermute x3, starting transfers between devices, shifted(): return lax.ppermute(x, axis, [(i, (i + k) % n) for i in range(n)])  4.65 us
    select_n x2, other arithmetic, local(): received = jnp.take(arrived, order, axis=0)  1.73 us
    select_n x3, other arithmetic, butterfly_gather(): jnp.where(mine_low, jnp.stack([held, other]), jnp.stack([other, held]))  1.62 us
    reshape x1, local copies, waits for them, and re-layouts, local(): pieces[:, :weight_len].reshape(n_fsdp * blocks_dev, block_size, block_size)  1.36 us
  transfers between devices with their start and end apart: 11, of which 8 were waited for; matrix products, arithmetic and copies ran while one was open for 11% of the time, Pallas kernels for 0%

profile of v7, /device:TPU:0, one launch (start us, length us, event | category | flops | bytes accessed | tf_op | source)
XLA Modules:
  0.0 64.4 jit_solution(15458166726576263485)
XLA Ops:
  0.6 0.7 %convert_element_type.48 = bf16[1,4,2]{1,2,0:T(2,128)(2,1)S(1)} convert(s32[1,4,2]{1,2,0:T(2,128)} %param.8) | non-fusion elementwise | flops 8 | bytes 48 | tf_op jit(solution)/shard_map/convert_element_type | solution.py:151
  1.5 0.9 %pad_maximum_fusion.1 = bf16[65544]{0:T(1024)(128)(2,1)S(1)} fusion(bf16[8]{0:T(256)(128)(2,1)S(1)} %convert_element_type.49, bf16[65536]{0:T(1024)(128)(2,1)} %bitcast.69), kind=kLoop, calls=%fused_computation.18 | loop fusion | flops 262176 | bytes 262176 | tf_op jit(solution)/shard_map/concatenate | solution.py:150
  2.4 0.7 %collective-permute-start = (bf16[65544]{0:T(1024)(128)(2,1)S(1)}, bf16[65544]{0:T(1024)(128)(2,1)S(1)}, u32[]{:S(2)}, u32[]{:S(2)}) collective-permute-start(bf16[65544]{0:T(1024)(128)(2,1)S(1)} %pad_maximum_fusion.1), channel_id=1, source_target_pairs={{0,0},{13,1},{10,2},{7,3},{4,4},{1,5},{14,6},{11,7},{8,8},{5,9},{2... | collective-permute-start | bytes 393272 | tf_op jit(solution)/shard_map/ppermute | solution.py:160
  3.3 12.0 %collective-permute-start.1 = (bf16[1,65544]{1,0:T(2,128)(2,1)S(1)}, bf16[1,65544]{1,0:T(2,128)(2,1)S(1)}, u32[]{:S(2)}, u32[]{:S(2)}) collective-permute-start(bf16[1,65544]{1,0:T(2,128)(2,1)S(1)} %stack.68), channel_id=1, source_target_pairs={{0,2},{1,3},{2,0},{3,1},{4,6},{5,7},{6,4},{7,5},{8,10},{9,11},{10,... | collective-permute-start | bytes 393272 | tf_op jit(solution)/shard_map/ppermute | solution.py:24
  15.2 0.7 %compare_select_fusion.2 = s32[4]{0:T(128)S(1)} fusion(s32[4]{0:T(128)} %param.9), kind=kLoop, calls=%fused_computation.38 | loop fusion | flops 12 | bytes 32 | tf_op jit(solution)/shard_map/jit(_take)/jit(_where)/select_n | solution.py:191
  16.0 4.4 %collective-permute-done.1 = bf16[1,65544]{1,0:T(2,128)(2,1)S(1)} collective-permute-done((bf16[1,65544]{1,0:T(2,128)(2,1)S(1)}, bf16[1,65544]{1,0:T(2,128)(2,1)S(1)}, u32[]{:S(2)}, u32[]{:S(2)}) %collective-permute-start.1) | collective-permute-done | bytes 131120 | tf_op jit(solution)/shard_map/ppermute | solution.py:24
  20.4 1.6 %broadcast_select_fusion = bf16[2,1,65544]{2,1,0:T(2,128)(2,1)S(1)} fusion(pred[]{:T(512)S(6)} %eq.24, bf16[1,1,65544]{2,1,0:T(2,128)(2,1)S(1)} %bitcast.56, bf16[1,1,65544]{2,1,0:T(2,128)(2,1)S(1)} %stack.67), kind=kLoop, calls=%fused_computation.3 | loop fusion | flops 393264 | bytes 524353 | tf_op jit(solution)/shard_map/jit(_where)/select_n | solution.py:125
  22.4 1.2 %fusion.1 = bf16[1,2,1,65544]{3,1,2,0:T(2,128)(2,1)S(1)} fusion(pred[]{:T(512)S(6)} %eq.24, bf16[1,1,65544]{2,1,0:T(2,128)(2,1)S(1)} %bitcast.57, bf16[1,1,65544]{2,1,0:T(2,128)(2,1)S(1)} %stack.67), kind=kLoop, calls=%fused_computation.12 | loop fusion | flops 1179792 | bytes 524353 | tf_op jit(solution)/shard_map/stack | solution.py:125
  23.9 0.9 %fusion = bf16[2,2,1,65544]{3,0,2,1:T(2,128)(2,1)S(1)} fusion(pred[]{:T(512)S(6)} %eq.12, bf16[1,2,1,65544]{3,1,2,0:T(2,128)(2,1)S(1)} %bitcast.64, bf16[1,2,1,65544]{3,1,2,0:T(2,128)(2,1)S(1)} %fusion.1), kind=kLoop, calls=%fused_computation.7 | loop fusion | flops 786528 | bytes 1048705 | tf_op jit(solution)/shard_map/transpose | solution.py:128
  25.3 0.9 %reshape_transpose_reshape.3 = bf16[4,65544]{1,0:T(4,128)(2,1)S(1)} reshape(bf16[2,2,1,65544]{3,1,0,2:T(2,128)(2,1)S(1)} %copy.37) | data formatting | bytes 1048704 | tf_op jit(solution)/shard_map/reshape;transpose;reshape | solution.py:164
  26.4 0.6 fusion.8
  27.1 0.8 %iota_reduce_fusion = (pred[16]{0:T(512)(128)(4,1)}, s32[16]{0:T(128)}) fusion(s32[16]{0:T(128)S(1)} %get-tuple-element.9.cols_ref), kind=kLoop, calls=%fused_computation.31 | loop fusion | flops 1936 | bytes 144 | tf_op jit(solution)/shard_map/block_pass/reduce | solution.py:86
  27.8 1.4 %reshape.388.w_ref = bf16[16,128,128]{2,1,0:T(8,128)(2,1)} reshape(bf16[4,65536]{1,0:T(4,128)(2,1)S(1)} %slice.50) | data formatting | bytes 1048576 | tf_op jit(solution)/shard_map/reshape | solution.py:165
  29.2 8.8 %shard_map.68 = (bf16[28,128,128]{2,1,0:T(8,128)(2,1)}, f32[16,128,128]{2,1,0:T(8,128)}) custom-call(s32[16]{0:T(128)} %get-tuple-element.10.rows_ref, s32[16]{0:T(128)} %copy-done.1, s32[16]{0:T(128)} %get-tuple-element.5.rep_ref, bf16[128,3584]{1,0:T(8,128)(2,1)} %bitcast.60, bf16[128,14336]{1,0:T(8,128)(2,1)} %bitcast.53, ...), custom_call_target="tpu_custom_call" | custom-call | flops 201326592 | bytes 3538944 | tf_op jit(solution)/shard_map/pallas_call | solution.py:90
  38.0 1.3 %constant_dynamic-slice_fusion.1 = (f32[4,4,2,1,32,128]{5,4,3,2,1,0:T(8,128)S(1)}, f32[4,4,2,1,32,128]{5,4,3,2,1,0:T(8,128)S(1)}) fusion(f32[4,4,2,2,32,128]{5,4,3,2,1,0:T(8,128)} %bitcast.59, s32[]{:T(128)S(6)} %select_n.147, s32[]{:T(128)S(6)} %select_n.148), kind=kLoop, calls=%fused_computation.42 | loop fusion | bytes 2097160 | tf_op jit(solution)/shard_map/jit(dynamic_index_in_dim)/dynamic_slice | solution.py:197
  40.0 0.5 copy-done
  40.5 0.6 %gather_fusion = bf16[16,128,128]{2,1,0:T(8,128)(2,1)S(1)} fusion(bf16[28,128,128]{2,1,0:T(8,128)(2,1)S(1)} %copy-done, s32[1024]{0:T(1024)S(1)} %pad_clamp_fusion.1), kind=kCustom, calls=%fused_computation | custom fusion | bytes 1048640 | tf_op jit(solution)/shard_map/jit(_take)/gather | solution.py:180
  41.6 1.8 %collective-permute-start.5 = (bf16[4,4,32,128]{3,2,1,0:T(8,128)(2,1)S(1)}, bf16[4,4,32,128]{3,2,1,0:T(8,128)(2,1)S(1)}, u32[]{:S(2)}, u32[]{:S(2)}) collective-permute-start(bf16[4,4,32,128]{3,2,1,0:T(8,128)(2,1)S(1)} %fusion.4), channel_id=1, source_target_pairs={{0,2},{1,3},{2,0},{3,1},{4,6},{5,7},{6,4},{7,5},{8,10},{9,11},{10,... | collective-permute-start | bytes 393224 | tf_op jit(solution)/shard_map/ppermute | solution.py:24
  43.4 1.3 %collective-permute-start.3 = (bf16[262160]{0:T(1024)(128)(2,1)S(1)}, bf16[262160]{0:T(1024)(128)(2,1)S(1)}, u32[]{:S(2)}, u32[]{:S(2)}) collective-permute-start(bf16[262160]{0:T(1024)(128)(2,1)S(1)} %pad_maximum_fusion), channel_id=1, source_target_pairs={{16,0},{17,1},{18,2},{19,3},{20,4},{21,5},{22,6},{23,7},{24,8},{25... | collective-permute-start | bytes 1572968 | tf_op jit(solution)/shard_map/ppermute | solution.py:14
  44.7 2.5 %collective-permute-done.5 = bf16[4,4,32,128]{3,2,1,0:T(8,128)(2,1)S(1)} collective-permute-done((bf16[4,4,32,128]{3,2,1,0:T(8,128)(2,1)S(1)}, bf16[4,4,32,128]{3,2,1,0:T(8,128)(2,1)S(1)}, u32[]{:S(2)}, u32[]{:S(2)}) %collective-permute-start.5) | collective-permute-done | bytes 131104 | tf_op jit(solution)/shard_map/ppermute | solution.py:24
  47.3 4.0 %collective-permute-start.6 = (bf16[4,32,128]{2,1,0:T(8,128)(2,1)S(1)}, bf16[4,32,128]{2,1,0:T(8,128)(2,1)S(1)}, u32[]{:S(2)}, u32[]{:S(2)}) collective-permute-start(bf16[4,32,128]{2,1,0:T(8,128)(2,1)S(1)} %get-tuple-element.15), channel_id=1, source_target_pairs={{0,12},{4,0},{8,4},{12,8},{1,13},{5,1},{9,5},{13,9},{2,14},{6,2},{... | collective-permute-start | bytes 98312 | tf_op jit(solution)/shard_map/ppermute | solution.py:19
  51.3 0.6 collective-permute-start.8
  51.9 0.9 %collective-permute-done.6 = bf16[4,32,128]{2,1,0:T(8,128)(2,1)S(1)} collective-permute-done((bf16[4,32,128]{2,1,0:T(8,128)(2,1)S(1)}, bf16[4,32,128]{2,1,0:T(8,128)(2,1)S(1)}, u32[]{:S(2)}, u32[]{:S(2)}) %collective-permute-start.6) | collective-permute-done | bytes 32800 | tf_op jit(solution)/shard_map/ppermute | solution.py:19
  52.9 3.2 %collective-permute-done.7 = bf16[4,32,128]{2,1,0:T(8,128)(2,1)S(1)} collective-permute-done((bf16[4,32,128]{2,1,0:T(8,128)(2,1)S(1)}, bf16[4,32,128]{2,1,0:T(8,128)(2,1)S(1)}, u32[]{:S(2)}, u32[]{:S(2)}) %collective-permute-start.7) | collective-permute-done | bytes 32800 | tf_op jit(solution)/shard_map/ppermute | solution.py:19
  56.1 0.9 %collective-permute-done.8 = bf16[4,32,128]{2,1,0:T(8,128)(2,1)S(1)} collective-permute-done((bf16[4,32,128]{2,1,0:T(8,128)(2,1)S(1)}, bf16[4,32,128]{2,1,0:T(8,128)(2,1)S(1)}, u32[]{:S(2)}, u32[]{:S(2)}) %collective-permute-start.8) | collective-permute-done | bytes 32800 | tf_op jit(solution)/shard_map/ppermute | solution.py:19
  57.0 1.8 %collective-permute-start.9 = (f32[4,32,128]{2,1,0:T(8,128)S(1)}, f32[4,32,128]{2,1,0:T(8,128)S(1)}, u32[]{:S(2)}, u32[]{:S(2)}) collective-permute-start(f32[4,32,128]{2,1,0:T(8,128)S(1)} %fusion.7), channel_id=1, source_target_pairs={{0,2},{1,3},{2,0},{3,1},{4,6},{5,7},{6,4},{7,5},{8,10},{9,11},{10,... | collective-permute-start | bytes 196616 | tf_op jit(solution)/shard_map/ppermute | solution.py:24
  59.3 1.1 %scatter_fusion = bf16[28,128,128]{2,1,0:T(8,128)(2,1)S(1)} fusion(bf16[28,128,128]{2,1,0:T(8,128)(2,1)S(1)} %broadcast_in_dim.31, s32[16]{0:T(128)S(1)} %compare_select_fusion.1, bf16[16,128,128]{2,1,0:T(8,128)(2,1)S(1)} %bitcast.54), kind=kCustom, calls=%fused_computation.2 | custom fusion | bytes 1572928 | tf_op jit(solution)/shard_map/scatter | solution.py:185
  60.5 0.6 copy.38
  61.1 0.5 reshape.390
  61.6 0.6 gather_fusion.1
  62.3 1.1 %bitcast_select_fusion = bf16[1,4,32,3584]{3,2,1,0:T(8,128)(2,1)} fusion(bf16[4,32,3584]{2,1,0:T(8,128)(2,1)S(1)} %gather_fusion.1, pred[4]{0:T(512)(128)(4,1)S(1)} %compare_and_fusion), kind=kLoop, calls=%fused_computation.5 | loop fusion | flops 458752 | bytes 1835012 | tf_op jit(solution)/shard_map/jit(_take)/select_n | solution.py:191
  63.7 0.7 %copy.42 = f32[4,4,32,128]{3,2,1,0:T(8,128)} copy(f32[4,4,32,128]{3,2,0,1:T(8,128)S(1)} %bitcast.58) | data formatting | bytes 524288 | tf_op jit(solution)/shard_map/div | solution.py:210
  (46 shorter events, 3.8 us)
Async XLA Ops:
  2.4 0.7 %collective-permute-start = (bf16[65544]{0:T(1024)(128)(2,1)S(1)}, bf16[65544]{0:T(1024)(128)(2,1)S(1)}, u32[]{:S(2)}, u32[]{:S(2)}) collective-permute-start(bf16[65544]{0:T(1024)(128)(2,1)S(1)} %pad_maximum_fusion.1), channel_id=1, source_target_pairs={{0,0},{13,1},{10,2},{7,3},{4,4},{1,5},{14,6},{11,7},{8,8},{5,9},{2... | collective-permute-start | bytes 393272 | tf_op jit(solution)/shard_map/ppermute | solution.py:160
  3.3 17.2 %collective-permute-start.1 = (bf16[1,65544]{1,0:T(2,128)(2,1)S(1)}, bf16[1,65544]{1,0:T(2,128)(2,1)S(1)}, u32[]{:S(2)}, u32[]{:S(2)}) collective-permute-start(bf16[1,65544]{1,0:T(2,128)(2,1)S(1)} %stack.68), channel_id=1, source_target_pairs={{0,2},{1,3},{2,0},{3,1},{4,6},{5,7},{6,4},{7,5},{8,10},{9,11},{10,... | collective-permute-start | bytes 393272 | tf_op jit(solution)/shard_map/ppermute | solution.py:24
  22.3 1.6 %collective-permute-start.2 = (bf16[2,1,65544]{2,0,1:T(2,128)(2,1)S(1)}, bf16[2,1,65544]{2,0,1:T(2,128)(2,1)S(1)}, u32[]{:S(2)}, u32[]{:S(2)}) collective-permute-start(bf16[2,1,65544]{2,0,1:T(2,128)(2,1)S(1)} %copy.36), channel_id=1, source_target_pairs={{0,1},{1,0},{2,3},{3,2},{4,5},{5,4},{6,7},{7,6},{8,9},{9,8},{10,11... | collective-permute-start | bytes 786536 | tf_op jit(solution)/shard_map/ppermute | solution.py:24
  27.1 2.1 %copy-start.1 = (s32[16]{0:T(128)}, s32[16]{0:T(128)S(1)}, u32[]{:S(2)}) copy-start(s32[16]{0:T(128)S(1)} %get-tuple-element.9.cols_ref) | copy-start | bytes 196
  38.0 1.6 %copy-start.3 = (s32[4]{0:T(128)S(1)}, s32[4]{0:T(128)}, u32[]{:S(2)}) copy-start(s32[4]{0:T(128)} %param.9) | copy-start | bytes 52
  39.3 0.7 %copy-start.2 = (s32[16]{0:T(128)S(1)}, s32[16]{0:T(128)}, u32[]{:S(2)}) copy-start(s32[16]{0:T(128)} %get-tuple-element.10.rows_ref) | copy-start | bytes 196
  39.4 1.2 %copy-start = (bf16[28,128,128]{2,1,0:T(8,128)(2,1)S(1)}, bf16[28,128,128]{2,1,0:T(8,128)(2,1)}, u32[]{:S(2)}) copy-start(bf16[28,128,128]{2,1,0:T(8,128)(2,1)} %get-tuple-element.6) | copy-start | bytes 2752516
  39.4 2.0 %collective-permute-start.4 = (f32[4,4,2,32,128]{4,3,1,0,2:T(8,128)S(1)}, f32[4,4,2,32,128]{4,3,1,0,2:T(8,128)S(1)}, u32[]{:S(2)}, u32[]{:S(2)}) collective-permute-start(f32[4,4,2,32,128]{4,3,1,0,2:T(8,128)S(1)} %bitcast.63), channel_id=1, source_target_pairs={{0,1},{1,0},{2,3},{3,2},{4,5},{5,4},{6,7},{7,6},{8,9},{9,8},{10,11... | collective-permute-start | bytes 1572872 | tf_op jit(solution)/shard_map/ppermute | solution.py:24
  41.6 5.6 %collective-permute-start.5 = (bf16[4,4,32,128]{3,2,1,0:T(8,128)(2,1)S(1)}, bf16[4,4,32,128]{3,2,1,0:T(8,128)(2,1)S(1)}, u32[]{:S(2)}, u32[]{:S(2)}) collective-permute-start(bf16[4,4,32,128]{3,2,1,0:T(8,128)(2,1)S(1)} %fusion.4), channel_id=1, source_target_pairs={{0,2},{1,3},{2,0},{3,1},{4,6},{5,7},{6,4},{7,5},{8,10},{9,11},{10,... | collective-permute-start | bytes 393224 | tf_op jit(solution)/shard_map/ppermute | solution.py:24
  43.4 15.7 %collective-permute-start.3 = (bf16[262160]{0:T(1024)(128)(2,1)S(1)}, bf16[262160]{0:T(1024)(128)(2,1)S(1)}, u32[]{:S(2)}, u32[]{:S(2)}) collective-permute-start(bf16[262160]{0:T(1024)(128)(2,1)S(1)} %pad_maximum_fusion), channel_id=1, source_target_pairs={{16,0},{17,1},{18,2},{19,3},{20,4},{21,5},{22,6},{23,7},{24,8},{25... | collective-permute-start | bytes 1572968 | tf_op jit(solution)/shard_map/ppermute | solution.py:14
  47.3 5.6 %collective-permute-start.6 = (bf16[4,32,128]{2,1,0:T(8,128)(2,1)S(1)}, bf16[4,32,128]{2,1,0:T(8,128)(2,1)S(1)}, u32[]{:S(2)}, u32[]{:S(2)}) collective-permute-start(bf16[4,32,128]{2,1,0:T(8,128)(2,1)S(1)} %get-tuple-element.15), channel_id=1, source_target_pairs={{0,12},{4,0},{8,4},{12,8},{1,13},{5,1},{9,5},{13,9},{2,14},{6,2},{... | collective-permute-start | bytes 98312 | tf_op jit(solution)/shard_map/ppermute | solution.py:19
  51.3 4.8 %collective-permute-start.7 = (bf16[4,32,128]{2,1,0:T(8,128)(2,1)S(1)}, bf16[4,32,128]{2,1,0:T(8,128)(2,1)S(1)}, u32[]{:S(2)}, u32[]{:S(2)}) collective-permute-start(bf16[4,32,128]{2,1,0:T(8,128)(2,1)S(1)} %get-tuple-element.17), channel_id=1, source_target_pairs={{0,8},{4,12},{8,0},{12,4},{1,9},{5,13},{9,1},{13,5},{2,10},{6,14},... | collective-permute-start | bytes 98312 | tf_op jit(solution)/shard_map/ppermute | solution.py:19
  51.3 5.7 %collective-permute-start.8 = (bf16[4,32,128]{2,1,0:T(8,128)(2,1)S(1)}, bf16[4,32,128]{2,1,0:T(8,128)(2,1)S(1)}, u32[]{:S(2)}, u32[]{:S(2)}) collective-permute-start(bf16[4,32,128]{2,1,0:T(8,128)(2,1)S(1)} %get-tuple-element.16), channel_id=1, source_target_pairs={{0,4},{4,8},{8,12},{12,0},{1,5},{5,9},{9,13},{13,1},{2,6},{6,10},{... | collective-permute-start | bytes 98312 | tf_op jit(solution)/shard_map/ppermute | solution.py:19
  57.0 5.2 %collective-permute-start.9 = (f32[4,32,128]{2,1,0:T(8,128)S(1)}, f32[4,32,128]{2,1,0:T(8,128)S(1)}, u32[]{:S(2)}, u32[]{:S(2)}) collective-permute-start(f32[4,32,128]{2,1,0:T(8,128)S(1)} %fusion.7), channel_id=1, source_target_pairs={{0,2},{1,3},{2,0},{3,1},{4,6},{5,7},{6,4},{7,5},{8,10},{9,11},{10,... | collective-permute-start | bytes 196616 | tf_op jit(solution)/shard_map/ppermute | solution.py:24
  62.2 1.4 %collective-permute-start.10 = (f32[2,4,32,128]{3,2,1,0:T(8,128)S(1)}, f32[2,4,32,128]{3,2,1,0:T(8,128)S(1)}, u32[]{:S(2)}, u32[]{:S(2)}) collective-permute-start(f32[2,4,32,128]{3,2,1,0:T(8,128)S(1)} %maximum_select_fusion.2), channel_id=1, source_target_pairs={{0,1},{1,0},{2,3},{3,2},{4,5},{5,4},{6,7},{7,6},{8,9},{9,8},{10,11... | collective-permute-start | bytes 393224 | tf_op jit(solution)/shard_map/ppermute | solution.py:24

commit v8 on v7

--- a/solution.py
+++ b/solution.py
@@ -146,10 +146,13 @@
 
     assert n_fsdp % n_dp == 0
     per_dp = n_fsdp // n_dp
-    weight_len = blocks_dev * block_size * block_size
-    payload = jnp.concatenate(
-        [own_blocks.reshape(-1), pattern[0].reshape(-1).astype(jnp.bfloat16)]
-    )
+    weight_rows = blocks_dev * block_size
+    assert 2 * blocks_dev <= block_size
+    index_tile = jnp.zeros((16, block_size), jnp.bfloat16)
+    index_tile = index_tile.at[0, : 2 * blocks_dev].set(
+        pattern[0].reshape(-1).astype(jnp.bfloat16)
+    )
+    payload = jnp.concatenate([own_blocks.reshape(weight_rows, block_size), index_tile])
     fetched = []
     for m in range(per_dp):
         pairs = []
@@ -160,10 +163,14 @@
         fetched.append(lax.ppermute(payload, ("fsdp", "dp"), pairs))
     fetched = jnp.stack(fetched)
     pieces = butterfly_gather(fetched, "dp", list(reversed(range(dp_bits))))
-    pieces = pieces.reshape((n_dp, per_dp, -1))
-    pieces = jnp.transpose(pieces, (1, 0, 2)).reshape(n_fsdp, -1)
-    weights = pieces[:, :weight_len].reshape(n_fsdp * blocks_dev, block_size, block_size)
-    all_indices = pieces[:, weight_len:].reshape(n_fsdp * blocks_dev, 2).astype(jnp.int32)
+    pieces = pieces.reshape((n_dp, per_dp) + payload.shape)
+    pieces = jnp.transpose(pieces, (1, 0, 2, 3)).reshape((n_fsdp,) + payload.shape)
+    weights = pieces[:, :weight_rows].reshape(n_fsdp * blocks_dev, block_size, block_size)
+    all_indices = (
+        pieces[:, weight_rows, : 2 * blocks_dev]
+        .reshape(n_fsdp * blocks_dev, 2)
+        .astype(jnp.int32)
+    )
 
     row_ids = all_indices[:, 0]
     col_ids = all_indices[:, 1]

time: 64.7 us -> 58.8 us (0.909)
  other arithmetic: 8.92 us -> 5.38 us
  local copies, waits for them, and re-layouts: 10.4 us -> 8.53 us
  waiting for transfers between devices: 12.8 us -> 11.6 us
  starting transfers between devices: 22.6 us -> 23.3 us
    select_n x3, other arithmetic: 1.62 us -> 0.05 us  [butterfly_gather(): jnp.where(mine_low, jnp.stack([held, other]), jnp.stack([other, held]))]
    reshape x1 -> x0, local copies, waits for them, and re-layouts: 1.36 us -> none  [local(): pieces[:, :weight_len].reshape(n_fsdp * blocks_dev, block_size, block_size)]
    another operation x3 -> x0, local copies, waits for them, and re-layouts: 1.18 us -> none  [the longest x1 0.9 us: local(): pieces = jnp.transpose(pieces, (1, 0, 2)).reshape(n_fsdp, -1)]
    another operation x1, other arithmetic: 1.18 us -> 0.03 us  [butterfly_gather(): jnp.stack([held, other])]
    ppermute x6, waiting for transfers between devices: 7.48 us -> 6.54 us  [swapped(): return lax.ppermute(x, axis, [(i, i ^ 1 << bit) for i in range(n)])]
    slice x1 -> x2, local copies, waits for them, and re-layouts: 0.18 us -> 1.07 us  [local(): pieces[:, :weight_rows].reshape(n_fsdp * blocks_dev, block_size, block_size)]
    transpose x1, other arithmetic: 0.92 us -> 0.09 us  [butterfly_gather(): return jnp.transpose(held, perm)]
  transfers between devices with their start and end apart: 11 -> 11, of which waited for: 8 -> 7; matrix products, arithmetic and copies ran while one was open for 11% -> 10% of each run, Pallas kernels for 0% -> 0%
where the time goes in v8:
time: 58.8 us; the launch traced here: 58.4 us
  starting transfers between devices  23.3 us (40%)
  waiting for transfers between devices  11.6 us (20%)
  Pallas kernels  8.72 us (15%)
  local copies, waits for them, and re-layouts  8.53 us (15%)
  other arithmetic  5.38 us (9%)
  between operations  0.9 us (2%)
    ppermute x6, starting transfers between devices, swapped(): return lax.ppermute(x, axis, [(i, i ^ 1 << bit) for i in range(n)])  16.2 us
    pallas_call x1, Pallas kernels, block_pass(): pl.pallas_call(block_kernel, out_shape=(jax.ShapeDtypeStruct((row_count,...  8.72 us
    ppermute x6, waiting for transfers between devices, swapped(): return lax.ppermute(x, axis, [(i, i ^ 1 << bit) for i in range(n)])  6.54 us
    ppermute x3, starting transfers between devices, shifted(): return lax.ppermute(x, axis, [(i, (i + k) % n) for i in range(n)])  5.08 us
    ppermute x3, waiting for transfers between devices, shifted(): return lax.ppermute(x, axis, [(i, (i + k) % n) for i in range(n)])  5.07 us
    select_n x2, other arithmetic, local(): received = jnp.take(arrived, order, axis=0)  1.74 us
    dynamic_slice x1, local copies, waits for them, and re-layouts, local(): keep = lax.dynamic_index_in_dim(held, mine, axis_at, keepdims=False)  1.31 us
    ppermute x1, starting transfers between devices, passed_along(): return lax.ppermute(block, axis, route)  1.29 us
  transfers between devices with their start and end apart: 11, of which 7 were waited for; matrix products, arithmetic and copies ran while one was open for 10% of the time, Pallas kernels for 0%

profile of v8, /device:TPU:0, one launch (start us, length us, event | category | flops | bytes accessed | tf_op | source)
XLA Modules:
  0.0 58.4 jit_solution(7436774732779730979)
XLA Ops:
  0.6 0.7 %convert_element_type.53 = bf16[1,4,2]{1,2,0:T(2,128)(2,1)S(1)} convert(s32[1,4,2]{1,2,0:T(2,128)} %param.10) | non-fusion elementwise | flops 8 | bytes 48 | tf_op jit(solution)/shard_map/convert_element_type | solution.py:153
  1.5 0.9 %fusion.5 = bf16[528,128]{1,0:T(8,128)(2,1)S(1)} fusion(bf16[1,8]{1,0:T(2,128)(2,1)S(1)} %convert_element_type.54, bf16[512,128]{1,0:T(8,128)(2,1)} %bitcast.79), kind=kLoop, calls=%fused_computation.20 | loop fusion | flops 405504 | bytes 266256 | tf_op jit(solution)/shard_map/concatenate | solution.py:155
  2.4 0.7 %collective-permute-start = (bf16[528,128]{1,0:T(8,128)(2,1)S(1)}, bf16[528,128]{1,0:T(8,128)(2,1)S(1)}, u32[]{:S(2)}, u32[]{:S(2)}) collective-permute-start(bf16[528,128]{1,0:T(8,128)(2,1)S(1)} %fusion.5), channel_id=1, source_target_pairs={{0,0},{13,1},{10,2},{7,3},{4,4},{1,5},{14,6},{11,7},{8,8},{5,9},{2... | collective-permute-start | bytes 405512 | tf_op jit(solution)/shard_map/ppermute | solution.py:163
  3.1 12.0 %collective-permute-start.1 = (bf16[1,528,128]{2,1,0:T(8,128)(2,1)S(1)}, bf16[1,528,128]{2,1,0:T(8,128)(2,1)S(1)}, u32[]{:S(2)}, u32[]{:S(2)}) collective-permute-start(bf16[1,528,128]{2,1,0:T(8,128)(2,1)S(1)} %bitcast.68), channel_id=1, source_target_pairs={{0,2},{1,3},{2,0},{3,1},{4,6},{5,7},{6,4},{7,5},{8,10},{9,11},{10,... | collective-permute-start | bytes 405512 | tf_op jit(solution)/shard_map/ppermute | solution.py:24
  15.1 3.0 %collective-permute-done.1 = bf16[1,528,128]{2,1,0:T(8,128)(2,1)S(1)} collective-permute-done((bf16[1,528,128]{2,1,0:T(8,128)(2,1)S(1)}, bf16[1,528,128]{2,1,0:T(8,128)(2,1)S(1)}, u32[]{:S(2)}, u32[]{:S(2)}) %collective-permute-start.1) | collective-permute-done | bytes 135200 | tf_op jit(solution)/shard_map/ppermute | solution.py:24
  18.2 0.7 %compare_select_fusion.2 = s32[4]{0:T(128)S(1)} fusion(s32[4]{0:T(128)} %param.11), kind=kLoop, calls=%fused_computation.40 | loop fusion | flops 12 | bytes 32 | tf_op jit(solution)/shard_map/jit(_take)/jit(_where)/select_n | solution.py:198
  18.9 0.8 %collective-permute-done.2 = bf16[2,1,528,128]{3,2,1,0:T(8,128)(2,1)S(1)} collective-permute-done((bf16[2,1,528,128]{3,2,1,0:T(8,128)(2,1)S(1)}, bf16[2,1,528,128]{3,2,1,0:T(8,128)(2,1)S(1)}, u32[]{:S(2)}, u32[]{:S(2)}) %collective-permute-start.2) | collective-permute-done | bytes 270368 | tf_op jit(solution)/shard_map/ppermute | solution.py:24
  19.8 0.4 copy.34
  20.5 0.6 %fusion.10 = (s32[16]{0:T(128)S(1)}, s32[16]{0:T(128)S(1)}, s32[16]{0:T(128)}) fusion(s32[16,2]{1,0:T(8,128)S(1)} %reshape.426), kind=kLoop, calls=%fused_computation.36 | loop fusion | flops 48 | bytes 320 | tf_op jit(solution)/shard_map/jit(_take)/jit(_where)/select_n | solution.py:187
  21.2 0.8 %iota_reduce_fusion = (pred[16]{0:T(512)(128)(4,1)}, s32[16]{0:T(128)}) fusion(s32[16]{0:T(128)S(1)} %get-tuple-element.21.cols_ref), kind=kLoop, calls=%fused_computation.33 | loop fusion | flops 1936 | bytes 144 | tf_op jit(solution)/shard_map/block_pass/reduce | solution.py:86
  21.9 0.9 %copy.35 = bf16[4,512,128]{2,1,0:T(8,128)(2,1)} copy(bf16[4,512,128]{2,0,1:T(4,128)(2,1)S(1)} %slice.66) | data formatting | bytes 1048576 | tf_op jit(solution)/shard_map/slice | solution.py:168
  22.8 8.7 %shard_map.68 = (bf16[28,128,128]{2,1,0:T(8,128)(2,1)}, f32[16,128,128]{2,1,0:T(8,128)}) custom-call(s32[16]{0:T(128)} %get-tuple-element.22.rows_ref, s32[16]{0:T(128)} %copy-done.1, s32[16]{0:T(128)} %get-tuple-element.17.rep_ref, bf16[128,3584]{1,0:T(8,128)(2,1)} %bitcast.65, bf16[128,14336]{1,0:T(8,128)(2,1)} %bitcast.57, bf16[16,128,128]{2,1,0:T(8,128)(2,1)} %bitcast.60), custom_call_target="tpu_custom_call" | custom-call | flops 201326592 | bytes 3538944 | tf_op jit(solution)/shard_map/pallas_call | solution.py:90
  31.6 1.3 %constant_dynamic-slice_fusion.1 = (f32[4,4,2,1,32,128]{5,4,3,2,1,0:T(8,128)S(1)}, f32[4,4,2,1,32,128]{5,4,3,2,1,0:T(8,128)S(1)}) fusion(f32[4,4,2,2,32,128]{5,4,3,2,1,0:T(8,128)} %bitcast.64, s32[]{:T(128)S(6)} %select_n.147, s32[]{:T(128)S(6)} %select_n.148), kind=kLoop, calls=%fused_computation.44 | loop fusion | bytes 2097160 | tf_op jit(solution)/shard_map/jit(dynamic_index_in_dim)/dynamic_slice | solution.py:204
  33.2 0.4 copy-done.2
  33.5 0.5 copy-done
  34.1 0.6 %gather_fusion = bf16[16,128,128]{2,1,0:T(8,128)(2,1)S(1)} fusion(bf16[28,128,128]{2,1,0:T(8,128)(2,1)S(1)} %copy-done, s32[1024]{0:T(1024)S(1)} %pad_clamp_fusion.1), kind=kCustom, calls=%fused_computation | custom fusion | bytes 1048640 | tf_op jit(solution)/shard_map/jit(_take)/gather | solution.py:187
  35.1 2.1 %collective-permute-start.5 = (bf16[4,4,32,128]{3,2,1,0:T(8,128)(2,1)S(1)}, bf16[4,4,32,128]{3,2,1,0:T(8,128)(2,1)S(1)}, u32[]{:S(2)}, u32[]{:S(2)}) collective-permute-start(bf16[4,4,32,128]{3,2,1,0:T(8,128)(2,1)S(1)} %fusion.6), channel_id=1, source_target_pairs={{0,2},{1,3},{2,0},{3,1},{4,6},{5,7},{6,4},{7,5},{8,10},{9,11},{10,... | collective-permute-start | bytes 393224 | tf_op jit(solution)/shard_map/ppermute | solution.py:24
  37.2 1.3 %collective-permute-start.3 = (bf16[262160]{0:T(1024)(128)(2,1)S(1)}, bf16[262160]{0:T(1024)(128)(2,1)S(1)}, u32[]{:S(2)}, u32[]{:S(2)}) collective-permute-start(bf16[262160]{0:T(1024)(128)(2,1)S(1)} %pad_maximum_fusion), channel_id=1, source_target_pairs={{16,0},{17,1},{18,2},{19,3},{20,4},{21,5},{22,6},{23,7},{24,8},{25... | collective-permute-start | bytes 1572968 | tf_op jit(solution)/shard_map/ppermute | solution.py:14
  38.5 2.5 %collective-permute-done.5 = bf16[4,4,32,128]{3,2,1,0:T(8,128)(2,1)S(1)} collective-permute-done((bf16[4,4,32,128]{3,2,1,0:T(8,128)(2,1)S(1)}, bf16[4,4,32,128]{3,2,1,0:T(8,128)(2,1)S(1)}, u32[]{:S(2)}, u32[]{:S(2)}) %collective-permute-start.5) | collective-permute-done | bytes 131104 | tf_op jit(solution)/shard_map/ppermute | solution.py:24
  41.1 4.4 %collective-permute-start.6 = (bf16[4,32,128]{2,1,0:T(8,128)(2,1)S(1)}, bf16[4,32,128]{2,1,0:T(8,128)(2,1)S(1)}, u32[]{:S(2)}, u32[]{:S(2)}) collective-permute-start(bf16[4,32,128]{2,1,0:T(8,128)(2,1)S(1)} %get-tuple-element.27), channel_id=1, source_target_pairs={{0,12},{4,0},{8,4},{12,8},{1,13},{5,1},{9,5},{13,9},{2,14},{6,2},{... | collective-permute-start | bytes 98312 | tf_op jit(solution)/shard_map/ppermute | solution.py:19
  45.5 0.6 %collective-permute-start.8 = (bf16[4,32,128]{2,1,0:T(8,128)(2,1)S(1)}, bf16[4,32,128]{2,1,0:T(8,128)(2,1)S(1)}, u32[]{:S(2)}, u32[]{:S(2)}) collective-permute-start(bf16[4,32,128]{2,1,0:T(8,128)(2,1)S(1)} %get-tuple-element.28), channel_id=1, source_target_pairs={{0,4},{4,8},{8,12},{12,0},{1,5},{5,9},{9,13},{13,1},{2,6},{6,10},{... | collective-permute-start | bytes 98312 | tf_op jit(solution)/shard_map/ppermute | solution.py:19
  46.2 0.9 %collective-permute-done.6 = bf16[4,32,128]{2,1,0:T(8,128)(2,1)S(1)} collective-permute-done((bf16[4,32,128]{2,1,0:T(8,128)(2,1)S(1)}, bf16[4,32,128]{2,1,0:T(8,128)(2,1)S(1)}, u32[]{:S(2)}, u32[]{:S(2)}) %collective-permute-start.6) | collective-permute-done | bytes 32800 | tf_op jit(solution)/shard_map/ppermute | solution.py:19
  47.1 3.2 %collective-permute-done.7 = bf16[4,32,128]{2,1,0:T(8,128)(2,1)S(1)} collective-permute-done((bf16[4,32,128]{2,1,0:T(8,128)(2,1)S(1)}, bf16[4,32,128]{2,1,0:T(8,128)(2,1)S(1)}, u32[]{:S(2)}, u32[]{:S(2)}) %collective-permute-start.7) | collective-permute-done | bytes 32800 | tf_op jit(solution)/shard_map/ppermute | solution.py:19
  50.3 0.9 %collective-permute-done.8 = bf16[4,32,128]{2,1,0:T(8,128)(2,1)S(1)} collective-permute-done((bf16[4,32,128]{2,1,0:T(8,128)(2,1)S(1)}, bf16[4,32,128]{2,1,0:T(8,128)(2,1)S(1)}, u32[]{:S(2)}, u32[]{:S(2)}) %collective-permute-start.8) | collective-permute-done | bytes 32800 | tf_op jit(solution)/shard_map/ppermute | solution.py:19
  51.2 1.8 %collective-permute-start.9 = (f32[4,32,128]{2,1,0:T(8,128)S(1)}, f32[4,32,128]{2,1,0:T(8,128)S(1)}, u32[]{:S(2)}, u32[]{:S(2)}) collective-permute-start(f32[4,32,128]{2,1,0:T(8,128)S(1)} %fusion.9), channel_id=1, source_target_pairs={{0,2},{1,3},{2,0},{3,1},{4,6},{5,7},{6,4},{7,5},{8,10},{9,11},{10,... | collective-permute-start | bytes 196616 | tf_op jit(solution)/shard_map/ppermute | solution.py:24
  53.3 1.1 %scatter_fusion = bf16[28,128,128]{2,1,0:T(8,128)(2,1)S(1)} fusion(bf16[28,128,128]{2,1,0:T(8,128)(2,1)S(1)} %broadcast_in_dim.32, s32[16]{0:T(128)S(1)} %compare_select_fusion.1, bf16[16,128,128]{2,1,0:T(8,128)(2,1)S(1)} %bitcast.61), kind=kCustom, calls=%fused_computation.2 | custom fusion | bytes 1572928 | tf_op jit(solution)/shard_map/scatter | solution.py:192
  54.5 0.6 %copy.36 = bf16[128,28,128]{2,1,0:T(8,128)(2,1)S(1)} copy(bf16[128,28,128]{2,0,1:T(8,128)(2,1)S(1)} %bitcast.56) | data formatting | bytes 1835008 | tf_op jit(solution)/shard_map/transpose | solution.py:195
  55.1 0.5 reshape.424
  55.6 0.6 %gather_fusion.1 = bf16[4,32,3584]{2,1,0:T(8,128)(2,1)S(1)} fusion(bf16[4,32,3584]{2,1,0:T(8,128)(2,1)S(1)} %reshape.424, s32[1024]{0:T(1024)S(1)} %pad_clamp_fusion), kind=kCustom, calls=%fused_computation.1 | custom fusion | bytes 1835024 | tf_op jit(solution)/shard_map/jit(_take)/gather | solution.py:198
  56.3 1.1 %bitcast_select_fusion = bf16[1,4,32,3584]{3,2,1,0:T(8,128)(2,1)} fusion(bf16[4,32,3584]{2,1,0:T(8,128)(2,1)S(1)} %gather_fusion.1, pred[4]{0:T(512)(128)(4,1)S(1)} %compare_and_fusion), kind=kLoop, calls=%fused_computation.3 | loop fusion | flops 458752 | bytes 1835012 | tf_op jit(solution)/shard_map/jit(_take)/select_n | solution.py:198
  57.4 0.2 collective-permute-done.10
  57.7 0.7 %copy.40 = f32[4,4,32,128]{3,2,1,0:T(8,128)} copy(f32[4,4,32,128]{3,2,0,1:T(8,128)S(1)} %bitcast.63) | data formatting | bytes 524288 | tf_op jit(solution)/shard_map/div | solution.py:217
  (42 shorter events, 1.8 us)
Async XLA Ops:
  2.4 0.7 %collective-permute-start = (bf16[528,128]{1,0:T(8,128)(2,1)S(1)}, bf16[528,128]{1,0:T(8,128)(2,1)S(1)}, u32[]{:S(2)}, u32[]{:S(2)}) collective-permute-start(bf16[528,128]{1,0:T(8,128)(2,1)S(1)} %fusion.5), channel_id=1, source_target_pairs={{0,0},{13,1},{10,2},{7,3},{4,4},{1,5},{14,6},{11,7},{8,8},{5,9},{2... | collective-permute-start | bytes 405512 | tf_op jit(solution)/shard_map/ppermute | solution.py:163
  3.1 15.0 %collective-permute-start.1 = (bf16[1,528,128]{2,1,0:T(8,128)(2,1)S(1)}, bf16[1,528,128]{2,1,0:T(8,128)(2,1)S(1)}, u32[]{:S(2)}, u32[]{:S(2)}) collective-permute-start(bf16[1,528,128]{2,1,0:T(8,128)(2,1)S(1)} %bitcast.68), channel_id=1, source_target_pairs={{0,2},{1,3},{2,0},{3,1},{4,6},{5,7},{6,4},{7,5},{8,10},{9,11},{10,... | collective-permute-start | bytes 405512 | tf_op jit(solution)/shard_map/ppermute | solution.py:24
  18.1 1.6 %collective-permute-start.2 = (bf16[2,1,528,128]{3,2,1,0:T(8,128)(2,1)S(1)}, bf16[2,1,528,128]{3,2,1,0:T(8,128)(2,1)S(1)}, u32[]{:S(2)}, u32[]{:S(2)}) collective-permute-start(bf16[2,1,528,128]{3,2,1,0:T(8,128)(2,1)S(1)} %maximum_select_fusion.2), channel_id=1, source_target_pairs={{0,1},{1,0},{2,3},{3,2},{4,5},{5,4},{6,7},{7,6},{8,9},{9,8},{10,11... | collective-permute-start | bytes 811016 | tf_op jit(solution)/shard_map/ppermute | solution.py:24
  21.2 1.7 %copy-start.1 = (s32[16]{0:T(128)}, s32[16]{0:T(128)S(1)}, u32[]{:S(2)}) copy-start(s32[16]{0:T(128)S(1)} %get-tuple-element.21.cols_ref) | copy-start | bytes 196
  31.6 1.6 %copy-start.3 = (s32[4]{0:T(128)S(1)}, s32[4]{0:T(128)}, u32[]{:S(2)}) copy-start(s32[4]{0:T(128)} %param.11) | copy-start | bytes 52
  32.9 0.7 %copy-start.2 = (s32[16]{0:T(128)S(1)}, s32[16]{0:T(128)}, u32[]{:S(2)}) copy-start(s32[16]{0:T(128)} %get-tuple-element.22.rows_ref) | copy-start | bytes 196
  32.9 1.2 %copy-start = (bf16[28,128,128]{2,1,0:T(8,128)(2,1)S(1)}, bf16[28,128,128]{2,1,0:T(8,128)(2,1)}, u32[]{:S(2)}) copy-start(bf16[28,128,128]{2,1,0:T(8,128)(2,1)} %get-tuple-element.18) | copy-start | bytes 2752516
  32.9 2.0 %collective-permute-start.4 = (f32[4,4,2,32,128]{4,3,1,0,2:T(8,128)S(1)}, f32[4,4,2,32,128]{4,3,1,0,2:T(8,128)S(1)}, u32[]{:S(2)}, u32[]{:S(2)}) collective-permute-start(f32[4,4,2,32,128]{4,3,1,0,2:T(8,128)S(1)} %bitcast.73), channel_id=1, source_target_pairs={{0,1},{1,0},{2,3},{3,2},{4,5},{5,4},{6,7},{7,6},{8,9},{9,8},{10,11... | collective-permute-start | bytes 1572872 | tf_op jit(solution)/shard_map/ppermute | solution.py:24
  35.1 5.9 %collective-permute-start.5 = (bf16[4,4,32,128]{3,2,1,0:T(8,128)(2,1)S(1)}, bf16[4,4,32,128]{3,2,1,0:T(8,128)(2,1)S(1)}, u32[]{:S(2)}, u32[]{:S(2)}) collective-permute-start(bf16[4,4,32,128]{3,2,1,0:T(8,128)(2,1)S(1)} %fusion.6), channel_id=1, source_target_pairs={{0,2},{1,3},{2,0},{3,1},{4,6},{5,7},{6,4},{7,5},{8,10},{9,11},{10,... | collective-permute-start | bytes 393224 | tf_op jit(solution)/shard_map/ppermute | solution.py:24
  37.2 15.8 %collective-permute-start.3 = (bf16[262160]{0:T(1024)(128)(2,1)S(1)}, bf16[262160]{0:T(1024)(128)(2,1)S(1)}, u32[]{:S(2)}, u32[]{:S(2)}) collective-permute-start(bf16[262160]{0:T(1024)(128)(2,1)S(1)} %pad_maximum_fusion), channel_id=1, source_target_pairs={{16,0},{17,1},{18,2},{19,3},{20,4},{21,5},{22,6},{23,7},{24,8},{25... | collective-permute-start | bytes 1572968 | tf_op jit(solution)/shard_map/ppermute | solution.py:14
  41.1 6.0 %collective-permute-start.6 = (bf16[4,32,128]{2,1,0:T(8,128)(2,1)S(1)}, bf16[4,32,128]{2,1,0:T(8,128)(2,1)S(1)}, u32[]{:S(2)}, u32[]{:S(2)}) collective-permute-start(bf16[4,32,128]{2,1,0:T(8,128)(2,1)S(1)} %get-tuple-element.27), channel_id=1, source_target_pairs={{0,12},{4,0},{8,4},{12,8},{1,13},{5,1},{9,5},{13,9},{2,14},{6,2},{... | collective-permute-start | bytes 98312 | tf_op jit(solution)/shard_map/ppermute | solution.py:19
  45.5 4.8 %collective-permute-start.7 = (bf16[4,32,128]{2,1,0:T(8,128)(2,1)S(1)}, bf16[4,32,128]{2,1,0:T(8,128)(2,1)S(1)}, u32[]{:S(2)}, u32[]{:S(2)}) collective-permute-start(bf16[4,32,128]{2,1,0:T(8,128)(2,1)S(1)} %get-tuple-element.29), channel_id=1, source_target_pairs={{0,8},{4,12},{8,0},{12,4},{1,9},{5,13},{9,1},{13,5},{2,10},{6,14},... | collective-permute-start | bytes 98312 | tf_op jit(solution)/shard_map/ppermute | solution.py:19
  45.5 5.7 %collective-permute-start.8 = (bf16[4,32,128]{2,1,0:T(8,128)(2,1)S(1)}, bf16[4,32,128]{2,1,0:T(8,128)(2,1)S(1)}, u32[]{:S(2)}, u32[]{:S(2)}) collective-permute-start(bf16[4,32,128]{2,1,0:T(8,128)(2,1)S(1)} %get-tuple-element.28), channel_id=1, source_target_pairs={{0,4},{4,8},{8,12},{12,0},{1,5},{5,9},{9,13},{13,1},{2,6},{6,10},{... | collective-permute-start | bytes 98312 | tf_op jit(solution)/shard_map/ppermute | solution.py:19
  51.2 4.9 %collective-permute-start.9 = (f32[4,32,128]{2,1,0:T(8,128)S(1)}, f32[4,32,128]{2,1,0:T(8,128)S(1)}, u32[]{:S(2)}, u32[]{:S(2)}) collective-permute-start(f32[4,32,128]{2,1,0:T(8,128)S(1)} %fusion.9), channel_id=1, source_target_pairs={{0,2},{1,3},{2,0},{3,1},{4,6},{5,7},{6,4},{7,5},{8,10},{9,11},{10,... | collective-permute-start | bytes 196616 | tf_op jit(solution)/shard_map/ppermute | solution.py:24
  56.2 1.4 %collective-permute-start.10 = (f32[2,4,32,128]{3,2,1,0:T(8,128)S(1)}, f32[2,4,32,128]{3,2,1,0:T(8,128)S(1)}, u32[]{:S(2)}, u32[]{:S(2)}) collective-permute-start(f32[2,4,32,128]{3,2,1,0:T(8,128)S(1)} %maximum_select_fusion.5), channel_id=1, source_target_pairs={{0,1},{1,0},{2,3},{3,2},{4,5},{5,4},{6,7},{7,6},{8,9},{9,8},{10,11... | collective-permute-start | bytes 393224 | tf_op jit(solution)/shard_map/ppermute | solution.py:24

commit v9 on v8

--- a/solution.py
+++ b/solution.py
@@ -207,9 +207,13 @@
             held = keep + swapped(send, "dp", bit)
         else:
             held = keep + swapped(send.astype(jnp.bfloat16), "dp", bit).astype(jnp.float32)
-    owned = held[0]
-    for k in range(1, n_fsdp):
-        owned = owned + shifted(held[k].astype(jnp.bfloat16), "fsdp", -k).astype(jnp.float32)
+    me_fsdp = lax.axis_index("fsdp")
+    to_device = (me_fsdp - jnp.arange(n_fsdp, dtype=jnp.int32)) % n_fsdp
+    outgoing = jnp.take(held, to_device, axis=0).astype(jnp.bfloat16)
+    incoming = lax.all_to_all(outgoing, "fsdp", 0, 0, tiled=True).astype(jnp.float32)
+    others = jnp.arange(n_fsdp, dtype=jnp.int32) != me_fsdp
+    incoming = jnp.where(others[:, None, None, None], incoming, 0.0)
+    owned = held[0] + jnp.sum(incoming, axis=0)
     full = butterfly_gather(owned, "dp", list(reversed(range(dp_bits))))
     full = full.reshape((n_dp, blocks_dev, chunk, block_size))
     full = jnp.transpose(full, (1, 0, 2, 3)).reshape(blocks_dev, block_size, block_size)

time: 58.8 us -> 71.1 us (1.21)
  waiting for transfers between devices: 11.6 us -> 20.9 us
  local copies, waits for them, and re-layouts: 8.53 us -> 10.2 us
  other arithmetic: 5.38 us -> 6.45 us
    ppermute x1, waiting for transfers between devices: 0.01 us -> 12.6 us  [passed_along(): return lax.ppermute(block, axis, route)]
    all_to_all x0 -> x1, starting transfers between devices: none -> 5.66 us  [local(): lax.all_to_all(outgoing, 'fsdp', 0, 0, tiled=True).astype(jnp.float32)]
    ppermute x3 -> x0, starting transfers between devices: 5.08 us -> none  [shifted(): return lax.ppermute(x, axis, [(i, (i + k) % n) for i in range(n)])]
    ppermute x3 -> x0, waiting for transfers between devices: 5.07 us -> none  [shifted(): return lax.ppermute(x, axis, [(i, (i + k) % n) for i in range(n)])]
    all_to_all x0 -> x1, waiting for transfers between devices: none -> 2.01 us  [local(): lax.all_to_all(outgoing, 'fsdp', 0, 0, tiled=True).astype(jnp.float32)]
    gather x1, local copies, waits for them, and re-layouts: 0.65 us -> 1.82 us  [local(): hit = jnp.take(input_grad, row_ids, axis=0)]
    unnamed x8 -> x6, local copies, waits for them, and re-layouts: 0.92 us -> 0.01 us
    slice x1 -> x2, local copies, waits for them, and re-layouts: 0.03 us -> 0.83 us  [local(): got = payload[:hit.size].reshape(hit.shape)]
  transfers between devices with their start and end apart: 11 -> 9, of which waited for: 7 -> 6; matrix products, arithmetic and copies ran while one was open for 10% -> 11% of each run, Pallas kernels for 0% -> 0%
where the time goes in v9:
time: 71.1 us; the launch traced here: 70.6 us
  starting transfers between devices  23.5 us (33%)
  waiting for transfers between devices  20.9 us (29%)
  local copies, waits for them, and re-layouts  10.2 us (14%)
  Pallas kernels  8.73 us (12%)
  other arithmetic  6.45 us (9%)
  between operations  0.91 us (1%)
    ppermute x6, starting transfers between devices, swapped(): return lax.ppermute(x, axis, [(i, i ^ 1 << bit) for i in range(n)])  15.9 us
    ppermute x1, waiting for transfers between devices, passed_along(): return lax.ppermute(block, axis, route)  12.6 us
    pallas_call x1, Pallas kernels, block_pass(): pl.pallas_call(block_kernel, out_shape=(jax.ShapeDtypeStruct((row_count,...  8.73 us
    ppermute x6, waiting for transfers between devices, swapped(): return lax.ppermute(x, axis, [(i, i ^ 1 << bit) for i in range(n)])  6.25 us
    all_to_all x1, starting transfers between devices, local(): lax.all_to_all(outgoing, 'fsdp', 0, 0, tiled=True).astype(jnp.float32)  5.66 us
    all_to_all x1, waiting for transfers between devices, local(): lax.all_to_all(outgoing, 'fsdp', 0, 0, tiled=True).astype(jnp.float32)  2.01 us
    gather x1, local copies, waits for them, and re-layouts, local(): hit = jnp.take(input_grad, row_ids, axis=0)  1.82 us
    select_n x2, other arithmetic, local(): received = jnp.take(arrived, order, axis=0)  1.74 us
  transfers between devices with their start and end apart: 9, of which 6 were waited for; matrix products, arithmetic and copies ran while one was open for 11% of the time, Pallas kernels for 0%

profile of v9, /device:TPU:0, one launch (start us, length us, event | category | flops | bytes accessed | tf_op | source)
XLA Modules:
  0.0 70.6 jit_solution(14640413065858448306)
XLA Ops:
  0.6 0.7 convert_element_type.38
  1.5 0.9 %fusion.5 = bf16[528,128]{1,0:T(8,128)(2,1)S(1)} fusion(bf16[1,8]{1,0:T(2,128)(2,1)S(1)} %convert_element_type.39, bf16[512,128]{1,0:T(8,128)(2,1)} %bitcast.68), kind=kLoop, calls=%fused_computation.23 | loop fusion | flops 405504 | bytes 266256 | tf_op jit(solution)/shard_map/concatenate | solution.py:155
  2.4 0.7 collective-permute-start
  3.1 0.7 compare_select_fusion.4
  3.8 11.3 %collective-permute-start.1 = (bf16[1,528,128]{2,1,0:T(8,128)(2,1)S(1)}, bf16[1,528,128]{2,1,0:T(8,128)(2,1)S(1)}, u32[]{:S(2)}, u32[]{:S(2)}) collective-permute-start(bf16[1,528,128]{2,1,0:T(8,128)(2,1)S(1)} %bitcast.57), channel_id=1, source_target_pairs={{0,2},{1,3},{2,0},{3,1},{4,6},{5,7},{6,4},{7,5},{8,10},{9,11},{10,... | collective-permute-start | bytes 405512 | tf_op jit(solution)/shard_map/ppermute | solution.py:24
  15.1 0.7 compare_and_fusion.1
  15.8 2.3 %collective-permute-done.1 = bf16[1,528,128]{2,1,0:T(8,128)(2,1)S(1)} collective-permute-done((bf16[1,528,128]{2,1,0:T(8,128)(2,1)S(1)}, bf16[1,528,128]{2,1,0:T(8,128)(2,1)S(1)}, u32[]{:S(2)}, u32[]{:S(2)}) %collective-permute-start.1) | collective-permute-done | bytes 135200 | tf_op jit(solution)/shard_map/ppermute | solution.py:24
  18.3 1.5 %collective-permute-done.2 = bf16[2,1,528,128]{3,2,1,0:T(8,128)(2,1)S(1)} collective-permute-done((bf16[2,1,528,128]{3,2,1,0:T(8,128)(2,1)S(1)}, bf16[2,1,528,128]{3,2,1,0:T(8,128)(2,1)S(1)}, u32[]{:S(2)}, u32[]{:S(2)}) %collective-permute-start.2) | collective-permute-done | bytes 270368 | tf_op jit(solution)/shard_map/ppermute | solution.py:24
  19.8 0.4 copy.34
  20.8 0.8 %iota_reduce_fusion = (pred[16]{0:T(512)(128)(4,1)}, s32[16]{0:T(128)}) fusion(s32[16]{0:T(128)S(1)} %get-tuple-element.21.cols_ref), kind=kLoop, calls=%fused_computation.31 | loop fusion | flops 1936 | bytes 144 | tf_op jit(solution)/shard_map/block_pass/reduce | solution.py:86
  21.6 0.9 %copy.35 = bf16[4,512,128]{2,1,0:T(8,128)(2,1)} copy(bf16[4,512,128]{2,0,1:T(4,128)(2,1)S(1)} %slice.53) | data formatting | bytes 1048576 | tf_op jit(solution)/shard_map/slice | solution.py:168
  22.5 8.7 %shard_map.68 = (bf16[28,128,128]{2,1,0:T(8,128)(2,1)}, f32[16,128,128]{2,1,0:T(8,128)}) custom-call(s32[16]{0:T(128)} %copy-done.2, s32[16]{0:T(128)} %copy-done.1, s32[16]{0:T(128)} %get-tuple-element.17.rep_ref, bf16[128,3584]{1,0:T(8,128)(2,1)} %bitcast.55, bf16[128,14336]{1,0:T(8,128)(2,1)} %bitcast.47, bf16[16,128,128]{2,1,0:T(8,128)(2,1)} %bitcast.50), custom_call_target="tpu_custom_call" | custom-call | flops 201326592 | bytes 3538944 | tf_op jit(solution)/shard_map/pallas_call | solution.py:90
  31.3 1.3 %constant_dynamic-slice_fusion.1 = (f32[4,4,2,1,32,128]{5,4,3,2,1,0:T(8,128)S(1)}, f32[4,4,2,1,32,128]{5,4,3,2,1,0:T(8,128)S(1)}) fusion(f32[4,4,2,2,32,128]{5,4,3,2,1,0:T(8,128)} %bitcast.54, s32[]{:T(128)S(6)} %select_n.188, s32[]{:T(128)S(6)} %select_n.189), kind=kLoop, calls=%fused_computation.52 | loop fusion | bytes 2097160 | tf_op jit(solution)/shard_map/jit(dynamic_index_in_dim)/dynamic_slice | solution.py:204
  32.6 0.2 collective-permute-start.4
  32.8 1.8 %gather_fusion = bf16[16,128,128]{2,1,0:T(8,128)(2,1)S(1)} fusion(bf16[28,128,128]{2,1,0:T(8,128)(2,1)} %get-tuple-element.18, s32[1024]{0:T(1024)S(1)} %pad_clamp_fusion.2), kind=kCustom, calls=%fused_computation | custom fusion | bytes 1048640 | tf_op jit(solution)/shard_map/jit(_take)/gather | solution.py:187
  34.8 1.3 %collective-permute-start.3 = (bf16[262160]{0:T(1024)(128)(2,1)S(1)}, bf16[262160]{0:T(1024)(128)(2,1)S(1)}, u32[]{:S(2)}, u32[]{:S(2)}) collective-permute-start(bf16[262160]{0:T(1024)(128)(2,1)S(1)} %pad_maximum_fusion), channel_id=1, source_target_pairs={{16,0},{17,1},{18,2},{19,3},{20,4},{21,5},{22,6},{23,7},{24,8},{25... | collective-permute-start | bytes 1572968 | tf_op jit(solution)/shard_map/ppermute | solution.py:14
  36.3 2.1 %collective-permute-start.5 = (bf16[4,4,32,128]{3,2,1,0:T(8,128)(2,1)S(1)}, bf16[4,4,32,128]{3,2,1,0:T(8,128)(2,1)S(1)}, u32[]{:S(2)}, u32[]{:S(2)}) collective-permute-start(bf16[4,4,32,128]{3,2,1,0:T(8,128)(2,1)S(1)} %fusion.6), channel_id=1, source_target_pairs={{0,2},{1,3},{2,0},{3,1},{4,6},{5,7},{6,4},{7,5},{8,10},{9,11},{10,... | collective-permute-start | bytes 393224 | tf_op jit(solution)/shard_map/ppermute | solution.py:24
  38.4 12.6 %collective-permute-done.3 = bf16[262160]{0:T(1024)(128)(2,1)S(1)} collective-permute-done((bf16[262160]{0:T(1024)(128)(2,1)S(1)}, bf16[262160]{0:T(1024)(128)(2,1)S(1)}, u32[]{:S(2)}, u32[]{:S(2)}) %collective-permute-start.3) | collective-permute-done | bytes 524352 | tf_op jit(solution)/shard_map/ppermute | solution.py:14
  51.0 0.6 gather_fusion.2
  51.6 0.7 %select_convert_fusion = bf16[4,4,32,128]{3,2,1,0:T(8,128)(2,1)} fusion(bf16[4,4,32,128]{3,2,1,0:T(8,128)(2,1)S(1)} %gather_fusion.2, pred[4]{0:T(512)(128)(4,1)S(1)} %compare_and_fusion), kind=kLoop, calls=%fused_computation.21 | loop fusion | flops 65536 | bytes 262148 | tf_op jit(solution)/shard_map/convert_element_type | solution.py:212
  52.3 5.7 %all-to-all-start = ((bf16[4,4,32,128]{3,2,1,0:T(8,128)(2,1)}), bf16[4,4,32,128]{3,2,1,0:T(8,128)(2,1)S(1)}, u32[]{:S(2)}, u32[]{:S(2)}) async-start(bf16[4,4,32,128]{3,2,1,0:T(8,128)(2,1)} %select_convert_fusion), calls=%async_computation | async-start | bytes 262144 | tf_op jit(solution)/shard_map/all_to_all | solution.py:213
  58.2 0.8 %slice-done = bf16[262144]{0:T(1024)(128)(2,1)S(1)} async-done(((bf16[262160]{0:T(1024)(128)(2,1)}), bf16[262144]{0:T(1024)(128)(2,1)S(1)}, s32[]{:S(2)}) %slice-start) | async-done | bytes 524312 | tf_op jit(solution)/shard_map/slice | solution.py:191
  59.0 1.1 %scatter_fusion = bf16[28,128,128]{2,1,0:T(8,128)(2,1)S(1)} fusion(bf16[28,128,128]{2,1,0:T(8,128)(2,1)S(1)} %broadcast_in_dim.55, s32[16]{0:T(128)S(1)} %compare_select_fusion.3, bf16[16,128,128]{2,1,0:T(8,128)(2,1)S(1)} %bitcast.51), kind=kCustom, calls=%fused_computation.3 | custom fusion | bytes 1572928 | tf_op jit(solution)/shard_map/scatter | solution.py:192
  60.2 0.6 copy.36
  60.8 0.5 reshape.478
  61.3 0.6 gather_fusion.1
  61.9 2.0 %all-to-all-done = bf16[4,4,32,128]{3,2,1,0:T(8,128)(2,1)S(1)} async-done(((bf16[4,4,32,128]{3,2,1,0:T(8,128)(2,1)}), bf16[4,4,32,128]{3,2,1,0:T(8,128)(2,1)S(1)}, u32[]{:S(2)}, u32[]{:S(2)}) %all-to-all-start) | async-done | bytes 131104 | tf_op jit(solution)/shard_map/all_to_all | solution.py:213
  64.0 2.1 %collective-permute-start.6 = (f32[4,32,128]{2,1,0:T(8,128)S(1)}, f32[4,32,128]{2,1,0:T(8,128)S(1)}, u32[]{:S(2)}, u32[]{:S(2)}) collective-permute-start(f32[4,32,128]{2,1,0:T(8,128)S(1)} %bitcast_add_fusion.2), channel_id=1, source_target_pairs={{0,2},{1,3},{2,0},{3,1},{4,6},{5,7},{6,4},{7,5},{8,10},{9,11},{10,... | collective-permute-start | bytes 196616 | tf_op jit(solution)/shard_map/ppermute | solution.py:24
  66.1 2.2 %collective-permute-done.6 = f32[4,32,128]{2,1,0:T(8,128)S(1)} collective-permute-done((f32[4,32,128]{2,1,0:T(8,128)S(1)}, f32[4,32,128]{2,1,0:T(8,128)S(1)}, u32[]{:S(2)}, u32[]{:S(2)}) %collective-permute-start.6) | collective-permute-done | bytes 65568 | tf_op jit(solution)/shard_map/ppermute | solution.py:24
  68.5 1.1 %bitcast_select_fusion = bf16[1,4,32,3584]{3,2,1,0:T(8,128)(2,1)} fusion(bf16[4,32,3584]{2,1,0:T(8,128)(2,1)S(1)} %gather_fusion.1, pred[4]{0:T(512)(128)(4,1)S(1)} %compare_and_fusion.1), kind=kLoop, calls=%fused_computation.4 | loop fusion | flops 458752 | bytes 1835012 | tf_op jit(solution)/shard_map/jit(_take)/select_n | solution.py:198
  69.6 0.2 collective-permute-done.7
  69.9 0.7 %copy.40 = f32[4,4,32,128]{3,2,1,0:T(8,128)} copy(f32[4,4,32,128]{3,2,0,1:T(8,128)S(1)} %bitcast.53) | data formatting | bytes 524288 | tf_op jit(solution)/shard_map/div | solution.py:221
  (44 shorter events, 1.8 us)
Async XLA Ops:
  2.4 1.3 %collective-permute-start = (bf16[528,128]{1,0:T(8,128)(2,1)S(1)}, bf16[528,128]{1,0:T(8,128)(2,1)S(1)}, u32[]{:S(2)}, u32[]{:S(2)}) collective-permute-start(bf16[528,128]{1,0:T(8,128)(2,1)S(1)} %fusion.5), channel_id=1, source_target_pairs={{0,0},{13,1},{10,2},{7,3},{4,4},{1,5},{14,6},{11,7},{8,8},{5,9},{2... | collective-permute-start | bytes 405512 | tf_op jit(solution)/shard_map/ppermute | solution.py:163
  3.8 14.3 %collective-permute-start.1 = (bf16[1,528,128]{2,1,0:T(8,128)(2,1)S(1)}, bf16[1,528,128]{2,1,0:T(8,128)(2,1)S(1)}, u32[]{:S(2)}, u32[]{:S(2)}) collective-permute-start(bf16[1,528,128]{2,1,0:T(8,128)(2,1)S(1)} %bitcast.57), channel_id=1, source_target_pairs={{0,2},{1,3},{2,0},{3,1},{4,6},{5,7},{6,4},{7,5},{8,10},{9,11},{10,... | collective-permute-start | bytes 405512 | tf_op jit(solution)/shard_map/ppermute | solution.py:24
  18.1 1.6 %collective-permute-start.2 = (bf16[2,1,528,128]{3,2,1,0:T(8,128)(2,1)S(1)}, bf16[2,1,528,128]{3,2,1,0:T(8,128)(2,1)S(1)}, u32[]{:S(2)}, u32[]{:S(2)}) collective-permute-start(bf16[2,1,528,128]{3,2,1,0:T(8,128)(2,1)S(1)} %maximum_select_fusion.2), channel_id=1, source_target_pairs={{0,1},{1,0},{2,3},{3,2},{4,5},{5,4},{6,7},{7,6},{8,9},{9,8},{10,11... | collective-permute-start | bytes 811016 | tf_op jit(solution)/shard_map/ppermute | solution.py:24
  20.7 1.8 %copy-start.1 = (s32[16]{0:T(128)}, s32[16]{0:T(128)S(1)}, u32[]{:S(2)}) copy-start(s32[16]{0:T(128)S(1)} %get-tuple-element.21.cols_ref) | copy-start | bytes 196
  20.7 1.8 %copy-start.2 = (s32[16]{0:T(128)}, s32[16]{0:T(128)S(1)}, u32[]{:S(2)}) copy-start(s32[16]{0:T(128)S(1)} %get-tuple-element.22.rows_ref) | copy-start | bytes 196
  32.6 3.5 %collective-permute-start.4 = (f32[4,4,2,32,128]{4,3,1,0,2:T(8,128)S(1)}, f32[4,4,2,32,128]{4,3,1,0,2:T(8,128)S(1)}, u32[]{:S(2)}, u32[]{:S(2)}) collective-permute-start(f32[4,4,2,32,128]{4,3,1,0,2:T(8,128)S(1)} %bitcast.62), channel_id=1, source_target_pairs={{0,1},{1,0},{2,3},{3,2},{4,5},{5,4},{6,7},{7,6},{8,9},{9,8},{10,11... | collective-permute-start | bytes 1572872 | tf_op jit(solution)/shard_map/ppermute | solution.py:24
  34.8 16.1 %collective-permute-start.3 = (bf16[262160]{0:T(1024)(128)(2,1)S(1)}, bf16[262160]{0:T(1024)(128)(2,1)S(1)}, u32[]{:S(2)}, u32[]{:S(2)}) collective-permute-start(bf16[262160]{0:T(1024)(128)(2,1)S(1)} %pad_maximum_fusion), channel_id=1, source_target_pairs={{16,0},{17,1},{18,2},{19,3},{20,4},{21,5},{22,6},{23,7},{24,8},{25... | collective-permute-start | bytes 1572968 | tf_op jit(solution)/shard_map/ppermute | solution.py:14
  36.3 14.7 %collective-permute-start.5 = (bf16[4,4,32,128]{3,2,1,0:T(8,128)(2,1)S(1)}, bf16[4,4,32,128]{3,2,1,0:T(8,128)(2,1)S(1)}, u32[]{:S(2)}, u32[]{:S(2)}) collective-permute-start(bf16[4,4,32,128]{3,2,1,0:T(8,128)(2,1)S(1)} %fusion.6), channel_id=1, source_target_pairs={{0,2},{1,3},{2,0},{3,1},{4,6},{5,7},{6,4},{7,5},{8,10},{9,11},{10,... | collective-permute-start | bytes 393224 | tf_op jit(solution)/shard_map/ppermute | solution.py:24
  51.0 7.0 %copy-start = (bf16[262160]{0:T(1024)(128)(2,1)}, bf16[262160]{0:T(1024)(128)(2,1)S(1)}, u32[]{:S(2)}) copy-start(bf16[262160]{0:T(1024)(128)(2,1)S(1)} %collective-permute-done.3) | copy-start | bytes 1572964
  52.3 11.6 %all-to-all-start = ((bf16[4,4,32,128]{3,2,1,0:T(8,128)(2,1)}), bf16[4,4,32,128]{3,2,1,0:T(8,128)(2,1)S(1)}, u32[]{:S(2)}, u32[]{:S(2)}) async-start(bf16[4,4,32,128]{3,2,1,0:T(8,128)(2,1)} %select_convert_fusion), calls=%async_computation | async-start | bytes 262144 | tf_op jit(solution)/shard_map/all_to_all | solution.py:213
  58.0 1.0 %slice-start = ((bf16[262160]{0:T(1024)(128)(2,1)}), bf16[262144]{0:T(1024)(128)(2,1)S(1)}, s32[]{:S(2)}) async-start(bf16[262160]{0:T(1024)(128)(2,1)} %copy-done), calls=%async_computation.1 | async-start | bytes 1048576 | tf_op jit(solution)/shard_map/slice | solution.py:191
  64.0 4.3 %collective-permute-start.6 = (f32[4,32,128]{2,1,0:T(8,128)S(1)}, f32[4,32,128]{2,1,0:T(8,128)S(1)}, u32[]{:S(2)}, u32[]{:S(2)}) collective-permute-start(f32[4,32,128]{2,1,0:T(8,128)S(1)} %bitcast_add_fusion.2), channel_id=1, source_target_pairs={{0,2},{1,3},{2,0},{3,1},{4,6},{5,7},{6,4},{7,5},{8,10},{9,11},{10,... | collective-permute-start | bytes 196616 | tf_op jit(solution)/shard_map/ppermute | solution.py:24
  68.4 1.4 %collective-permute-start.7 = (f32[2,4,32,128]{3,2,1,0:T(8,128)S(1)}, f32[2,4,32,128]{3,2,1,0:T(8,128)S(1)}, u32[]{:S(2)}, u32[]{:S(2)}) collective-permute-start(f32[2,4,32,128]{3,2,1,0:T(8,128)S(1)} %maximum_select_fusion.5), channel_id=1, source_target_pairs={{0,1},{1,0},{2,3},{3,2},{4,5},{5,4},{6,7},{7,6},{8,9},{9,8},{10,11... | collective-permute-start | bytes 393224 | tf_op jit(solution)/shard_map/ppermute | solution.py:24

commit v10 on v8

--- a/solution.py
+++ b/solution.py
@@ -29,30 +29,19 @@
     return sigmoid_val * (1.0 + pre_act * (1.0 - sigmoid_val))
 
 
-def block_kernel(rows_ref, cols_ref, rep_ref, feat_hbm, hid_hbm, w_ref, ig_ref, pg_ref,
-                 xs, hs, pr, acc, sems):
+def block_kernel(rows_ref, cols_ref, rep_ref, feat_ref, hid_ref, w_ref, ig_ref, pg_ref,
+                 xs, hs, pr, acc):
     block_count = w_ref.shape[0]
     width = w_ref.shape[-1]
 
-    def copies(b):
+    acc[...] = jnp.zeros(acc.shape, acc.dtype)
+
+    @pl.loop(0, block_count)
+    def _(b):
         r = pl.multiple_of(rows_ref[b] * width, width)
         c = pl.multiple_of(cols_ref[b] * width, width)
-        return (
-            pltpu.make_async_copy(feat_hbm.at[:, pl.ds(r, width)], xs.at[b], sems.at[0, b]),
-            pltpu.make_async_copy(hid_hbm.at[:, pl.ds(c, width)], hs.at[b], sems.at[1, b]),
-        )
-
-    @pl.loop(0, block_count)
-    def _(b):
-        for cp in copies(b):
-            cp.start()
-
-    acc[...] = jnp.zeros(acc.shape, acc.dtype)
-
-    @pl.loop(0, block_count)
-    def _(b):
-        for cp in copies(b):
-            cp.wait()
+        xs[b] = feat_ref[:, pl.ds(r, width)]
+        hs[b] = hid_ref[:, pl.ds(c, width)]
         pr[b] = jnp.dot(xs[b], w_ref[b], preferred_element_type=jnp.float32)
 
     @pl.loop(0, block_count)
@@ -85,7 +74,6 @@
     same = col_ids[:, None] == col_ids[None, :]
     first = jnp.argmax(same, axis=1).astype(jnp.int32)
     smem = pl.BlockSpec(memory_space=pltpu.SMEM)
-    anyspace = pl.BlockSpec(memory_space=pl.ANY)
     vmem = pl.BlockSpec(memory_space=pltpu.VMEM)
     return pl.pallas_call(
         block_kernel,
@@ -93,14 +81,13 @@
             jax.ShapeDtypeStruct((row_count, tokens, width), jnp.bfloat16),
             jax.ShapeDtypeStruct((block_count, width, width), jnp.float32),
         ),
-        in_specs=[smem, smem, smem, anyspace, anyspace, vmem],
+        in_specs=[smem, smem, smem, vmem, vmem, vmem],
         out_specs=(vmem, vmem),
         scratch_shapes=[
             pltpu.VMEM((block_count, tokens, width), jnp.bfloat16),
             pltpu.VMEM((block_count, tokens, width), jnp.bfloat16),
             pltpu.VMEM((block_count, tokens, width), jnp.float32),
             pltpu.VMEM((row_count, tokens, width), jnp.float32),
-            pltpu.SemaphoreType.DMA((2, block_count)),
         ],
         cost_estimate=pl.CostEstimate(
             flops=6 * block_count * tokens * width * width,

time: 58.8 us -> 59.1 us (level)
  no operation moved by 1% of the time
where the time goes in v10:
time: 59.1 us; the launch traced here: 58.9 us
  starting transfers between devices  23.3 us (39%)
  waiting for transfers between devices  11.6 us (20%)
  Pallas kernels  9.2 us (16%)
  local copies, waits for them, and re-layouts  8.52 us (14%)
  other arithmetic  5.38 us (9%)
  between operations  0.89 us (2%)
    ppermute x6, starting transfers between devices, swapped(): return lax.ppermute(x, axis, [(i, i ^ 1 << bit) for i in range(n)])  16.2 us
    pallas_call x1, Pallas kernels, block_pass(): pl.pallas_call(block_kernel, out_shape=(jax.ShapeDtypeStruct((row_count,...  9.2 us
    ppermute x6, waiting for transfers between devices, swapped(): return lax.ppermute(x, axis, [(i, i ^ 1 << bit) for i in range(n)])  6.54 us
    ppermute x3, starting transfers between devices, shifted(): return lax.ppermute(x, axis, [(i, (i + k) % n) for i in range(n)])  5.14 us
    ppermute x3, waiting for transfers between devices, shifted(): return lax.ppermute(x, axis, [(i, (i + k) % n) for i in range(n)])  5.07 us
    select_n x2, other arithmetic, local(): received = jnp.take(arrived, order, axis=0)  1.74 us
    dynamic_slice x1, local copies, waits for them, and re-layouts, local(): keep = lax.dynamic_index_in_dim(held, mine, axis_at, keepdims=False)  1.31 us
    ppermute x1, starting transfers between devices, passed_along(): return lax.ppermute(block, axis, route)  1.29 us
  transfers between devices with their start and end apart: 11, of which 7 were waited for; matrix products, arithmetic and copies ran while one was open for 10% of the time, Pallas kernels for 0%

profile of v10, /device:TPU:0, one launch (start us, length us, event | category | flops | bytes accessed | tf_op | source)
XLA Modules:
  0.0 58.9 jit_solution(16150666263741574312)
XLA Ops:
  0.6 0.7 %convert_element_type.53 = bf16[1,4,2]{1,2,0:T(2,128)(2,1)S(1)} convert(s32[1,4,2]{1,2,0:T(2,128)} %param.10) | non-fusion elementwise | flops 8 | bytes 48 | tf_op jit(solution)/shard_map/convert_element_type | solution.py:140
  1.5 0.9 %fusion.5 = bf16[528,128]{1,0:T(8,128)(2,1)S(1)} fusion(bf16[1,8]{1,0:T(2,128)(2,1)S(1)} %convert_element_type.54, bf16[512,128]{1,0:T(8,128)(2,1)} %bitcast.79), kind=kLoop, calls=%fused_computation.20 | loop fusion | flops 405504 | bytes 266256 | tf_op jit(solution)/shard_map/concatenate | solution.py:142
  2.4 0.7 %collective-permute-start = (bf16[528,128]{1,0:T(8,128)(2,1)S(1)}, bf16[528,128]{1,0:T(8,128)(2,1)S(1)}, u32[]{:S(2)}, u32[]{:S(2)}) collective-permute-start(bf16[528,128]{1,0:T(8,128)(2,1)S(1)} %fusion.5), channel_id=1, source_target_pairs={{0,0},{13,1},{10,2},{7,3},{4,4},{1,5},{14,6},{11,7},{8,8},{5,9},{2... | collective-permute-start | bytes 405512 | tf_op jit(solution)/shard_map/ppermute | solution.py:150
  3.1 12.0 %collective-permute-start.1 = (bf16[1,528,128]{2,1,0:T(8,128)(2,1)S(1)}, bf16[1,528,128]{2,1,0:T(8,128)(2,1)S(1)}, u32[]{:S(2)}, u32[]{:S(2)}) collective-permute-start(bf16[1,528,128]{2,1,0:T(8,128)(2,1)S(1)} %bitcast.68), channel_id=1, source_target_pairs={{0,2},{1,3},{2,0},{3,1},{4,6},{5,7},{6,4},{7,5},{8,10},{9,11},{10,... | collective-permute-start | bytes 405512 | tf_op jit(solution)/shard_map/ppermute | solution.py:24
  15.1 3.0 %collective-permute-done.1 = bf16[1,528,128]{2,1,0:T(8,128)(2,1)S(1)} collective-permute-done((bf16[1,528,128]{2,1,0:T(8,128)(2,1)S(1)}, bf16[1,528,128]{2,1,0:T(8,128)(2,1)S(1)}, u32[]{:S(2)}, u32[]{:S(2)}) %collective-permute-start.1) | collective-permute-done | bytes 135200 | tf_op jit(solution)/shard_map/ppermute | solution.py:24
  18.2 0.7 %compare_select_fusion.2 = s32[4]{0:T(128)S(1)} fusion(s32[4]{0:T(128)} %param.11), kind=kLoop, calls=%fused_computation.40 | loop fusion | flops 12 | bytes 32 | tf_op jit(solution)/shard_map/jit(_take)/jit(_where)/select_n | solution.py:185
  18.9 0.8 %collective-permute-done.2 = bf16[2,1,528,128]{3,2,1,0:T(8,128)(2,1)S(1)} collective-permute-done((bf16[2,1,528,128]{3,2,1,0:T(8,128)(2,1)S(1)}, bf16[2,1,528,128]{3,2,1,0:T(8,128)(2,1)S(1)}, u32[]{:S(2)}, u32[]{:S(2)}) %collective-permute-start.2) | collective-permute-done | bytes 270368 | tf_op jit(solution)/shard_map/ppermute | solution.py:24
  19.8 0.4 copy.34
  20.5 0.6 %fusion.10 = (s32[16]{0:T(128)S(1)}, s32[16]{0:T(128)S(1)}, s32[16]{0:T(128)}) fusion(s32[16,2]{1,0:T(8,128)S(1)} %reshape.426), kind=kLoop, calls=%fused_computation.36 | loop fusion | flops 48 | bytes 320 | tf_op jit(solution)/shard_map/jit(_take)/jit(_where)/select_n | solution.py:174
  21.2 0.8 %iota_reduce_fusion = (pred[16]{0:T(512)(128)(4,1)}, s32[16]{0:T(128)}) fusion(s32[16]{0:T(128)S(1)} %get-tuple-element.21.cols_ref), kind=kLoop, calls=%fused_computation.33 | loop fusion | flops 1936 | bytes 144 | tf_op jit(solution)/shard_map/block_pass/reduce | solution.py:75
  21.9 0.9 %copy.35 = bf16[4,512,128]{2,1,0:T(8,128)(2,1)} copy(bf16[4,512,128]{2,0,1:T(4,128)(2,1)S(1)} %slice.66) | data formatting | bytes 1048576 | tf_op jit(solution)/shard_map/slice | solution.py:155
  22.8 9.2 %shard_map.68 = (bf16[28,128,128]{2,1,0:T(8,128)(2,1)}, f32[16,128,128]{2,1,0:T(8,128)}) custom-call(s32[16]{0:T(128)} %get-tuple-element.22.rows_ref, s32[16]{0:T(128)} %copy-done.1, s32[16]{0:T(128)} %get-tuple-element.17.rep_ref, bf16[128,3584]{1,0:T(8,128)(2,1)} %bitcast.65, bf16[128,14336]{1,0:T(8,128)(2,1)} %bitcast.57, bf16[16,128,128]{2,1,0:T(8,128)(2,1)} %bitcast.60), custom_call_target="tpu_custom_call" | custom-call | flops 201326592 | bytes 3538944 | tf_op jit(solution)/shard_map/pallas_call | solution.py:78
  32.0 1.3 %constant_dynamic-slice_fusion.1 = (f32[4,4,2,1,32,128]{5,4,3,2,1,0:T(8,128)S(1)}, f32[4,4,2,1,32,128]{5,4,3,2,1,0:T(8,128)S(1)}) fusion(f32[4,4,2,2,32,128]{5,4,3,2,1,0:T(8,128)} %bitcast.64, s32[]{:T(128)S(6)} %select_n.147, s32[]{:T(128)S(6)} %select_n.148), kind=kLoop, calls=%fused_computation.44 | loop fusion | bytes 2097160 | tf_op jit(solution)/shard_map/jit(dynamic_index_in_dim)/dynamic_slice | solution.py:191
  33.6 0.4 copy-done.2
  34.0 0.5 copy-done
  34.5 0.6 %gather_fusion = bf16[16,128,128]{2,1,0:T(8,128)(2,1)S(1)} fusion(bf16[28,128,128]{2,1,0:T(8,128)(2,1)S(1)} %copy-done, s32[1024]{0:T(1024)S(1)} %pad_clamp_fusion.1), kind=kCustom, calls=%fused_computation | custom fusion | bytes 1048640 | tf_op jit(solution)/shard_map/jit(_take)/gather | solution.py:174
  35.6 2.1 %collective-permute-start.5 = (bf16[4,4,32,128]{3,2,1,0:T(8,128)(2,1)S(1)}, bf16[4,4,32,128]{3,2,1,0:T(8,128)(2,1)S(1)}, u32[]{:S(2)}, u32[]{:S(2)}) collective-permute-start(bf16[4,4,32,128]{3,2,1,0:T(8,128)(2,1)S(1)} %fusion.6), channel_id=1, source_target_pairs={{0,2},{1,3},{2,0},{3,1},{4,6},{5,7},{6,4},{7,5},{8,10},{9,11},{10,... | collective-permute-start | bytes 393224 | tf_op jit(solution)/shard_map/ppermute | solution.py:24
  37.7 1.3 %collective-permute-start.3 = (bf16[262160]{0:T(1024)(128)(2,1)S(1)}, bf16[262160]{0:T(1024)(128)(2,1)S(1)}, u32[]{:S(2)}, u32[]{:S(2)}) collective-permute-start(bf16[262160]{0:T(1024)(128)(2,1)S(1)} %pad_maximum_fusion), channel_id=1, source_target_pairs={{16,0},{17,1},{18,2},{19,3},{20,4},{21,5},{22,6},{23,7},{24,8},{25... | collective-permute-start | bytes 1572968 | tf_op jit(solution)/shard_map/ppermute | solution.py:14
  39.0 2.5 %collective-permute-done.5 = bf16[4,4,32,128]{3,2,1,0:T(8,128)(2,1)S(1)} collective-permute-done((bf16[4,4,32,128]{3,2,1,0:T(8,128)(2,1)S(1)}, bf16[4,4,32,128]{3,2,1,0:T(8,128)(2,1)S(1)}, u32[]{:S(2)}, u32[]{:S(2)}) %collective-permute-start.5) | collective-permute-done | bytes 131104 | tf_op jit(solution)/shard_map/ppermute | solution.py:24
  41.5 4.5 %collective-permute-start.6 = (bf16[4,32,128]{2,1,0:T(8,128)(2,1)S(1)}, bf16[4,32,128]{2,1,0:T(8,128)(2,1)S(1)}, u32[]{:S(2)}, u32[]{:S(2)}) collective-permute-start(bf16[4,32,128]{2,1,0:T(8,128)(2,1)S(1)} %get-tuple-element.27), channel_id=1, source_target_pairs={{0,12},{4,0},{8,4},{12,8},{1,13},{5,1},{9,5},{13,9},{2,14},{6,2},{... | collective-permute-start | bytes 98312 | tf_op jit(solution)/shard_map/ppermute | solution.py:19
  46.0 0.6 %collective-permute-start.8 = (bf16[4,32,128]{2,1,0:T(8,128)(2,1)S(1)}, bf16[4,32,128]{2,1,0:T(8,128)(2,1)S(1)}, u32[]{:S(2)}, u32[]{:S(2)}) collective-permute-start(bf16[4,32,128]{2,1,0:T(8,128)(2,1)S(1)} %get-tuple-element.28), channel_id=1, source_target_pairs={{0,4},{4,8},{8,12},{12,0},{1,5},{5,9},{9,13},{13,1},{2,6},{6,10},{... | collective-permute-start | bytes 98312 | tf_op jit(solution)/shard_map/ppermute | solution.py:19
  46.7 0.9 %collective-permute-done.6 = bf16[4,32,128]{2,1,0:T(8,128)(2,1)S(1)} collective-permute-done((bf16[4,32,128]{2,1,0:T(8,128)(2,1)S(1)}, bf16[4,32,128]{2,1,0:T(8,128)(2,1)S(1)}, u32[]{:S(2)}, u32[]{:S(2)}) %collective-permute-start.6) | collective-permute-done | bytes 32800 | tf_op jit(solution)/shard_map/ppermute | solution.py:19
  47.6 3.2 %collective-permute-done.7 = bf16[4,32,128]{2,1,0:T(8,128)(2,1)S(1)} collective-permute-done((bf16[4,32,128]{2,1,0:T(8,128)(2,1)S(1)}, bf16[4,32,128]{2,1,0:T(8,128)(2,1)S(1)}, u32[]{:S(2)}, u32[]{:S(2)}) %collective-permute-start.7) | collective-permute-done | bytes 32800 | tf_op jit(solution)/shard_map/ppermute | solution.py:19
  50.8 0.9 %collective-permute-done.8 = bf16[4,32,128]{2,1,0:T(8,128)(2,1)S(1)} collective-permute-done((bf16[4,32,128]{2,1,0:T(8,128)(2,1)S(1)}, bf16[4,32,128]{2,1,0:T(8,128)(2,1)S(1)}, u32[]{:S(2)}, u32[]{:S(2)}) %collective-permute-start.8) | collective-permute-done | bytes 32800 | tf_op jit(solution)/shard_map/ppermute | solution.py:19
  51.8 1.8 %collective-permute-start.9 = (f32[4,32,128]{2,1,0:T(8,128)S(1)}, f32[4,32,128]{2,1,0:T(8,128)S(1)}, u32[]{:S(2)}, u32[]{:S(2)}) collective-permute-start(f32[4,32,128]{2,1,0:T(8,128)S(1)} %fusion.9), channel_id=1, source_target_pairs={{0,2},{1,3},{2,0},{3,1},{4,6},{5,7},{6,4},{7,5},{8,10},{9,11},{10,... | collective-permute-start | bytes 196616 | tf_op jit(solution)/shard_map/ppermute | solution.py:24
  53.8 1.1 %scatter_fusion = bf16[28,128,128]{2,1,0:T(8,128)(2,1)S(1)} fusion(bf16[28,128,128]{2,1,0:T(8,128)(2,1)S(1)} %broadcast_in_dim.32, s32[16]{0:T(128)S(1)} %compare_select_fusion.1, bf16[16,128,128]{2,1,0:T(8,128)(2,1)S(1)} %bitcast.61), kind=kCustom, calls=%fused_computation.2 | custom fusion | bytes 1572928 | tf_op jit(solution)/shard_map/scatter | solution.py:179
  55.0 0.6 %copy.36 = bf16[128,28,128]{2,1,0:T(8,128)(2,1)S(1)} copy(bf16[128,28,128]{2,0,1:T(8,128)(2,1)S(1)} %bitcast.56) | data formatting | bytes 1835008 | tf_op jit(solution)/shard_map/transpose | solution.py:182
  55.6 0.5 reshape.424
  56.1 0.6 %gather_fusion.1 = bf16[4,32,3584]{2,1,0:T(8,128)(2,1)S(1)} fusion(bf16[4,32,3584]{2,1,0:T(8,128)(2,1)S(1)} %reshape.424, s32[1024]{0:T(1024)S(1)} %pad_clamp_fusion), kind=kCustom, calls=%fused_computation.1 | custom fusion | bytes 1835024 | tf_op jit(solution)/shard_map/jit(_take)/gather | solution.py:185
  56.8 1.1 %bitcast_select_fusion = bf16[1,4,32,3584]{3,2,1,0:T(8,128)(2,1)} fusion(bf16[4,32,3584]{2,1,0:T(8,128)(2,1)S(1)} %gather_fusion.1, pred[4]{0:T(512)(128)(4,1)S(1)} %compare_and_fusion), kind=kLoop, calls=%fused_computation.3 | loop fusion | flops 458752 | bytes 1835012 | tf_op jit(solution)/shard_map/jit(_take)/select_n | solution.py:185
  57.9 0.2 collective-permute-done.10
  58.2 0.7 %copy.40 = f32[4,4,32,128]{3,2,1,0:T(8,128)} copy(f32[4,4,32,128]{3,2,0,1:T(8,128)S(1)} %bitcast.63) | data formatting | bytes 524288 | tf_op jit(solution)/shard_map/div | solution.py:204
  (42 shorter events, 1.8 us)
Async XLA Ops:
  2.4 0.7 %collective-permute-start = (bf16[528,128]{1,0:T(8,128)(2,1)S(1)}, bf16[528,128]{1,0:T(8,128)(2,1)S(1)}, u32[]{:S(2)}, u32[]{:S(2)}) collective-permute-start(bf16[528,128]{1,0:T(8,128)(2,1)S(1)} %fusion.5), channel_id=1, source_target_pairs={{0,0},{13,1},{10,2},{7,3},{4,4},{1,5},{14,6},{11,7},{8,8},{5,9},{2... | collective-permute-start | bytes 405512 | tf_op jit(solution)/shard_map/ppermute | solution.py:150
  3.1 15.0 %collective-permute-start.1 = (bf16[1,528,128]{2,1,0:T(8,128)(2,1)S(1)}, bf16[1,528,128]{2,1,0:T(8,128)(2,1)S(1)}, u32[]{:S(2)}, u32[]{:S(2)}) collective-permute-start(bf16[1,528,128]{2,1,0:T(8,128)(2,1)S(1)} %bitcast.68), channel_id=1, source_target_pairs={{0,2},{1,3},{2,0},{3,1},{4,6},{5,7},{6,4},{7,5},{8,10},{9,11},{10,... | collective-permute-start | bytes 405512 | tf_op jit(solution)/shard_map/ppermute | solution.py:24
  18.1 1.6 %collective-permute-start.2 = (bf16[2,1,528,128]{3,2,1,0:T(8,128)(2,1)S(1)}, bf16[2,1,528,128]{3,2,1,0:T(8,128)(2,1)S(1)}, u32[]{:S(2)}, u32[]{:S(2)}) collective-permute-start(bf16[2,1,528,128]{3,2,1,0:T(8,128)(2,1)S(1)} %maximum_select_fusion.2), channel_id=1, source_target_pairs={{0,1},{1,0},{2,3},{3,2},{4,5},{5,4},{6,7},{7,6},{8,9},{9,8},{10,11... | collective-permute-start | bytes 811016 | tf_op jit(solution)/shard_map/ppermute | solution.py:24
  21.2 1.7 %copy-start.1 = (s32[16]{0:T(128)}, s32[16]{0:T(128)S(1)}, u32[]{:S(2)}) copy-start(s32[16]{0:T(128)S(1)} %get-tuple-element.21.cols_ref) | copy-start | bytes 196
  32.0 1.6 %copy-start.3 = (s32[4]{0:T(128)S(1)}, s32[4]{0:T(128)}, u32[]{:S(2)}) copy-start(s32[4]{0:T(128)} %param.11) | copy-start | bytes 52
  33.3 0.7 %copy-start.2 = (s32[16]{0:T(128)S(1)}, s32[16]{0:T(128)}, u32[]{:S(2)}) copy-start(s32[16]{0:T(128)} %get-tuple-element.22.rows_ref) | copy-start | bytes 196
  33.4 1.2 %copy-start = (bf16[28,128,128]{2,1,0:T(8,128)(2,1)S(1)}, bf16[28,128,128]{2,1,0:T(8,128)(2,1)}, u32[]{:S(2)}) copy-start(bf16[28,128,128]{2,1,0:T(8,128)(2,1)} %get-tuple-element.18) | copy-start | bytes 2752516
  33.4 2.0 %collective-permute-start.4 = (f32[4,4,2,32,128]{4,3,1,0,2:T(8,128)S(1)}, f32[4,4,2,32,128]{4,3,1,0,2:T(8,128)S(1)}, u32[]{:S(2)}, u32[]{:S(2)}) collective-permute-start(f32[4,4,2,32,128]{4,3,1,0,2:T(8,128)S(1)} %bitcast.73), channel_id=1, source_target_pairs={{0,1},{1,0},{2,3},{3,2},{4,5},{5,4},{6,7},{7,6},{8,9},{9,8},{10,11... | collective-permute-start | bytes 1572872 | tf_op jit(solution)/shard_map/ppermute | solution.py:24
  35.6 5.9 %collective-permute-start.5 = (bf16[4,4,32,128]{3,2,1,0:T(8,128)(2,1)S(1)}, bf16[4,4,32,128]{3,2,1,0:T(8,128)(2,1)S(1)}, u32[]{:S(2)}, u32[]{:S(2)}) collective-permute-start(bf16[4,4,32,128]{3,2,1,0:T(8,128)(2,1)S(1)} %fusion.6), channel_id=1, source_target_pairs={{0,2},{1,3},{2,0},{3,1},{4,6},{5,7},{6,4},{7,5},{8,10},{9,11},{10,... | collective-permute-start | bytes 393224 | tf_op jit(solution)/shard_map/ppermute | solution.py:24
  37.7 15.9 %collective-permute-start.3 = (bf16[262160]{0:T(1024)(128)(2,1)S(1)}, bf16[262160]{0:T(1024)(128)(2,1)S(1)}, u32[]{:S(2)}, u32[]{:S(2)}) collective-permute-start(bf16[262160]{0:T(1024)(128)(2,1)S(1)} %pad_maximum_fusion), channel_id=1, source_target_pairs={{16,0},{17,1},{18,2},{19,3},{20,4},{21,5},{22,6},{23,7},{24,8},{25... | collective-permute-start | bytes 1572968 | tf_op jit(solution)/shard_map/ppermute | solution.py:14
  41.5 6.1 %collective-permute-start.6 = (bf16[4,32,128]{2,1,0:T(8,128)(2,1)S(1)}, bf16[4,32,128]{2,1,0:T(8,128)(2,1)S(1)}, u32[]{:S(2)}, u32[]{:S(2)}) collective-permute-start(bf16[4,32,128]{2,1,0:T(8,128)(2,1)S(1)} %get-tuple-element.27), channel_id=1, source_target_pairs={{0,12},{4,0},{8,4},{12,8},{1,13},{5,1},{9,5},{13,9},{2,14},{6,2},{... | collective-permute-start | bytes 98312 | tf_op jit(solution)/shard_map/ppermute | solution.py:19
  46.0 4.8 %collective-permute-start.7 = (bf16[4,32,128]{2,1,0:T(8,128)(2,1)S(1)}, bf16[4,32,128]{2,1,0:T(8,128)(2,1)S(1)}, u32[]{:S(2)}, u32[]{:S(2)}) collective-permute-start(bf16[4,32,128]{2,1,0:T(8,128)(2,1)S(1)} %get-tuple-element.29), channel_id=1, source_target_pairs={{0,8},{4,12},{8,0},{12,4},{1,9},{5,13},{9,1},{13,5},{2,10},{6,14},... | collective-permute-start | bytes 98312 | tf_op jit(solution)/shard_map/ppermute | solution.py:19
  46.0 5.7 %collective-permute-start.8 = (bf16[4,32,128]{2,1,0:T(8,128)(2,1)S(1)}, bf16[4,32,128]{2,1,0:T(8,128)(2,1)S(1)}, u32[]{:S(2)}, u32[]{:S(2)}) collective-permute-start(bf16[4,32,128]{2,1,0:T(8,128)(2,1)S(1)} %get-tuple-element.28), channel_id=1, source_target_pairs={{0,4},{4,8},{8,12},{12,0},{1,5},{5,9},{9,13},{13,1},{2,6},{6,10},{... | collective-permute-start | bytes 98312 | tf_op jit(solution)/shard_map/ppermute | solution.py:19
  51.8 4.9 %collective-permute-start.9 = (f32[4,32,128]{2,1,0:T(8,128)S(1)}, f32[4,32,128]{2,1,0:T(8,128)S(1)}, u32[]{:S(2)}, u32[]{:S(2)}) collective-permute-start(f32[4,32,128]{2,1,0:T(8,128)S(1)} %fusion.9), channel_id=1, source_target_pairs={{0,2},{1,3},{2,0},{3,1},{4,6},{5,7},{6,4},{7,5},{8,10},{9,11},{10,... | collective-permute-start | bytes 196616 | tf_op jit(solution)/shard_map/ppermute | solution.py:24
  56.7 1.4 %collective-permute-start.10 = (f32[2,4,32,128]{3,2,1,0:T(8,128)S(1)}, f32[2,4,32,128]{3,2,1,0:T(8,128)S(1)}, u32[]{:S(2)}, u32[]{:S(2)}) collective-permute-start(f32[2,4,32,128]{3,2,1,0:T(8,128)S(1)} %maximum_select_fusion.5), channel_id=1, source_target_pairs={{0,1},{1,0},{2,3},{3,2},{4,5},{5,4},{6,7},{7,6},{8,9},{9,8},{10,11... | collective-permute-start | bytes 393224 | tf_op jit(solution)/shard_map/ppermute | solution.py:24

commit v11 on v8

--- a/solution.py
+++ b/solution.py
@@ -29,8 +29,8 @@
     return sigmoid_val * (1.0 + pre_act * (1.0 - sigmoid_val))
 
 
-def block_kernel(rows_ref, cols_ref, rep_ref, feat_hbm, hid_hbm, w_ref, ig_ref, pg_ref,
-                 xs, hs, pr, acc, sems):
+def block_kernel(rows_ref, cols_ref, rep_ref, feat_hbm, feat_t_hbm, hid_hbm, w_ref, ig_ref, pg_ref,
+                 xs, xts, hs, pr, acc, sems):
     block_count = w_ref.shape[0]
     width = w_ref.shape[-1]
 
@@ -40,6 +40,7 @@
         return (
             pltpu.make_async_copy(feat_hbm.at[:, pl.ds(r, width)], xs.at[b], sems.at[0, b]),
             pltpu.make_async_copy(hid_hbm.at[:, pl.ds(c, width)], hs.at[b], sems.at[1, b]),
+            pltpu.make_async_copy(feat_t_hbm.at[pl.ds(r, width), :], xts.at[b], sems.at[2, b]),
         )
 
     @pl.loop(0, block_count)
@@ -72,9 +73,7 @@
         )
         row = rows_ref[b]
         acc[row] = acc[row] + back
-        pg_ref[b] = lax.dot_general(
-            xs[b], act, (((0,), (0,)), ((), ())), preferred_element_type=jnp.float32
-        )
+        pg_ref[b] = jnp.dot(xts[b], act, preferred_element_type=jnp.float32)
 
     ig_ref[...] = acc[...].astype(ig_ref.dtype)
 
@@ -93,14 +92,15 @@
             jax.ShapeDtypeStruct((row_count, tokens, width), jnp.bfloat16),
             jax.ShapeDtypeStruct((block_count, width, width), jnp.float32),
         ),
-        in_specs=[smem, smem, smem, anyspace, anyspace, vmem],
+        in_specs=[smem, smem, smem, anyspace, anyspace, anyspace, vmem],
         out_specs=(vmem, vmem),
         scratch_shapes=[
             pltpu.VMEM((block_count, tokens, width), jnp.bfloat16),
+            pltpu.VMEM((block_count, width, tokens), jnp.bfloat16),
             pltpu.VMEM((block_count, tokens, width), jnp.bfloat16),
             pltpu.VMEM((block_count, tokens, width), jnp.float32),
             pltpu.VMEM((row_count, tokens, width), jnp.float32),
-            pltpu.SemaphoreType.DMA((2, block_count)),
+            pltpu.SemaphoreType.DMA((3, block_count)),
         ],
         cost_estimate=pl.CostEstimate(
             flops=6 * block_count * tokens * width * width,
@@ -108,7 +108,7 @@
             bytes_accessed=block_count * width * (4 * tokens + 6 * width)
             + row_count * tokens * width * 2,
         ),
-    )(row_ids, col_ids, first, features, hidden_grad, weights)
+    )(row_ids, col_ids, first, features, features.T, hidden_grad, weights)
 
 
 def gather_over(x, axis):

time: 58.8 us -> 58.7 us (level)
  local copies, waits for them, and re-layouts: 8.53 us -> 10.7 us
  waiting for transfers between devices: 11.6 us -> 10 us
  other arithmetic: 5.38 us -> 4.74 us
    another operation x0 -> x1, local copies, waits for them, and re-layouts: none -> 2.22 us  [local(): activations[0].reshape(tok_rows, -1)]
    ppermute x6, waiting for transfers between devices: 6.54 us -> 4.96 us  [swapped(): return lax.ppermute(x, axis, [(i, i ^ 1 << bit) for i in range(n)])]
    select_n x2, other arithmetic: 1.74 us -> 1.08 us  [local(): received = jnp.take(arrived, order, axis=0)]
  transfers between devices with their start and end apart: 11 -> 11, of which waited for: 7 -> 7; matrix products, arithmetic and copies ran while one was open for 10% -> 13% of each run, Pallas kernels for 0% -> 0%
where the time goes in v11:
time: 58.7 us; the launch traced here: 58.3 us
  starting transfers between devices  23.2 us (40%)
  local copies, waits for them, and re-layouts  10.7 us (18%)
  waiting for transfers between devices  10 us (17%)
  Pallas kernels  8.68 us (15%)
  other arithmetic  4.74 us (8%)
  between operations  0.91 us (2%)
    ppermute x6, starting transfers between devices, swapped(): return lax.ppermute(x, axis, [(i, i ^ 1 << bit) for i in range(n)])  16.2 us
    pallas_call x1, Pallas kernels, block_pass(): pl.pallas_call(block_kernel, out_shape=(jax.ShapeDtypeStruct((row_count,...  8.68 us
    ppermute x3, waiting for transfers between devices, shifted(): return lax.ppermute(x, axis, [(i, (i + k) % n) for i in range(n)])  5.07 us
    ppermute x3, starting transfers between devices, shifted(): return lax.ppermute(x, axis, [(i, (i + k) % n) for i in range(n)])  5.02 us
    ppermute x6, waiting for transfers between devices, swapped(): return lax.ppermute(x, axis, [(i, i ^ 1 << bit) for i in range(n)])  4.96 us
    another operation x1, local copies, waits for them, and re-layouts, local(): activations[0].reshape(tok_rows, -1)  2.22 us
    dynamic_slice x1, local copies, waits for them, and re-layouts, local(): keep = lax.dynamic_index_in_dim(held, mine, axis_at, keepdims=False)  1.31 us
    ppermute x1, starting transfers between devices, passed_along(): return lax.ppermute(block, axis, route)  1.29 us
  transfers between devices with their start and end apart: 11, of which 7 were waited for; matrix products, arithmetic and copies ran while one was open for 13% of the time, Pallas kernels for 0%

profile of v11, /device:TPU:0, one launch (start us, length us, event | category | flops | bytes accessed | tf_op | source)
XLA Modules:
  0.0 58.3 jit_solution(8223293509352606567)
XLA Ops:
  0.6 0.7 %convert_element_type.53 = bf16[1,4,2]{1,2,0:T(2,128)(2,1)S(1)} convert(s32[1,4,2]{1,2,0:T(2,128)} %param.10) | non-fusion elementwise | flops 8 | bytes 48 | tf_op jit(solution)/shard_map/convert_element_type | solution.py:153
  1.5 0.9 %fusion.5 = bf16[528,128]{1,0:T(8,128)(2,1)S(1)} fusion(bf16[1,8]{1,0:T(2,128)(2,1)S(1)} %convert_element_type.54, bf16[512,128]{1,0:T(8,128)(2,1)} %bitcast.82), kind=kLoop, calls=%fused_computation.20 | loop fusion | flops 405504 | bytes 266256 | tf_op jit(solution)/shard_map/concatenate | solution.py:155
  2.4 0.7 %collective-permute-start = (bf16[528,128]{1,0:T(8,128)(2,1)S(1)}, bf16[528,128]{1,0:T(8,128)(2,1)S(1)}, u32[]{:S(2)}, u32[]{:S(2)}) collective-permute-start(bf16[528,128]{1,0:T(8,128)(2,1)S(1)} %fusion.5), channel_id=1, source_target_pairs={{0,0},{13,1},{10,2},{7,3},{4,4},{1,5},{14,6},{11,7},{8,8},{5,9},{2... | collective-permute-start | bytes 405512 | tf_op jit(solution)/shard_map/ppermute | solution.py:163
  3.1 12.0 %collective-permute-start.1 = (bf16[1,528,128]{2,1,0:T(8,128)(2,1)S(1)}, bf16[1,528,128]{2,1,0:T(8,128)(2,1)S(1)}, u32[]{:S(2)}, u32[]{:S(2)}) collective-permute-start(bf16[1,528,128]{2,1,0:T(8,128)(2,1)S(1)} %bitcast.71), channel_id=1, source_target_pairs={{0,2},{1,3},{2,0},{3,1},{4,6},{5,7},{6,4},{7,5},{8,10},{9,11},{10,... | collective-permute-start | bytes 405512 | tf_op jit(solution)/shard_map/ppermute | solution.py:24
  15.1 2.2 %copy.40 = bf16[128,3584]{0,1:T(8,128)(2,1)} copy(bf16[128,3584]{1,0:T(8,128)(2,1)} %bitcast.59) | data formatting | bytes 1835008 | tf_op jit(solution)/shard_map/reshape;squeeze | solution.py:178
  17.3 0.8 %collective-permute-done.1 = bf16[1,528,128]{2,1,0:T(8,128)(2,1)S(1)} collective-permute-done((bf16[1,528,128]{2,1,0:T(8,128)(2,1)S(1)}, bf16[1,528,128]{2,1,0:T(8,128)(2,1)S(1)}, u32[]{:S(2)}, u32[]{:S(2)}) %collective-permute-start.1) | collective-permute-done | bytes 135200 | tf_op jit(solution)/shard_map/ppermute | solution.py:24
  18.3 1.5 %collective-permute-done.2 = bf16[2,1,528,128]{3,2,1,0:T(8,128)(2,1)S(1)} collective-permute-done((bf16[2,1,528,128]{3,2,1,0:T(8,128)(2,1)S(1)}, bf16[2,1,528,128]{3,2,1,0:T(8,128)(2,1)S(1)}, u32[]{:S(2)}, u32[]{:S(2)}) %collective-permute-start.2) | collective-permute-done | bytes 270368 | tf_op jit(solution)/shard_map/ppermute | solution.py:24
  19.8 0.4 copy.39
  20.5 0.6 %fusion.10 = (s32[16]{0:T(128)S(1)}, s32[16]{0:T(128)S(1)}, s32[16]{0:T(128)}) fusion(s32[16,2]{1,0:T(8,128)S(1)} %reshape.426), kind=kLoop, calls=%fused_computation.36 | loop fusion | flops 48 | bytes 320 | tf_op jit(solution)/shard_map/jit(_take)/jit(_where)/select_n | solution.py:187
  21.2 0.8 %iota_reduce_fusion = (pred[16]{0:T(512)(128)(4,1)}, s32[16]{0:T(128)}) fusion(s32[16]{0:T(128)S(1)} %get-tuple-element.21.cols_ref), kind=kLoop, calls=%fused_computation.33 | loop fusion | flops 1936 | bytes 144 | tf_op jit(solution)/shard_map/block_pass/reduce | solution.py:85
  21.9 0.9 %copy.41 = bf16[4,512,128]{2,1,0:T(8,128)(2,1)} copy(bf16[4,512,128]{2,0,1:T(4,128)(2,1)S(1)} %slice.66) | data formatting | bytes 1048576 | tf_op jit(solution)/shard_map/slice | solution.py:168
  22.8 8.7 %shard_map.68 = (bf16[28,128,128]{2,1,0:T(8,128)(2,1)}, f32[16,128,128]{2,1,0:T(8,128)}) custom-call(s32[16]{0:T(128)} %get-tuple-element.22.rows_ref, s32[16]{0:T(128)} %copy-done.1, s32[16]{0:T(128)} %get-tuple-element.17.rep_ref, bf16[128,3584]{1,0:T(8,128)(2,1)} %bitcast.60, bf16[3584,128]{1,0:T(8,128)(2,1)} %bitcast.61, bf16[128,14336]{1,0:T(8,128)(2,1)} %bitcast.58, ...), custom_call_target="tpu_custom_call" | custom-call | flops 201326592 | bytes 3538944 | tf_op jit(solution)/shard_map/pallas_call | solution.py:89
  31.5 1.3 %constant_dynamic-slice_fusion.1 = (f32[4,4,2,1,32,128]{5,4,3,2,1,0:T(8,128)S(1)}, f32[4,4,2,1,32,128]{5,4,3,2,1,0:T(8,128)S(1)}) fusion(f32[4,4,2,2,32,128]{5,4,3,2,1,0:T(8,128)} %bitcast.68, s32[]{:T(128)S(6)} %select_n.147, s32[]{:T(128)S(6)} %select_n.148), kind=kLoop, calls=%fused_computation.44 | loop fusion | bytes 2097160 | tf_op jit(solution)/shard_map/jit(dynamic_index_in_dim)/dynamic_slice | solution.py:204
  33.1 0.4 copy-done.2
  33.5 0.5 copy-done
  34.0 0.6 %gather_fusion = bf16[16,128,128]{2,1,0:T(8,128)(2,1)S(1)} fusion(bf16[28,128,128]{2,1,0:T(8,128)(2,1)S(1)} %copy-done, s32[1024]{0:T(1024)S(1)} %pad_clamp_fusion.1), kind=kCustom, calls=%fused_computation | custom fusion | bytes 1048640 | tf_op jit(solution)/shard_map/jit(_take)/gather | solution.py:187
  35.1 2.1 %collective-permute-start.5 = (bf16[4,4,32,128]{3,2,1,0:T(8,128)(2,1)S(1)}, bf16[4,4,32,128]{3,2,1,0:T(8,128)(2,1)S(1)}, u32[]{:S(2)}, u32[]{:S(2)}) collective-permute-start(bf16[4,4,32,128]{3,2,1,0:T(8,128)(2,1)S(1)} %fusion.6), channel_id=1, source_target_pairs={{0,2},{1,3},{2,0},{3,1},{4,6},{5,7},{6,4},{7,5},{8,10},{9,11},{10,... | collective-permute-start | bytes 393224 | tf_op jit(solution)/shard_map/ppermute | solution.py:24
  37.2 1.3 %collective-permute-start.3 = (bf16[262160]{0:T(1024)(128)(2,1)S(1)}, bf16[262160]{0:T(1024)(128)(2,1)S(1)}, u32[]{:S(2)}, u32[]{:S(2)}) collective-permute-start(bf16[262160]{0:T(1024)(128)(2,1)S(1)} %pad_maximum_fusion), channel_id=1, source_target_pairs={{16,0},{17,1},{18,2},{19,3},{20,4},{21,5},{22,6},{23,7},{24,8},{25... | collective-permute-start | bytes 1572968 | tf_op jit(solution)/shard_map/ppermute | solution.py:14
  38.5 2.5 %collective-permute-done.5 = bf16[4,4,32,128]{3,2,1,0:T(8,128)(2,1)S(1)} collective-permute-done((bf16[4,4,32,128]{3,2,1,0:T(8,128)(2,1)S(1)}, bf16[4,4,32,128]{3,2,1,0:T(8,128)(2,1)S(1)}, u32[]{:S(2)}, u32[]{:S(2)}) %collective-permute-start.5) | collective-permute-done | bytes 131104 | tf_op jit(solution)/shard_map/ppermute | solution.py:24
  41.0 4.4 %collective-permute-start.6 = (bf16[4,32,128]{2,1,0:T(8,128)(2,1)S(1)}, bf16[4,32,128]{2,1,0:T(8,128)(2,1)S(1)}, u32[]{:S(2)}, u32[]{:S(2)}) collective-permute-start(bf16[4,32,128]{2,1,0:T(8,128)(2,1)S(1)} %get-tuple-element.27), channel_id=1, source_target_pairs={{0,12},{4,0},{8,4},{12,8},{1,13},{5,1},{9,5},{13,9},{2,14},{6,2},{... | collective-permute-start | bytes 98312 | tf_op jit(solution)/shard_map/ppermute | solution.py:19
  45.4 0.6 %collective-permute-start.8 = (bf16[4,32,128]{2,1,0:T(8,128)(2,1)S(1)}, bf16[4,32,128]{2,1,0:T(8,128)(2,1)S(1)}, u32[]{:S(2)}, u32[]{:S(2)}) collective-permute-start(bf16[4,32,128]{2,1,0:T(8,128)(2,1)S(1)} %get-tuple-element.28), channel_id=1, source_target_pairs={{0,4},{4,8},{8,12},{12,0},{1,5},{5,9},{9,13},{13,1},{2,6},{6,10},{... | collective-permute-start | bytes 98312 | tf_op jit(solution)/shard_map/ppermute | solution.py:19
  46.1 0.9 %collective-permute-done.6 = bf16[4,32,128]{2,1,0:T(8,128)(2,1)S(1)} collective-permute-done((bf16[4,32,128]{2,1,0:T(8,128)(2,1)S(1)}, bf16[4,32,128]{2,1,0:T(8,128)(2,1)S(1)}, u32[]{:S(2)}, u32[]{:S(2)}) %collective-permute-start.6) | collective-permute-done | bytes 32800 | tf_op jit(solution)/shard_map/ppermute | solution.py:19
  47.0 3.2 %collective-permute-done.7 = bf16[4,32,128]{2,1,0:T(8,128)(2,1)S(1)} collective-permute-done((bf16[4,32,128]{2,1,0:T(8,128)(2,1)S(1)}, bf16[4,32,128]{2,1,0:T(8,128)(2,1)S(1)}, u32[]{:S(2)}, u32[]{:S(2)}) %collective-permute-start.7) | collective-permute-done | bytes 32800 | tf_op jit(solution)/shard_map/ppermute | solution.py:19
  50.2 0.9 %collective-permute-done.8 = bf16[4,32,128]{2,1,0:T(8,128)(2,1)S(1)} collective-permute-done((bf16[4,32,128]{2,1,0:T(8,128)(2,1)S(1)}, bf16[4,32,128]{2,1,0:T(8,128)(2,1)S(1)}, u32[]{:S(2)}, u32[]{:S(2)}) %collective-permute-start.8) | collective-permute-done | bytes 32800 | tf_op jit(solution)/shard_map/ppermute | solution.py:19
  51.1 1.8 %collective-permute-start.9 = (f32[4,32,128]{2,1,0:T(8,128)S(1)}, f32[4,32,128]{2,1,0:T(8,128)S(1)}, u32[]{:S(2)}, u32[]{:S(2)}) collective-permute-start(f32[4,32,128]{2,1,0:T(8,128)S(1)} %fusion.9), channel_id=1, source_target_pairs={{0,2},{1,3},{2,0},{3,1},{4,6},{5,7},{6,4},{7,5},{8,10},{9,11},{10,... | collective-permute-start | bytes 196616 | tf_op jit(solution)/shard_map/ppermute | solution.py:24
  53.2 1.1 %scatter_fusion = bf16[28,128,128]{2,1,0:T(8,128)(2,1)S(1)} fusion(bf16[28,128,128]{2,1,0:T(8,128)(2,1)S(1)} %broadcast_in_dim.32, s32[16]{0:T(128)S(1)} %compare_select_fusion.1, bf16[16,128,128]{2,1,0:T(8,128)(2,1)S(1)} %bitcast.64), kind=kCustom, calls=%fused_computation.2 | custom fusion | bytes 1572928 | tf_op jit(solution)/shard_map/scatter | solution.py:192
  54.4 0.6 %copy.42 = bf16[128,28,128]{2,1,0:T(8,128)(2,1)S(1)} copy(bf16[128,28,128]{2,0,1:T(8,128)(2,1)S(1)} %bitcast.57) | data formatting | bytes 1835008 | tf_op jit(solution)/shard_map/transpose | solution.py:195
  55.0 0.5 reshape.424
  55.5 0.6 %gather_fusion.1 = bf16[4,32,3584]{2,1,0:T(8,128)(2,1)S(1)} fusion(bf16[4,32,3584]{2,1,0:T(8,128)(2,1)S(1)} %reshape.424, s32[1024]{0:T(1024)S(1)} %pad_clamp_fusion), kind=kCustom, calls=%fused_computation.1 | custom fusion | bytes 1835024 | tf_op jit(solution)/shard_map/jit(_take)/gather | solution.py:198
  56.2 1.1 %bitcast_select_fusion = bf16[1,4,32,3584]{3,2,1,0:T(8,128)(2,1)} fusion(bf16[4,32,3584]{2,1,0:T(8,128)(2,1)S(1)} %gather_fusion.1, pred[4]{0:T(512)(128)(4,1)S(1)} %compare_and_fusion), kind=kLoop, calls=%fused_computation.3 | loop fusion | flops 458752 | bytes 1835012 | tf_op jit(solution)/shard_map/jit(_take)/select_n | solution.py:198
  57.3 0.2 collective-permute-done.10
  57.6 0.7 %copy.46 = f32[4,4,32,128]{3,2,1,0:T(8,128)} copy(f32[4,4,32,128]{3,2,0,1:T(8,128)S(1)} %bitcast.67) | data formatting | bytes 524288 | tf_op jit(solution)/shard_map/div | solution.py:217
  (43 shorter events, 1.8 us)
Async XLA Ops:
  2.4 0.7 %collective-permute-start = (bf16[528,128]{1,0:T(8,128)(2,1)S(1)}, bf16[528,128]{1,0:T(8,128)(2,1)S(1)}, u32[]{:S(2)}, u32[]{:S(2)}) collective-permute-start(bf16[528,128]{1,0:T(8,128)(2,1)S(1)} %fusion.5), channel_id=1, source_target_pairs={{0,0},{13,1},{10,2},{7,3},{4,4},{1,5},{14,6},{11,7},{8,8},{5,9},{2... | collective-permute-start | bytes 405512 | tf_op jit(solution)/shard_map/ppermute | solution.py:163
  3.1 15.0 %collective-permute-start.1 = (bf16[1,528,128]{2,1,0:T(8,128)(2,1)S(1)}, bf16[1,528,128]{2,1,0:T(8,128)(2,1)S(1)}, u32[]{:S(2)}, u32[]{:S(2)}) collective-permute-start(bf16[1,528,128]{2,1,0:T(8,128)(2,1)S(1)} %bitcast.71), channel_id=1, source_target_pairs={{0,2},{1,3},{2,0},{3,1},{4,6},{5,7},{6,4},{7,5},{8,10},{9,11},{10,... | collective-permute-start | bytes 405512 | tf_op jit(solution)/shard_map/ppermute | solution.py:24
  15.1 3.1 %copy-start.3 = (s32[4]{0:T(128)S(1)}, s32[4]{0:T(128)}, u32[]{:S(2)}) copy-start(s32[4]{0:T(128)} %param.11) | copy-start | bytes 52
  18.1 1.6 %collective-permute-start.2 = (bf16[2,1,528,128]{3,2,1,0:T(8,128)(2,1)S(1)}, bf16[2,1,528,128]{3,2,1,0:T(8,128)(2,1)S(1)}, u32[]{:S(2)}, u32[]{:S(2)}) collective-permute-start(bf16[2,1,528,128]{3,2,1,0:T(8,128)(2,1)S(1)} %maximum_select_fusion.2), channel_id=1, source_target_pairs={{0,1},{1,0},{2,3},{3,2},{4,5},{5,4},{6,7},{7,6},{8,9},{9,8},{10,11... | collective-permute-start | bytes 811016 | tf_op jit(solution)/shard_map/ppermute | solution.py:24
  21.2 1.7 %copy-start.1 = (s32[16]{0:T(128)}, s32[16]{0:T(128)S(1)}, u32[]{:S(2)}) copy-start(s32[16]{0:T(128)S(1)} %get-tuple-element.21.cols_ref) | copy-start | bytes 196
  32.8 0.7 %copy-start.2 = (s32[16]{0:T(128)S(1)}, s32[16]{0:T(128)}, u32[]{:S(2)}) copy-start(s32[16]{0:T(128)} %get-tuple-element.22.rows_ref) | copy-start | bytes 196
  32.8 1.2 %copy-start = (bf16[28,128,128]{2,1,0:T(8,128)(2,1)S(1)}, bf16[28,128,128]{2,1,0:T(8,128)(2,1)}, u32[]{:S(2)}) copy-start(bf16[28,128,128]{2,1,0:T(8,128)(2,1)} %get-tuple-element.18) | copy-start | bytes 2752516
  32.9 2.0 %collective-permute-start.4 = (f32[4,4,2,32,128]{4,3,1,0,2:T(8,128)S(1)}, f32[4,4,2,32,128]{4,3,1,0,2:T(8,128)S(1)}, u32[]{:S(2)}, u32[]{:S(2)}) collective-permute-start(f32[4,4,2,32,128]{4,3,1,0,2:T(8,128)S(1)} %bitcast.76), channel_id=1, source_target_pairs={{0,1},{1,0},{2,3},{3,2},{4,5},{5,4},{6,7},{7,6},{8,9},{9,8},{10,11... | collective-permute-start | bytes 1572872 | tf_op jit(solution)/shard_map/ppermute | solution.py:24
  35.1 5.9 %collective-permute-start.5 = (bf16[4,4,32,128]{3,2,1,0:T(8,128)(2,1)S(1)}, bf16[4,4,32,128]{3,2,1,0:T(8,128)(2,1)S(1)}, u32[]{:S(2)}, u32[]{:S(2)}) collective-permute-start(bf16[4,4,32,128]{3,2,1,0:T(8,128)(2,1)S(1)} %fusion.6), channel_id=1, source_target_pairs={{0,2},{1,3},{2,0},{3,1},{4,6},{5,7},{6,4},{7,5},{8,10},{9,11},{10,... | collective-permute-start | bytes 393224 | tf_op jit(solution)/shard_map/ppermute | solution.py:24
  37.2 15.8 %collective-permute-start.3 = (bf16[262160]{0:T(1024)(128)(2,1)S(1)}, bf16[262160]{0:T(1024)(128)(2,1)S(1)}, u32[]{:S(2)}, u32[]{:S(2)}) collective-permute-start(bf16[262160]{0:T(1024)(128)(2,1)S(1)} %pad_maximum_fusion), channel_id=1, source_target_pairs={{16,0},{17,1},{18,2},{19,3},{20,4},{21,5},{22,6},{23,7},{24,8},{25... | collective-permute-start | bytes 1572968 | tf_op jit(solution)/shard_map/ppermute | solution.py:14
  41.0 6.0 %collective-permute-start.6 = (bf16[4,32,128]{2,1,0:T(8,128)(2,1)S(1)}, bf16[4,32,128]{2,1,0:T(8,128)(2,1)S(1)}, u32[]{:S(2)}, u32[]{:S(2)}) collective-permute-start(bf16[4,32,128]{2,1,0:T(8,128)(2,1)S(1)} %get-tuple-element.27), channel_id=1, source_target_pairs={{0,12},{4,0},{8,4},{12,8},{1,13},{5,1},{9,5},{13,9},{2,14},{6,2},{... | collective-permute-start | bytes 98312 | tf_op jit(solution)/shard_map/ppermute | solution.py:19
  45.4 4.8 %collective-permute-start.7 = (bf16[4,32,128]{2,1,0:T(8,128)(2,1)S(1)}, bf16[4,32,128]{2,1,0:T(8,128)(2,1)S(1)}, u32[]{:S(2)}, u32[]{:S(2)}) collective-permute-start(bf16[4,32,128]{2,1,0:T(8,128)(2,1)S(1)} %get-tuple-element.29), channel_id=1, source_target_pairs={{0,8},{4,12},{8,0},{12,4},{1,9},{5,13},{9,1},{13,5},{2,10},{6,14},... | collective-permute-start | bytes 98312 | tf_op jit(solution)/shard_map/ppermute | solution.py:19
  45.4 5.7 %collective-permute-start.8 = (bf16[4,32,128]{2,1,0:T(8,128)(2,1)S(1)}, bf16[4,32,128]{2,1,0:T(8,128)(2,1)S(1)}, u32[]{:S(2)}, u32[]{:S(2)}) collective-permute-start(bf16[4,32,128]{2,1,0:T(8,128)(2,1)S(1)} %get-tuple-element.28), channel_id=1, source_target_pairs={{0,4},{4,8},{8,12},{12,0},{1,5},{5,9},{9,13},{13,1},{2,6},{6,10},{... | collective-permute-start | bytes 98312 | tf_op jit(solution)/shard_map/ppermute | solution.py:19
  51.1 4.9 %collective-permute-start.9 = (f32[4,32,128]{2,1,0:T(8,128)S(1)}, f32[4,32,128]{2,1,0:T(8,128)S(1)}, u32[]{:S(2)}, u32[]{:S(2)}) collective-permute-start(f32[4,32,128]{2,1,0:T(8,128)S(1)} %fusion.9), channel_id=1, source_target_pairs={{0,2},{1,3},{2,0},{3,1},{4,6},{5,7},{6,4},{7,5},{8,10},{9,11},{10,... | collective-permute-start | bytes 196616 | tf_op jit(solution)/shard_map/ppermute | solution.py:24
  56.1 1.4 %collective-permute-start.10 = (f32[2,4,32,128]{3,2,1,0:T(8,128)S(1)}, f32[2,4,32,128]{3,2,1,0:T(8,128)S(1)}, u32[]{:S(2)}, u32[]{:S(2)}) collective-permute-start(f32[2,4,32,128]{3,2,1,0:T(8,128)S(1)} %maximum_select_fusion.5), channel_id=1, source_target_pairs={{0,1},{1,0},{2,3},{3,2},{4,5},{5,4},{6,7},{7,6},{8,9},{9,8},{10,11... | collective-permute-start | bytes 393224 | tf_op jit(solution)/shard_map/ppermute | solution.py:24

commit v12 on v8

--- a/solution.py
+++ b/solution.py
@@ -33,6 +33,13 @@
                  xs, hs, pr, acc, sems):
     block_count = w_ref.shape[0]
     width = w_ref.shape[-1]
+
+    def block_loop(body):
+        def step(b, carry):
+            body(b)
+            return carry
+
+        lax.fori_loop(0, block_count, step, 0, unroll=min(block_count, 16))
 
     def copies(b):
         r = pl.multiple_of(rows_ref[b] * width, width)
@@ -42,20 +49,20 @@
             pltpu.make_async_copy(hid_hbm.at[:, pl.ds(c, width)], hs.at[b], sems.at[1, b]),
         )
 
-    @pl.loop(0, block_count)
+    @block_loop
     def _(b):
         for cp in copies(b):
             cp.start()
 
     acc[...] = jnp.zeros(acc.shape, acc.dtype)
 
-    @pl.loop(0, block_count)
+    @block_loop
     def _(b):
         for cp in copies(b):
             cp.wait()
         pr[b] = jnp.dot(xs[b], w_ref[b], preferred_element_type=jnp.float32)
 
-    @pl.loop(0, block_count)
+    @block_loop
     def _(b):
         first = rep_ref[b]
 
@@ -63,7 +70,7 @@
         def _():
             pr[first] = pr[first] + pr[b]
 
-    @pl.loop(0, block_count)
+    @block_loop
     def _(b):
         pre_act = pr[rep_ref[b]]
         act = (hs[b].astype(jnp.float32) * silu_slope(pre_act)).astype(jnp.bfloat16)

time: 58.8 us -> 56.6 us (0.963)
  Pallas kernels: 8.72 us -> 6.55 us
    pallas_call x1, Pallas kernels: 8.72 us -> 6.55 us  [block_pass(): pl.pallas_call(block_kernel, out_shape=(jax.ShapeDtypeStruct((row_count,...]
where the time goes in v12:
time: 56.6 us; the launch traced here: 56.3 us
  starting transfers between devices  23.3 us (41%)
  waiting for transfers between devices  11.6 us (20%)
  local copies, waits for them, and re-layouts  8.52 us (15%)
  Pallas kernels  6.55 us (12%)
  other arithmetic  5.38 us (10%)
  between operations  0.9 us (2%)
    ppermute x6, starting transfers between devices, swapped(): return lax.ppermute(x, axis, [(i, i ^ 1 << bit) for i in range(n)])  16.2 us
    pallas_call x1, Pallas kernels, block_pass(): pl.pallas_call(block_kernel, out_shape=(jax.ShapeDtypeStruct((row_count,...  6.55 us
    ppermute x6, waiting for transfers between devices, swapped(): return lax.ppermute(x, axis, [(i, i ^ 1 << bit) for i in range(n)])  6.55 us
    ppermute x3, starting transfers between devices, shifted(): return lax.ppermute(x, axis, [(i, (i + k) % n) for i in range(n)])  5.1 us
    ppermute x3, waiting for transfers between devices, shifted(): return lax.ppermute(x, axis, [(i, (i + k) % n) for i in range(n)])  5.07 us
    select_n x2, other arithmetic, local(): received = jnp.take(arrived, order, axis=0)  1.74 us
    dynamic_slice x1, local copies, waits for them, and re-layouts, local(): keep = lax.dynamic_index_in_dim(held, mine, axis_at, keepdims=False)  1.31 us
    ppermute x1, starting transfers between devices, passed_along(): return lax.ppermute(block, axis, route)  1.29 us
  transfers between devices with their start and end apart: 11, of which 7 were waited for; matrix products, arithmetic and copies ran while one was open for 10% of the time, Pallas kernels for 0%

profile of v12, /device:TPU:0, one launch (start us, length us, event | category | flops | bytes accessed | tf_op | source)
XLA Modules:
  0.0 56.3 jit_solution(17407929761228313116)
XLA Ops:
  0.6 0.7 %convert_element_type.53 = bf16[1,4,2]{1,2,0:T(2,128)(2,1)S(1)} convert(s32[1,4,2]{1,2,0:T(2,128)} %param.10) | non-fusion elementwise | flops 8 | bytes 48 | tf_op jit(solution)/shard_map/convert_element_type | solution.py:160
  1.5 0.9 %fusion.5 = bf16[528,128]{1,0:T(8,128)(2,1)S(1)} fusion(bf16[1,8]{1,0:T(2,128)(2,1)S(1)} %convert_element_type.54, bf16[512,128]{1,0:T(8,128)(2,1)} %bitcast.79), kind=kLoop, calls=%fused_computation.20 | loop fusion | flops 405504 | bytes 266256 | tf_op jit(solution)/shard_map/concatenate | solution.py:162
  2.4 0.7 %collective-permute-start = (bf16[528,128]{1,0:T(8,128)(2,1)S(1)}, bf16[528,128]{1,0:T(8,128)(2,1)S(1)}, u32[]{:S(2)}, u32[]{:S(2)}) collective-permute-start(bf16[528,128]{1,0:T(8,128)(2,1)S(1)} %fusion.5), channel_id=1, source_target_pairs={{0,0},{13,1},{10,2},{7,3},{4,4},{1,5},{14,6},{11,7},{8,8},{5,9},{2... | collective-permute-start | bytes 405512 | tf_op jit(solution)/shard_map/ppermute | solution.py:170
  3.1 12.0 %collective-permute-start.1 = (bf16[1,528,128]{2,1,0:T(8,128)(2,1)S(1)}, bf16[1,528,128]{2,1,0:T(8,128)(2,1)S(1)}, u32[]{:S(2)}, u32[]{:S(2)}) collective-permute-start(bf16[1,528,128]{2,1,0:T(8,128)(2,1)S(1)} %bitcast.68), channel_id=1, source_target_pairs={{0,2},{1,3},{2,0},{3,1},{4,6},{5,7},{6,4},{7,5},{8,10},{9,11},{10,... | collective-permute-start | bytes 405512 | tf_op jit(solution)/shard_map/ppermute | solution.py:24
  15.1 3.0 %collective-permute-done.1 = bf16[1,528,128]{2,1,0:T(8,128)(2,1)S(1)} collective-permute-done((bf16[1,528,128]{2,1,0:T(8,128)(2,1)S(1)}, bf16[1,528,128]{2,1,0:T(8,128)(2,1)S(1)}, u32[]{:S(2)}, u32[]{:S(2)}) %collective-permute-start.1) | collective-permute-done | bytes 135200 | tf_op jit(solution)/shard_map/ppermute | solution.py:24
  18.2 0.7 %compare_select_fusion.2 = s32[4]{0:T(128)S(1)} fusion(s32[4]{0:T(128)} %param.11), kind=kLoop, calls=%fused_computation.40 | loop fusion | flops 12 | bytes 32 | tf_op jit(solution)/shard_map/jit(_take)/jit(_where)/select_n | solution.py:205
  18.9 0.8 %collective-permute-done.2 = bf16[2,1,528,128]{3,2,1,0:T(8,128)(2,1)S(1)} collective-permute-done((bf16[2,1,528,128]{3,2,1,0:T(8,128)(2,1)S(1)}, bf16[2,1,528,128]{3,2,1,0:T(8,128)(2,1)S(1)}, u32[]{:S(2)}, u32[]{:S(2)}) %collective-permute-start.2) | collective-permute-done | bytes 270368 | tf_op jit(solution)/shard_map/ppermute | solution.py:24
  19.8 0.4 copy.34
  20.5 0.6 %fusion.10 = (s32[16]{0:T(128)S(1)}, s32[16]{0:T(128)S(1)}, s32[16]{0:T(128)}) fusion(s32[16,2]{1,0:T(8,128)S(1)} %reshape.426), kind=kLoop, calls=%fused_computation.36 | loop fusion | flops 48 | bytes 320 | tf_op jit(solution)/shard_map/jit(_take)/jit(_where)/select_n | solution.py:194
  21.2 0.8 %iota_reduce_fusion = (pred[16]{0:T(512)(128)(4,1)}, s32[16]{0:T(128)}) fusion(s32[16]{0:T(128)S(1)} %get-tuple-element.21.cols_ref), kind=kLoop, calls=%fused_computation.33 | loop fusion | flops 1936 | bytes 144 | tf_op jit(solution)/shard_map/block_pass/reduce | solution.py:93
  21.9 0.9 %copy.35 = bf16[4,512,128]{2,1,0:T(8,128)(2,1)} copy(bf16[4,512,128]{2,0,1:T(4,128)(2,1)S(1)} %slice.66) | data formatting | bytes 1048576 | tf_op jit(solution)/shard_map/slice | solution.py:175
  22.8 6.6 %shard_map.68 = (bf16[28,128,128]{2,1,0:T(8,128)(2,1)}, f32[16,128,128]{2,1,0:T(8,128)}) custom-call(s32[16]{0:T(128)} %get-tuple-element.22.rows_ref, s32[16]{0:T(128)} %copy-done.1, s32[16]{0:T(128)} %get-tuple-element.17.rep_ref, bf16[128,3584]{1,0:T(8,128)(2,1)} %bitcast.65, bf16[128,14336]{1,0:T(8,128)(2,1)} %bitcast.57, bf16[16,128,128]{2,1,0:T(8,128)(2,1)} %bitcast.60), custom_call_target="tpu_custom_call" | custom-call | flops 201326592 | bytes 3538944 | tf_op jit(solution)/shard_map/pallas_call | solution.py:97
  29.4 1.3 %constant_dynamic-slice_fusion.1 = (f32[4,4,2,1,32,128]{5,4,3,2,1,0:T(8,128)S(1)}, f32[4,4,2,1,32,128]{5,4,3,2,1,0:T(8,128)S(1)}) fusion(f32[4,4,2,2,32,128]{5,4,3,2,1,0:T(8,128)} %bitcast.64, s32[]{:T(128)S(6)} %select_n.147, s32[]{:T(128)S(6)} %select_n.148), kind=kLoop, calls=%fused_computation.44 | loop fusion | bytes 2097160 | tf_op jit(solution)/shard_map/jit(dynamic_index_in_dim)/dynamic_slice | solution.py:211
  31.0 0.4 copy-done.2
  31.4 0.5 copy-done
  31.9 0.6 %gather_fusion = bf16[16,128,128]{2,1,0:T(8,128)(2,1)S(1)} fusion(bf16[28,128,128]{2,1,0:T(8,128)(2,1)S(1)} %copy-done, s32[1024]{0:T(1024)S(1)} %pad_clamp_fusion.1), kind=kCustom, calls=%fused_computation | custom fusion | bytes 1048640 | tf_op jit(solution)/shard_map/jit(_take)/gather | solution.py:194
  32.9 2.1 %collective-permute-start.5 = (bf16[4,4,32,128]{3,2,1,0:T(8,128)(2,1)S(1)}, bf16[4,4,32,128]{3,2,1,0:T(8,128)(2,1)S(1)}, u32[]{:S(2)}, u32[]{:S(2)}) collective-permute-start(bf16[4,4,32,128]{3,2,1,0:T(8,128)(2,1)S(1)} %fusion.6), channel_id=1, source_target_pairs={{0,2},{1,3},{2,0},{3,1},{4,6},{5,7},{6,4},{7,5},{8,10},{9,11},{10,... | collective-permute-start | bytes 393224 | tf_op jit(solution)/shard_map/ppermute | solution.py:24
  35.1 1.3 %collective-permute-start.3 = (bf16[262160]{0:T(1024)(128)(2,1)S(1)}, bf16[262160]{0:T(1024)(128)(2,1)S(1)}, u32[]{:S(2)}, u32[]{:S(2)}) collective-permute-start(bf16[262160]{0:T(1024)(128)(2,1)S(1)} %pad_maximum_fusion), channel_id=1, source_target_pairs={{16,0},{17,1},{18,2},{19,3},{20,4},{21,5},{22,6},{23,7},{24,8},{25... | collective-permute-start | bytes 1572968 | tf_op jit(solution)/shard_map/ppermute | solution.py:14
  36.4 2.5 %collective-permute-done.5 = bf16[4,4,32,128]{3,2,1,0:T(8,128)(2,1)S(1)} collective-permute-done((bf16[4,4,32,128]{3,2,1,0:T(8,128)(2,1)S(1)}, bf16[4,4,32,128]{3,2,1,0:T(8,128)(2,1)S(1)}, u32[]{:S(2)}, u32[]{:S(2)}) %collective-permute-start.5) | collective-permute-done | bytes 131104 | tf_op jit(solution)/shard_map/ppermute | solution.py:24
  38.9 4.5 %collective-permute-start.6 = (bf16[4,32,128]{2,1,0:T(8,128)(2,1)S(1)}, bf16[4,32,128]{2,1,0:T(8,128)(2,1)S(1)}, u32[]{:S(2)}, u32[]{:S(2)}) collective-permute-start(bf16[4,32,128]{2,1,0:T(8,128)(2,1)S(1)} %get-tuple-element.27), channel_id=1, source_target_pairs={{0,12},{4,0},{8,4},{12,8},{1,13},{5,1},{9,5},{13,9},{2,14},{6,2},{... | collective-permute-start | bytes 98312 | tf_op jit(solution)/shard_map/ppermute | solution.py:19
  43.4 0.6 %collective-permute-start.8 = (bf16[4,32,128]{2,1,0:T(8,128)(2,1)S(1)}, bf16[4,32,128]{2,1,0:T(8,128)(2,1)S(1)}, u32[]{:S(2)}, u32[]{:S(2)}) collective-permute-start(bf16[4,32,128]{2,1,0:T(8,128)(2,1)S(1)} %get-tuple-element.28), channel_id=1, source_target_pairs={{0,4},{4,8},{8,12},{12,0},{1,5},{5,9},{9,13},{13,1},{2,6},{6,10},{... | collective-permute-start | bytes 98312 | tf_op jit(solution)/shard_map/ppermute | solution.py:19
  44.0 0.9 %collective-permute-done.6 = bf16[4,32,128]{2,1,0:T(8,128)(2,1)S(1)} collective-permute-done((bf16[4,32,128]{2,1,0:T(8,128)(2,1)S(1)}, bf16[4,32,128]{2,1,0:T(8,128)(2,1)S(1)}, u32[]{:S(2)}, u32[]{:S(2)}) %collective-permute-start.6) | collective-permute-done | bytes 32800 | tf_op jit(solution)/shard_map/ppermute | solution.py:19
  45.0 3.2 %collective-permute-done.7 = bf16[4,32,128]{2,1,0:T(8,128)(2,1)S(1)} collective-permute-done((bf16[4,32,128]{2,1,0:T(8,128)(2,1)S(1)}, bf16[4,32,128]{2,1,0:T(8,128)(2,1)S(1)}, u32[]{:S(2)}, u32[]{:S(2)}) %collective-permute-start.7) | collective-permute-done | bytes 32800 | tf_op jit(solution)/shard_map/ppermute | solution.py:19
  48.2 0.9 %collective-permute-done.8 = bf16[4,32,128]{2,1,0:T(8,128)(2,1)S(1)} collective-permute-done((bf16[4,32,128]{2,1,0:T(8,128)(2,1)S(1)}, bf16[4,32,128]{2,1,0:T(8,128)(2,1)S(1)}, u32[]{:S(2)}, u32[]{:S(2)}) %collective-permute-start.8) | collective-permute-done | bytes 32800 | tf_op jit(solution)/shard_map/ppermute | solution.py:19
  49.1 1.8 %collective-permute-start.9 = (f32[4,32,128]{2,1,0:T(8,128)S(1)}, f32[4,32,128]{2,1,0:T(8,128)S(1)}, u32[]{:S(2)}, u32[]{:S(2)}) collective-permute-start(f32[4,32,128]{2,1,0:T(8,128)S(1)} %fusion.9), channel_id=1, source_target_pairs={{0,2},{1,3},{2,0},{3,1},{4,6},{5,7},{6,4},{7,5},{8,10},{9,11},{10,... | collective-permute-start | bytes 196616 | tf_op jit(solution)/shard_map/ppermute | solution.py:24
  51.2 1.1 %scatter_fusion = bf16[28,128,128]{2,1,0:T(8,128)(2,1)S(1)} fusion(bf16[28,128,128]{2,1,0:T(8,128)(2,1)S(1)} %broadcast_in_dim.32, s32[16]{0:T(128)S(1)} %compare_select_fusion.1, bf16[16,128,128]{2,1,0:T(8,128)(2,1)S(1)} %bitcast.61), kind=kCustom, calls=%fused_computation.2 | custom fusion | bytes 1572928 | tf_op jit(solution)/shard_map/scatter | solution.py:199
  52.3 0.6 %copy.36 = bf16[128,28,128]{2,1,0:T(8,128)(2,1)S(1)} copy(bf16[128,28,128]{2,0,1:T(8,128)(2,1)S(1)} %bitcast.56) | data formatting | bytes 1835008 | tf_op jit(solution)/shard_map/transpose | solution.py:202
  52.9 0.5 reshape.424
  53.4 0.6 %gather_fusion.1 = bf16[4,32,3584]{2,1,0:T(8,128)(2,1)S(1)} fusion(bf16[4,32,3584]{2,1,0:T(8,128)(2,1)S(1)} %reshape.424, s32[1024]{0:T(1024)S(1)} %pad_clamp_fusion), kind=kCustom, calls=%fused_computation.1 | custom fusion | bytes 1835024 | tf_op jit(solution)/shard_map/jit(_take)/gather | solution.py:205
  54.2 1.1 %bitcast_select_fusion = bf16[1,4,32,3584]{3,2,1,0:T(8,128)(2,1)} fusion(bf16[4,32,3584]{2,1,0:T(8,128)(2,1)S(1)} %gather_fusion.1, pred[4]{0:T(512)(128)(4,1)S(1)} %compare_and_fusion), kind=kLoop, calls=%fused_computation.3 | loop fusion | flops 458752 | bytes 1835012 | tf_op jit(solution)/shard_map/jit(_take)/select_n | solution.py:205
  55.2 0.2 collective-permute-done.10
  55.5 0.7 %copy.40 = f32[4,4,32,128]{3,2,1,0:T(8,128)} copy(f32[4,4,32,128]{3,2,0,1:T(8,128)S(1)} %bitcast.63) | data formatting | bytes 524288 | tf_op jit(solution)/shard_map/div | solution.py:224
  (42 shorter events, 1.8 us)
Async XLA Ops:
  2.4 0.7 %collective-permute-start = (bf16[528,128]{1,0:T(8,128)(2,1)S(1)}, bf16[528,128]{1,0:T(8,128)(2,1)S(1)}, u32[]{:S(2)}, u32[]{:S(2)}) collective-permute-start(bf16[528,128]{1,0:T(8,128)(2,1)S(1)} %fusion.5), channel_id=1, source_target_pairs={{0,0},{13,1},{10,2},{7,3},{4,4},{1,5},{14,6},{11,7},{8,8},{5,9},{2... | collective-permute-start | bytes 405512 | tf_op jit(solution)/shard_map/ppermute | solution.py:170
  3.1 15.0 %collective-permute-start.1 = (bf16[1,528,128]{2,1,0:T(8,128)(2,1)S(1)}, bf16[1,528,128]{2,1,0:T(8,128)(2,1)S(1)}, u32[]{:S(2)}, u32[]{:S(2)}) collective-permute-start(bf16[1,528,128]{2,1,0:T(8,128)(2,1)S(1)} %bitcast.68), channel_id=1, source_target_pairs={{0,2},{1,3},{2,0},{3,1},{4,6},{5,7},{6,4},{7,5},{8,10},{9,11},{10,... | collective-permute-start | bytes 405512 | tf_op jit(solution)/shard_map/ppermute | solution.py:24
  18.1 1.6 %collective-permute-start.2 = (bf16[2,1,528,128]{3,2,1,0:T(8,128)(2,1)S(1)}, bf16[2,1,528,128]{3,2,1,0:T(8,128)(2,1)S(1)}, u32[]{:S(2)}, u32[]{:S(2)}) collective-permute-start(bf16[2,1,528,128]{3,2,1,0:T(8,128)(2,1)S(1)} %maximum_select_fusion.2), channel_id=1, source_target_pairs={{0,1},{1,0},{2,3},{3,2},{4,5},{5,4},{6,7},{7,6},{8,9},{9,8},{10,11... | collective-permute-start | bytes 811016 | tf_op jit(solution)/shard_map/ppermute | solution.py:24
  21.2 1.7 %copy-start.1 = (s32[16]{0:T(128)}, s32[16]{0:T(128)S(1)}, u32[]{:S(2)}) copy-start(s32[16]{0:T(128)S(1)} %get-tuple-element.21.cols_ref) | copy-start | bytes 196
  29.4 1.6 %copy-start.3 = (s32[4]{0:T(128)S(1)}, s32[4]{0:T(128)}, u32[]{:S(2)}) copy-start(s32[4]{0:T(128)} %param.11) | copy-start | bytes 52
  30.7 0.7 %copy-start.2 = (s32[16]{0:T(128)S(1)}, s32[16]{0:T(128)}, u32[]{:S(2)}) copy-start(s32[16]{0:T(128)} %get-tuple-element.22.rows_ref) | copy-start | bytes 196
  30.7 1.2 %copy-start = (bf16[28,128,128]{2,1,0:T(8,128)(2,1)S(1)}, bf16[28,128,128]{2,1,0:T(8,128)(2,1)}, u32[]{:S(2)}) copy-start(bf16[28,128,128]{2,1,0:T(8,128)(2,1)} %get-tuple-element.18) | copy-start | bytes 2752516
  30.8 2.0 %collective-permute-start.4 = (f32[4,4,2,32,128]{4,3,1,0,2:T(8,128)S(1)}, f32[4,4,2,32,128]{4,3,1,0,2:T(8,128)S(1)}, u32[]{:S(2)}, u32[]{:S(2)}) collective-permute-start(f32[4,4,2,32,128]{4,3,1,0,2:T(8,128)S(1)} %bitcast.73), channel_id=1, source_target_pairs={{0,1},{1,0},{2,3},{3,2},{4,5},{5,4},{6,7},{7,6},{8,9},{9,8},{10,11... | collective-permute-start | bytes 1572872 | tf_op jit(solution)/shard_map/ppermute | solution.py:24
  32.9 5.9 %collective-permute-start.5 = (bf16[4,4,32,128]{3,2,1,0:T(8,128)(2,1)S(1)}, bf16[4,4,32,128]{3,2,1,0:T(8,128)(2,1)S(1)}, u32[]{:S(2)}, u32[]{:S(2)}) collective-permute-start(bf16[4,4,32,128]{3,2,1,0:T(8,128)(2,1)S(1)} %fusion.6), channel_id=1, source_target_pairs={{0,2},{1,3},{2,0},{3,1},{4,6},{5,7},{6,4},{7,5},{8,10},{9,11},{10,... | collective-permute-start | bytes 393224 | tf_op jit(solution)/shard_map/ppermute | solution.py:24
  35.1 15.8 %collective-permute-start.3 = (bf16[262160]{0:T(1024)(128)(2,1)S(1)}, bf16[262160]{0:T(1024)(128)(2,1)S(1)}, u32[]{:S(2)}, u32[]{:S(2)}) collective-permute-start(bf16[262160]{0:T(1024)(128)(2,1)S(1)} %pad_maximum_fusion), channel_id=1, source_target_pairs={{16,0},{17,1},{18,2},{19,3},{20,4},{21,5},{22,6},{23,7},{24,8},{25... | collective-permute-start | bytes 1572968 | tf_op jit(solution)/shard_map/ppermute | solution.py:14
  38.9 6.1 %collective-permute-start.6 = (bf16[4,32,128]{2,1,0:T(8,128)(2,1)S(1)}, bf16[4,32,128]{2,1,0:T(8,128)(2,1)S(1)}, u32[]{:S(2)}, u32[]{:S(2)}) collective-permute-start(bf16[4,32,128]{2,1,0:T(8,128)(2,1)S(1)} %get-tuple-element.27), channel_id=1, source_target_pairs={{0,12},{4,0},{8,4},{12,8},{1,13},{5,1},{9,5},{13,9},{2,14},{6,2},{... | collective-permute-start | bytes 98312 | tf_op jit(solution)/shard_map/ppermute | solution.py:19
  43.4 4.8 %collective-permute-start.7 = (bf16[4,32,128]{2,1,0:T(8,128)(2,1)S(1)}, bf16[4,32,128]{2,1,0:T(8,128)(2,1)S(1)}, u32[]{:S(2)}, u32[]{:S(2)}) collective-permute-start(bf16[4,32,128]{2,1,0:T(8,128)(2,1)S(1)} %get-tuple-element.29), channel_id=1, source_target_pairs={{0,8},{4,12},{8,0},{12,4},{1,9},{5,13},{9,1},{13,5},{2,10},{6,14},... | collective-permute-start | bytes 98312 | tf_op jit(solution)/shard_map/ppermute | solution.py:19
  43.4 5.7 %collective-permute-start.8 = (bf16[4,32,128]{2,1,0:T(8,128)(2,1)S(1)}, bf16[4,32,128]{2,1,0:T(8,128)(2,1)S(1)}, u32[]{:S(2)}, u32[]{:S(2)}) collective-permute-start(bf16[4,32,128]{2,1,0:T(8,128)(2,1)S(1)} %get-tuple-element.28), channel_id=1, source_target_pairs={{0,4},{4,8},{8,12},{12,0},{1,5},{5,9},{9,13},{13,1},{2,6},{6,10},{... | collective-permute-start | bytes 98312 | tf_op jit(solution)/shard_map/ppermute | solution.py:19
  49.1 4.9 %collective-permute-start.9 = (f32[4,32,128]{2,1,0:T(8,128)S(1)}, f32[4,32,128]{2,1,0:T(8,128)S(1)}, u32[]{:S(2)}, u32[]{:S(2)}) collective-permute-start(f32[4,32,128]{2,1,0:T(8,128)S(1)} %fusion.9), channel_id=1, source_target_pairs={{0,2},{1,3},{2,0},{3,1},{4,6},{5,7},{6,4},{7,5},{8,10},{9,11},{10,... | collective-permute-start | bytes 196616 | tf_op jit(solution)/shard_map/ppermute | solution.py:24
  54.1 1.4 %collective-permute-start.10 = (f32[2,4,32,128]{3,2,1,0:T(8,128)S(1)}, f32[2,4,32,128]{3,2,1,0:T(8,128)S(1)}, u32[]{:S(2)}, u32[]{:S(2)}) collective-permute-start(f32[2,4,32,128]{3,2,1,0:T(8,128)S(1)} %maximum_select_fusion.5), channel_id=1, source_target_pairs={{0,1},{1,0},{2,3},{3,2},{4,5},{5,4},{6,7},{7,6},{8,9},{9,8},{10,11... | collective-permute-start | bytes 393224 | tf_op jit(solution)/shard_map/ppermute | solution.py:24

commit v13 on v12

--- a/solution.py
+++ b/solution.py
@@ -1,3 +1,4 @@
+import functools
 import math
 
 import jax
@@ -29,10 +30,11 @@
     return sigmoid_val * (1.0 + pre_act * (1.0 - sigmoid_val))
 
 
-def block_kernel(rows_ref, cols_ref, rep_ref, feat_hbm, hid_hbm, w_ref, ig_ref, pg_ref,
-                 xs, hs, pr, acc, sems):
+def block_kernel(compact, chunk, rows_ref, cols_ref, rep_ref, bit_ref, feat_hbm, hid_hbm, w_ref,
+                 ig_ref, keep_ref, send_ref, xs, hs, pr, acc, pgs, sems):
     block_count = w_ref.shape[0]
     width = w_ref.shape[-1]
+    halves = keep_ref.shape[1]
 
     def block_loop(body):
         def step(b, carry):
@@ -54,7 +56,12 @@
         for cp in copies(b):
             cp.start()
 
-    acc[...] = jnp.zeros(acc.shape, acc.dtype)
+    if compact:
+        @block_loop
+        def _(b):
+            acc[rows_ref[b]] = jnp.zeros(acc.shape[1:], acc.dtype)
+    else:
+        acc[...] = jnp.zeros(acc.shape, acc.dtype)
 
     @block_loop
     def _(b):
@@ -69,6 +76,8 @@
         @pl.when(first != b)
         def _():
             pr[first] = pr[first] + pr[b]
+
+    mine = bit_ref[0]
 
     @block_loop
     def _(b):
@@ -79,34 +88,50 @@
         )
         row = rows_ref[b]
         acc[row] = acc[row] + back
-        pg_ref[b] = lax.dot_general(
+        pgs[b] = lax.dot_general(
             xs[b], act, (((0,), (0,)), ((), ())), preferred_element_type=jnp.float32
         )
-
-    ig_ref[...] = acc[...].astype(ig_ref.dtype)
-
-
-def block_pass(features, hidden_grad, weights, row_ids, col_ids, row_count):
+        for h in range(halves):
+            kept = pl.multiple_of((2 * h + mine) * chunk, chunk)
+            sent = pl.multiple_of((2 * h + 1 - mine) * chunk, chunk)
+            keep_ref[b, h] = pgs[b, pl.ds(kept, chunk), :]
+            send_ref[b, h] = pgs[b, pl.ds(sent, chunk), :]
+
+    if compact:
+        @block_loop
+        def _(b):
+            ig_ref[b] = acc[rows_ref[b]].astype(ig_ref.dtype)
+    else:
+        ig_ref[...] = acc[...].astype(ig_ref.dtype)
+
+
+def block_pass(features, hidden_grad, weights, row_ids, col_ids, row_count, low_bit, parts):
     tokens = features.shape[0]
     block_count, width, _ = weights.shape
+    chunk = width // parts
+    compact = block_count < row_count
     same = col_ids[:, None] == col_ids[None, :]
     first = jnp.argmax(same, axis=1).astype(jnp.int32)
     smem = pl.BlockSpec(memory_space=pltpu.SMEM)
     anyspace = pl.BlockSpec(memory_space=pl.ANY)
     vmem = pl.BlockSpec(memory_space=pltpu.VMEM)
+    ig_rows = block_count if compact else row_count
+    half = jax.ShapeDtypeStruct((block_count, parts // 2, chunk, width), jnp.float32)
     return pl.pallas_call(
-        block_kernel,
+        functools.partial(block_kernel, compact, chunk),
         out_shape=(
-            jax.ShapeDtypeStruct((row_count, tokens, width), jnp.bfloat16),
-            jax.ShapeDtypeStruct((block_count, width, width), jnp.float32),
+            jax.ShapeDtypeStruct((ig_rows, tokens, width), jnp.bfloat16),
+            half,
+            half,
         ),
-        in_specs=[smem, smem, smem, anyspace, anyspace, vmem],
-        out_specs=(vmem, vmem),
+        in_specs=[smem, smem, smem, smem, anyspace, anyspace, vmem],
+        out_specs=(vmem, vmem, vmem),
         scratch_shapes=[
             pltpu.VMEM((block_count, tokens, width), jnp.bfloat16),
             pltpu.VMEM((block_count, tokens, width), jnp.bfloat16),
             pltpu.VMEM((block_count, tokens, width), jnp.float32),
             pltpu.VMEM((row_count, tokens, width), jnp.float32),
+            pltpu.VMEM((block_count, width, width), jnp.float32),
             pltpu.SemaphoreType.DMA((2, block_count)),
         ],
         cost_estimate=pl.CostEstimate(
@@ -115,7 +140,7 @@
             bytes_accessed=block_count * width * (4 * tokens + 6 * width)
             + row_count * tokens * width * 2,
         ),
-    )(row_ids, col_ids, first, features, hidden_grad, weights)
+    )(row_ids, col_ids, first, low_bit, features, hidden_grad, weights)
 
 
 def gather_over(x, axis):
@@ -181,22 +206,25 @@
 
     row_ids = all_indices[:, 0]
     col_ids = all_indices[:, 1]
-    input_grad, partial = block_pass(
+    low_bit = (me_dp & 1).astype(jnp.int32).reshape(1)
+    input_grad, keep, send = block_pass(
         activations[0].reshape(tok_rows, -1),
         out_grad[0].reshape(tok_rows, -1),
         weights,
         row_ids,
         col_ids,
         row_count,
+        low_bit,
+        n_dp,
     )
     block_count = row_ids.shape[0]
     if block_count < row_count:
-        hit = jnp.take(input_grad, row_ids, axis=0)
-        payload = jnp.concatenate([hit.reshape(-1), row_ids.astype(jnp.bfloat16)])
+        payload = jnp.concatenate([input_grad.reshape(-1), row_ids.astype(jnp.bfloat16)])
         payload = passed_along(payload, "section", -1)
-        got_rows = payload[hit.size:].astype(jnp.int32)
-        got = payload[: hit.size].reshape(hit.shape)
-        arrived = jnp.zeros_like(input_grad).at[got_rows].set(got)
+        got_rows = payload[input_grad.size :].astype(jnp.int32)
+        got = payload[: input_grad.size].reshape(input_grad.shape)
+        arrived = jnp.zeros((row_count,) + input_grad.shape[1:], jnp.bfloat16)
+        arrived = arrived.at[got_rows].set(got)
     else:
         arrived = passed_along(input_grad, "section", -1)
     arrived = jnp.transpose(arrived, (1, 0, 2)).reshape(
@@ -204,16 +232,14 @@
     )
     received = jnp.take(arrived, order, axis=0)
 
-    held = partial.reshape((n_fsdp, blocks_dev) + (2,) * dp_bits + (chunk, block_size))
-    for bit in range(dp_bits):
+    held = keep + swapped(send, "dp", 0)
+    held = held.reshape((n_fsdp, blocks_dev) + (2,) * (dp_bits - 1) + (chunk, block_size))
+    for bit in range(1, dp_bits):
         axis_at = 2 + (dp_bits - 1 - bit)
         mine = (me_dp >> bit) & 1
         keep = lax.dynamic_index_in_dim(held, mine, axis_at, keepdims=False)
         send = lax.dynamic_index_in_dim(held, 1 - mine, axis_at, keepdims=False)
-        if bit == 0:
-            held = keep + swapped(send, "dp", bit)
-        else:
-            held = keep + swapped(send.astype(jnp.bfloat16), "dp", bit).astype(jnp.float32)
+        held = keep + swapped(send.astype(jnp.bfloat16), "dp", bit).astype(jnp.float32)
     owned = held[0]
     for k in range(1, n_fsdp):
         owned = owned + shifted(held[k].astype(jnp.bfloat16), "fsdp", -k).astype(jnp.float32)

time: 56.6 us -> 56.2 us (level)
  waiting for transfers between devices: 11.6 us -> 14.2 us
  local copies, waits for them, and re-layouts: 8.52 us -> 6.22 us
    ppermute x6, waiting for transfers between devices: 6.55 us -> 9.13 us  [swapped(): return lax.ppermute(x, axis, [(i, i ^ 1 << bit) for i in range(n)])]
    dynamic_slice x2 -> x0, local copies, waits for them, and re-layouts: 1.34 us -> none  [the longest x1 1.31 us: local(): keep = lax.dynamic_index_in_dim(held, mine, axis_at, keepdims=False)]
    add x1, other arithmetic: 0.08 us -> 1.12 us  [local(): held = keep + swapped(send, 'dp', 0)]
    unnamed x8, local copies, waits for them, and re-layouts: 0.91 us -> 0.02 us
    select_n x3 -> x1, other arithmetic: 0.76 us -> 0.01 us  [local(): arrived = arrived.at[got_rows].set(got)]
    select_n x2, other arithmetic: 1.74 us -> 1.08 us  [local(): received = jnp.take(arrived, order, axis=0)]
    gather x1 -> x0, local copies, waits for them, and re-layouts: 0.65 us -> none  [local(): hit = jnp.take(input_grad, row_ids, axis=0)]
    slice x1 -> x2, local copies, waits for them, and re-layouts: 0.03 us -> 0.67 us  [the longest x1 0.63 us: local(): col_ids = all_indices[:, 1]]
  transfers between devices with their start and end apart: 11 -> 11, of which waited for: 7 -> 8; matrix products, arithmetic and copies ran while one was open for 10% -> 8% of each run, Pallas kernels for 0% -> 0%
where the time goes in v13:
time: 56.2 us; the launch traced here: 55.9 us
  starting transfers between devices  23.3 us (41%)
  waiting for transfers between devices  14.2 us (25%)
  Pallas kernels  6.49 us (12%)
  local copies, waits for them, and re-layouts  6.22 us (11%)
  other arithmetic  4.84 us (9%)
  between operations  0.86 us (2%)
    ppermute x6, starting transfers between devices, swapped(): return lax.ppermute(x, axis, [(i, i ^ 1 << bit) for i in range(n)])  16.2 us
    ppermute x6, waiting for transfers between devices, swapped(): return lax.ppermute(x, axis, [(i, i ^ 1 << bit) for i in range(n)])  9.13 us
    pallas_call x1, Pallas kernels, block_pass(): pl.pallas_call(functools.partial(block_kernel, compact, chunk), out_shape...  6.49 us
    ppermute x3, starting transfers between devices, shifted(): return lax.ppermute(x, axis, [(i, (i + k) % n) for i in range(n)])  5.08 us
    ppermute x3, waiting for transfers between devices, shifted(): return lax.ppermute(x, axis, [(i, (i + k) % n) for i in range(n)])  5.07 us
    ppermute x1, starting transfers between devices, passed_along(): return lax.ppermute(block, axis, route)  1.29 us
    scatter x1, local copies, waits for them, and re-layouts, local(): arrived = arrived.at[got_rows].set(got)  1.14 us
  transfers between devices with their start and end apart: 11, of which 8 were waited for; matrix products, arithmetic and copies ran while one was open for 8% of the time, Pallas kernels for 0%

profile of v13, /device:TPU:0, one launch (start us, length us, event | category | flops | bytes accessed | tf_op | source)
XLA Modules:
  0.0 55.9 jit_solution(11300012991575251940)
XLA Ops:
  0.6 0.7 %convert_element_type.53 = bf16[1,4,2]{1,2,0:T(2,128)(2,1)S(1)} convert(s32[1,4,2]{1,2,0:T(2,128)} %param.10) | non-fusion elementwise | flops 8 | bytes 48 | tf_op jit(solution)/shard_map/convert_element_type | solution.py:185
  1.5 0.9 %fusion.4 = bf16[528,128]{1,0:T(8,128)(2,1)S(1)} fusion(bf16[1,8]{1,0:T(2,128)(2,1)S(1)} %convert_element_type.54, bf16[512,128]{1,0:T(8,128)(2,1)} %bitcast.87), kind=kLoop, calls=%fused_computation.15 | loop fusion | flops 405504 | bytes 266256 | tf_op jit(solution)/shard_map/concatenate | solution.py:187
  2.4 0.7 %collective-permute-start = (bf16[528,128]{1,0:T(8,128)(2,1)S(1)}, bf16[528,128]{1,0:T(8,128)(2,1)S(1)}, u32[]{:S(2)}, u32[]{:S(2)}) collective-permute-start(bf16[528,128]{1,0:T(8,128)(2,1)S(1)} %fusion.4), channel_id=1, source_target_pairs={{0,0},{13,1},{10,2},{7,3},{4,4},{1,5},{14,6},{11,7},{8,8},{5,9},{2... | collective-permute-start | bytes 405512 | tf_op jit(solution)/shard_map/ppermute | solution.py:195
  3.1 12.0 %collective-permute-start.1 = (bf16[1,528,128]{2,1,0:T(8,128)(2,1)S(1)}, bf16[1,528,128]{2,1,0:T(8,128)(2,1)S(1)}, u32[]{:S(2)}, u32[]{:S(2)}) collective-permute-start(bf16[1,528,128]{2,1,0:T(8,128)(2,1)S(1)} %bitcast.76), channel_id=1, source_target_pairs={{0,2},{1,3},{2,0},{3,1},{4,6},{5,7},{6,4},{7,5},{8,10},{9,11},{10,... | collective-permute-start | bytes 405512 | tf_op jit(solution)/shard_map/ppermute | solution.py:25
  15.1 3.0 %collective-permute-done.1 = bf16[1,528,128]{2,1,0:T(8,128)(2,1)S(1)} collective-permute-done((bf16[1,528,128]{2,1,0:T(8,128)(2,1)S(1)}, bf16[1,528,128]{2,1,0:T(8,128)(2,1)S(1)}, u32[]{:S(2)}, u32[]{:S(2)}) %collective-permute-start.1) | collective-permute-done | bytes 135200 | tf_op jit(solution)/shard_map/ppermute | solution.py:25
  18.2 1.5 %collective-permute-done.2 = bf16[2,1,528,128]{3,2,1,0:T(8,128)(2,1)S(1)} collective-permute-done((bf16[2,1,528,128]{3,2,1,0:T(8,128)(2,1)S(1)}, bf16[2,1,528,128]{3,2,1,0:T(8,128)(2,1)S(1)}, u32[]{:S(2)}, u32[]{:S(2)}) %collective-permute-start.2) | collective-permute-done | bytes 270368 | tf_op jit(solution)/shard_map/ppermute | solution.py:25
  19.8 0.4 copy.25
  20.3 0.2 slice.64
  20.5 0.6 %slice_reduce_fusion = (s32[16]{0:T(128)S(1)}, s32[16]{0:T(128)}) fusion(s32[16,2]{1,0:T(8,128)S(1)} %reshape.425), kind=kLoop, calls=%fused_computation.28 | loop fusion | bytes 256 | tf_op jit(solution)/shard_map/slice | solution.py:208
  21.2 0.7 %iota_reduce_fusion = (pred[16]{0:T(512)(128)(4,1)}, s32[16]{0:T(128)}) fusion(s32[16]{0:T(128)S(1)} %get-tuple-element.22.cols_ref), kind=kLoop, calls=%fused_computation.30 | loop fusion | flops 1936 | bytes 144 | tf_op jit(solution)/shard_map/block_pass/reduce | solution.py:114
  21.9 0.9 %copy.26 = bf16[4,512,128]{2,1,0:T(8,128)(2,1)} copy(bf16[4,512,128]{2,0,1:T(4,128)(2,1)S(1)} %slice.64) | data formatting | bytes 1048576 | tf_op jit(solution)/shard_map/slice | solution.py:200
  22.7 6.5 %shard_map.68 = (bf16[16,128,128]{2,1,0:T(8,128)(2,1)}, f32[16,2,32,128]{3,2,1,0:T(8,128)}, f32[16,2,32,128]{3,2,1,0:T(8,128)}) custom-call(s32[16]{0:T(128)} %get-tuple-element.23.rows_ref, s32[16]{0:T(128)} %copy-done.1, s32[16]{0:T(128)} %get-tuple-element.18.rep_ref, s32[1]{0:T(128)} %bitcast.8.bit_ref, bf16[128,3584]{1,0:T(8,128)(2,1)} %bitcast.73, ...), custom_call_target="tpu_custom_call" | custom-call | flops 201326592 | bytes 3538944 | tf_op jit(solution)/shard_map/pallas_call | solution.py:120
  29.3 0.2 collective-permute-start.4
  29.5 1.9 %collective-permute-done.4 = f32[16,2,32,128]{3,2,1,0:T(8,128)S(1)} collective-permute-done((f32[16,2,32,128]{3,2,1,0:T(8,128)}, f32[16,2,32,128]{3,2,1,0:T(8,128)S(1)}, u32[]{:S(2)}, u32[]{:S(2)}) %collective-permute-start.4) | collective-permute-done | bytes 524320 | tf_op jit(solution)/shard_map/ppermute | solution.py:25
  31.4 1.1 %add.36 = f32[16,2,32,128]{3,2,1,0:T(8,128)S(1)} add(f32[16,2,32,128]{3,2,1,0:T(8,128)} %get-tuple-element.20, f32[16,2,32,128]{3,2,1,0:T(8,128)S(1)} %collective-permute-done.4) | non-fusion elementwise | flops 131072 | bytes 1572864 | tf_op jit(solution)/shard_map/add | solution.py:235
  32.6 2.1 %collective-permute-start.5 = (bf16[4,4,32,128]{3,2,1,0:T(8,128)(2,1)S(1)}, bf16[4,4,32,128]{3,2,1,0:T(8,128)(2,1)S(1)}, u32[]{:S(2)}, u32[]{:S(2)}) collective-permute-start(bf16[4,4,32,128]{3,2,1,0:T(8,128)(2,1)S(1)} %fusion.5), channel_id=1, source_target_pairs={{0,2},{1,3},{2,0},{3,1},{4,6},{5,7},{6,4},{7,5},{8,10},{9,11},{10,... | collective-permute-start | bytes 393224 | tf_op jit(solution)/shard_map/ppermute | solution.py:25
  34.7 1.3 %collective-permute-start.3 = (bf16[262160]{0:T(1024)(128)(2,1)S(1)}, bf16[262160]{0:T(1024)(128)(2,1)S(1)}, u32[]{:S(2)}, u32[]{:S(2)}) collective-permute-start(bf16[262160]{0:T(1024)(128)(2,1)S(1)} %pad_maximum_fusion), channel_id=1, source_target_pairs={{16,0},{17,1},{18,2},{19,3},{20,4},{21,5},{22,6},{23,7},{24,8},{25... | collective-permute-start | bytes 1572968 | tf_op jit(solution)/shard_map/ppermute | solution.py:15
  36.0 2.5 %collective-permute-done.5 = bf16[4,4,32,128]{3,2,1,0:T(8,128)(2,1)S(1)} collective-permute-done((bf16[4,4,32,128]{3,2,1,0:T(8,128)(2,1)S(1)}, bf16[4,4,32,128]{3,2,1,0:T(8,128)(2,1)S(1)}, u32[]{:S(2)}, u32[]{:S(2)}) %collective-permute-start.5) | collective-permute-done | bytes 131104 | tf_op jit(solution)/shard_map/ppermute | solution.py:25
  38.6 4.4 %collective-permute-start.6 = (bf16[4,32,128]{2,1,0:T(8,128)(2,1)S(1)}, bf16[4,32,128]{2,1,0:T(8,128)(2,1)S(1)}, u32[]{:S(2)}, u32[]{:S(2)}) collective-permute-start(bf16[4,32,128]{2,1,0:T(8,128)(2,1)S(1)} %get-tuple-element.26), channel_id=1, source_target_pairs={{0,12},{4,0},{8,4},{12,8},{1,13},{5,1},{9,5},{13,9},{2,14},{6,2},{... | collective-permute-start | bytes 98312 | tf_op jit(solution)/shard_map/ppermute | solution.py:20
  43.0 0.6 %collective-permute-start.8 = (bf16[4,32,128]{2,1,0:T(8,128)(2,1)S(1)}, bf16[4,32,128]{2,1,0:T(8,128)(2,1)S(1)}, u32[]{:S(2)}, u32[]{:S(2)}) collective-permute-start(bf16[4,32,128]{2,1,0:T(8,128)(2,1)S(1)} %get-tuple-element.27), channel_id=1, source_target_pairs={{0,4},{4,8},{8,12},{12,0},{1,5},{5,9},{9,13},{13,1},{2,6},{6,10},{... | collective-permute-start | bytes 98312 | tf_op jit(solution)/shard_map/ppermute | solution.py:20
  43.7 0.9 %collective-permute-done.6 = bf16[4,32,128]{2,1,0:T(8,128)(2,1)S(1)} collective-permute-done((bf16[4,32,128]{2,1,0:T(8,128)(2,1)S(1)}, bf16[4,32,128]{2,1,0:T(8,128)(2,1)S(1)}, u32[]{:S(2)}, u32[]{:S(2)}) %collective-permute-start.6) | collective-permute-done | bytes 32800 | tf_op jit(solution)/shard_map/ppermute | solution.py:20
  44.6 3.2 %collective-permute-done.7 = bf16[4,32,128]{2,1,0:T(8,128)(2,1)S(1)} collective-permute-done((bf16[4,32,128]{2,1,0:T(8,128)(2,1)S(1)}, bf16[4,32,128]{2,1,0:T(8,128)(2,1)S(1)}, u32[]{:S(2)}, u32[]{:S(2)}) %collective-permute-start.7) | collective-permute-done | bytes 32800 | tf_op jit(solution)/shard_map/ppermute | solution.py:20
  47.8 0.9 %collective-permute-done.8 = bf16[4,32,128]{2,1,0:T(8,128)(2,1)S(1)} collective-permute-done((bf16[4,32,128]{2,1,0:T(8,128)(2,1)S(1)}, bf16[4,32,128]{2,1,0:T(8,128)(2,1)S(1)}, u32[]{:S(2)}, u32[]{:S(2)}) %collective-permute-start.8) | collective-permute-done | bytes 32800 | tf_op jit(solution)/shard_map/ppermute | solution.py:20
  48.7 1.8 %collective-permute-start.9 = (f32[4,32,128]{2,1,0:T(8,128)S(1)}, f32[4,32,128]{2,1,0:T(8,128)S(1)}, u32[]{:S(2)}, u32[]{:S(2)}) collective-permute-start(f32[4,32,128]{2,1,0:T(8,128)S(1)} %fusion.9), channel_id=1, source_target_pairs={{0,2},{1,3},{2,0},{3,1},{4,6},{5,7},{6,4},{7,5},{8,10},{9,11},{10,... | collective-permute-start | bytes 196616 | tf_op jit(solution)/shard_map/ppermute | solution.py:25
  50.6 0.2 broadcast_in_dim.22
  50.8 1.1 %scatter_fusion = bf16[28,128,128]{2,1,0:T(8,128)(2,1)S(1)} fusion(bf16[28,128,128]{2,1,0:T(8,128)(2,1)S(1)} %broadcast_in_dim.22, s32[16]{0:T(128)S(1)} %compare_select_fusion, bf16[16,128,128]{2,1,0:T(8,128)(2,1)S(1)} %bitcast.69), kind=kCustom, calls=%fused_computation.1 | custom fusion | bytes 1572928 | tf_op jit(solution)/shard_map/scatter | solution.py:227
  52.0 0.6 %copy.27 = bf16[128,28,128]{2,1,0:T(8,128)(2,1)S(1)} copy(bf16[128,28,128]{2,0,1:T(8,128)(2,1)S(1)} %bitcast.64) | data formatting | bytes 1835008 | tf_op jit(solution)/shard_map/transpose | solution.py:230
  52.6 0.5 reshape.423
  53.1 0.6 %gather_fusion = bf16[4,32,3584]{2,1,0:T(8,128)(2,1)S(1)} fusion(bf16[4,32,3584]{2,1,0:T(8,128)(2,1)S(1)} %reshape.423, s32[1024]{0:T(1024)S(1)} %pad_clamp_fusion), kind=kCustom, calls=%fused_computation | custom fusion | bytes 1835024 | tf_op jit(solution)/shard_map/jit(_take)/gather | solution.py:233
  53.8 1.1 %bitcast_select_fusion = bf16[1,4,32,3584]{3,2,1,0:T(8,128)(2,1)} fusion(bf16[4,32,3584]{2,1,0:T(8,128)(2,1)S(1)} %gather_fusion, pred[4]{0:T(512)(128)(4,1)S(1)} %compare_and_fusion), kind=kLoop, calls=%fused_computation.2 | loop fusion | flops 458752 | bytes 1835012 | tf_op jit(solution)/shard_map/jit(_take)/select_n | solution.py:233
  54.9 0.2 collective-permute-done.10
  55.2 0.7 %copy.31 = f32[4,4,32,128]{3,2,1,0:T(8,128)} copy(f32[4,4,32,128]{3,2,0,1:T(8,128)S(1)} %bitcast.72) | data formatting | bytes 524288 | tf_op jit(solution)/shard_map/div | solution.py:250
  (35 shorter events, 0.8 us)
Async XLA Ops:
  2.4 0.7 %collective-permute-start = (bf16[528,128]{1,0:T(8,128)(2,1)S(1)}, bf16[528,128]{1,0:T(8,128)(2,1)S(1)}, u32[]{:S(2)}, u32[]{:S(2)}) collective-permute-start(bf16[528,128]{1,0:T(8,128)(2,1)S(1)} %fusion.4), channel_id=1, source_target_pairs={{0,0},{13,1},{10,2},{7,3},{4,4},{1,5},{14,6},{11,7},{8,8},{5,9},{2... | collective-permute-start | bytes 405512 | tf_op jit(solution)/shard_map/ppermute | solution.py:195
  3.1 15.0 %collective-permute-start.1 = (bf16[1,528,128]{2,1,0:T(8,128)(2,1)S(1)}, bf16[1,528,128]{2,1,0:T(8,128)(2,1)S(1)}, u32[]{:S(2)}, u32[]{:S(2)}) collective-permute-start(bf16[1,528,128]{2,1,0:T(8,128)(2,1)S(1)} %bitcast.76), channel_id=1, source_target_pairs={{0,2},{1,3},{2,0},{3,1},{4,6},{5,7},{6,4},{7,5},{8,10},{9,11},{10,... | collective-permute-start | bytes 405512 | tf_op jit(solution)/shard_map/ppermute | solution.py:25
  18.1 1.6 %collective-permute-start.2 = (bf16[2,1,528,128]{3,2,1,0:T(8,128)(2,1)S(1)}, bf16[2,1,528,128]{3,2,1,0:T(8,128)(2,1)S(1)}, u32[]{:S(2)}, u32[]{:S(2)}) collective-permute-start(bf16[2,1,528,128]{3,2,1,0:T(8,128)(2,1)S(1)} %maximum_select_fusion.2), channel_id=1, source_target_pairs={{0,1},{1,0},{2,3},{3,2},{4,5},{5,4},{6,7},{7,6},{8,9},{9,8},{10,11... | collective-permute-start | bytes 811016 | tf_op jit(solution)/shard_map/ppermute | solution.py:25
  21.2 1.6 %copy-start.1 = (s32[16]{0:T(128)}, s32[16]{0:T(128)S(1)}, u32[]{:S(2)}) copy-start(s32[16]{0:T(128)S(1)} %get-tuple-element.22.cols_ref) | copy-start | bytes 196
  22.7 6.7 %copy-start.3 = (s32[4]{0:T(128)S(1)}, s32[4]{0:T(128)}, u32[]{:S(2)}) copy-start(s32[4]{0:T(128)} %param.11) | copy-start | bytes 52
  22.7 6.7 %copy-start.2 = (s32[16]{0:T(128)S(1)}, s32[16]{0:T(128)}, u32[]{:S(2)}) copy-start(s32[16]{0:T(128)} %get-tuple-element.23.rows_ref) | copy-start | bytes 196
  29.3 5.4 %copy-start = (bf16[16,128,128]{2,1,0:T(8,128)(2,1)S(1)}, bf16[16,128,128]{2,1,0:T(8,128)(2,1)}, u32[]{:S(2)}) copy-start(bf16[16,128,128]{2,1,0:T(8,128)(2,1)} %get-tuple-element.19) | copy-start | bytes 1572868
  29.3 2.2 %collective-permute-start.4 = (f32[16,2,32,128]{3,2,1,0:T(8,128)}, f32[16,2,32,128]{3,2,1,0:T(8,128)S(1)}, u32[]{:S(2)}, u32[]{:S(2)}) collective-permute-start(f32[16,2,32,128]{3,2,1,0:T(8,128)} %get-tuple-element.21), channel_id=1, source_target_pairs={{0,1},{1,0},{2,3},{3,2},{4,5},{5,4},{6,7},{7,6},{8,9},{9,8},{10,11... | collective-permute-start | bytes 1572872 | tf_op jit(solution)/shard_map/ppermute | solution.py:25
  32.6 5.9 %collective-permute-start.5 = (bf16[4,4,32,128]{3,2,1,0:T(8,128)(2,1)S(1)}, bf16[4,4,32,128]{3,2,1,0:T(8,128)(2,1)S(1)}, u32[]{:S(2)}, u32[]{:S(2)}) collective-permute-start(bf16[4,4,32,128]{3,2,1,0:T(8,128)(2,1)S(1)} %fusion.5), channel_id=1, source_target_pairs={{0,2},{1,3},{2,0},{3,1},{4,6},{5,7},{6,4},{7,5},{8,10},{9,11},{10,... | collective-permute-start | bytes 393224 | tf_op jit(solution)/shard_map/ppermute | solution.py:25
  34.7 15.8 %collective-permute-start.3 = (bf16[262160]{0:T(1024)(128)(2,1)S(1)}, bf16[262160]{0:T(1024)(128)(2,1)S(1)}, u32[]{:S(2)}, u32[]{:S(2)}) collective-permute-start(bf16[262160]{0:T(1024)(128)(2,1)S(1)} %pad_maximum_fusion), channel_id=1, source_target_pairs={{16,0},{17,1},{18,2},{19,3},{20,4},{21,5},{22,6},{23,7},{24,8},{25... | collective-permute-start | bytes 1572968 | tf_op jit(solution)/shard_map/ppermute | solution.py:15
  38.6 6.0 %collective-permute-start.6 = (bf16[4,32,128]{2,1,0:T(8,128)(2,1)S(1)}, bf16[4,32,128]{2,1,0:T(8,128)(2,1)S(1)}, u32[]{:S(2)}, u32[]{:S(2)}) collective-permute-start(bf16[4,32,128]{2,1,0:T(8,128)(2,1)S(1)} %get-tuple-element.26), channel_id=1, source_target_pairs={{0,12},{4,0},{8,4},{12,8},{1,13},{5,1},{9,5},{13,9},{2,14},{6,2},{... | collective-permute-start | bytes 98312 | tf_op jit(solution)/shard_map/ppermute | solution.py:20
  43.0 4.8 %collective-permute-start.7 = (bf16[4,32,128]{2,1,0:T(8,128)(2,1)S(1)}, bf16[4,32,128]{2,1,0:T(8,128)(2,1)S(1)}, u32[]{:S(2)}, u32[]{:S(2)}) collective-permute-start(bf16[4,32,128]{2,1,0:T(8,128)(2,1)S(1)} %get-tuple-element.28), channel_id=1, source_target_pairs={{0,8},{4,12},{8,0},{12,4},{1,9},{5,13},{9,1},{13,5},{2,10},{6,14},... | collective-permute-start | bytes 98312 | tf_op jit(solution)/shard_map/ppermute | solution.py:20
  43.0 5.7 %collective-permute-start.8 = (bf16[4,32,128]{2,1,0:T(8,128)(2,1)S(1)}, bf16[4,32,128]{2,1,0:T(8,128)(2,1)S(1)}, u32[]{:S(2)}, u32[]{:S(2)}) collective-permute-start(bf16[4,32,128]{2,1,0:T(8,128)(2,1)S(1)} %get-tuple-element.27), channel_id=1, source_target_pairs={{0,4},{4,8},{8,12},{12,0},{1,5},{5,9},{9,13},{13,1},{2,6},{6,10},{... | collective-permute-start | bytes 98312 | tf_op jit(solution)/shard_map/ppermute | solution.py:20
  48.7 4.9 %collective-permute-start.9 = (f32[4,32,128]{2,1,0:T(8,128)S(1)}, f32[4,32,128]{2,1,0:T(8,128)S(1)}, u32[]{:S(2)}, u32[]{:S(2)}) collective-permute-start(f32[4,32,128]{2,1,0:T(8,128)S(1)} %fusion.9), channel_id=1, source_target_pairs={{0,2},{1,3},{2,0},{3,1},{4,6},{5,7},{6,4},{7,5},{8,10},{9,11},{10,... | collective-permute-start | bytes 196616 | tf_op jit(solution)/shard_map/ppermute | solution.py:25
  53.7 1.4 %collective-permute-start.10 = (f32[2,4,32,128]{3,2,1,0:T(8,128)S(1)}, f32[2,4,32,128]{3,2,1,0:T(8,128)S(1)}, u32[]{:S(2)}, u32[]{:S(2)}) collective-permute-start(f32[2,4,32,128]{3,2,1,0:T(8,128)S(1)} %maximum_select_fusion.4), channel_id=1, source_target_pairs={{0,1},{1,0},{2,3},{3,2},{4,5},{5,4},{6,7},{7,6},{8,9},{9,8},{10,11... | collective-permute-start | bytes 393224 | tf_op jit(solution)/shard_map/ppermute | solution.py:25

commit v14 on v13

--- a/solution.py
+++ b/solution.py
@@ -143,6 +143,47 @@
     )(row_ids, col_ids, first, low_bit, features, hidden_grad, weights)
 
 
+def unpack_kernel(rows_ref, order_ref, got_ref, out_ref, where_ref):
+    block_count, tok_rows, width = got_ref.shape
+    micro_count, tok_mb, _ = out_ref.shape
+    row_count = out_ref.shape[2] // width
+    for r in range(row_count):
+        where_ref[r] = -1
+    for b in range(block_count):
+        where_ref[rows_ref[b]] = b
+    for r in range(row_count):
+        src = where_ref[r]
+        for i in range(micro_count):
+            start = pl.multiple_of(order_ref[i] * tok_mb, tok_mb)
+
+            @pl.when(src >= 0)
+            def _():
+                out_ref[i, :, r * width : (r + 1) * width] = got_ref[
+                    src, pl.ds(start, tok_mb), :
+                ]
+
+            @pl.when(src < 0)
+            def _():
+                out_ref[i, :, r * width : (r + 1) * width] = jnp.zeros(
+                    (tok_mb, width), out_ref.dtype
+                )
+
+
+def unpack_rows(got_rows, order, got, micro_count, row_count):
+    block_count, tok_rows, width = got.shape
+    smem = pl.BlockSpec(memory_space=pltpu.SMEM)
+    vmem = pl.BlockSpec(memory_space=pltpu.VMEM)
+    return pl.pallas_call(
+        unpack_kernel,
+        out_shape=jax.ShapeDtypeStruct(
+            (micro_count, tok_rows // micro_count, row_count * width), got.dtype
+        ),
+        in_specs=[smem, smem, vmem],
+        out_specs=vmem,
+        scratch_shapes=[pltpu.SMEM((row_count,), jnp.int32)],
+    )(got_rows, order, got)
+
+
 def gather_over(x, axis):
     n = lax.axis_size(axis)
     return jnp.stack([x] + [shifted(x, axis, k) for k in range(1, n)])
@@ -223,14 +264,13 @@
         payload = passed_along(payload, "section", -1)
         got_rows = payload[input_grad.size :].astype(jnp.int32)
         got = payload[: input_grad.size].reshape(input_grad.shape)
-        arrived = jnp.zeros((row_count,) + input_grad.shape[1:], jnp.bfloat16)
-        arrived = arrived.at[got_rows].set(got)
+        received = unpack_rows(got_rows, order, got, micro_count, row_count)
     else:
         arrived = passed_along(input_grad, "section", -1)
-    arrived = jnp.transpose(arrived, (1, 0, 2)).reshape(
-        micro_count, activations.shape[2], activations.shape[3]
-    )
-    received = jnp.take(arrived, order, axis=0)
+        arrived = jnp.transpose(arrived, (1, 0, 2)).reshape(
+            micro_count, activations.shape[2], activations.shape[3]
+        )
+        received = jnp.take(arrived, order, axis=0)
 
     held = keep + swapped(send, "dp", 0)
     held = held.reshape((n_fsdp, blocks_dev) + (2,) * (dp_bits - 1) + (chunk, block_size))

time: 56.2 us -> 58.7 us (1.044)
  Pallas kernels: 6.49 us -> 9.51 us
  waiting for transfers between devices: 14.2 us -> 16.5 us
  local copies, waits for them, and re-layouts: 6.22 us -> 3.95 us
    pallas_call x0 -> x1, Pallas kernels: none -> 3.03 us  [unpack_rows(): pl.pallas_call(unpack_kernel, out_shape=jax.ShapeDtypeStruct((micro_count...]
    ppermute x6, waiting for transfers between devices: 9.13 us -> 11.4 us  [swapped(): return lax.ppermute(x, axis, [(i, i ^ 1 << bit) for i in range(n)])]
    scatter x1 -> x0, local copies, waits for them, and re-layouts: 1.14 us -> none  [local(): arrived = arrived.at[got_rows].set(got)]
    select_n x3 -> x0, other arithmetic: 1.08 us -> none  [the longest x2 1.08 us: local(): received = jnp.take(arrived, order, axis=0)]
    slice x1, local copies, waits for them, and re-layouts: 0.03 us -> 0.81 us  [local(): got = payload[:input_grad.size].reshape(input_grad.shape)]
    transpose x1 -> x0, local copies, waits for them, and re-layouts: 0.61 us -> none  [local(): jnp.transpose(arrived, (1, 0, 2))]
    gather x1 -> x0, local copies, waits for them, and re-layouts: 0.61 us -> none  [local(): received = jnp.take(arrived, order, axis=0)]
  transfers between devices with their start and end apart: 11 -> 11, of which waited for: 8 -> 8; matrix products, arithmetic and copies ran while one was open for 8% -> 3% of each run, Pallas kernels for 0% -> 5%
where the time goes in v14:
time: 58.7 us; the launch traced here: 58.3 us
  starting transfers between devices  23.3 us (40%)
  waiting for transfers between devices  16.5 us (28%)
  Pallas kernels  9.51 us (16%)
  other arithmetic  4.29 us (7%)
  local copies, waits for them, and re-layouts  3.95 us (7%)
  between operations  0.81 us (1%)
    ppermute x6, starting transfers between devices, swapped(): return lax.ppermute(x, axis, [(i, i ^ 1 << bit) for i in range(n)])  16.2 us
    ppermute x6, waiting for transfers between devices, swapped(): return lax.ppermute(x, axis, [(i, i ^ 1 << bit) for i in range(n)])  11.4 us
    pallas_call x1, Pallas kernels, block_pass(): pl.pallas_call(functools.partial(block_kernel, compact, chunk), out_shape...  6.48 us
    ppermute x3, starting transfers between devices, shifted(): return lax.ppermute(x, axis, [(i, (i + k) % n) for i in range(n)])  5.08 us
    ppermute x3, waiting for transfers between devices, shifted(): return lax.ppermute(x, axis, [(i, (i + k) % n) for i in range(n)])  5.07 us
    pallas_call x1, Pallas kernels, unpack_rows(): pl.pallas_call(unpack_kernel, out_shape=jax.ShapeDtypeStruct((micro_count...  3.03 us
    ppermute x1, starting transfers between devices, passed_along(): return lax.ppermute(block, axis, route)  1.29 us
  transfers between devices with their start and end apart: 11, of which 8 were waited for; matrix products, arithmetic and copies ran while one was open for 3% of the time, Pallas kernels for 5%

profile of v14, /device:TPU:0, one launch (start us, length us, event | category | flops | bytes accessed | tf_op | source)
XLA Modules:
  0.0 58.3 jit_solution(16668163640091154975)
XLA Ops:
  0.6 0.7 %convert_element_type.53 = bf16[1,4,2]{1,2,0:T(2,128)(2,1)S(1)} convert(s32[1,4,2]{1,2,0:T(2,128)} %param.10) | non-fusion elementwise | flops 8 | bytes 48 | tf_op jit(solution)/shard_map/convert_element_type | solution.py:226
  1.3 0.1 copy.23
  1.4 0.1 convert_element_type.54
  1.5 0.9 %fusion.4 = bf16[528,128]{1,0:T(8,128)(2,1)S(1)} fusion(bf16[1,8]{1,0:T(2,128)(2,1)S(1)} %convert_element_type.54, bf16[512,128]{1,0:T(8,128)(2,1)} %bitcast.85), kind=kLoop, calls=%fused_computation.12 | loop fusion | flops 405504 | bytes 266256 | tf_op jit(solution)/shard_map/concatenate | solution.py:228
  2.4 0.7 %collective-permute-start = (bf16[528,128]{1,0:T(8,128)(2,1)S(1)}, bf16[528,128]{1,0:T(8,128)(2,1)S(1)}, u32[]{:S(2)}, u32[]{:S(2)}) collective-permute-start(bf16[528,128]{1,0:T(8,128)(2,1)S(1)} %fusion.4), channel_id=1, source_target_pairs={{0,0},{13,1},{10,2},{7,3},{4,4},{1,5},{14,6},{11,7},{8,8},{5,9},{2... | collective-permute-start | bytes 405512 | tf_op jit(solution)/shard_map/ppermute | solution.py:236
  3.1 12.0 %collective-permute-start.1 = (bf16[1,528,128]{2,1,0:T(8,128)(2,1)S(1)}, bf16[1,528,128]{2,1,0:T(8,128)(2,1)S(1)}, u32[]{:S(2)}, u32[]{:S(2)}) collective-permute-start(bf16[1,528,128]{2,1,0:T(8,128)(2,1)S(1)} %bitcast.74), channel_id=1, source_target_pairs={{0,2},{1,3},{2,0},{3,1},{4,6},{5,7},{6,4},{7,5},{8,10},{9,11},{10,... | collective-permute-start | bytes 405512 | tf_op jit(solution)/shard_map/ppermute | solution.py:25
  15.1 3.0 %collective-permute-done.1 = bf16[1,528,128]{2,1,0:T(8,128)(2,1)S(1)} collective-permute-done((bf16[1,528,128]{2,1,0:T(8,128)(2,1)S(1)}, bf16[1,528,128]{2,1,0:T(8,128)(2,1)S(1)}, u32[]{:S(2)}, u32[]{:S(2)}) %collective-permute-start.1) | collective-permute-done | bytes 135200 | tf_op jit(solution)/shard_map/ppermute | solution.py:25
  18.2 1.5 %collective-permute-done.2 = bf16[2,1,528,128]{3,2,1,0:T(8,128)(2,1)S(1)} collective-permute-done((bf16[2,1,528,128]{3,2,1,0:T(8,128)(2,1)S(1)}, bf16[2,1,528,128]{3,2,1,0:T(8,128)(2,1)S(1)}, u32[]{:S(2)}, u32[]{:S(2)}) %collective-permute-start.2) | collective-permute-done | bytes 270368 | tf_op jit(solution)/shard_map/ppermute | solution.py:25
  19.7 0.1 fusion
  19.8 0.4 copy.24
  20.3 0.2 slice.62
  20.5 0.6 %slice_reduce_fusion = (s32[16]{0:T(128)S(1)}, s32[16]{0:T(128)}) fusion(s32[16,2]{1,0:T(8,128)S(1)} %reshape.409), kind=kLoop, calls=%fused_computation.25 | loop fusion | bytes 256 | tf_op jit(solution)/shard_map/slice | solution.py:249
  21.2 0.8 %iota_reduce_fusion = (pred[16]{0:T(512)(128)(4,1)}, s32[16]{0:T(128)}) fusion(s32[16]{0:T(128)S(1)} %get-tuple-element.22.cols_ref), kind=kLoop, calls=%fused_computation.27 | loop fusion | flops 1936 | bytes 144 | tf_op jit(solution)/shard_map/block_pass/reduce | solution.py:114
  21.9 0.9 %copy.25 = bf16[4,512,128]{2,1,0:T(8,128)(2,1)} copy(bf16[4,512,128]{2,0,1:T(4,128)(2,1)S(1)} %slice.62) | data formatting | bytes 1048576 | tf_op jit(solution)/shard_map/slice | solution.py:241
  22.8 6.5 %shard_map.68 = (bf16[16,128,128]{2,1,0:T(8,128)(2,1)}, f32[16,2,32,128]{3,2,1,0:T(8,128)}, f32[16,2,32,128]{3,2,1,0:T(8,128)}) custom-call(s32[16]{0:T(128)} %get-tuple-element.23.rows_ref, s32[16]{0:T(128)} %copy-done.1, s32[16]{0:T(128)} %get-tuple-element.18.rep_ref, s32[1]{0:T(128)} %bitcast.8.bit_ref, bf16[128,3584]{1,0:T(8,128)(2,1)} %bitcast.70, ...), custom_call_target="tpu_custom_call" | custom-call | flops 201326592 | bytes 3538944 | tf_op jit(solution)/shard_map/pallas_call | solution.py:120
  29.3 0.2 collective-permute-start.4
  29.5 2.0 %collective-permute-done.4 = f32[16,2,32,128]{3,2,1,0:T(8,128)S(1)} collective-permute-done((f32[16,2,32,128]{3,2,1,0:T(8,128)}, f32[16,2,32,128]{3,2,1,0:T(8,128)S(1)}, u32[]{:S(2)}, u32[]{:S(2)}) %collective-permute-start.4) | collective-permute-done | bytes 524320 | tf_op jit(solution)/shard_map/ppermute | solution.py:25
  31.5 1.1 %add.27 = f32[16,2,32,128]{3,2,1,0:T(8,128)S(1)} add(f32[16,2,32,128]{3,2,1,0:T(8,128)} %get-tuple-element.20, f32[16,2,32,128]{3,2,1,0:T(8,128)S(1)} %collective-permute-done.4) | non-fusion elementwise | flops 131072 | bytes 1572864 | tf_op jit(solution)/shard_map/add | solution.py:275
  32.6 2.1 %collective-permute-start.5 = (bf16[4,4,32,128]{3,2,1,0:T(8,128)(2,1)S(1)}, bf16[4,4,32,128]{3,2,1,0:T(8,128)(2,1)S(1)}, u32[]{:S(2)}, u32[]{:S(2)}) collective-permute-start(bf16[4,4,32,128]{3,2,1,0:T(8,128)(2,1)S(1)} %fusion.5), channel_id=1, source_target_pairs={{0,2},{1,3},{2,0},{3,1},{4,6},{5,7},{6,4},{7,5},{8,10},{9,11},{10,... | collective-permute-start | bytes 393224 | tf_op jit(solution)/shard_map/ppermute | solution.py:25
  34.8 1.3 %collective-permute-start.3 = (bf16[262160]{0:T(1024)(128)(2,1)S(1)}, bf16[262160]{0:T(1024)(128)(2,1)S(1)}, u32[]{:S(2)}, u32[]{:S(2)}) collective-permute-start(bf16[262160]{0:T(1024)(128)(2,1)S(1)} %pad_maximum_fusion), channel_id=1, source_target_pairs={{16,0},{17,1},{18,2},{19,3},{20,4},{21,5},{22,6},{23,7},{24,8},{25... | collective-permute-start | bytes 1572968 | tf_op jit(solution)/shard_map/ppermute | solution.py:15
  36.1 2.5 %collective-permute-done.5 = bf16[4,4,32,128]{3,2,1,0:T(8,128)(2,1)S(1)} collective-permute-done((bf16[4,4,32,128]{3,2,1,0:T(8,128)(2,1)S(1)}, bf16[4,4,32,128]{3,2,1,0:T(8,128)(2,1)S(1)}, u32[]{:S(2)}, u32[]{:S(2)}) %collective-permute-start.5) | collective-permute-done | bytes 131104 | tf_op jit(solution)/shard_map/ppermute | solution.py:25
  38.6 4.4 %collective-permute-start.6 = (bf16[4,32,128]{2,1,0:T(8,128)(2,1)S(1)}, bf16[4,32,128]{2,1,0:T(8,128)(2,1)S(1)}, u32[]{:S(2)}, u32[]{:S(2)}) collective-permute-start(bf16[4,32,128]{2,1,0:T(8,128)(2,1)S(1)} %get-tuple-element.26), channel_id=1, source_target_pairs={{0,12},{4,0},{8,4},{12,8},{1,13},{5,1},{9,5},{13,9},{2,14},{6,2},{... | collective-permute-start | bytes 98312 | tf_op jit(solution)/shard_map/ppermute | solution.py:20
  43.0 0.6 %collective-permute-start.8 = (bf16[4,32,128]{2,1,0:T(8,128)(2,1)S(1)}, bf16[4,32,128]{2,1,0:T(8,128)(2,1)S(1)}, u32[]{:S(2)}, u32[]{:S(2)}) collective-permute-start(bf16[4,32,128]{2,1,0:T(8,128)(2,1)S(1)} %get-tuple-element.27), channel_id=1, source_target_pairs={{0,4},{4,8},{8,12},{12,0},{1,5},{5,9},{9,13},{13,1},{2,6},{6,10},{... | collective-permute-start | bytes 98312 | tf_op jit(solution)/shard_map/ppermute | solution.py:20
  43.7 1.0 %collective-permute-done.6 = bf16[4,32,128]{2,1,0:T(8,128)(2,1)S(1)} collective-permute-done((bf16[4,32,128]{2,1,0:T(8,128)(2,1)S(1)}, bf16[4,32,128]{2,1,0:T(8,128)(2,1)S(1)}, u32[]{:S(2)}, u32[]{:S(2)}) %collective-permute-start.6) | collective-permute-done | bytes 32800 | tf_op jit(solution)/shard_map/ppermute | solution.py:20
  44.6 3.2 %collective-permute-done.7 = bf16[4,32,128]{2,1,0:T(8,128)(2,1)S(1)} collective-permute-done((bf16[4,32,128]{2,1,0:T(8,128)(2,1)S(1)}, bf16[4,32,128]{2,1,0:T(8,128)(2,1)S(1)}, u32[]{:S(2)}, u32[]{:S(2)}) %collective-permute-start.7) | collective-permute-done | bytes 32800 | tf_op jit(solution)/shard_map/ppermute | solution.py:20
  47.8 0.9 %collective-permute-done.8 = bf16[4,32,128]{2,1,0:T(8,128)(2,1)S(1)} collective-permute-done((bf16[4,32,128]{2,1,0:T(8,128)(2,1)S(1)}, bf16[4,32,128]{2,1,0:T(8,128)(2,1)S(1)}, u32[]{:S(2)}, u32[]{:S(2)}) %collective-permute-start.8) | collective-permute-done | bytes 32800 | tf_op jit(solution)/shard_map/ppermute | solution.py:20
  48.8 1.8 %collective-permute-start.9 = (f32[4,32,128]{2,1,0:T(8,128)S(1)}, f32[4,32,128]{2,1,0:T(8,128)S(1)}, u32[]{:S(2)}, u32[]{:S(2)}) collective-permute-start(f32[4,32,128]{2,1,0:T(8,128)S(1)} %fusion.9), channel_id=1, source_target_pairs={{0,2},{1,3},{2,0},{3,1},{4,6},{5,7},{6,4},{7,5},{8,10},{9,11},{10,... | collective-permute-start | bytes 196616 | tf_op jit(solution)/shard_map/ppermute | solution.py:25
  50.6 2.5 %collective-permute-done.9 = f32[4,32,128]{2,1,0:T(8,128)S(1)} collective-permute-done((f32[4,32,128]{2,1,0:T(8,128)S(1)}, f32[4,32,128]{2,1,0:T(8,128)S(1)}, u32[]{:S(2)}, u32[]{:S(2)}) %collective-permute-start.9) | collective-permute-done | bytes 65568 | tf_op jit(solution)/shard_map/ppermute | solution.py:25
  53.2 0.5 slice_convert_fusion.1.rows_ref
  53.7 0.8 %slice.64 = bf16[262144]{0:T(1024)(128)(2,1)} slice(bf16[262160]{0:T(1024)(128)(2,1)S(1)} %collective-permute-done.3), slice={[0:262144]} | slice | bytes 1048576 | tf_op jit(solution)/shard_map/slice | solution.py:266
  54.5 3.0 %shard_map.69 = bf16[4,32,3584]{2,1,0:T(8,128)(2,1)} custom-call(s32[16]{0:T(128)} %slice_convert_fusion.1.rows_ref, s32[4]{0:T(128)} %order_ref.1, bf16[16,128,128]{2,1,0:T(8,128)(2,1)} %bitcast.66), custom_call_target="tpu_custom_call" | custom-call | tf_op jit(solution)/shard_map/pallas_call | solution.py:176
  57.6 0.7 %copy.29 = f32[4,4,32,128]{3,2,1,0:T(8,128)} copy(f32[4,4,32,128]{3,2,0,1:T(8,128)S(1)} %bitcast.69) | data formatting | bytes 524288 | tf_op jit(solution)/shard_map/div | solution.py:290
  (25 shorter events, 0.5 us)
Async XLA Ops:
  2.4 0.7 %collective-permute-start = (bf16[528,128]{1,0:T(8,128)(2,1)S(1)}, bf16[528,128]{1,0:T(8,128)(2,1)S(1)}, u32[]{:S(2)}, u32[]{:S(2)}) collective-permute-start(bf16[528,128]{1,0:T(8,128)(2,1)S(1)} %fusion.4), channel_id=1, source_target_pairs={{0,0},{13,1},{10,2},{7,3},{4,4},{1,5},{14,6},{11,7},{8,8},{5,9},{2... | collective-permute-start | bytes 405512 | tf_op jit(solution)/shard_map/ppermute | solution.py:236
  3.1 15.0 %collective-permute-start.1 = (bf16[1,528,128]{2,1,0:T(8,128)(2,1)S(1)}, bf16[1,528,128]{2,1,0:T(8,128)(2,1)S(1)}, u32[]{:S(2)}, u32[]{:S(2)}) collective-permute-start(bf16[1,528,128]{2,1,0:T(8,128)(2,1)S(1)} %bitcast.74), channel_id=1, source_target_pairs={{0,2},{1,3},{2,0},{3,1},{4,6},{5,7},{6,4},{7,5},{8,10},{9,11},{10,... | collective-permute-start | bytes 405512 | tf_op jit(solution)/shard_map/ppermute | solution.py:25
  18.1 1.6 %collective-permute-start.2 = (bf16[2,1,528,128]{3,2,1,0:T(8,128)(2,1)S(1)}, bf16[2,1,528,128]{3,2,1,0:T(8,128)(2,1)S(1)}, u32[]{:S(2)}, u32[]{:S(2)}) collective-permute-start(bf16[2,1,528,128]{3,2,1,0:T(8,128)(2,1)S(1)} %maximum_select_fusion.2), channel_id=1, source_target_pairs={{0,1},{1,0},{2,3},{3,2},{4,5},{5,4},{6,7},{7,6},{8,9},{9,8},{10,11... | collective-permute-start | bytes 811016 | tf_op jit(solution)/shard_map/ppermute | solution.py:25
  21.2 1.6 %copy-start.1 = (s32[16]{0:T(128)}, s32[16]{0:T(128)S(1)}, u32[]{:S(2)}) copy-start(s32[16]{0:T(128)S(1)} %get-tuple-element.22.cols_ref) | copy-start | bytes 196
  22.8 6.7 %copy-start.2 = (s32[16]{0:T(128)S(1)}, s32[16]{0:T(128)}, u32[]{:S(2)}) copy-start(s32[16]{0:T(128)} %get-tuple-element.23.rows_ref) | copy-start | bytes 196
  29.3 5.4 %copy-start = (bf16[16,128,128]{2,1,0:T(8,128)(2,1)S(1)}, bf16[16,128,128]{2,1,0:T(8,128)(2,1)}, u32[]{:S(2)}) copy-start(bf16[16,128,128]{2,1,0:T(8,128)(2,1)} %get-tuple-element.19) | copy-start | bytes 1572868
  29.3 2.2 %collective-permute-start.4 = (f32[16,2,32,128]{3,2,1,0:T(8,128)}, f32[16,2,32,128]{3,2,1,0:T(8,128)S(1)}, u32[]{:S(2)}, u32[]{:S(2)}) collective-permute-start(f32[16,2,32,128]{3,2,1,0:T(8,128)} %get-tuple-element.21), channel_id=1, source_target_pairs={{0,1},{1,0},{2,3},{3,2},{4,5},{5,4},{6,7},{7,6},{8,9},{9,8},{10,11... | collective-permute-start | bytes 1572872 | tf_op jit(solution)/shard_map/ppermute | solution.py:25
  32.6 5.9 %collective-permute-start.5 = (bf16[4,4,32,128]{3,2,1,0:T(8,128)(2,1)S(1)}, bf16[4,4,32,128]{3,2,1,0:T(8,128)(2,1)S(1)}, u32[]{:S(2)}, u32[]{:S(2)}) collective-permute-start(bf16[4,4,32,128]{3,2,1,0:T(8,128)(2,1)S(1)} %fusion.5), channel_id=1, source_target_pairs={{0,2},{1,3},{2,0},{3,1},{4,6},{5,7},{6,4},{7,5},{8,10},{9,11},{10,... | collective-permute-start | bytes 393224 | tf_op jit(solution)/shard_map/ppermute | solution.py:25
  34.8 18.4 %collective-permute-start.3 = (bf16[262160]{0:T(1024)(128)(2,1)S(1)}, bf16[262160]{0:T(1024)(128)(2,1)S(1)}, u32[]{:S(2)}, u32[]{:S(2)}) collective-permute-start(bf16[262160]{0:T(1024)(128)(2,1)S(1)} %pad_maximum_fusion), channel_id=1, source_target_pairs={{16,0},{17,1},{18,2},{19,3},{20,4},{21,5},{22,6},{23,7},{24,8},{25... | collective-permute-start | bytes 1572968 | tf_op jit(solution)/shard_map/ppermute | solution.py:15
  38.6 6.0 %collective-permute-start.6 = (bf16[4,32,128]{2,1,0:T(8,128)(2,1)S(1)}, bf16[4,32,128]{2,1,0:T(8,128)(2,1)S(1)}, u32[]{:S(2)}, u32[]{:S(2)}) collective-permute-start(bf16[4,32,128]{2,1,0:T(8,128)(2,1)S(1)} %get-tuple-element.26), channel_id=1, source_target_pairs={{0,12},{4,0},{8,4},{12,8},{1,13},{5,1},{9,5},{13,9},{2,14},{6,2},{... | collective-permute-start | bytes 98312 | tf_op jit(solution)/shard_map/ppermute | solution.py:20
  43.0 4.8 %collective-permute-start.7 = (bf16[4,32,128]{2,1,0:T(8,128)(2,1)S(1)}, bf16[4,32,128]{2,1,0:T(8,128)(2,1)S(1)}, u32[]{:S(2)}, u32[]{:S(2)}) collective-permute-start(bf16[4,32,128]{2,1,0:T(8,128)(2,1)S(1)} %get-tuple-element.28), channel_id=1, source_target_pairs={{0,8},{4,12},{8,0},{12,4},{1,9},{5,13},{9,1},{13,5},{2,10},{6,14},... | collective-permute-start | bytes 98312 | tf_op jit(solution)/shard_map/ppermute | solution.py:20
  43.0 5.7 %collective-permute-start.8 = (bf16[4,32,128]{2,1,0:T(8,128)(2,1)S(1)}, bf16[4,32,128]{2,1,0:T(8,128)(2,1)S(1)}, u32[]{:S(2)}, u32[]{:S(2)}) collective-permute-start(bf16[4,32,128]{2,1,0:T(8,128)(2,1)S(1)} %get-tuple-element.27), channel_id=1, source_target_pairs={{0,4},{4,8},{8,12},{12,0},{1,5},{5,9},{9,13},{13,1},{2,6},{6,10},{... | collective-permute-start | bytes 98312 | tf_op jit(solution)/shard_map/ppermute | solution.py:20
  48.8 4.3 %collective-permute-start.9 = (f32[4,32,128]{2,1,0:T(8,128)S(1)}, f32[4,32,128]{2,1,0:T(8,128)S(1)}, u32[]{:S(2)}, u32[]{:S(2)}) collective-permute-start(f32[4,32,128]{2,1,0:T(8,128)S(1)} %fusion.9), channel_id=1, source_target_pairs={{0,2},{1,3},{2,0},{3,1},{4,6},{5,7},{6,4},{7,5},{8,10},{9,11},{10,... | collective-permute-start | bytes 196616 | tf_op jit(solution)/shard_map/ppermute | solution.py:25
  53.1 4.5 %collective-permute-start.10 = (f32[2,4,32,128]{3,2,1,0:T(8,128)S(1)}, f32[2,4,32,128]{3,2,1,0:T(8,128)S(1)}, u32[]{:S(2)}, u32[]{:S(2)}) collective-permute-start(f32[2,4,32,128]{3,2,1,0:T(8,128)S(1)} %maximum_select_fusion.4), channel_id=1, source_target_pairs={{0,1},{1,0},{2,3},{3,2},{4,5},{5,4},{6,7},{7,6},{8,9},{9,8},{10,11... | collective-permute-start | bytes 393224 | tf_op jit(solution)/shard_map/ppermute | solution.py:25

commit v15 on v13

--- a/solution.py
+++ b/solution.py
@@ -243,8 +243,9 @@
     owned = held[0]
     for k in range(1, n_fsdp):
         owned = owned + shifted(held[k].astype(jnp.bfloat16), "fsdp", -k).astype(jnp.float32)
-    full = butterfly_gather(owned, "dp", list(reversed(range(dp_bits))))
-    full = full.reshape((n_dp, blocks_dev, chunk, block_size))
+    relative = gather_over(owned, "dp")
+    from_device = (me_dp - jnp.arange(n_dp, dtype=jnp.int32)) % n_dp
+    full = jnp.take(relative, from_device, axis=0)
     full = jnp.transpose(full, (1, 0, 2, 3)).reshape(blocks_dev, block_size, block_size)
     grad_scale = jnp.sqrt(jnp.float32(tok_rows * n_fsdp * n_dp))
     return (received[None], (full / grad_scale)[None])

time: 56.2 us -> 60.5 us (1.077)
  waiting for transfers between devices: 14.2 us -> 17.7 us
    ppermute x1, waiting for transfers between devices: 0.01 us -> 6.71 us  [passed_along(): return lax.ppermute(block, axis, route)]
    ppermute x3 -> x6, waiting for transfers between devices: 5.07 us -> 2.21 us  [shifted(): return lax.ppermute(x, axis, [(i, (i + k) % n) for i in range(n)])]
    ppermute x6 -> x4, starting transfers between devices: 16.2 us -> 14.4 us  [swapped(): return lax.ppermute(x, axis, [(i, i ^ 1 << bit) for i in range(n)])]
    ppermute x3 -> x6, starting transfers between devices: 5.08 us -> 6.9 us  [shifted(): return lax.ppermute(x, axis, [(i, (i + k) % n) for i in range(n)])]
    ppermute x6 -> x4, waiting for transfers between devices: 9.13 us -> 8.82 us  [swapped(): return lax.ppermute(x, axis, [(i, i ^ 1 << bit) for i in range(n)])]
  transfers between devices with their start and end apart: 11 -> 12, of which waited for: 8 -> 7; matrix products, arithmetic and copies ran while one was open for 8% -> 7% of each run, Pallas kernels for 0% -> 0%
where the time goes in v15:
time: 60.5 us; the launch traced here: 60.1 us
  starting transfers between devices  23.2 us (38%)
  waiting for transfers between devices  17.7 us (29%)
  local copies, waits for them, and re-layouts  6.78 us (11%)
  Pallas kernels  6.49 us (11%)
  other arithmetic  4.91 us (8%)
  between operations  0.91 us (2%)
    ppermute x4, starting transfers between devices, swapped(): return lax.ppermute(x, axis, [(i, i ^ 1 << bit) for i in range(n)])  14.4 us
    ppermute x4, waiting for transfers between devices, swapped(): return lax.ppermute(x, axis, [(i, i ^ 1 << bit) for i in range(n)])  8.82 us
    ppermute x6, starting transfers between devices, shifted(): return lax.ppermute(x, axis, [(i, (i + k) % n) for i in range(n)])  6.9 us
    ppermute x1, waiting for transfers between devices, passed_along(): return lax.ppermute(block, axis, route)  6.71 us
    pallas_call x1, Pallas kernels, block_pass(): pl.pallas_call(functools.partial(block_kernel, compact, chunk), out_shape...  6.49 us
    ppermute x6, waiting for transfers between devices, shifted(): return lax.ppermute(x, axis, [(i, (i + k) % n) for i in range(n)])  2.21 us
    ppermute x1, starting transfers between devices, passed_along(): return lax.ppermute(block, axis, route)  1.29 us
  transfers between devices with their start and end apart: 12, of which 7 were waited for; matrix products, arithmetic and copies ran while one was open for 7% of the time, Pallas kernels for 0%

profile of v15, /device:TPU:0, one launch (start us, length us, event | category | flops | bytes accessed | tf_op | source)
XLA Modules:
  0.0 60.1 jit_solution(1594723523209892700)
XLA Ops:
  0.6 0.7 %convert_element_type.53 = bf16[1,4,2]{1,2,0:T(2,128)(2,1)S(1)} convert(s32[1,4,2]{1,2,0:T(2,128)} %param.10) | non-fusion elementwise | flops 8 | bytes 48 | tf_op jit(solution)/shard_map/convert_element_type | solution.py:185
  1.5 0.9 %fusion.3 = bf16[528,128]{1,0:T(8,128)(2,1)S(1)} fusion(bf16[1,8]{1,0:T(2,128)(2,1)S(1)} %convert_element_type.54, bf16[512,128]{1,0:T(8,128)(2,1)} %bitcast.68), kind=kLoop, calls=%fused_computation.16 | loop fusion | flops 405504 | bytes 266256 | tf_op jit(solution)/shard_map/concatenate | solution.py:187
  2.4 0.7 %collective-permute-start = (bf16[528,128]{1,0:T(8,128)(2,1)S(1)}, bf16[528,128]{1,0:T(8,128)(2,1)S(1)}, u32[]{:S(2)}, u32[]{:S(2)}) collective-permute-start(bf16[528,128]{1,0:T(8,128)(2,1)S(1)} %fusion.3), channel_id=1, source_target_pairs={{0,0},{13,1},{10,2},{7,3},{4,4},{1,5},{14,6},{11,7},{8,8},{5,9},{2... | collective-permute-start | bytes 405512 | tf_op jit(solution)/shard_map/ppermute | solution.py:195
  3.1 12.0 %collective-permute-start.1 = (bf16[1,528,128]{2,1,0:T(8,128)(2,1)S(1)}, bf16[1,528,128]{2,1,0:T(8,128)(2,1)S(1)}, u32[]{:S(2)}, u32[]{:S(2)}) collective-permute-start(bf16[1,528,128]{2,1,0:T(8,128)(2,1)S(1)} %bitcast.59), channel_id=1, source_target_pairs={{0,2},{1,3},{2,0},{3,1},{4,6},{5,7},{6,4},{7,5},{8,10},{9,11},{10,... | collective-permute-start | bytes 405512 | tf_op jit(solution)/shard_map/ppermute | solution.py:25
  15.1 3.0 %collective-permute-done.1 = bf16[1,528,128]{2,1,0:T(8,128)(2,1)S(1)} collective-permute-done((bf16[1,528,128]{2,1,0:T(8,128)(2,1)S(1)}, bf16[1,528,128]{2,1,0:T(8,128)(2,1)S(1)}, u32[]{:S(2)}, u32[]{:S(2)}) %collective-permute-start.1) | collective-permute-done | bytes 135200 | tf_op jit(solution)/shard_map/ppermute | solution.py:25
  18.3 1.5 %collective-permute-done.2 = bf16[2,1,528,128]{3,2,1,0:T(8,128)(2,1)S(1)} collective-permute-done((bf16[2,1,528,128]{3,2,1,0:T(8,128)(2,1)S(1)}, bf16[2,1,528,128]{3,2,1,0:T(8,128)(2,1)S(1)}, u32[]{:S(2)}, u32[]{:S(2)}) %collective-permute-start.2) | collective-permute-done | bytes 270368 | tf_op jit(solution)/shard_map/ppermute | solution.py:25
  19.8 0.4 copy.21
  20.5 0.6 %slice_reduce_fusion = (s32[16]{0:T(128)S(1)}, s32[16]{0:T(128)}) fusion(s32[16,2]{1,0:T(8,128)S(1)} %reshape.417), kind=kLoop, calls=%fused_computation.25 | loop fusion | bytes 256 | tf_op jit(solution)/shard_map/slice | solution.py:208
  21.2 0.7 %iota_reduce_fusion = (pred[16]{0:T(512)(128)(4,1)}, s32[16]{0:T(128)}) fusion(s32[16]{0:T(128)S(1)} %get-tuple-element.22.cols_ref), kind=kLoop, calls=%fused_computation.27 | loop fusion | flops 1936 | bytes 144 | tf_op jit(solution)/shard_map/block_pass/reduce | solution.py:114
  21.9 0.9 %copy.22 = bf16[4,512,128]{2,1,0:T(8,128)(2,1)} copy(bf16[4,512,128]{2,0,1:T(4,128)(2,1)S(1)} %slice.66) | data formatting | bytes 1048576 | tf_op jit(solution)/shard_map/slice | solution.py:200
  22.7 6.5 %shard_map.68 = (bf16[16,128,128]{2,1,0:T(8,128)(2,1)}, f32[16,2,32,128]{3,2,1,0:T(8,128)}, f32[16,2,32,128]{3,2,1,0:T(8,128)}) custom-call(s32[16]{0:T(128)} %get-tuple-element.23.rows_ref, s32[16]{0:T(128)} %copy-done.1, s32[16]{0:T(128)} %get-tuple-element.18.rep_ref, s32[1]{0:T(128)} %bitcast.8.bit_ref, bf16[128,3584]{1,0:T(8,128)(2,1)} %bitcast.58, ...), custom_call_target="tpu_custom_call" | custom-call | flops 201326592 | bytes 3538944 | tf_op jit(solution)/shard_map/pallas_call | solution.py:120
  29.2 0.2 collective-permute-start.4
  29.5 1.9 %collective-permute-done.4 = f32[16,2,32,128]{3,2,1,0:T(8,128)S(1)} collective-permute-done((f32[16,2,32,128]{3,2,1,0:T(8,128)}, f32[16,2,32,128]{3,2,1,0:T(8,128)S(1)}, u32[]{:S(2)}, u32[]{:S(2)}) %collective-permute-start.4) | collective-permute-done | bytes 524320 | tf_op jit(solution)/shard_map/ppermute | solution.py:25
  31.4 1.1 %add.70 = f32[16,2,32,128]{3,2,1,0:T(8,128)S(1)} add(f32[16,2,32,128]{3,2,1,0:T(8,128)} %get-tuple-element.20, f32[16,2,32,128]{3,2,1,0:T(8,128)S(1)} %collective-permute-done.4) | non-fusion elementwise | flops 131072 | bytes 1572864 | tf_op jit(solution)/shard_map/add | solution.py:235
  32.6 2.1 %collective-permute-start.5 = (bf16[4,4,32,128]{3,2,1,0:T(8,128)(2,1)S(1)}, bf16[4,4,32,128]{3,2,1,0:T(8,128)(2,1)S(1)}, u32[]{:S(2)}, u32[]{:S(2)}) collective-permute-start(bf16[4,4,32,128]{3,2,1,0:T(8,128)(2,1)S(1)} %fusion.4), channel_id=1, source_target_pairs={{0,2},{1,3},{2,0},{3,1},{4,6},{5,7},{6,4},{7,5},{8,10},{9,11},{10,... | collective-permute-start | bytes 393224 | tf_op jit(solution)/shard_map/ppermute | solution.py:25
  34.7 1.3 %collective-permute-start.3 = (bf16[262160]{0:T(1024)(128)(2,1)S(1)}, bf16[262160]{0:T(1024)(128)(2,1)S(1)}, u32[]{:S(2)}, u32[]{:S(2)}) collective-permute-start(bf16[262160]{0:T(1024)(128)(2,1)S(1)} %pad_maximum_fusion), channel_id=1, source_target_pairs={{16,0},{17,1},{18,2},{19,3},{20,4},{21,5},{22,6},{23,7},{24,8},{25... | collective-permute-start | bytes 1572968 | tf_op jit(solution)/shard_map/ppermute | solution.py:15
  36.0 2.4 %collective-permute-done.5 = bf16[4,4,32,128]{3,2,1,0:T(8,128)(2,1)S(1)} collective-permute-done((bf16[4,4,32,128]{3,2,1,0:T(8,128)(2,1)S(1)}, bf16[4,4,32,128]{3,2,1,0:T(8,128)(2,1)S(1)}, u32[]{:S(2)}, u32[]{:S(2)}) %collective-permute-start.5) | collective-permute-done | bytes 131104 | tf_op jit(solution)/shard_map/ppermute | solution.py:25
  38.6 4.4 %collective-permute-start.6 = (bf16[4,32,128]{2,1,0:T(8,128)(2,1)S(1)}, bf16[4,32,128]{2,1,0:T(8,128)(2,1)S(1)}, u32[]{:S(2)}, u32[]{:S(2)}) collective-permute-start(bf16[4,32,128]{2,1,0:T(8,128)(2,1)S(1)} %get-tuple-element.26), channel_id=1, source_target_pairs={{0,12},{4,0},{8,4},{12,8},{1,13},{5,1},{9,5},{13,9},{2,14},{6,2},{... | collective-permute-start | bytes 98312 | tf_op jit(solution)/shard_map/ppermute | solution.py:20
  43.0 0.6 %collective-permute-start.8 = (bf16[4,32,128]{2,1,0:T(8,128)(2,1)S(1)}, bf16[4,32,128]{2,1,0:T(8,128)(2,1)S(1)}, u32[]{:S(2)}, u32[]{:S(2)}) collective-permute-start(bf16[4,32,128]{2,1,0:T(8,128)(2,1)S(1)} %get-tuple-element.27), channel_id=1, source_target_pairs={{0,4},{4,8},{8,12},{12,0},{1,5},{5,9},{9,13},{13,1},{2,6},{6,10},{... | collective-permute-start | bytes 98312 | tf_op jit(solution)/shard_map/ppermute | solution.py:20
  43.6 6.7 %collective-permute-done.3 = bf16[262160]{0:T(1024)(128)(2,1)S(1)} collective-permute-done((bf16[262160]{0:T(1024)(128)(2,1)S(1)}, bf16[262160]{0:T(1024)(128)(2,1)S(1)}, u32[]{:S(2)}, u32[]{:S(2)}) %collective-permute-start.3) | collective-permute-done | bytes 524352 | tf_op jit(solution)/shard_map/ppermute | solution.py:15
  50.4 0.2 broadcast_in_dim.32
  50.6 1.1 %scatter_fusion = bf16[28,128,128]{2,1,0:T(8,128)(2,1)S(1)} fusion(bf16[28,128,128]{2,1,0:T(8,128)(2,1)S(1)} %broadcast_in_dim.32, s32[16]{0:T(128)S(1)} %compare_select_fusion.2, bf16[16,128,128]{2,1,0:T(8,128)(2,1)S(1)} %bitcast.55), kind=kCustom, calls=%fused_computation.2 | custom fusion | bytes 1572928 | tf_op jit(solution)/shard_map/scatter | solution.py:227
  51.8 0.6 %copy.23 = bf16[128,28,128]{2,1,0:T(8,128)(2,1)S(1)} copy(bf16[128,28,128]{2,0,1:T(8,128)(2,1)S(1)} %bitcast.50) | data formatting | bytes 1835008 | tf_op jit(solution)/shard_map/transpose | solution.py:230
  52.4 0.5 reshape.415
  52.9 0.6 %gather_fusion = bf16[4,32,3584]{2,1,0:T(8,128)(2,1)S(1)} fusion(bf16[4,32,3584]{2,1,0:T(8,128)(2,1)S(1)} %reshape.415, s32[1024]{0:T(1024)S(1)} %pad_clamp_fusion.1), kind=kCustom, calls=%fused_computation | custom fusion | bytes 1835024 | tf_op jit(solution)/shard_map/jit(_take)/gather | solution.py:233
  53.6 0.4 collective-permute-start.10
  54.0 1.4 %collective-permute-start.11 = (f32[4,32,128]{2,1,0:T(8,128)S(1)}, f32[4,32,128]{2,1,0:T(8,128)S(1)}, u32[]{:S(2)}, u32[]{:S(2)}) collective-permute-start(f32[4,32,128]{2,1,0:T(8,128)S(1)} %fusion.7), channel_id=1, source_target_pairs={{0,3},{1,0},{2,1},{3,2},{4,7},{5,4},{6,5},{7,6},{8,11},{9,8},{10,9... | collective-permute-start | bytes 196616 | tf_op jit(solution)/shard_map/ppermute | solution.py:20
  55.4 1.1 %bitcast_select_fusion = bf16[1,4,32,3584]{3,2,1,0:T(8,128)(2,1)} fusion(bf16[4,32,3584]{2,1,0:T(8,128)(2,1)S(1)} %gather_fusion, pred[4]{0:T(512)(128)(4,1)S(1)} %get-tuple-element.30), kind=kLoop, calls=%fused_computation.3 | loop fusion | flops 458752 | bytes 1835012 | tf_op jit(solution)/shard_map/jit(_take)/select_n | solution.py:233
  56.4 0.9 %collective-permute-done.9 = f32[4,32,128]{2,1,0:T(8,128)S(1)} collective-permute-done((f32[4,32,128]{2,1,0:T(8,128)S(1)}, f32[4,32,128]{2,1,0:T(8,128)S(1)}, u32[]{:S(2)}, u32[]{:S(2)}) %collective-permute-start.9) | collective-permute-done | bytes 65568 | tf_op jit(solution)/shard_map/ppermute | solution.py:20
  57.3 1.3 %collective-permute-done.10 = f32[4,32,128]{2,1,0:T(8,128)S(1)} collective-permute-done((f32[4,32,128]{2,1,0:T(8,128)S(1)}, f32[4,32,128]{2,1,0:T(8,128)S(1)}, u32[]{:S(2)}, u32[]{:S(2)}) %collective-permute-start.10) | collective-permute-done | bytes 65568 | tf_op jit(solution)/shard_map/ppermute | solution.py:20
  58.7 0.6 gather_fusion.1
  59.3 0.7 %copy.24 = f32[4,4,32,128]{3,2,1,0:T(8,128)} copy(f32[4,4,32,128]{3,2,0,1:T(8,128)S(1)} %multiply_bitcast_fusion) | data formatting | bytes 524288 | tf_op jit(solution)/shard_map/div | solution.py:251
  (39 shorter events, 1.1 us)
Async XLA Ops:
  2.4 0.7 %collective-permute-start = (bf16[528,128]{1,0:T(8,128)(2,1)S(1)}, bf16[528,128]{1,0:T(8,128)(2,1)S(1)}, u32[]{:S(2)}, u32[]{:S(2)}) collective-permute-start(bf16[528,128]{1,0:T(8,128)(2,1)S(1)} %fusion.3), channel_id=1, source_target_pairs={{0,0},{13,1},{10,2},{7,3},{4,4},{1,5},{14,6},{11,7},{8,8},{5,9},{2... | collective-permute-start | bytes 405512 | tf_op jit(solution)/shard_map/ppermute | solution.py:195
  3.1 15.0 %collective-permute-start.1 = (bf16[1,528,128]{2,1,0:T(8,128)(2,1)S(1)}, bf16[1,528,128]{2,1,0:T(8,128)(2,1)S(1)}, u32[]{:S(2)}, u32[]{:S(2)}) collective-permute-start(bf16[1,528,128]{2,1,0:T(8,128)(2,1)S(1)} %bitcast.59), channel_id=1, source_target_pairs={{0,2},{1,3},{2,0},{3,1},{4,6},{5,7},{6,4},{7,5},{8,10},{9,11},{10,... | collective-permute-start | bytes 405512 | tf_op jit(solution)/shard_map/ppermute | solution.py:25
  18.1 1.6 %collective-permute-start.2 = (bf16[2,1,528,128]{3,2,1,0:T(8,128)(2,1)S(1)}, bf16[2,1,528,128]{3,2,1,0:T(8,128)(2,1)S(1)}, u32[]{:S(2)}, u32[]{:S(2)}) collective-permute-start(bf16[2,1,528,128]{3,2,1,0:T(8,128)(2,1)S(1)} %maximum_select_fusion.2), channel_id=1, source_target_pairs={{0,1},{1,0},{2,3},{3,2},{4,5},{5,4},{6,7},{7,6},{8,9},{9,8},{10,11... | collective-permute-start | bytes 811016 | tf_op jit(solution)/shard_map/ppermute | solution.py:25
  21.2 1.6 %copy-start.1 = (s32[16]{0:T(128)}, s32[16]{0:T(128)S(1)}, u32[]{:S(2)}) copy-start(s32[16]{0:T(128)S(1)} %get-tuple-element.22.cols_ref) | copy-start | bytes 196
  22.7 6.7 %copy-start.3 = (s32[4]{0:T(128)S(1)}, s32[4]{0:T(128)}, u32[]{:S(2)}) copy-start(s32[4]{0:T(128)} %param.11) | copy-start | bytes 52
  22.7 6.8 %copy-start.2 = (s32[16]{0:T(128)S(1)}, s32[16]{0:T(128)}, u32[]{:S(2)}) copy-start(s32[16]{0:T(128)} %get-tuple-element.23.rows_ref) | copy-start | bytes 196
  29.2 5.5 %copy-start = (bf16[16,128,128]{2,1,0:T(8,128)(2,1)S(1)}, bf16[16,128,128]{2,1,0:T(8,128)(2,1)}, u32[]{:S(2)}) copy-start(bf16[16,128,128]{2,1,0:T(8,128)(2,1)} %get-tuple-element.19) | copy-start | bytes 1572868
  29.2 2.2 %collective-permute-start.4 = (f32[16,2,32,128]{3,2,1,0:T(8,128)}, f32[16,2,32,128]{3,2,1,0:T(8,128)S(1)}, u32[]{:S(2)}, u32[]{:S(2)}) collective-permute-start(f32[16,2,32,128]{3,2,1,0:T(8,128)} %get-tuple-element.21), channel_id=1, source_target_pairs={{0,1},{1,0},{2,3},{3,2},{4,5},{5,4},{6,7},{7,6},{8,9},{9,8},{10,11... | collective-permute-start | bytes 1572872 | tf_op jit(solution)/shard_map/ppermute | solution.py:25
  32.6 5.9 %collective-permute-start.5 = (bf16[4,4,32,128]{3,2,1,0:T(8,128)(2,1)S(1)}, bf16[4,4,32,128]{3,2,1,0:T(8,128)(2,1)S(1)}, u32[]{:S(2)}, u32[]{:S(2)}) collective-permute-start(bf16[4,4,32,128]{3,2,1,0:T(8,128)(2,1)S(1)} %fusion.4), channel_id=1, source_target_pairs={{0,2},{1,3},{2,0},{3,1},{4,6},{5,7},{6,4},{7,5},{8,10},{9,11},{10,... | collective-permute-start | bytes 393224 | tf_op jit(solution)/shard_map/ppermute | solution.py:25
  34.7 15.6 %collective-permute-start.3 = (bf16[262160]{0:T(1024)(128)(2,1)S(1)}, bf16[262160]{0:T(1024)(128)(2,1)S(1)}, u32[]{:S(2)}, u32[]{:S(2)}) collective-permute-start(bf16[262160]{0:T(1024)(128)(2,1)S(1)} %pad_maximum_fusion), channel_id=1, source_target_pairs={{16,0},{17,1},{18,2},{19,3},{20,4},{21,5},{22,6},{23,7},{24,8},{25... | collective-permute-start | bytes 1572968 | tf_op jit(solution)/shard_map/ppermute | solution.py:15
  38.6 14.9 %collective-permute-start.6 = (bf16[4,32,128]{2,1,0:T(8,128)(2,1)S(1)}, bf16[4,32,128]{2,1,0:T(8,128)(2,1)S(1)}, u32[]{:S(2)}, u32[]{:S(2)}) collective-permute-start(bf16[4,32,128]{2,1,0:T(8,128)(2,1)S(1)} %get-tuple-element.26), channel_id=1, source_target_pairs={{0,12},{4,0},{8,4},{12,8},{1,13},{5,1},{9,5},{13,9},{2,14},{6,2},{... | collective-permute-start | bytes 98312 | tf_op jit(solution)/shard_map/ppermute | solution.py:20
  43.0 10.5 %collective-permute-start.7 = (bf16[4,32,128]{2,1,0:T(8,128)(2,1)S(1)}, bf16[4,32,128]{2,1,0:T(8,128)(2,1)S(1)}, u32[]{:S(2)}, u32[]{:S(2)}) collective-permute-start(bf16[4,32,128]{2,1,0:T(8,128)(2,1)S(1)} %get-tuple-element.28), channel_id=1, source_target_pairs={{0,8},{4,12},{8,0},{12,4},{1,9},{5,13},{9,1},{13,5},{2,10},{6,14},... | collective-permute-start | bytes 98312 | tf_op jit(solution)/shard_map/ppermute | solution.py:20
  43.0 10.5 %collective-permute-start.8 = (bf16[4,32,128]{2,1,0:T(8,128)(2,1)S(1)}, bf16[4,32,128]{2,1,0:T(8,128)(2,1)S(1)}, u32[]{:S(2)}, u32[]{:S(2)}) collective-permute-start(bf16[4,32,128]{2,1,0:T(8,128)(2,1)S(1)} %get-tuple-element.27), channel_id=1, source_target_pairs={{0,4},{4,8},{8,12},{12,0},{1,5},{5,9},{9,13},{13,1},{2,6},{6,10},{... | collective-permute-start | bytes 98312 | tf_op jit(solution)/shard_map/ppermute | solution.py:20
  53.5 3.8 %collective-permute-start.9 = (f32[4,32,128]{2,1,0:T(8,128)S(1)}, f32[4,32,128]{2,1,0:T(8,128)S(1)}, u32[]{:S(2)}, u32[]{:S(2)}) collective-permute-start(f32[4,32,128]{2,1,0:T(8,128)S(1)} %fusion.7), channel_id=1, source_target_pairs={{0,1},{1,2},{2,3},{3,0},{4,5},{5,6},{6,7},{7,4},{8,9},{9,10},{10,1... | collective-permute-start | bytes 196616 | tf_op jit(solution)/shard_map/ppermute | solution.py:20
  53.6 5.0 %collective-permute-start.10 = (f32[4,32,128]{2,1,0:T(8,128)S(1)}, f32[4,32,128]{2,1,0:T(8,128)S(1)}, u32[]{:S(2)}, u32[]{:S(2)}) collective-permute-start(f32[4,32,128]{2,1,0:T(8,128)S(1)} %fusion.7), channel_id=1, source_target_pairs={{0,2},{1,3},{2,0},{3,1},{4,6},{5,7},{6,4},{7,5},{8,10},{9,11},{10,... | collective-permute-start | bytes 196616 | tf_op jit(solution)/shard_map/ppermute | solution.py:20
  54.0 4.7 %collective-permute-start.11 = (f32[4,32,128]{2,1,0:T(8,128)S(1)}, f32[4,32,128]{2,1,0:T(8,128)S(1)}, u32[]{:S(2)}, u32[]{:S(2)}) collective-permute-start(f32[4,32,128]{2,1,0:T(8,128)S(1)} %fusion.7), channel_id=1, source_target_pairs={{0,3},{1,0},{2,1},{3,2},{4,7},{5,4},{6,5},{7,6},{8,11},{9,8},{10,9... | collective-permute-start | bytes 196616 | tf_op jit(solution)/shard_map/ppermute | solution.py:20

commit v16 on v13

--- a/solution.py
+++ b/solution.py
@@ -30,10 +30,15 @@
     return sigmoid_val * (1.0 + pre_act * (1.0 - sigmoid_val))
 
 
-def block_kernel(compact, chunk, rows_ref, cols_ref, rep_ref, bit_ref, feat_hbm, hid_hbm, w_ref,
-                 ig_ref, keep_ref, send_ref, xs, hs, pr, acc, pgs, sems):
-    block_count = w_ref.shape[0]
-    width = w_ref.shape[-1]
+def block_kernel(compact, chunk, rows_ref, cols_ref, bit_ref, feat_hbm, hid_hbm, pieces_ref,
+                 ig_ref, keep_ref, send_ref, xs, hs, pr, acc, pgs, rep_ref, sems):
+    width = pieces_ref.shape[-1]
+    per_piece = (pieces_ref.shape[1] - 16) // width
+    block_count = pieces_ref.shape[0] * per_piece
+
+    def w_of(b):
+        start = pl.multiple_of((b % per_piece) * width, width)
+        return pieces_ref[b // per_piece, pl.ds(start, width), :]
     halves = keep_ref.shape[1]
 
     def block_loop(body):
@@ -56,6 +61,14 @@
         for cp in copies(b):
             cp.start()
 
+    for b in range(block_count):
+        rep_ref[b] = b
+    for b in range(block_count - 1, -1, -1):
+        for a in range(b - 1, -1, -1):
+            @pl.when(cols_ref[a] == cols_ref[b])
+            def _():
+                rep_ref[b] = a
+
     if compact:
         @block_loop
         def _(b):
@@ -67,7 +80,7 @@
     def _(b):
         for cp in copies(b):
             cp.wait()
-        pr[b] = jnp.dot(xs[b], w_ref[b], preferred_element_type=jnp.float32)
+        pr[b] = jnp.dot(xs[b], w_of(b), preferred_element_type=jnp.float32)
 
     @block_loop
     def _(b):
@@ -84,7 +97,7 @@
         pre_act = pr[rep_ref[b]]
         act = (hs[b].astype(jnp.float32) * silu_slope(pre_act)).astype(jnp.bfloat16)
         back = lax.dot_general(
-            act, w_ref[b], (((1,), (1,)), ((), ())), preferred_element_type=jnp.float32
+            act, w_of(b), (((1,), (1,)), ((), ())), preferred_element_type=jnp.float32
         )
         row = rows_ref[b]
         acc[row] = acc[row] + back
@@ -105,13 +118,12 @@
         ig_ref[...] = acc[...].astype(ig_ref.dtype)
 
 
-def block_pass(features, hidden_grad, weights, row_ids, col_ids, row_count, low_bit, parts):
+def block_pass(features, hidden_grad, pieces, row_ids, col_ids, row_count, low_bit, parts):
     tokens = features.shape[0]
-    block_count, width, _ = weights.shape
+    width = pieces.shape[-1]
+    block_count = row_ids.shape[0]
     chunk = width // parts
     compact = block_count < row_count
-    same = col_ids[:, None] == col_ids[None, :]
-    first = jnp.argmax(same, axis=1).astype(jnp.int32)
     smem = pl.BlockSpec(memory_space=pltpu.SMEM)
     anyspace = pl.BlockSpec(memory_space=pl.ANY)
     vmem = pl.BlockSpec(memory_space=pltpu.VMEM)
@@ -124,7 +136,7 @@
             half,
             half,
         ),
-        in_specs=[smem, smem, smem, smem, anyspace, anyspace, vmem],
+        in_specs=[smem, smem, smem, anyspace, anyspace, vmem],
         out_specs=(vmem, vmem, vmem),
         scratch_shapes=[
             pltpu.VMEM((block_count, tokens, width), jnp.bfloat16),
@@ -132,6 +144,7 @@
             pltpu.VMEM((block_count, tokens, width), jnp.float32),
             pltpu.VMEM((row_count, tokens, width), jnp.float32),
             pltpu.VMEM((block_count, width, width), jnp.float32),
+            pltpu.SMEM((block_count,), jnp.int32),
             pltpu.SemaphoreType.DMA((2, block_count)),
         ],
         cost_estimate=pl.CostEstimate(
@@ -140,7 +153,7 @@
             bytes_accessed=block_count * width * (4 * tokens + 6 * width)
             + row_count * tokens * width * 2,
         ),
-    )(row_ids, col_ids, first, low_bit, features, hidden_grad, weights)
+    )(row_ids, col_ids, low_bit, features, hidden_grad, pieces)
 
 
 def gather_over(x, axis):
@@ -197,7 +210,6 @@
     pieces = butterfly_gather(fetched, "dp", list(reversed(range(dp_bits))))
     pieces = pieces.reshape((n_dp, per_dp) + payload.shape)
     pieces = jnp.transpose(pieces, (1, 0, 2, 3)).reshape((n_fsdp,) + payload.shape)
-    weights = pieces[:, :weight_rows].reshape(n_fsdp * blocks_dev, block_size, block_size)
     all_indices = (
         pieces[:, weight_rows, : 2 * blocks_dev]
         .reshape(n_fsdp * blocks_dev, 2)
@@ -210,7 +222,7 @@
     input_grad, keep, send = block_pass(
         activations[0].reshape(tok_rows, -1),
         out_grad[0].reshape(tok_rows, -1),
-        weights,
+        pieces,
         row_ids,
         col_ids,
         row_count,

time: 56.2 us -> 54.1 us (0.963)
  local copies, waits for them, and re-layouts: 6.22 us -> 4.9 us
  other arithmetic: 4.84 us -> 4.1 us
    slice x2 -> x0, local copies, waits for them, and re-layouts: 1.04 us -> none  [local(): pieces[:, :weight_rows].reshape(n_fsdp * blocks_dev, block_size, block_size)]
    another operation x2 -> x1, other arithmetic: 0.77 us -> 0.05 us  [the longest x1 0.72 us: block_pass(): first = jnp.argmax(same, axis=1).astype(jnp.int32)]
where the time goes in v16:
time: 54.1 us; the launch traced here: 53.8 us
  starting transfers between devices  23.3 us (43%)
  waiting for transfers between devices  14.2 us (26%)
  Pallas kernels  6.47 us (12%)
  local copies, waits for them, and re-layouts  4.9 us (9%)
  other arithmetic  4.1 us (8%)
  between operations  0.85 us (2%)
    ppermute x6, starting transfers between devices, swapped(): return lax.ppermute(x, axis, [(i, i ^ 1 << bit) for i in range(n)])  16.2 us
    ppermute x6, waiting for transfers between devices, swapped(): return lax.ppermute(x, axis, [(i, i ^ 1 << bit) for i in range(n)])  9.14 us
    pallas_call x1, Pallas kernels, block_pass(): pl.pallas_call(functools.partial(block_kernel, compact, chunk), out_shape...  6.47 us
    ppermute x3, starting transfers between devices, shifted(): return lax.ppermute(x, axis, [(i, (i + k) % n) for i in range(n)])  5.08 us
    ppermute x3, waiting for transfers between devices, shifted(): return lax.ppermute(x, axis, [(i, (i + k) % n) for i in range(n)])  5.07 us
    ppermute x1, starting transfers between devices, passed_along(): return lax.ppermute(block, axis, route)  1.29 us
    scatter x1, local copies, waits for them, and re-layouts, local(): arrived = arrived.at[got_rows].set(got)  1.14 us
    add x1, other arithmetic, local(): held = keep + swapped(send, 'dp', 0)  1.12 us
  transfers between devices with their start and end apart: 11, of which 8 were waited for; matrix products, arithmetic and copies ran while one was open for 8% of the time, Pallas kernels for 0%

profile of v16, /device:TPU:0, one launch (start us, length us, event | category | flops | bytes accessed | tf_op | source)
XLA Modules:
  0.0 53.8 jit_solution(12226701214349832745)
XLA Ops:
  0.6 0.7 %convert_element_type.53 = bf16[1,4,2]{1,2,0:T(2,128)(2,1)S(1)} convert(s32[1,4,2]{1,2,0:T(2,128)} %param.10) | non-fusion elementwise | flops 8 | bytes 48 | tf_op jit(solution)/shard_map/convert_element_type | solution.py:198
  1.3 0.1 copy.12
  1.4 0.1 convert_element_type.54
  1.5 0.9 %fusion.3 = bf16[528,128]{1,0:T(8,128)(2,1)S(1)} fusion(bf16[1,8]{1,0:T(2,128)(2,1)S(1)} %convert_element_type.54, bf16[512,128]{1,0:T(8,128)(2,1)} %bitcast.83), kind=kLoop, calls=%fused_computation.14 | loop fusion | flops 405504 | bytes 266256 | tf_op jit(solution)/shard_map/concatenate | solution.py:200
  2.4 0.7 %collective-permute-start = (bf16[528,128]{1,0:T(8,128)(2,1)S(1)}, bf16[528,128]{1,0:T(8,128)(2,1)S(1)}, u32[]{:S(2)}, u32[]{:S(2)}) collective-permute-start(bf16[528,128]{1,0:T(8,128)(2,1)S(1)} %fusion.3), channel_id=1, source_target_pairs={{0,0},{13,1},{10,2},{7,3},{4,4},{1,5},{14,6},{11,7},{8,8},{5,9},{2... | collective-permute-start | bytes 405512 | tf_op jit(solution)/shard_map/ppermute | solution.py:208
  3.1 12.0 %collective-permute-start.1 = (bf16[1,528,128]{2,1,0:T(8,128)(2,1)S(1)}, bf16[1,528,128]{2,1,0:T(8,128)(2,1)S(1)}, u32[]{:S(2)}, u32[]{:S(2)}) collective-permute-start(bf16[1,528,128]{2,1,0:T(8,128)(2,1)S(1)} %bitcast.72), channel_id=1, source_target_pairs={{0,2},{1,3},{2,0},{3,1},{4,6},{5,7},{6,4},{7,5},{8,10},{9,11},{10,... | collective-permute-start | bytes 405512 | tf_op jit(solution)/shard_map/ppermute | solution.py:25
  15.1 3.0 %collective-permute-done.1 = bf16[1,528,128]{2,1,0:T(8,128)(2,1)S(1)} collective-permute-done((bf16[1,528,128]{2,1,0:T(8,128)(2,1)S(1)}, bf16[1,528,128]{2,1,0:T(8,128)(2,1)S(1)}, u32[]{:S(2)}, u32[]{:S(2)}) %collective-permute-start.1) | collective-permute-done | bytes 135200 | tf_op jit(solution)/shard_map/ppermute | solution.py:25
  18.2 1.5 %collective-permute-done.2 = bf16[2,1,528,128]{3,2,0,1:T(8,128)(2,1)S(1)} collective-permute-done((bf16[2,1,528,128]{3,2,0,1:T(8,128)(2,1)S(1)}, bf16[2,1,528,128]{3,2,0,1:T(8,128)(2,1)S(1)}, u32[]{:S(2)}, u32[]{:S(2)}) %collective-permute-start.2) | collective-permute-done | bytes 270368 | tf_op jit(solution)/shard_map/ppermute | solution.py:25
  19.8 0.1 reshape.420
  19.9 0.8 %slice_reduce_fusion = (s32[16]{0:T(128)}, s32[16]{0:T(128)}) fusion(s32[16,2]{1,0:T(8,128)S(1)} %reshape.420), kind=kLoop, calls=%fused_computation.27 | loop fusion | bytes 256 | tf_op jit(solution)/shard_map/slice | solution.py:220
  20.7 6.5 %shard_map.68 = (bf16[16,128,128]{2,1,0:T(8,128)(2,1)}, f32[16,2,32,128]{3,2,1,0:T(8,128)}, f32[16,2,32,128]{3,2,1,0:T(8,128)}) custom-call(s32[16]{0:T(128)} %get-tuple-element.21.rows_ref, s32[16]{0:T(128)} %get-tuple-element.20.cols_ref, s32[1]{0:T(128)} %bitcast.8.bit_ref, bf16[128,3584]{1,0:T(8,128)(2,1)} %bitcast.69, bf16[128,14336]{1,0:T(8,128)(2,1)} %bitcast.62, ...), custom_call_target="tpu_custom_call" | custom-call | flops 201326592 | bytes 3538944 | tf_op jit(solution)/shard_map/pallas_call | solution.py:132
  27.2 0.2 collective-permute-start.4
  27.4 2.0 %collective-permute-done.4 = f32[16,2,32,128]{3,2,1,0:T(8,128)S(1)} collective-permute-done((f32[16,2,32,128]{3,2,1,0:T(8,128)}, f32[16,2,32,128]{3,2,1,0:T(8,128)S(1)}, u32[]{:S(2)}, u32[]{:S(2)}) %collective-permute-start.4) | collective-permute-done | bytes 524320 | tf_op jit(solution)/shard_map/ppermute | solution.py:25
  29.4 1.1 %add.36 = f32[16,2,32,128]{3,2,1,0:T(8,128)S(1)} add(f32[16,2,32,128]{3,2,1,0:T(8,128)} %get-tuple-element.18, f32[16,2,32,128]{3,2,1,0:T(8,128)S(1)} %collective-permute-done.4) | non-fusion elementwise | flops 131072 | bytes 1572864 | tf_op jit(solution)/shard_map/add | solution.py:247
  30.5 2.1 %collective-permute-start.5 = (bf16[4,4,32,128]{3,2,1,0:T(8,128)(2,1)S(1)}, bf16[4,4,32,128]{3,2,1,0:T(8,128)(2,1)S(1)}, u32[]{:S(2)}, u32[]{:S(2)}) collective-permute-start(bf16[4,4,32,128]{3,2,1,0:T(8,128)(2,1)S(1)} %fusion.4), channel_id=1, source_target_pairs={{0,2},{1,3},{2,0},{3,1},{4,6},{5,7},{6,4},{7,5},{8,10},{9,11},{10,... | collective-permute-start | bytes 393224 | tf_op jit(solution)/shard_map/ppermute | solution.py:25
  32.7 1.3 %collective-permute-start.3 = (bf16[262160]{0:T(1024)(128)(2,1)S(1)}, bf16[262160]{0:T(1024)(128)(2,1)S(1)}, u32[]{:S(2)}, u32[]{:S(2)}) collective-permute-start(bf16[262160]{0:T(1024)(128)(2,1)S(1)} %pad_maximum_fusion), channel_id=1, source_target_pairs={{16,0},{17,1},{18,2},{19,3},{20,4},{21,5},{22,6},{23,7},{24,8},{25... | collective-permute-start | bytes 1572968 | tf_op jit(solution)/shard_map/ppermute | solution.py:15
  34.0 2.5 %collective-permute-done.5 = bf16[4,4,32,128]{3,2,1,0:T(8,128)(2,1)S(1)} collective-permute-done((bf16[4,4,32,128]{3,2,1,0:T(8,128)(2,1)S(1)}, bf16[4,4,32,128]{3,2,1,0:T(8,128)(2,1)S(1)}, u32[]{:S(2)}, u32[]{:S(2)}) %collective-permute-start.5) | collective-permute-done | bytes 131104 | tf_op jit(solution)/shard_map/ppermute | solution.py:25
  36.5 4.4 %collective-permute-start.6 = (bf16[4,32,128]{2,1,0:T(8,128)(2,1)S(1)}, bf16[4,32,128]{2,1,0:T(8,128)(2,1)S(1)}, u32[]{:S(2)}, u32[]{:S(2)}) collective-permute-start(bf16[4,32,128]{2,1,0:T(8,128)(2,1)S(1)} %get-tuple-element.24), channel_id=1, source_target_pairs={{0,12},{4,0},{8,4},{12,8},{1,13},{5,1},{9,5},{13,9},{2,14},{6,2},{... | collective-permute-start | bytes 98312 | tf_op jit(solution)/shard_map/ppermute | solution.py:20
  40.9 0.6 %collective-permute-start.8 = (bf16[4,32,128]{2,1,0:T(8,128)(2,1)S(1)}, bf16[4,32,128]{2,1,0:T(8,128)(2,1)S(1)}, u32[]{:S(2)}, u32[]{:S(2)}) collective-permute-start(bf16[4,32,128]{2,1,0:T(8,128)(2,1)S(1)} %get-tuple-element.25), channel_id=1, source_target_pairs={{0,4},{4,8},{8,12},{12,0},{1,5},{5,9},{9,13},{13,1},{2,6},{6,10},{... | collective-permute-start | bytes 98312 | tf_op jit(solution)/shard_map/ppermute | solution.py:20
  41.6 0.9 %collective-permute-done.6 = bf16[4,32,128]{2,1,0:T(8,128)(2,1)S(1)} collective-permute-done((bf16[4,32,128]{2,1,0:T(8,128)(2,1)S(1)}, bf16[4,32,128]{2,1,0:T(8,128)(2,1)S(1)}, u32[]{:S(2)}, u32[]{:S(2)}) %collective-permute-start.6) | collective-permute-done | bytes 32800 | tf_op jit(solution)/shard_map/ppermute | solution.py:20
  42.5 3.2 %collective-permute-done.7 = bf16[4,32,128]{2,1,0:T(8,128)(2,1)S(1)} collective-permute-done((bf16[4,32,128]{2,1,0:T(8,128)(2,1)S(1)}, bf16[4,32,128]{2,1,0:T(8,128)(2,1)S(1)}, u32[]{:S(2)}, u32[]{:S(2)}) %collective-permute-start.7) | collective-permute-done | bytes 32800 | tf_op jit(solution)/shard_map/ppermute | solution.py:20
  45.7 0.9 %collective-permute-done.8 = bf16[4,32,128]{2,1,0:T(8,128)(2,1)S(1)} collective-permute-done((bf16[4,32,128]{2,1,0:T(8,128)(2,1)S(1)}, bf16[4,32,128]{2,1,0:T(8,128)(2,1)S(1)}, u32[]{:S(2)}, u32[]{:S(2)}) %collective-permute-start.8) | collective-permute-done | bytes 32800 | tf_op jit(solution)/shard_map/ppermute | solution.py:20
  46.6 1.8 %collective-permute-start.9 = (f32[4,32,128]{2,1,0:T(8,128)S(1)}, f32[4,32,128]{2,1,0:T(8,128)S(1)}, u32[]{:S(2)}, u32[]{:S(2)}) collective-permute-start(f32[4,32,128]{2,1,0:T(8,128)S(1)} %fusion.8), channel_id=1, source_target_pairs={{0,2},{1,3},{2,0},{3,1},{4,6},{5,7},{6,4},{7,5},{8,10},{9,11},{10,... | collective-permute-start | bytes 196616 | tf_op jit(solution)/shard_map/ppermute | solution.py:25
  48.5 0.2 broadcast_in_dim.22
  48.7 1.1 %scatter_fusion = bf16[28,128,128]{2,1,0:T(8,128)(2,1)S(1)} fusion(bf16[28,128,128]{2,1,0:T(8,128)(2,1)S(1)} %broadcast_in_dim.22, s32[16]{0:T(128)S(1)} %compare_select_fusion, bf16[16,128,128]{2,1,0:T(8,128)(2,1)S(1)} %bitcast.65), kind=kCustom, calls=%fused_computation.1 | custom fusion | bytes 1572928 | tf_op jit(solution)/shard_map/scatter | solution.py:239
  49.9 0.6 %copy.13 = bf16[128,28,128]{2,1,0:T(8,128)(2,1)S(1)} copy(bf16[128,28,128]{2,0,1:T(8,128)(2,1)S(1)} %bitcast.61) | data formatting | bytes 1835008 | tf_op jit(solution)/shard_map/transpose | solution.py:242
  50.5 0.5 reshape.418
  51.0 0.6 %gather_fusion = bf16[4,32,3584]{2,1,0:T(8,128)(2,1)S(1)} fusion(bf16[4,32,3584]{2,1,0:T(8,128)(2,1)S(1)} %reshape.418, s32[1024]{0:T(1024)S(1)} %pad_clamp_fusion), kind=kCustom, calls=%fused_computation | custom fusion | bytes 1835024 | tf_op jit(solution)/shard_map/jit(_take)/gather | solution.py:245
  51.6 0.1 collective-permute-start.10
  51.7 1.1 %bitcast_select_fusion = bf16[1,4,32,3584]{3,2,1,0:T(8,128)(2,1)} fusion(bf16[4,32,3584]{2,1,0:T(8,128)(2,1)S(1)} %gather_fusion, pred[4]{0:T(512)(128)(4,1)S(1)} %compare_and_fusion), kind=kLoop, calls=%fused_computation.2 | loop fusion | flops 458752 | bytes 1835012 | tf_op jit(solution)/shard_map/jit(_take)/select_n | solution.py:245
  52.8 0.2 collective-permute-done.10
  53.1 0.7 %copy.17 = f32[4,4,32,128]{3,2,1,0:T(8,128)} copy(f32[4,4,32,128]{3,2,0,1:T(8,128)S(1)} %bitcast.68) | data formatting | bytes 524288 | tf_op jit(solution)/shard_map/div | solution.py:262
  (31 shorter events, 0.5 us)
Async XLA Ops:
  2.4 0.7 %collective-permute-start = (bf16[528,128]{1,0:T(8,128)(2,1)S(1)}, bf16[528,128]{1,0:T(8,128)(2,1)S(1)}, u32[]{:S(2)}, u32[]{:S(2)}) collective-permute-start(bf16[528,128]{1,0:T(8,128)(2,1)S(1)} %fusion.3), channel_id=1, source_target_pairs={{0,0},{13,1},{10,2},{7,3},{4,4},{1,5},{14,6},{11,7},{8,8},{5,9},{2... | collective-permute-start | bytes 405512 | tf_op jit(solution)/shard_map/ppermute | solution.py:208
  3.1 15.0 %collective-permute-start.1 = (bf16[1,528,128]{2,1,0:T(8,128)(2,1)S(1)}, bf16[1,528,128]{2,1,0:T(8,128)(2,1)S(1)}, u32[]{:S(2)}, u32[]{:S(2)}) collective-permute-start(bf16[1,528,128]{2,1,0:T(8,128)(2,1)S(1)} %bitcast.72), channel_id=1, source_target_pairs={{0,2},{1,3},{2,0},{3,1},{4,6},{5,7},{6,4},{7,5},{8,10},{9,11},{10,... | collective-permute-start | bytes 405512 | tf_op jit(solution)/shard_map/ppermute | solution.py:25
  18.1 1.6 %collective-permute-start.2 = (bf16[2,1,528,128]{3,2,0,1:T(8,128)(2,1)S(1)}, bf16[2,1,528,128]{3,2,0,1:T(8,128)(2,1)S(1)}, u32[]{:S(2)}, u32[]{:S(2)}) collective-permute-start(bf16[2,1,528,128]{3,2,0,1:T(8,128)(2,1)S(1)} %maximum_select_fusion.2), channel_id=1, source_target_pairs={{0,1},{1,0},{2,3},{3,2},{4,5},{5,4},{6,7},{7,6},{8,9},{9,8},{10,11... | collective-permute-start | bytes 811016 | tf_op jit(solution)/shard_map/ppermute | solution.py:25
  19.8 0.9 %copy-start = (bf16[2,2,1,528,128]{4,3,0,1,2:T(8,128)(2,1)}, bf16[2,2,1,528,128]{4,3,0,1,2:T(8,128)(2,1)S(1)}, u32[]{:S(2)}) copy-start(bf16[2,2,1,528,128]{4,3,0,1,2:T(8,128)(2,1)S(1)} %maximum_select_fusion) | copy-start | bytes 1622020
  20.7 6.7 %copy-start.3 = (s32[4]{0:T(128)S(1)}, s32[4]{0:T(128)}, u32[]{:S(2)}) copy-start(s32[4]{0:T(128)} %param.11) | copy-start | bytes 52
  20.7 6.7 %copy-start.2 = (s32[16]{0:T(128)S(1)}, s32[16]{0:T(128)}, u32[]{:S(2)}) copy-start(s32[16]{0:T(128)} %get-tuple-element.21.rows_ref) | copy-start | bytes 196
  27.2 5.4 %copy-start.1 = (bf16[16,128,128]{2,1,0:T(8,128)(2,1)S(1)}, bf16[16,128,128]{2,1,0:T(8,128)(2,1)}, u32[]{:S(2)}) copy-start(bf16[16,128,128]{2,1,0:T(8,128)(2,1)} %get-tuple-element.17) | copy-start | bytes 1572868
  27.2 2.2 %collective-permute-start.4 = (f32[16,2,32,128]{3,2,1,0:T(8,128)}, f32[16,2,32,128]{3,2,1,0:T(8,128)S(1)}, u32[]{:S(2)}, u32[]{:S(2)}) collective-permute-start(f32[16,2,32,128]{3,2,1,0:T(8,128)} %get-tuple-element.19), channel_id=1, source_target_pairs={{0,1},{1,0},{2,3},{3,2},{4,5},{5,4},{6,7},{7,6},{8,9},{9,8},{10,11... | collective-permute-start | bytes 1572872 | tf_op jit(solution)/shard_map/ppermute | solution.py:25
  30.5 5.9 %collective-permute-start.5 = (bf16[4,4,32,128]{3,2,1,0:T(8,128)(2,1)S(1)}, bf16[4,4,32,128]{3,2,1,0:T(8,128)(2,1)S(1)}, u32[]{:S(2)}, u32[]{:S(2)}) collective-permute-start(bf16[4,4,32,128]{3,2,1,0:T(8,128)(2,1)S(1)} %fusion.4), channel_id=1, source_target_pairs={{0,2},{1,3},{2,0},{3,1},{4,6},{5,7},{6,4},{7,5},{8,10},{9,11},{10,... | collective-permute-start | bytes 393224 | tf_op jit(solution)/shard_map/ppermute | solution.py:25
  32.7 15.8 %collective-permute-start.3 = (bf16[262160]{0:T(1024)(128)(2,1)S(1)}, bf16[262160]{0:T(1024)(128)(2,1)S(1)}, u32[]{:S(2)}, u32[]{:S(2)}) collective-permute-start(bf16[262160]{0:T(1024)(128)(2,1)S(1)} %pad_maximum_fusion), channel_id=1, source_target_pairs={{16,0},{17,1},{18,2},{19,3},{20,4},{21,5},{22,6},{23,7},{24,8},{25... | collective-permute-start | bytes 1572968 | tf_op jit(solution)/shard_map/ppermute | solution.py:15
  36.5 6.0 %collective-permute-start.6 = (bf16[4,32,128]{2,1,0:T(8,128)(2,1)S(1)}, bf16[4,32,128]{2,1,0:T(8,128)(2,1)S(1)}, u32[]{:S(2)}, u32[]{:S(2)}) collective-permute-start(bf16[4,32,128]{2,1,0:T(8,128)(2,1)S(1)} %get-tuple-element.24), channel_id=1, source_target_pairs={{0,12},{4,0},{8,4},{12,8},{1,13},{5,1},{9,5},{13,9},{2,14},{6,2},{... | collective-permute-start | bytes 98312 | tf_op jit(solution)/shard_map/ppermute | solution.py:20
  40.9 4.8 %collective-permute-start.7 = (bf16[4,32,128]{2,1,0:T(8,128)(2,1)S(1)}, bf16[4,32,128]{2,1,0:T(8,128)(2,1)S(1)}, u32[]{:S(2)}, u32[]{:S(2)}) collective-permute-start(bf16[4,32,128]{2,1,0:T(8,128)(2,1)S(1)} %get-tuple-element.26), channel_id=1, source_target_pairs={{0,8},{4,12},{8,0},{12,4},{1,9},{5,13},{9,1},{13,5},{2,10},{6,14},... | collective-permute-start | bytes 98312 | tf_op jit(solution)/shard_map/ppermute | solution.py:20
  40.9 5.7 %collective-permute-start.8 = (bf16[4,32,128]{2,1,0:T(8,128)(2,1)S(1)}, bf16[4,32,128]{2,1,0:T(8,128)(2,1)S(1)}, u32[]{:S(2)}, u32[]{:S(2)}) collective-permute-start(bf16[4,32,128]{2,1,0:T(8,128)(2,1)S(1)} %get-tuple-element.25), channel_id=1, source_target_pairs={{0,4},{4,8},{8,12},{12,0},{1,5},{5,9},{9,13},{13,1},{2,6},{6,10},{... | collective-permute-start | bytes 98312 | tf_op jit(solution)/shard_map/ppermute | solution.py:20
  46.6 4.9 %collective-permute-start.9 = (f32[4,32,128]{2,1,0:T(8,128)S(1)}, f32[4,32,128]{2,1,0:T(8,128)S(1)}, u32[]{:S(2)}, u32[]{:S(2)}) collective-permute-start(f32[4,32,128]{2,1,0:T(8,128)S(1)} %fusion.8), channel_id=1, source_target_pairs={{0,2},{1,3},{2,0},{3,1},{4,6},{5,7},{6,4},{7,5},{8,10},{9,11},{10,... | collective-permute-start | bytes 196616 | tf_op jit(solution)/shard_map/ppermute | solution.py:25
  51.6 1.4 %collective-permute-start.10 = (f32[2,4,32,128]{3,2,1,0:T(8,128)S(1)}, f32[2,4,32,128]{3,2,1,0:T(8,128)S(1)}, u32[]{:S(2)}, u32[]{:S(2)}) collective-permute-start(f32[2,4,32,128]{3,2,1,0:T(8,128)S(1)} %maximum_select_fusion.4), channel_id=1, source_target_pairs={{0,1},{1,0},{2,3},{3,2},{4,5},{5,4},{6,7},{7,6},{8,9},{9,8},{10,11... | collective-permute-start | bytes 393224 | tf_op jit(solution)/shard_map/ppermute | solution.py:25

commit v17 on v16

--- a/solution.py
+++ b/solution.py
@@ -91,6 +91,7 @@
             pr[first] = pr[first] + pr[b]
 
     mine = bit_ref[0]
+    high = bit_ref[1]
 
     @block_loop
     def _(b):
@@ -105,8 +106,9 @@
             xs[b], act, (((0,), (0,)), ((), ())), preferred_element_type=jnp.float32
         )
         for h in range(halves):
-            kept = pl.multiple_of((2 * h + mine) * chunk, chunk)
-            sent = pl.multiple_of((2 * h + 1 - mine) * chunk, chunk)
+            half = h ^ high
+            kept = pl.multiple_of((2 * half + mine) * chunk, chunk)
+            sent = pl.multiple_of((2 * half + 1 - mine) * chunk, chunk)
             keep_ref[b, h] = pgs[b, pl.ds(kept, chunk), :]
             send_ref[b, h] = pgs[b, pl.ds(sent, chunk), :]
 
@@ -218,7 +220,8 @@
 
     row_ids = all_indices[:, 0]
     col_ids = all_indices[:, 1]
-    low_bit = (me_dp & 1).astype(jnp.int32).reshape(1)
+    assert n_dp == 4
+    low_bit = jnp.stack([me_dp & 1, (me_dp >> 1) & 1]).astype(jnp.int32)
     input_grad, keep, send = block_pass(
         activations[0].reshape(tok_rows, -1),
         out_grad[0].reshape(tok_rows, -1),
@@ -245,13 +248,10 @@
     received = jnp.take(arrived, order, axis=0)
 
     held = keep + swapped(send, "dp", 0)
-    held = held.reshape((n_fsdp, blocks_dev) + (2,) * (dp_bits - 1) + (chunk, block_size))
-    for bit in range(1, dp_bits):
-        axis_at = 2 + (dp_bits - 1 - bit)
-        mine = (me_dp >> bit) & 1
-        keep = lax.dynamic_index_in_dim(held, mine, axis_at, keepdims=False)
-        send = lax.dynamic_index_in_dim(held, 1 - mine, axis_at, keepdims=False)
-        held = keep + swapped(send.astype(jnp.bfloat16), "dp", bit).astype(jnp.float32)
+    held = held.reshape((n_fsdp, blocks_dev, 2, chunk, block_size))
+    held = held[:, :, 0] + swapped(held[:, :, 1].astype(jnp.bfloat16), "dp", 1).astype(
+        jnp.float32
+    )
     owned = held[0]
     for k in range(1, n_fsdp):
         owned = owned + shifted(held[k].astype(jnp.bfloat16), "fsdp", -k).astype(jnp.float32)

time: 54.1 us -> 54.1 us (level)
  other arithmetic: 4.1 us -> 4.75 us
  waiting for transfers between devices: 14.2 us -> 13.6 us
    ppermute x6, waiting for transfers between devices: 9.14 us -> 8.49 us  [swapped(): return lax.ppermute(x, axis, [(i, i ^ 1 << bit) for i in range(n)])]
    another operation x1 -> x2, other arithmetic: 0.05 us -> 0.7 us  [the longest x1 0.65 us: local(): low_bit = jnp.stack([me_dp & 1, me_dp >> 1 & 1]).astype(jnp.int32)]
  transfers between devices with their start and end apart: 11 -> 11, of which waited for: 8 -> 8; matrix products, arithmetic and copies ran while one was open for 8% -> 9% of each run, Pallas kernels for 0% -> 0%
where the time goes in v17:
time: 54.1 us; the launch traced here: 53.8 us
  starting transfers between devices  23.3 us (43%)
  waiting for transfers between devices  13.6 us (25%)
  Pallas kernels  6.47 us (12%)
  local copies, waits for them, and re-layouts  4.89 us (9%)
  other arithmetic  4.75 us (9%)
  between operations  0.84 us (2%)
    ppermute x6, starting transfers between devices, swapped(): return lax.ppermute(x, axis, [(i, i ^ 1 << bit) for i in range(n)])  16.3 us
    ppermute x6, waiting for transfers between devices, swapped(): return lax.ppermute(x, axis, [(i, i ^ 1 << bit) for i in range(n)])  8.49 us
    pallas_call x1, Pallas kernels, block_pass(): pl.pallas_call(functools.partial(block_kernel, compact, chunk), out_shape...  6.47 us
    ppermute x3, starting transfers between devices, shifted(): return lax.ppermute(x, axis, [(i, (i + k) % n) for i in range(n)])  5.08 us
    ppermute x3, waiting for transfers between devices, shifted(): return lax.ppermute(x, axis, [(i, (i + k) % n) for i in range(n)])  5.07 us
    ppermute x1, starting transfers between devices, passed_along(): return lax.ppermute(block, axis, route)  1.29 us
    scatter x1, local copies, waits for them, and re-layouts, local(): arrived = arrived.at[got_rows].set(got)  1.14 us
    add x1, other arithmetic, local(): held = keep + swapped(send, 'dp', 0)  1.12 us
  transfers between devices with their start and end apart: 11, of which 8 were waited for; matrix products, arithmetic and copies ran while one was open for 9% of the time, Pallas kernels for 0%

profile of v17, /device:TPU:0, one launch (start us, length us, event | category | flops | bytes accessed | tf_op | source)
XLA Modules:
  0.0 53.8 jit_solution(6683939579377539077)
XLA Ops:
  0.6 0.7 %convert_element_type.51 = bf16[1,4,2]{1,2,0:T(2,128)(2,1)S(1)} convert(s32[1,4,2]{1,2,0:T(2,128)} %param.10) | non-fusion elementwise | flops 8 | bytes 48 | tf_op jit(solution)/shard_map/convert_element_type | solution.py:200
  1.3 0.1 copy.14
  1.4 0.1 convert_element_type.52
  1.5 0.9 %fusion.4 = bf16[528,128]{1,0:T(8,128)(2,1)S(1)} fusion(bf16[1,8]{1,0:T(2,128)(2,1)S(1)} %convert_element_type.52, bf16[512,128]{1,0:T(8,128)(2,1)} %bitcast.82), kind=kLoop, calls=%fused_computation.15 | loop fusion | flops 405504 | bytes 266256 | tf_op jit(solution)/shard_map/concatenate | solution.py:202
  2.4 0.7 %collective-permute-start = (bf16[528,128]{1,0:T(8,128)(2,1)S(1)}, bf16[528,128]{1,0:T(8,128)(2,1)S(1)}, u32[]{:S(2)}, u32[]{:S(2)}) collective-permute-start(bf16[528,128]{1,0:T(8,128)(2,1)S(1)} %fusion.4), channel_id=1, source_target_pairs={{0,0},{13,1},{10,2},{7,3},{4,4},{1,5},{14,6},{11,7},{8,8},{5,9},{2... | collective-permute-start | bytes 405512 | tf_op jit(solution)/shard_map/ppermute | solution.py:210
  3.1 12.0 %collective-permute-start.1 = (bf16[1,528,128]{2,1,0:T(8,128)(2,1)S(1)}, bf16[1,528,128]{2,1,0:T(8,128)(2,1)S(1)}, u32[]{:S(2)}, u32[]{:S(2)}) collective-permute-start(bf16[1,528,128]{2,1,0:T(8,128)(2,1)S(1)} %bitcast.71), channel_id=1, source_target_pairs={{0,2},{1,3},{2,0},{3,1},{4,6},{5,7},{6,4},{7,5},{8,10},{9,11},{10,... | collective-permute-start | bytes 405512 | tf_op jit(solution)/shard_map/ppermute | solution.py:25
  15.1 3.0 %collective-permute-done.1 = bf16[1,528,128]{2,1,0:T(8,128)(2,1)S(1)} collective-permute-done((bf16[1,528,128]{2,1,0:T(8,128)(2,1)S(1)}, bf16[1,528,128]{2,1,0:T(8,128)(2,1)S(1)}, u32[]{:S(2)}, u32[]{:S(2)}) %collective-permute-start.1) | collective-permute-done | bytes 135200 | tf_op jit(solution)/shard_map/ppermute | solution.py:25
  18.2 0.7 %pad_add_fusion.bit_ref = s32[2]{0:T(128)} fusion(s32[1]{0:T(128)} %bitcast.9, s32[1]{0:T(128)} %bitcast.8), kind=kLoop, calls=%fused_computation.37 | loop fusion | flops 2 | bytes 16 | tf_op jit(solution)/shard_map/stack | solution.py:224
  18.9 0.8 %collective-permute-done.2 = bf16[2,1,528,128]{3,2,0,1:T(8,128)(2,1)S(1)} collective-permute-done((bf16[2,1,528,128]{3,2,0,1:T(8,128)(2,1)S(1)}, bf16[2,1,528,128]{3,2,0,1:T(8,128)(2,1)S(1)}, u32[]{:S(2)}, u32[]{:S(2)}) %collective-permute-start.2) | collective-permute-done | bytes 270368 | tf_op jit(solution)/shard_map/ppermute | solution.py:25
  19.8 0.1 reshape.416
  19.9 0.8 %slice_reduce_fusion = (s32[16]{0:T(128)}, s32[16]{0:T(128)}) fusion(s32[16,2]{1,0:T(8,128)S(1)} %reshape.416), kind=kLoop, calls=%fused_computation.28 | loop fusion | bytes 256 | tf_op jit(solution)/shard_map/slice | solution.py:222
  20.7 6.5 %shard_map.68 = (bf16[16,128,128]{2,1,0:T(8,128)(2,1)}, f32[16,2,32,128]{3,2,1,0:T(8,128)}, f32[16,2,32,128]{3,2,1,0:T(8,128)}) custom-call(s32[16]{0:T(128)} %get-tuple-element.21.rows_ref, s32[16]{0:T(128)} %get-tuple-element.20.cols_ref, s32[2]{0:T(128)} %pad_add_fusion.bit_ref, bf16[128,3584]{1,0:T(8,128)(2,1)} %bitcast.68, bf16[128,14336]{1,0:T(8,128)(2,1)} %bitcast.61, ...), custom_call_target="tpu_custom_call" | custom-call | flops 201326592 | bytes 3538944 | tf_op jit(solution)/shard_map/pallas_call | solution.py:134
  27.2 0.2 collective-permute-start.4
  27.4 1.9 %collective-permute-done.4 = f32[16,2,32,128]{3,2,1,0:T(8,128)S(1)} collective-permute-done((f32[16,2,32,128]{3,2,1,0:T(8,128)}, f32[16,2,32,128]{3,2,1,0:T(8,128)S(1)}, u32[]{:S(2)}, u32[]{:S(2)}) %collective-permute-start.4) | collective-permute-done | bytes 524320 | tf_op jit(solution)/shard_map/ppermute | solution.py:25
  29.4 1.1 %add.28 = f32[16,2,32,128]{3,2,1,0:T(8,128)S(1)} add(f32[16,2,32,128]{3,2,1,0:T(8,128)} %get-tuple-element.18, f32[16,2,32,128]{3,2,1,0:T(8,128)S(1)} %collective-permute-done.4) | non-fusion elementwise | flops 131072 | bytes 1572864 | tf_op jit(solution)/shard_map/add | solution.py:250
  30.5 2.1 %collective-permute-start.5 = (bf16[4,4,32,128]{3,2,1,0:T(8,128)(2,1)S(1)}, bf16[4,4,32,128]{3,2,1,0:T(8,128)(2,1)S(1)}, u32[]{:S(2)}, u32[]{:S(2)}) collective-permute-start(bf16[4,4,32,128]{3,2,1,0:T(8,128)(2,1)S(1)} %fusion.5), channel_id=1, source_target_pairs={{0,2},{1,3},{2,0},{3,1},{4,6},{5,7},{6,4},{7,5},{8,10},{9,11},{10,... | collective-permute-start | bytes 393224 | tf_op jit(solution)/shard_map/ppermute | solution.py:25
  32.7 1.3 %collective-permute-start.3 = (bf16[262160]{0:T(1024)(128)(2,1)S(1)}, bf16[262160]{0:T(1024)(128)(2,1)S(1)}, u32[]{:S(2)}, u32[]{:S(2)}) collective-permute-start(bf16[262160]{0:T(1024)(128)(2,1)S(1)} %pad_maximum_fusion), channel_id=1, source_target_pairs={{16,0},{17,1},{18,2},{19,3},{20,4},{21,5},{22,6},{23,7},{24,8},{25... | collective-permute-start | bytes 1572968 | tf_op jit(solution)/shard_map/ppermute | solution.py:15
  34.0 2.5 %collective-permute-done.5 = bf16[4,4,32,128]{3,2,1,0:T(8,128)(2,1)S(1)} collective-permute-done((bf16[4,4,32,128]{3,2,1,0:T(8,128)(2,1)S(1)}, bf16[4,4,32,128]{3,2,1,0:T(8,128)(2,1)S(1)}, u32[]{:S(2)}, u32[]{:S(2)}) %collective-permute-start.5) | collective-permute-done | bytes 131104 | tf_op jit(solution)/shard_map/ppermute | solution.py:25
  36.5 4.4 %collective-permute-start.6 = (bf16[4,32,128]{2,1,0:T(8,128)(2,1)S(1)}, bf16[4,32,128]{2,1,0:T(8,128)(2,1)S(1)}, u32[]{:S(2)}, u32[]{:S(2)}) collective-permute-start(bf16[4,32,128]{2,1,0:T(8,128)(2,1)S(1)} %get-tuple-element.24), channel_id=1, source_target_pairs={{0,12},{4,0},{8,4},{12,8},{1,13},{5,1},{9,5},{13,9},{2,14},{6,2},{... | collective-permute-start | bytes 98312 | tf_op jit(solution)/shard_map/ppermute | solution.py:20
  40.9 0.6 %collective-permute-start.8 = (bf16[4,32,128]{2,1,0:T(8,128)(2,1)S(1)}, bf16[4,32,128]{2,1,0:T(8,128)(2,1)S(1)}, u32[]{:S(2)}, u32[]{:S(2)}) collective-permute-start(bf16[4,32,128]{2,1,0:T(8,128)(2,1)S(1)} %get-tuple-element.25), channel_id=1, source_target_pairs={{0,4},{4,8},{8,12},{12,0},{1,5},{5,9},{9,13},{13,1},{2,6},{6,10},{... | collective-permute-start | bytes 98312 | tf_op jit(solution)/shard_map/ppermute | solution.py:20
  41.6 0.9 %collective-permute-done.6 = bf16[4,32,128]{2,1,0:T(8,128)(2,1)S(1)} collective-permute-done((bf16[4,32,128]{2,1,0:T(8,128)(2,1)S(1)}, bf16[4,32,128]{2,1,0:T(8,128)(2,1)S(1)}, u32[]{:S(2)}, u32[]{:S(2)}) %collective-permute-start.6) | collective-permute-done | bytes 32800 | tf_op jit(solution)/shard_map/ppermute | solution.py:20
  42.5 3.2 %collective-permute-done.7 = bf16[4,32,128]{2,1,0:T(8,128)(2,1)S(1)} collective-permute-done((bf16[4,32,128]{2,1,0:T(8,128)(2,1)S(1)}, bf16[4,32,128]{2,1,0:T(8,128)(2,1)S(1)}, u32[]{:S(2)}, u32[]{:S(2)}) %collective-permute-start.7) | collective-permute-done | bytes 32800 | tf_op jit(solution)/shard_map/ppermute | solution.py:20
  45.8 0.9 %collective-permute-done.8 = bf16[4,32,128]{2,1,0:T(8,128)(2,1)S(1)} collective-permute-done((bf16[4,32,128]{2,1,0:T(8,128)(2,1)S(1)}, bf16[4,32,128]{2,1,0:T(8,128)(2,1)S(1)}, u32[]{:S(2)}, u32[]{:S(2)}) %collective-permute-start.8) | collective-permute-done | bytes 32800 | tf_op jit(solution)/shard_map/ppermute | solution.py:20
  46.7 1.8 %collective-permute-start.9 = (f32[4,32,128]{2,1,0:T(8,128)S(1)}, f32[4,32,128]{2,1,0:T(8,128)S(1)}, u32[]{:S(2)}, u32[]{:S(2)}) collective-permute-start(f32[4,32,128]{2,1,0:T(8,128)S(1)} %fusion.9), channel_id=1, source_target_pairs={{0,2},{1,3},{2,0},{3,1},{4,6},{5,7},{6,4},{7,5},{8,10},{9,11},{10,... | collective-permute-start | bytes 196616 | tf_op jit(solution)/shard_map/ppermute | solution.py:25
  48.5 0.2 broadcast_in_dim.22
  48.7 1.1 %scatter_fusion = bf16[28,128,128]{2,1,0:T(8,128)(2,1)S(1)} fusion(bf16[28,128,128]{2,1,0:T(8,128)(2,1)S(1)} %broadcast_in_dim.22, s32[16]{0:T(128)S(1)} %compare_select_fusion, bf16[16,128,128]{2,1,0:T(8,128)(2,1)S(1)} %bitcast.64), kind=kCustom, calls=%fused_computation.1 | custom fusion | bytes 1572928 | tf_op jit(solution)/shard_map/scatter | solution.py:242
  49.9 0.6 %copy.15 = bf16[128,28,128]{2,1,0:T(8,128)(2,1)S(1)} copy(bf16[128,28,128]{2,0,1:T(8,128)(2,1)S(1)} %bitcast.60) | data formatting | bytes 1835008 | tf_op jit(solution)/shard_map/transpose | solution.py:245
  50.5 0.5 reshape.414
  51.0 0.6 %gather_fusion = bf16[4,32,3584]{2,1,0:T(8,128)(2,1)S(1)} fusion(bf16[4,32,3584]{2,1,0:T(8,128)(2,1)S(1)} %reshape.414, s32[1024]{0:T(1024)S(1)} %pad_clamp_fusion), kind=kCustom, calls=%fused_computation | custom fusion | bytes 1835024 | tf_op jit(solution)/shard_map/jit(_take)/gather | solution.py:248
  51.7 1.1 %bitcast_select_fusion = bf16[1,4,32,3584]{3,2,1,0:T(8,128)(2,1)} fusion(bf16[4,32,3584]{2,1,0:T(8,128)(2,1)S(1)} %gather_fusion, pred[4]{0:T(512)(128)(4,1)S(1)} %compare_and_fusion), kind=kLoop, calls=%fused_computation.2 | loop fusion | flops 458752 | bytes 1835012 | tf_op jit(solution)/shard_map/jit(_take)/select_n | solution.py:248
  52.8 0.2 collective-permute-done.10
  53.1 0.7 %copy.20 = f32[4,4,32,128]{3,2,1,0:T(8,128)} copy(f32[4,4,32,128]{3,2,0,1:T(8,128)S(1)} %bitcast.67) | data formatting | bytes 524288 | tf_op jit(solution)/shard_map/div | solution.py:262
  (32 shorter events, 0.5 us)
Async XLA Ops:
  2.4 0.7 %collective-permute-start = (bf16[528,128]{1,0:T(8,128)(2,1)S(1)}, bf16[528,128]{1,0:T(8,128)(2,1)S(1)}, u32[]{:S(2)}, u32[]{:S(2)}) collective-permute-start(bf16[528,128]{1,0:T(8,128)(2,1)S(1)} %fusion.4), channel_id=1, source_target_pairs={{0,0},{13,1},{10,2},{7,3},{4,4},{1,5},{14,6},{11,7},{8,8},{5,9},{2... | collective-permute-start | bytes 405512 | tf_op jit(solution)/shard_map/ppermute | solution.py:210
  3.1 15.0 %collective-permute-start.1 = (bf16[1,528,128]{2,1,0:T(8,128)(2,1)S(1)}, bf16[1,528,128]{2,1,0:T(8,128)(2,1)S(1)}, u32[]{:S(2)}, u32[]{:S(2)}) collective-permute-start(bf16[1,528,128]{2,1,0:T(8,128)(2,1)S(1)} %bitcast.71), channel_id=1, source_target_pairs={{0,2},{1,3},{2,0},{3,1},{4,6},{5,7},{6,4},{7,5},{8,10},{9,11},{10,... | collective-permute-start | bytes 405512 | tf_op jit(solution)/shard_map/ppermute | solution.py:25
  18.1 1.6 %collective-permute-start.2 = (bf16[2,1,528,128]{3,2,0,1:T(8,128)(2,1)S(1)}, bf16[2,1,528,128]{3,2,0,1:T(8,128)(2,1)S(1)}, u32[]{:S(2)}, u32[]{:S(2)}) collective-permute-start(bf16[2,1,528,128]{3,2,0,1:T(8,128)(2,1)S(1)} %maximum_select_fusion.2), channel_id=1, source_target_pairs={{0,1},{1,0},{2,3},{3,2},{4,5},{5,4},{6,7},{7,6},{8,9},{9,8},{10,11... | collective-permute-start | bytes 811016 | tf_op jit(solution)/shard_map/ppermute | solution.py:25
  19.8 0.9 %copy-start = (bf16[2,2,1,528,128]{4,3,0,1,2:T(8,128)(2,1)}, bf16[2,2,1,528,128]{4,3,0,1,2:T(8,128)(2,1)S(1)}, u32[]{:S(2)}) copy-start(bf16[2,2,1,528,128]{4,3,0,1,2:T(8,128)(2,1)S(1)} %maximum_select_fusion) | copy-start | bytes 1622020
  20.7 6.7 %copy-start.3 = (s32[4]{0:T(128)S(1)}, s32[4]{0:T(128)}, u32[]{:S(2)}) copy-start(s32[4]{0:T(128)} %param.11) | copy-start | bytes 52
  20.7 6.7 %copy-start.2 = (s32[16]{0:T(128)S(1)}, s32[16]{0:T(128)}, u32[]{:S(2)}) copy-start(s32[16]{0:T(128)} %get-tuple-element.21.rows_ref) | copy-start | bytes 196
  27.2 5.5 %copy-start.1 = (bf16[16,128,128]{2,1,0:T(8,128)(2,1)S(1)}, bf16[16,128,128]{2,1,0:T(8,128)(2,1)}, u32[]{:S(2)}) copy-start(bf16[16,128,128]{2,1,0:T(8,128)(2,1)} %get-tuple-element.17) | copy-start | bytes 1572868
  27.2 2.2 %collective-permute-start.4 = (f32[16,2,32,128]{3,2,1,0:T(8,128)}, f32[16,2,32,128]{3,2,1,0:T(8,128)S(1)}, u32[]{:S(2)}, u32[]{:S(2)}) collective-permute-start(f32[16,2,32,128]{3,2,1,0:T(8,128)} %get-tuple-element.19), channel_id=1, source_target_pairs={{0,1},{1,0},{2,3},{3,2},{4,5},{5,4},{6,7},{7,6},{8,9},{9,8},{10,11... | collective-permute-start | bytes 1572872 | tf_op jit(solution)/shard_map/ppermute | solution.py:25
  30.5 5.9 %collective-permute-start.5 = (bf16[4,4,32,128]{3,2,1,0:T(8,128)(2,1)S(1)}, bf16[4,4,32,128]{3,2,1,0:T(8,128)(2,1)S(1)}, u32[]{:S(2)}, u32[]{:S(2)}) collective-permute-start(bf16[4,4,32,128]{3,2,1,0:T(8,128)(2,1)S(1)} %fusion.5), channel_id=1, source_target_pairs={{0,2},{1,3},{2,0},{3,1},{4,6},{5,7},{6,4},{7,5},{8,10},{9,11},{10,... | collective-permute-start | bytes 393224 | tf_op jit(solution)/shard_map/ppermute | solution.py:25
  32.7 15.8 %collective-permute-start.3 = (bf16[262160]{0:T(1024)(128)(2,1)S(1)}, bf16[262160]{0:T(1024)(128)(2,1)S(1)}, u32[]{:S(2)}, u32[]{:S(2)}) collective-permute-start(bf16[262160]{0:T(1024)(128)(2,1)S(1)} %pad_maximum_fusion), channel_id=1, source_target_pairs={{16,0},{17,1},{18,2},{19,3},{20,4},{21,5},{22,6},{23,7},{24,8},{25... | collective-permute-start | bytes 1572968 | tf_op jit(solution)/shard_map/ppermute | solution.py:15
  36.5 6.0 %collective-permute-start.6 = (bf16[4,32,128]{2,1,0:T(8,128)(2,1)S(1)}, bf16[4,32,128]{2,1,0:T(8,128)(2,1)S(1)}, u32[]{:S(2)}, u32[]{:S(2)}) collective-permute-start(bf16[4,32,128]{2,1,0:T(8,128)(2,1)S(1)} %get-tuple-element.24), channel_id=1, source_target_pairs={{0,12},{4,0},{8,4},{12,8},{1,13},{5,1},{9,5},{13,9},{2,14},{6,2},{... | collective-permute-start | bytes 98312 | tf_op jit(solution)/shard_map/ppermute | solution.py:20
  40.9 4.8 %collective-permute-start.7 = (bf16[4,32,128]{2,1,0:T(8,128)(2,1)S(1)}, bf16[4,32,128]{2,1,0:T(8,128)(2,1)S(1)}, u32[]{:S(2)}, u32[]{:S(2)}) collective-permute-start(bf16[4,32,128]{2,1,0:T(8,128)(2,1)S(1)} %get-tuple-element.26), channel_id=1, source_target_pairs={{0,8},{4,12},{8,0},{12,4},{1,9},{5,13},{9,1},{13,5},{2,10},{6,14},... | collective-permute-start | bytes 98312 | tf_op jit(solution)/shard_map/ppermute | solution.py:20
  40.9 5.7 %collective-permute-start.8 = (bf16[4,32,128]{2,1,0:T(8,128)(2,1)S(1)}, bf16[4,32,128]{2,1,0:T(8,128)(2,1)S(1)}, u32[]{:S(2)}, u32[]{:S(2)}) collective-permute-start(bf16[4,32,128]{2,1,0:T(8,128)(2,1)S(1)} %get-tuple-element.25), channel_id=1, source_target_pairs={{0,4},{4,8},{8,12},{12,0},{1,5},{5,9},{9,13},{13,1},{2,6},{6,10},{... | collective-permute-start | bytes 98312 | tf_op jit(solution)/shard_map/ppermute | solution.py:20
  46.7 4.9 %collective-permute-start.9 = (f32[4,32,128]{2,1,0:T(8,128)S(1)}, f32[4,32,128]{2,1,0:T(8,128)S(1)}, u32[]{:S(2)}, u32[]{:S(2)}) collective-permute-start(f32[4,32,128]{2,1,0:T(8,128)S(1)} %fusion.9), channel_id=1, source_target_pairs={{0,2},{1,3},{2,0},{3,1},{4,6},{5,7},{6,4},{7,5},{8,10},{9,11},{10,... | collective-permute-start | bytes 196616 | tf_op jit(solution)/shard_map/ppermute | solution.py:25
  51.6 1.4 %collective-permute-start.10 = (f32[2,4,32,128]{3,2,1,0:T(8,128)S(1)}, f32[2,4,32,128]{3,2,1,0:T(8,128)S(1)}, u32[]{:S(2)}, u32[]{:S(2)}) collective-permute-start(f32[2,4,32,128]{3,2,1,0:T(8,128)S(1)} %maximum_select_fusion.4), channel_id=1, source_target_pairs={{0,1},{1,0},{2,3},{3,2},{4,5},{5,4},{6,7},{7,6},{8,9},{9,8},{10,11... | collective-permute-start | bytes 393224 | tf_op jit(solution)/shard_map/ppermute | solution.py:25

commit v18 on v16

--- a/solution.py
+++ b/solution.py
@@ -255,11 +255,11 @@
     owned = held[0]
     for k in range(1, n_fsdp):
         owned = owned + shifted(held[k].astype(jnp.bfloat16), "fsdp", -k).astype(jnp.float32)
-    full = butterfly_gather(owned, "dp", list(reversed(range(dp_bits))))
+    grad_scale = jnp.sqrt(jnp.float32(tok_rows * n_fsdp * n_dp))
+    full = butterfly_gather(owned / grad_scale, "dp", list(reversed(range(dp_bits))))
     full = full.reshape((n_dp, blocks_dev, chunk, block_size))
     full = jnp.transpose(full, (1, 0, 2, 3)).reshape(blocks_dev, block_size, block_size)
-    grad_scale = jnp.sqrt(jnp.float32(tok_rows * n_fsdp * n_dp))
-    return (received[None], (full / grad_scale)[None])
+    return (received[None], full[None])
 
 
 def solution(mesh):

time: 54.1 us -> 54.1 us (level)
    div x1 -> x0, local copies, waits for them, and re-layouts: 0.72 us -> none  [local(): return (received[None], (full / grad_scale)[None])]
    transpose x0 -> x1, local copies, waits for them, and re-layouts: none -> 0.72 us  [local(): jnp.transpose(full, (1, 0, 2, 3))]
where the time goes in v18:
time: 54.1 us; the launch traced here: 53.8 us
  starting transfers between devices  23.3 us (43%)
  waiting for transfers between devices  14.2 us (26%)
  Pallas kernels  6.46 us (12%)
  local copies, waits for them, and re-layouts  4.9 us (9%)
  other arithmetic  4.1 us (8%)
  between operations  0.84 us (2%)
    ppermute x6, starting transfers between devices, swapped(): return lax.ppermute(x, axis, [(i, i ^ 1 << bit) for i in range(n)])  16.2 us
    ppermute x6, waiting for transfers between devices, swapped(): return lax.ppermute(x, axis, [(i, i ^ 1 << bit) for i in range(n)])  9.13 us
    pallas_call x1, Pallas kernels, block_pass(): pl.pallas_call(functools.partial(block_kernel, compact, chunk), out_shape...  6.46 us
    ppermute x3, starting transfers between devices, shifted(): return lax.ppermute(x, axis, [(i, (i + k) % n) for i in range(n)])  5.08 us
    ppermute x3, waiting for transfers between devices, shifted(): return lax.ppermute(x, axis, [(i, (i + k) % n) for i in range(n)])  5.07 us
    ppermute x1, starting transfers between devices, passed_along(): return lax.ppermute(block, axis, route)  1.29 us
    scatter x1, local copies, waits for them, and re-layouts, local(): arrived = arrived.at[got_rows].set(got)  1.14 us
    add x1, other arithmetic, local(): held = keep + swapped(send, 'dp', 0)  1.12 us
  transfers between devices with their start and end apart: 11, of which 8 were waited for; matrix products, arithmetic and copies ran while one was open for 8% of the time, Pallas kernels for 0%

profile of v18, /device:TPU:0, one launch (start us, length us, event | category | flops | bytes accessed | tf_op | source)
XLA Modules:
  0.0 53.8 jit_solution(567179137710143105)
XLA Ops:
  0.6 0.7 %convert_element_type.53 = bf16[1,4,2]{1,2,0:T(2,128)(2,1)S(1)} convert(s32[1,4,2]{1,2,0:T(2,128)} %param.10) | non-fusion elementwise | flops 8 | bytes 48 | tf_op jit(solution)/shard_map/convert_element_type | solution.py:198
  1.3 0.1 copy.12
  1.4 0.1 convert_element_type.54
  1.5 0.9 %fusion.2 = bf16[528,128]{1,0:T(8,128)(2,1)S(1)} fusion(bf16[1,8]{1,0:T(2,128)(2,1)S(1)} %convert_element_type.54, bf16[512,128]{1,0:T(8,128)(2,1)} %bitcast.85), kind=kLoop, calls=%fused_computation.13 | loop fusion | flops 405504 | bytes 266256 | tf_op jit(solution)/shard_map/concatenate | solution.py:200
  2.4 0.7 %collective-permute-start = (bf16[528,128]{1,0:T(8,128)(2,1)S(1)}, bf16[528,128]{1,0:T(8,128)(2,1)S(1)}, u32[]{:S(2)}, u32[]{:S(2)}) collective-permute-start(bf16[528,128]{1,0:T(8,128)(2,1)S(1)} %fusion.2), channel_id=1, source_target_pairs={{0,0},{13,1},{10,2},{7,3},{4,4},{1,5},{14,6},{11,7},{8,8},{5,9},{2... | collective-permute-start | bytes 405512 | tf_op jit(solution)/shard_map/ppermute | solution.py:208
  3.1 12.0 %collective-permute-start.1 = (bf16[1,528,128]{2,1,0:T(8,128)(2,1)S(1)}, bf16[1,528,128]{2,1,0:T(8,128)(2,1)S(1)}, u32[]{:S(2)}, u32[]{:S(2)}) collective-permute-start(bf16[1,528,128]{2,1,0:T(8,128)(2,1)S(1)} %bitcast.74), channel_id=1, source_target_pairs={{0,2},{1,3},{2,0},{3,1},{4,6},{5,7},{6,4},{7,5},{8,10},{9,11},{10,... | collective-permute-start | bytes 405512 | tf_op jit(solution)/shard_map/ppermute | solution.py:25
  15.1 3.0 %collective-permute-done.1 = bf16[1,528,128]{2,1,0:T(8,128)(2,1)S(1)} collective-permute-done((bf16[1,528,128]{2,1,0:T(8,128)(2,1)S(1)}, bf16[1,528,128]{2,1,0:T(8,128)(2,1)S(1)}, u32[]{:S(2)}, u32[]{:S(2)}) %collective-permute-start.1) | collective-permute-done | bytes 135200 | tf_op jit(solution)/shard_map/ppermute | solution.py:25
  18.1 0.1 collective-permute-start.2
  18.2 1.5 %collective-permute-done.2 = bf16[2,1,528,128]{3,2,0,1:T(8,128)(2,1)S(1)} collective-permute-done((bf16[2,1,528,128]{3,2,0,1:T(8,128)(2,1)S(1)}, bf16[2,1,528,128]{3,2,0,1:T(8,128)(2,1)S(1)}, u32[]{:S(2)}, u32[]{:S(2)}) %collective-permute-start.2) | collective-permute-done | bytes 270368 | tf_op jit(solution)/shard_map/ppermute | solution.py:25
  19.8 0.1 reshape.408
  19.9 0.8 %slice_reduce_fusion = (s32[16]{0:T(128)}, s32[16]{0:T(128)}) fusion(s32[16,2]{1,0:T(8,128)S(1)} %reshape.408), kind=kLoop, calls=%fused_computation.27 | loop fusion | bytes 256 | tf_op jit(solution)/shard_map/slice | solution.py:220
  20.7 6.5 %shard_map.68 = (bf16[16,128,128]{2,1,0:T(8,128)(2,1)}, f32[16,2,32,128]{3,2,1,0:T(8,128)}, f32[16,2,32,128]{3,2,1,0:T(8,128)}) custom-call(s32[16]{0:T(128)} %get-tuple-element.21.rows_ref, s32[16]{0:T(128)} %get-tuple-element.20.cols_ref, s32[1]{0:T(128)} %bitcast.8.bit_ref, bf16[128,3584]{1,0:T(8,128)(2,1)} %bitcast.71, bf16[128,14336]{1,0:T(8,128)(2,1)} %bitcast.64, ...), custom_call_target="tpu_custom_call" | custom-call | flops 201326592 | bytes 3538944 | tf_op jit(solution)/shard_map/pallas_call | solution.py:132
  27.2 0.2 collective-permute-start.4
  27.4 1.9 %collective-permute-done.4 = f32[16,2,32,128]{3,2,1,0:T(8,128)S(1)} collective-permute-done((f32[16,2,32,128]{3,2,1,0:T(8,128)}, f32[16,2,32,128]{3,2,1,0:T(8,128)S(1)}, u32[]{:S(2)}, u32[]{:S(2)}) %collective-permute-start.4) | collective-permute-done | bytes 524320 | tf_op jit(solution)/shard_map/ppermute | solution.py:25
  29.3 1.1 %add.36 = f32[16,2,32,128]{3,2,1,0:T(8,128)S(1)} add(f32[16,2,32,128]{3,2,1,0:T(8,128)} %get-tuple-element.18, f32[16,2,32,128]{3,2,1,0:T(8,128)S(1)} %collective-permute-done.4) | non-fusion elementwise | flops 131072 | bytes 1572864 | tf_op jit(solution)/shard_map/add | solution.py:247
  30.5 2.1 %collective-permute-start.5 = (bf16[4,4,32,128]{3,2,1,0:T(8,128)(2,1)S(1)}, bf16[4,4,32,128]{3,2,1,0:T(8,128)(2,1)S(1)}, u32[]{:S(2)}, u32[]{:S(2)}) collective-permute-start(bf16[4,4,32,128]{3,2,1,0:T(8,128)(2,1)S(1)} %fusion.3), channel_id=1, source_target_pairs={{0,2},{1,3},{2,0},{3,1},{4,6},{5,7},{6,4},{7,5},{8,10},{9,11},{10,... | collective-permute-start | bytes 393224 | tf_op jit(solution)/shard_map/ppermute | solution.py:25
  32.6 1.3 %collective-permute-start.3 = (bf16[262160]{0:T(1024)(128)(2,1)S(1)}, bf16[262160]{0:T(1024)(128)(2,1)S(1)}, u32[]{:S(2)}, u32[]{:S(2)}) collective-permute-start(bf16[262160]{0:T(1024)(128)(2,1)S(1)} %pad_maximum_fusion), channel_id=1, source_target_pairs={{16,0},{17,1},{18,2},{19,3},{20,4},{21,5},{22,6},{23,7},{24,8},{25... | collective-permute-start | bytes 1572968 | tf_op jit(solution)/shard_map/ppermute | solution.py:15
  33.9 2.5 %collective-permute-done.5 = bf16[4,4,32,128]{3,2,1,0:T(8,128)(2,1)S(1)} collective-permute-done((bf16[4,4,32,128]{3,2,1,0:T(8,128)(2,1)S(1)}, bf16[4,4,32,128]{3,2,1,0:T(8,128)(2,1)S(1)}, u32[]{:S(2)}, u32[]{:S(2)}) %collective-permute-start.5) | collective-permute-done | bytes 131104 | tf_op jit(solution)/shard_map/ppermute | solution.py:25
  36.5 4.4 %collective-permute-start.6 = (bf16[4,32,128]{2,1,0:T(8,128)(2,1)S(1)}, bf16[4,32,128]{2,1,0:T(8,128)(2,1)S(1)}, u32[]{:S(2)}, u32[]{:S(2)}) collective-permute-start(bf16[4,32,128]{2,1,0:T(8,128)(2,1)S(1)} %get-tuple-element.24), channel_id=1, source_target_pairs={{0,12},{4,0},{8,4},{12,8},{1,13},{5,1},{9,5},{13,9},{2,14},{6,2},{... | collective-permute-start | bytes 98312 | tf_op jit(solution)/shard_map/ppermute | solution.py:20
  40.9 0.6 %collective-permute-start.8 = (bf16[4,32,128]{2,1,0:T(8,128)(2,1)S(1)}, bf16[4,32,128]{2,1,0:T(8,128)(2,1)S(1)}, u32[]{:S(2)}, u32[]{:S(2)}) collective-permute-start(bf16[4,32,128]{2,1,0:T(8,128)(2,1)S(1)} %get-tuple-element.25), channel_id=1, source_target_pairs={{0,4},{4,8},{8,12},{12,0},{1,5},{5,9},{9,13},{13,1},{2,6},{6,10},{... | collective-permute-start | bytes 98312 | tf_op jit(solution)/shard_map/ppermute | solution.py:20
  41.6 0.9 %collective-permute-done.6 = bf16[4,32,128]{2,1,0:T(8,128)(2,1)S(1)} collective-permute-done((bf16[4,32,128]{2,1,0:T(8,128)(2,1)S(1)}, bf16[4,32,128]{2,1,0:T(8,128)(2,1)S(1)}, u32[]{:S(2)}, u32[]{:S(2)}) %collective-permute-start.6) | collective-permute-done | bytes 32800 | tf_op jit(solution)/shard_map/ppermute | solution.py:20
  42.5 3.2 %collective-permute-done.7 = bf16[4,32,128]{2,1,0:T(8,128)(2,1)S(1)} collective-permute-done((bf16[4,32,128]{2,1,0:T(8,128)(2,1)S(1)}, bf16[4,32,128]{2,1,0:T(8,128)(2,1)S(1)}, u32[]{:S(2)}, u32[]{:S(2)}) %collective-permute-start.7) | collective-permute-done | bytes 32800 | tf_op jit(solution)/shard_map/ppermute | solution.py:20
  45.7 0.9 %collective-permute-done.8 = bf16[4,32,128]{2,1,0:T(8,128)(2,1)S(1)} collective-permute-done((bf16[4,32,128]{2,1,0:T(8,128)(2,1)S(1)}, bf16[4,32,128]{2,1,0:T(8,128)(2,1)S(1)}, u32[]{:S(2)}, u32[]{:S(2)}) %collective-permute-start.8) | collective-permute-done | bytes 32800 | tf_op jit(solution)/shard_map/ppermute | solution.py:20
  46.7 1.8 %collective-permute-start.9 = (f32[4,32,128]{2,1,0:T(8,128)S(1)}, f32[4,32,128]{2,1,0:T(8,128)S(1)}, u32[]{:S(2)}, u32[]{:S(2)}) collective-permute-start(f32[4,32,128]{2,1,0:T(8,128)S(1)} %fusion.8), channel_id=1, source_target_pairs={{0,2},{1,3},{2,0},{3,1},{4,6},{5,7},{6,4},{7,5},{8,10},{9,11},{10,... | collective-permute-start | bytes 196616 | tf_op jit(solution)/shard_map/ppermute | solution.py:25
  48.5 0.2 broadcast_in_dim.21
  48.7 1.1 %scatter_fusion = bf16[28,128,128]{2,1,0:T(8,128)(2,1)S(1)} fusion(bf16[28,128,128]{2,1,0:T(8,128)(2,1)S(1)} %broadcast_in_dim.21, s32[16]{0:T(128)S(1)} %compare_select_fusion, bf16[16,128,128]{2,1,0:T(8,128)(2,1)S(1)} %bitcast.67), kind=kCustom, calls=%fused_computation.1 | custom fusion | bytes 1572928 | tf_op jit(solution)/shard_map/scatter | solution.py:239
  49.9 0.6 %copy.13 = bf16[128,28,128]{2,1,0:T(8,128)(2,1)S(1)} copy(bf16[128,28,128]{2,0,1:T(8,128)(2,1)S(1)} %bitcast.63) | data formatting | bytes 1835008 | tf_op jit(solution)/shard_map/transpose | solution.py:242
  50.5 0.5 reshape.405
  51.0 0.6 %gather_fusion = bf16[4,32,3584]{2,1,0:T(8,128)(2,1)S(1)} fusion(bf16[4,32,3584]{2,1,0:T(8,128)(2,1)S(1)} %reshape.405, s32[1024]{0:T(1024)S(1)} %pad_clamp_fusion), kind=kCustom, calls=%fused_computation | custom fusion | bytes 1835024 | tf_op jit(solution)/shard_map/jit(_take)/gather | solution.py:245
  51.7 1.1 %bitcast_select_fusion = bf16[1,4,32,3584]{3,2,1,0:T(8,128)(2,1)} fusion(bf16[4,32,3584]{2,1,0:T(8,128)(2,1)S(1)} %gather_fusion, pred[4]{0:T(512)(128)(4,1)S(1)} %compare_and_fusion), kind=kLoop, calls=%fused_computation.2 | loop fusion | flops 458752 | bytes 1835012 | tf_op jit(solution)/shard_map/jit(_take)/select_n | solution.py:245
  52.8 0.2 collective-permute-done.10
  53.1 0.7 %copy.17 = f32[4,4,32,128]{3,2,1,0:T(8,128)} copy(f32[4,4,32,128]{3,2,0,1:T(8,128)S(1)} %bitcast.70) | data formatting | bytes 524288 | tf_op jit(solution)/shard_map/transpose | solution.py:261
  (31 shorter events, 0.5 us)
Async XLA Ops:
  2.4 0.7 %collective-permute-start = (bf16[528,128]{1,0:T(8,128)(2,1)S(1)}, bf16[528,128]{1,0:T(8,128)(2,1)S(1)}, u32[]{:S(2)}, u32[]{:S(2)}) collective-permute-start(bf16[528,128]{1,0:T(8,128)(2,1)S(1)} %fusion.2), channel_id=1, source_target_pairs={{0,0},{13,1},{10,2},{7,3},{4,4},{1,5},{14,6},{11,7},{8,8},{5,9},{2... | collective-permute-start | bytes 405512 | tf_op jit(solution)/shard_map/ppermute | solution.py:208
  3.1 15.0 %collective-permute-start.1 = (bf16[1,528,128]{2,1,0:T(8,128)(2,1)S(1)}, bf16[1,528,128]{2,1,0:T(8,128)(2,1)S(1)}, u32[]{:S(2)}, u32[]{:S(2)}) collective-permute-start(bf16[1,528,128]{2,1,0:T(8,128)(2,1)S(1)} %bitcast.74), channel_id=1, source_target_pairs={{0,2},{1,3},{2,0},{3,1},{4,6},{5,7},{6,4},{7,5},{8,10},{9,11},{10,... | collective-permute-start | bytes 405512 | tf_op jit(solution)/shard_map/ppermute | solution.py:25
  18.1 1.6 %collective-permute-start.2 = (bf16[2,1,528,128]{3,2,0,1:T(8,128)(2,1)S(1)}, bf16[2,1,528,128]{3,2,0,1:T(8,128)(2,1)S(1)}, u32[]{:S(2)}, u32[]{:S(2)}) collective-permute-start(bf16[2,1,528,128]{3,2,0,1:T(8,128)(2,1)S(1)} %maximum_select_fusion.2), channel_id=1, source_target_pairs={{0,1},{1,0},{2,3},{3,2},{4,5},{5,4},{6,7},{7,6},{8,9},{9,8},{10,11... | collective-permute-start | bytes 811016 | tf_op jit(solution)/shard_map/ppermute | solution.py:25
  19.8 0.9 %copy-start = (bf16[2,2,1,528,128]{4,3,0,1,2:T(8,128)(2,1)}, bf16[2,2,1,528,128]{4,3,0,1,2:T(8,128)(2,1)S(1)}, u32[]{:S(2)}) copy-start(bf16[2,2,1,528,128]{4,3,0,1,2:T(8,128)(2,1)S(1)} %maximum_select_fusion) | copy-start | bytes 1622020
  20.7 6.7 %copy-start.3 = (s32[4]{0:T(128)S(1)}, s32[4]{0:T(128)}, u32[]{:S(2)}) copy-start(s32[4]{0:T(128)} %param.11) | copy-start | bytes 52
  20.7 6.7 %copy-start.2 = (s32[16]{0:T(128)S(1)}, s32[16]{0:T(128)}, u32[]{:S(2)}) copy-start(s32[16]{0:T(128)} %get-tuple-element.21.rows_ref) | copy-start | bytes 196
  27.1 5.4 %copy-start.1 = (bf16[16,128,128]{2,1,0:T(8,128)(2,1)S(1)}, bf16[16,128,128]{2,1,0:T(8,128)(2,1)}, u32[]{:S(2)}) copy-start(bf16[16,128,128]{2,1,0:T(8,128)(2,1)} %get-tuple-element.17) | copy-start | bytes 1572868
  27.2 2.2 %collective-permute-start.4 = (f32[16,2,32,128]{3,2,1,0:T(8,128)}, f32[16,2,32,128]{3,2,1,0:T(8,128)S(1)}, u32[]{:S(2)}, u32[]{:S(2)}) collective-permute-start(f32[16,2,32,128]{3,2,1,0:T(8,128)} %get-tuple-element.19), channel_id=1, source_target_pairs={{0,1},{1,0},{2,3},{3,2},{4,5},{5,4},{6,7},{7,6},{8,9},{9,8},{10,11... | collective-permute-start | bytes 1572872 | tf_op jit(solution)/shard_map/ppermute | solution.py:25
  30.5 5.9 %collective-permute-start.5 = (bf16[4,4,32,128]{3,2,1,0:T(8,128)(2,1)S(1)}, bf16[4,4,32,128]{3,2,1,0:T(8,128)(2,1)S(1)}, u32[]{:S(2)}, u32[]{:S(2)}) collective-permute-start(bf16[4,4,32,128]{3,2,1,0:T(8,128)(2,1)S(1)} %fusion.3), channel_id=1, source_target_pairs={{0,2},{1,3},{2,0},{3,1},{4,6},{5,7},{6,4},{7,5},{8,10},{9,11},{10,... | collective-permute-start | bytes 393224 | tf_op jit(solution)/shard_map/ppermute | solution.py:25
  32.6 15.8 %collective-permute-start.3 = (bf16[262160]{0:T(1024)(128)(2,1)S(1)}, bf16[262160]{0:T(1024)(128)(2,1)S(1)}, u32[]{:S(2)}, u32[]{:S(2)}) collective-permute-start(bf16[262160]{0:T(1024)(128)(2,1)S(1)} %pad_maximum_fusion), channel_id=1, source_target_pairs={{16,0},{17,1},{18,2},{19,3},{20,4},{21,5},{22,6},{23,7},{24,8},{25... | collective-permute-start | bytes 1572968 | tf_op jit(solution)/shard_map/ppermute | solution.py:15
  36.5 6.0 %collective-permute-start.6 = (bf16[4,32,128]{2,1,0:T(8,128)(2,1)S(1)}, bf16[4,32,128]{2,1,0:T(8,128)(2,1)S(1)}, u32[]{:S(2)}, u32[]{:S(2)}) collective-permute-start(bf16[4,32,128]{2,1,0:T(8,128)(2,1)S(1)} %get-tuple-element.24), channel_id=1, source_target_pairs={{0,12},{4,0},{8,4},{12,8},{1,13},{5,1},{9,5},{13,9},{2,14},{6,2},{... | collective-permute-start | bytes 98312 | tf_op jit(solution)/shard_map/ppermute | solution.py:20
  40.9 4.8 %collective-permute-start.7 = (bf16[4,32,128]{2,1,0:T(8,128)(2,1)S(1)}, bf16[4,32,128]{2,1,0:T(8,128)(2,1)S(1)}, u32[]{:S(2)}, u32[]{:S(2)}) collective-permute-start(bf16[4,32,128]{2,1,0:T(8,128)(2,1)S(1)} %get-tuple-element.26), channel_id=1, source_target_pairs={{0,8},{4,12},{8,0},{12,4},{1,9},{5,13},{9,1},{13,5},{2,10},{6,14},... | collective-permute-start | bytes 98312 | tf_op jit(solution)/shard_map/ppermute | solution.py:20
  40.9 5.7 %collective-permute-start.8 = (bf16[4,32,128]{2,1,0:T(8,128)(2,1)S(1)}, bf16[4,32,128]{2,1,0:T(8,128)(2,1)S(1)}, u32[]{:S(2)}, u32[]{:S(2)}) collective-permute-start(bf16[4,32,128]{2,1,0:T(8,128)(2,1)S(1)} %get-tuple-element.25), channel_id=1, source_target_pairs={{0,4},{4,8},{8,12},{12,0},{1,5},{5,9},{9,13},{13,1},{2,6},{6,10},{... | collective-permute-start | bytes 98312 | tf_op jit(solution)/shard_map/ppermute | solution.py:20
  46.7 4.9 %collective-permute-start.9 = (f32[4,32,128]{2,1,0:T(8,128)S(1)}, f32[4,32,128]{2,1,0:T(8,128)S(1)}, u32[]{:S(2)}, u32[]{:S(2)}) collective-permute-start(f32[4,32,128]{2,1,0:T(8,128)S(1)} %fusion.8), channel_id=1, source_target_pairs={{0,2},{1,3},{2,0},{3,1},{4,6},{5,7},{6,4},{7,5},{8,10},{9,11},{10,... | collective-permute-start | bytes 196616 | tf_op jit(solution)/shard_map/ppermute | solution.py:25
  51.6 1.4 %collective-permute-start.10 = (f32[2,4,32,128]{3,2,1,0:T(8,128)S(1)}, f32[2,4,32,128]{3,2,1,0:T(8,128)S(1)}, u32[]{:S(2)}, u32[]{:S(2)}) collective-permute-start(f32[2,4,32,128]{3,2,1,0:T(8,128)S(1)} %maximum_select_fusion.4), channel_id=1, source_target_pairs={{0,1},{1,0},{2,3},{3,2},{4,5},{5,4},{6,7},{7,6},{8,9},{9,8},{10,11... | collective-permute-start | bytes 393224 | tf_op jit(solution)/shard_map/ppermute | solution.py:25

commit v19 on v16

--- a/solution.py
+++ b/solution.py
@@ -255,9 +255,15 @@
     owned = held[0]
     for k in range(1, n_fsdp):
         owned = owned + shifted(held[k].astype(jnp.bfloat16), "fsdp", -k).astype(jnp.float32)
-    full = butterfly_gather(owned, "dp", list(reversed(range(dp_bits))))
-    full = full.reshape((n_dp, blocks_dev, chunk, block_size))
-    full = jnp.transpose(full, (1, 0, 2, 3)).reshape(blocks_dev, block_size, block_size)
+    full = owned
+    for level, bit in enumerate(reversed(range(dp_bits))):
+        other = swapped(full, "dp", bit)
+        mine_low = ((me_dp >> bit) & 1) == 0
+        at = 1 + level
+        full = jnp.where(
+            mine_low, jnp.stack([full, other], axis=at), jnp.stack([other, full], axis=at)
+        )
+    full = full.reshape(blocks_dev, block_size, block_size)
     grad_scale = jnp.sqrt(jnp.float32(tok_rows * n_fsdp * n_dp))
     return (received[None], (full / grad_scale)[None])
 

time: 54.1 us -> 54.1 us (level)
  no operation moved by 1% of the time
where the time goes in v19:
time: 54.1 us; the launch traced here: 53.8 us
  starting transfers between devices  23.3 us (43%)
  waiting for transfers between devices  14.2 us (26%)
  Pallas kernels  6.47 us (12%)
  local copies, waits for them, and re-layouts  4.9 us (9%)
  other arithmetic  4.1 us (8%)
  between operations  0.85 us (2%)
    ppermute x6, starting transfers between devices, swapped(): return lax.ppermute(x, axis, [(i, i ^ 1 << bit) for i in range(n)])  16.2 us
    ppermute x6, waiting for transfers between devices, swapped(): return lax.ppermute(x, axis, [(i, i ^ 1 << bit) for i in range(n)])  9.13 us
    pallas_call x1, Pallas kernels, block_pass(): pl.pallas_call(functools.partial(block_kernel, compact, chunk), out_shape...  6.47 us
    ppermute x3, starting transfers between devices, shifted(): return lax.ppermute(x, axis, [(i, (i + k) % n) for i in range(n)])  5.08 us
    ppermute x3, waiting for transfers between devices, shifted(): return lax.ppermute(x, axis, [(i, (i + k) % n) for i in range(n)])  5.07 us
    ppermute x1, starting transfers between devices, passed_along(): return lax.ppermute(block, axis, route)  1.29 us
    scatter x1, local copies, waits for them, and re-layouts, local(): arrived = arrived.at[got_rows].set(got)  1.15 us
    add x1, other arithmetic, local(): held = keep + swapped(send, 'dp', 0)  1.12 us
  transfers between devices with their start and end apart: 11, of which 8 were waited for; matrix products, arithmetic and copies ran while one was open for 8% of the time, Pallas kernels for 0%

profile of v19, /device:TPU:0, one launch (start us, length us, event | category | flops | bytes accessed | tf_op | source)
XLA Modules:
  0.0 53.8 jit_solution(16753120700554493987)
XLA Ops:
  0.6 0.7 %convert_element_type.53 = bf16[1,4,2]{1,2,0:T(2,128)(2,1)S(1)} convert(s32[1,4,2]{1,2,0:T(2,128)} %param.10) | non-fusion elementwise | flops 8 | bytes 48 | tf_op jit(solution)/shard_map/convert_element_type | solution.py:198
  1.3 0.1 copy.11
  1.4 0.1 convert_element_type.54
  1.5 0.9 %fusion.3 = bf16[528,128]{1,0:T(8,128)(2,1)S(1)} fusion(bf16[1,8]{1,0:T(2,128)(2,1)S(1)} %convert_element_type.54, bf16[512,128]{1,0:T(8,128)(2,1)} %bitcast.65), kind=kLoop, calls=%fused_computation.14 | loop fusion | flops 405504 | bytes 266256 | tf_op jit(solution)/shard_map/concatenate | solution.py:200
  2.4 0.7 %collective-permute-start = (bf16[528,128]{1,0:T(8,128)(2,1)S(1)}, bf16[528,128]{1,0:T(8,128)(2,1)S(1)}, u32[]{:S(2)}, u32[]{:S(2)}) collective-permute-start(bf16[528,128]{1,0:T(8,128)(2,1)S(1)} %fusion.3), channel_id=1, source_target_pairs={{0,0},{13,1},{10,2},{7,3},{4,4},{1,5},{14,6},{11,7},{8,8},{5,9},{2... | collective-permute-start | bytes 405512 | tf_op jit(solution)/shard_map/ppermute | solution.py:208
  3.1 12.0 %collective-permute-start.1 = (bf16[1,528,128]{2,1,0:T(8,128)(2,1)S(1)}, bf16[1,528,128]{2,1,0:T(8,128)(2,1)S(1)}, u32[]{:S(2)}, u32[]{:S(2)}) collective-permute-start(bf16[1,528,128]{2,1,0:T(8,128)(2,1)S(1)} %bitcast.54), channel_id=1, source_target_pairs={{0,2},{1,3},{2,0},{3,1},{4,6},{5,7},{6,4},{7,5},{8,10},{9,11},{10,... | collective-permute-start | bytes 405512 | tf_op jit(solution)/shard_map/ppermute | solution.py:25
  15.1 3.0 %collective-permute-done.1 = bf16[1,528,128]{2,1,0:T(8,128)(2,1)S(1)} collective-permute-done((bf16[1,528,128]{2,1,0:T(8,128)(2,1)S(1)}, bf16[1,528,128]{2,1,0:T(8,128)(2,1)S(1)}, u32[]{:S(2)}, u32[]{:S(2)}) %collective-permute-start.1) | collective-permute-done | bytes 135200 | tf_op jit(solution)/shard_map/ppermute | solution.py:25
  18.2 1.5 %collective-permute-done.2 = bf16[2,1,528,128]{3,2,0,1:T(8,128)(2,1)S(1)} collective-permute-done((bf16[2,1,528,128]{3,2,0,1:T(8,128)(2,1)S(1)}, bf16[2,1,528,128]{3,2,0,1:T(8,128)(2,1)S(1)}, u32[]{:S(2)}, u32[]{:S(2)}) %collective-permute-start.2) | collective-permute-done | bytes 270368 | tf_op jit(solution)/shard_map/ppermute | solution.py:25
  19.8 0.1 reshape.431
  19.9 0.8 %slice_reduce_fusion = (s32[16]{0:T(128)}, s32[16]{0:T(128)}) fusion(s32[16,2]{1,0:T(8,128)S(1)} %reshape.431), kind=kLoop, calls=%fused_computation.25 | loop fusion | bytes 256 | tf_op jit(solution)/shard_map/slice | solution.py:220
  20.7 6.5 %shard_map.68 = (bf16[16,128,128]{2,1,0:T(8,128)(2,1)}, f32[16,2,32,128]{3,2,1,0:T(8,128)}, f32[16,2,32,128]{3,2,1,0:T(8,128)}) custom-call(s32[16]{0:T(128)} %get-tuple-element.21.rows_ref, s32[16]{0:T(128)} %get-tuple-element.20.cols_ref, s32[1]{0:T(128)} %bitcast.8.bit_ref, bf16[128,3584]{1,0:T(8,128)(2,1)} %bitcast.51, bf16[128,14336]{1,0:T(8,128)(2,1)} %bitcast.45, ...), custom_call_target="tpu_custom_call" | custom-call | flops 201326592 | bytes 3538944 | tf_op jit(solution)/shard_map/pallas_call | solution.py:132
  27.2 0.2 collective-permute-start.4
  27.4 1.9 %collective-permute-done.4 = f32[16,2,32,128]{3,2,1,0:T(8,128)S(1)} collective-permute-done((f32[16,2,32,128]{3,2,1,0:T(8,128)}, f32[16,2,32,128]{3,2,1,0:T(8,128)S(1)}, u32[]{:S(2)}, u32[]{:S(2)}) %collective-permute-start.4) | collective-permute-done | bytes 524320 | tf_op jit(solution)/shard_map/ppermute | solution.py:25
  29.4 1.1 %add.36 = f32[16,2,32,128]{3,2,1,0:T(8,128)S(1)} add(f32[16,2,32,128]{3,2,1,0:T(8,128)} %get-tuple-element.18, f32[16,2,32,128]{3,2,1,0:T(8,128)S(1)} %collective-permute-done.4) | non-fusion elementwise | flops 131072 | bytes 1572864 | tf_op jit(solution)/shard_map/add | solution.py:247
  30.5 2.1 %collective-permute-start.5 = (bf16[4,4,32,128]{3,2,1,0:T(8,128)(2,1)S(1)}, bf16[4,4,32,128]{3,2,1,0:T(8,128)(2,1)S(1)}, u32[]{:S(2)}, u32[]{:S(2)}) collective-permute-start(bf16[4,4,32,128]{3,2,1,0:T(8,128)(2,1)S(1)} %fusion.4), channel_id=1, source_target_pairs={{0,2},{1,3},{2,0},{3,1},{4,6},{5,7},{6,4},{7,5},{8,10},{9,11},{10,... | collective-permute-start | bytes 393224 | tf_op jit(solution)/shard_map/ppermute | solution.py:25
  32.6 1.3 %collective-permute-start.3 = (bf16[262160]{0:T(1024)(128)(2,1)S(1)}, bf16[262160]{0:T(1024)(128)(2,1)S(1)}, u32[]{:S(2)}, u32[]{:S(2)}) collective-permute-start(bf16[262160]{0:T(1024)(128)(2,1)S(1)} %pad_maximum_fusion), channel_id=1, source_target_pairs={{16,0},{17,1},{18,2},{19,3},{20,4},{21,5},{22,6},{23,7},{24,8},{25... | collective-permute-start | bytes 1572968 | tf_op jit(solution)/shard_map/ppermute | solution.py:15
  33.9 2.5 %collective-permute-done.5 = bf16[4,4,32,128]{3,2,1,0:T(8,128)(2,1)S(1)} collective-permute-done((bf16[4,4,32,128]{3,2,1,0:T(8,128)(2,1)S(1)}, bf16[4,4,32,128]{3,2,1,0:T(8,128)(2,1)S(1)}, u32[]{:S(2)}, u32[]{:S(2)}) %collective-permute-start.5) | collective-permute-done | bytes 131104 | tf_op jit(solution)/shard_map/ppermute | solution.py:25
  36.5 4.4 %collective-permute-start.6 = (bf16[4,32,128]{2,1,0:T(8,128)(2,1)S(1)}, bf16[4,32,128]{2,1,0:T(8,128)(2,1)S(1)}, u32[]{:S(2)}, u32[]{:S(2)}) collective-permute-start(bf16[4,32,128]{2,1,0:T(8,128)(2,1)S(1)} %get-tuple-element.24), channel_id=1, source_target_pairs={{0,12},{4,0},{8,4},{12,8},{1,13},{5,1},{9,5},{13,9},{2,14},{6,2},{... | collective-permute-start | bytes 98312 | tf_op jit(solution)/shard_map/ppermute | solution.py:20
  40.9 0.6 %collective-permute-start.8 = (bf16[4,32,128]{2,1,0:T(8,128)(2,1)S(1)}, bf16[4,32,128]{2,1,0:T(8,128)(2,1)S(1)}, u32[]{:S(2)}, u32[]{:S(2)}) collective-permute-start(bf16[4,32,128]{2,1,0:T(8,128)(2,1)S(1)} %get-tuple-element.25), channel_id=1, source_target_pairs={{0,4},{4,8},{8,12},{12,0},{1,5},{5,9},{9,13},{13,1},{2,6},{6,10},{... | collective-permute-start | bytes 98312 | tf_op jit(solution)/shard_map/ppermute | solution.py:20
  41.6 0.9 %collective-permute-done.6 = bf16[4,32,128]{2,1,0:T(8,128)(2,1)S(1)} collective-permute-done((bf16[4,32,128]{2,1,0:T(8,128)(2,1)S(1)}, bf16[4,32,128]{2,1,0:T(8,128)(2,1)S(1)}, u32[]{:S(2)}, u32[]{:S(2)}) %collective-permute-start.6) | collective-permute-done | bytes 32800 | tf_op jit(solution)/shard_map/ppermute | solution.py:20
  42.5 3.2 %collective-permute-done.7 = bf16[4,32,128]{2,1,0:T(8,128)(2,1)S(1)} collective-permute-done((bf16[4,32,128]{2,1,0:T(8,128)(2,1)S(1)}, bf16[4,32,128]{2,1,0:T(8,128)(2,1)S(1)}, u32[]{:S(2)}, u32[]{:S(2)}) %collective-permute-start.7) | collective-permute-done | bytes 32800 | tf_op jit(solution)/shard_map/ppermute | solution.py:20
  45.7 0.9 %collective-permute-done.8 = bf16[4,32,128]{2,1,0:T(8,128)(2,1)S(1)} collective-permute-done((bf16[4,32,128]{2,1,0:T(8,128)(2,1)S(1)}, bf16[4,32,128]{2,1,0:T(8,128)(2,1)S(1)}, u32[]{:S(2)}, u32[]{:S(2)}) %collective-permute-start.8) | collective-permute-done | bytes 32800 | tf_op jit(solution)/shard_map/ppermute | solution.py:20
  46.7 1.8 %collective-permute-start.9 = (f32[4,32,128]{2,1,0:T(8,128)S(1)}, f32[4,32,128]{2,1,0:T(8,128)S(1)}, u32[]{:S(2)}, u32[]{:S(2)}) collective-permute-start(f32[4,32,128]{2,1,0:T(8,128)S(1)} %fusion.7), channel_id=1, source_target_pairs={{0,2},{1,3},{2,0},{3,1},{4,6},{5,7},{6,4},{7,5},{8,10},{9,11},{10,... | collective-permute-start | bytes 196616 | tf_op jit(solution)/shard_map/ppermute | solution.py:25
  48.5 0.2 broadcast_in_dim.22
  48.7 1.1 %scatter_fusion = bf16[28,128,128]{2,1,0:T(8,128)(2,1)S(1)} fusion(bf16[28,128,128]{2,1,0:T(8,128)(2,1)S(1)} %broadcast_in_dim.22, s32[16]{0:T(128)S(1)} %compare_select_fusion, bf16[16,128,128]{2,1,0:T(8,128)(2,1)S(1)} %bitcast.48), kind=kCustom, calls=%fused_computation.1 | custom fusion | bytes 1572928 | tf_op jit(solution)/shard_map/scatter | solution.py:239
  49.9 0.6 %copy.12 = bf16[128,28,128]{2,1,0:T(8,128)(2,1)S(1)} copy(bf16[128,28,128]{2,0,1:T(8,128)(2,1)S(1)} %bitcast.44) | data formatting | bytes 1835008 | tf_op jit(solution)/shard_map/transpose | solution.py:242
  50.5 0.5 reshape.429
  51.0 0.6 %gather_fusion = bf16[4,32,3584]{2,1,0:T(8,128)(2,1)S(1)} fusion(bf16[4,32,3584]{2,1,0:T(8,128)(2,1)S(1)} %reshape.429, s32[1024]{0:T(1024)S(1)} %pad_clamp_fusion), kind=kCustom, calls=%fused_computation | custom fusion | bytes 1835024 | tf_op jit(solution)/shard_map/jit(_take)/gather | solution.py:245
  51.6 0.1 collective-permute-start.10
  51.7 1.1 %bitcast_select_fusion = bf16[1,4,32,3584]{3,2,1,0:T(8,128)(2,1)} fusion(bf16[4,32,3584]{2,1,0:T(8,128)(2,1)S(1)} %gather_fusion, pred[4]{0:T(512)(128)(4,1)S(1)} %compare_and_fusion), kind=kLoop, calls=%fused_computation.2 | loop fusion | flops 458752 | bytes 1835012 | tf_op jit(solution)/shard_map/jit(_take)/select_n | solution.py:245
  52.8 0.2 collective-permute-done.10
  53.1 0.7 %copy.13 = f32[4,2,2,32,128]{4,3,2,1,0:T(8,128)} copy(f32[4,2,2,32,128]{4,3,0,1,2:T(8,128)S(1)} %fusion.2) | data formatting | bytes 524288 | tf_op jit(solution)/shard_map/div | solution.py:268
  (31 shorter events, 0.5 us)
Async XLA Ops:
  2.4 0.7 %collective-permute-start = (bf16[528,128]{1,0:T(8,128)(2,1)S(1)}, bf16[528,128]{1,0:T(8,128)(2,1)S(1)}, u32[]{:S(2)}, u32[]{:S(2)}) collective-permute-start(bf16[528,128]{1,0:T(8,128)(2,1)S(1)} %fusion.3), channel_id=1, source_target_pairs={{0,0},{13,1},{10,2},{7,3},{4,4},{1,5},{14,6},{11,7},{8,8},{5,9},{2... | collective-permute-start | bytes 405512 | tf_op jit(solution)/shard_map/ppermute | solution.py:208
  3.1 15.0 %collective-permute-start.1 = (bf16[1,528,128]{2,1,0:T(8,128)(2,1)S(1)}, bf16[1,528,128]{2,1,0:T(8,128)(2,1)S(1)}, u32[]{:S(2)}, u32[]{:S(2)}) collective-permute-start(bf16[1,528,128]{2,1,0:T(8,128)(2,1)S(1)} %bitcast.54), channel_id=1, source_target_pairs={{0,2},{1,3},{2,0},{3,1},{4,6},{5,7},{6,4},{7,5},{8,10},{9,11},{10,... | collective-permute-start | bytes 405512 | tf_op jit(solution)/shard_map/ppermute | solution.py:25
  18.1 1.6 %collective-permute-start.2 = (bf16[2,1,528,128]{3,2,0,1:T(8,128)(2,1)S(1)}, bf16[2,1,528,128]{3,2,0,1:T(8,128)(2,1)S(1)}, u32[]{:S(2)}, u32[]{:S(2)}) collective-permute-start(bf16[2,1,528,128]{3,2,0,1:T(8,128)(2,1)S(1)} %maximum_select_fusion.2), channel_id=1, source_target_pairs={{0,1},{1,0},{2,3},{3,2},{4,5},{5,4},{6,7},{7,6},{8,9},{9,8},{10,11... | collective-permute-start | bytes 811016 | tf_op jit(solution)/shard_map/ppermute | solution.py:25
  19.8 0.9 %copy-start = (bf16[2,2,1,528,128]{4,3,0,1,2:T(8,128)(2,1)}, bf16[2,2,1,528,128]{4,3,0,1,2:T(8,128)(2,1)S(1)}, u32[]{:S(2)}) copy-start(bf16[2,2,1,528,128]{4,3,0,1,2:T(8,128)(2,1)S(1)} %maximum_select_fusion) | copy-start | bytes 1622020
  20.7 6.7 %copy-start.3 = (s32[4]{0:T(128)S(1)}, s32[4]{0:T(128)}, u32[]{:S(2)}) copy-start(s32[4]{0:T(128)} %param.11) | copy-start | bytes 52
  20.7 6.7 %copy-start.2 = (s32[16]{0:T(128)S(1)}, s32[16]{0:T(128)}, u32[]{:S(2)}) copy-start(s32[16]{0:T(128)} %get-tuple-element.21.rows_ref) | copy-start | bytes 196
  27.2 5.4 %copy-start.1 = (bf16[16,128,128]{2,1,0:T(8,128)(2,1)S(1)}, bf16[16,128,128]{2,1,0:T(8,128)(2,1)}, u32[]{:S(2)}) copy-start(bf16[16,128,128]{2,1,0:T(8,128)(2,1)} %get-tuple-element.17) | copy-start | bytes 1572868
  27.2 2.2 %collective-permute-start.4 = (f32[16,2,32,128]{3,2,1,0:T(8,128)}, f32[16,2,32,128]{3,2,1,0:T(8,128)S(1)}, u32[]{:S(2)}, u32[]{:S(2)}) collective-permute-start(f32[16,2,32,128]{3,2,1,0:T(8,128)} %get-tuple-element.19), channel_id=1, source_target_pairs={{0,1},{1,0},{2,3},{3,2},{4,5},{5,4},{6,7},{7,6},{8,9},{9,8},{10,11... | collective-permute-start | bytes 1572872 | tf_op jit(solution)/shard_map/ppermute | solution.py:25
  30.5 5.9 %collective-permute-start.5 = (bf16[4,4,32,128]{3,2,1,0:T(8,128)(2,1)S(1)}, bf16[4,4,32,128]{3,2,1,0:T(8,128)(2,1)S(1)}, u32[]{:S(2)}, u32[]{:S(2)}) collective-permute-start(bf16[4,4,32,128]{3,2,1,0:T(8,128)(2,1)S(1)} %fusion.4), channel_id=1, source_target_pairs={{0,2},{1,3},{2,0},{3,1},{4,6},{5,7},{6,4},{7,5},{8,10},{9,11},{10,... | collective-permute-start | bytes 393224 | tf_op jit(solution)/shard_map/ppermute | solution.py:25
  32.6 15.8 %collective-permute-start.3 = (bf16[262160]{0:T(1024)(128)(2,1)S(1)}, bf16[262160]{0:T(1024)(128)(2,1)S(1)}, u32[]{:S(2)}, u32[]{:S(2)}) collective-permute-start(bf16[262160]{0:T(1024)(128)(2,1)S(1)} %pad_maximum_fusion), channel_id=1, source_target_pairs={{16,0},{17,1},{18,2},{19,3},{20,4},{21,5},{22,6},{23,7},{24,8},{25... | collective-permute-start | bytes 1572968 | tf_op jit(solution)/shard_map/ppermute | solution.py:15
  36.5 6.0 %collective-permute-start.6 = (bf16[4,32,128]{2,1,0:T(8,128)(2,1)S(1)}, bf16[4,32,128]{2,1,0:T(8,128)(2,1)S(1)}, u32[]{:S(2)}, u32[]{:S(2)}) collective-permute-start(bf16[4,32,128]{2,1,0:T(8,128)(2,1)S(1)} %get-tuple-element.24), channel_id=1, source_target_pairs={{0,12},{4,0},{8,4},{12,8},{1,13},{5,1},{9,5},{13,9},{2,14},{6,2},{... | collective-permute-start | bytes 98312 | tf_op jit(solution)/shard_map/ppermute | solution.py:20
  40.9 4.8 %collective-permute-start.7 = (bf16[4,32,128]{2,1,0:T(8,128)(2,1)S(1)}, bf16[4,32,128]{2,1,0:T(8,128)(2,1)S(1)}, u32[]{:S(2)}, u32[]{:S(2)}) collective-permute-start(bf16[4,32,128]{2,1,0:T(8,128)(2,1)S(1)} %get-tuple-element.26), channel_id=1, source_target_pairs={{0,8},{4,12},{8,0},{12,4},{1,9},{5,13},{9,1},{13,5},{2,10},{6,14},... | collective-permute-start | bytes 98312 | tf_op jit(solution)/shard_map/ppermute | solution.py:20
  40.9 5.7 %collective-permute-start.8 = (bf16[4,32,128]{2,1,0:T(8,128)(2,1)S(1)}, bf16[4,32,128]{2,1,0:T(8,128)(2,1)S(1)}, u32[]{:S(2)}, u32[]{:S(2)}) collective-permute-start(bf16[4,32,128]{2,1,0:T(8,128)(2,1)S(1)} %get-tuple-element.25), channel_id=1, source_target_pairs={{0,4},{4,8},{8,12},{12,0},{1,5},{5,9},{9,13},{13,1},{2,6},{6,10},{... | collective-permute-start | bytes 98312 | tf_op jit(solution)/shard_map/ppermute | solution.py:20
  46.7 4.9 %collective-permute-start.9 = (f32[4,32,128]{2,1,0:T(8,128)S(1)}, f32[4,32,128]{2,1,0:T(8,128)S(1)}, u32[]{:S(2)}, u32[]{:S(2)}) collective-permute-start(f32[4,32,128]{2,1,0:T(8,128)S(1)} %fusion.7), channel_id=1, source_target_pairs={{0,2},{1,3},{2,0},{3,1},{4,6},{5,7},{6,4},{7,5},{8,10},{9,11},{10,... | collective-permute-start | bytes 196616 | tf_op jit(solution)/shard_map/ppermute | solution.py:25
  51.6 1.4 %collective-permute-start.10 = (f32[4,2,32,128]{3,2,0,1:T(8,128)S(1)}, f32[4,2,32,128]{3,2,0,1:T(8,128)S(1)}, u32[]{:S(2)}, u32[]{:S(2)}) collective-permute-start(f32[4,2,32,128]{3,2,0,1:T(8,128)S(1)} %maximum_select_fusion.5), channel_id=1, source_target_pairs={{0,1},{1,0},{2,3},{3,2},{4,5},{5,4},{6,7},{7,6},{8,9},{9,8},{10,11... | collective-permute-start | bytes 393224 | tf_op jit(solution)/shard_map/ppermute | solution.py:25
